TPU v7x, 32 devices: a whole 2x2x4 slice. The times are simulated.
32 devices in a mesh: rep: 2 (over y), grp: 4 (over z), sub: 4 (over x, core).
Axes of the slice: x: 2, y: 2, z: 4, core: 2. Of those that a mesh axis runs over, the one named last changes fastest.
Arguments:
- volume: bfloat16 [256, 8, 8, 128], P(None, ('rep', 'grp'), 'sub'), parts along dimension 1, may hold values from -6 to 6
- cotangent: bfloat16 [256, 8, 8, 128], P(None, ('rep', 'grp'), 'sub'), parts along dimension 1, may hold values from -6 to 6
- first_weight: bfloat16 [256, 256], replicated, may hold values from -0.375 to 0.375
- group_weight: bfloat16 [256, 8, 3, 3, 3], replicated, may hold values from -0.4375 to 0.4375
- third_weight: bfloat16 [256, 256], replicated, may hold values from -0.375 to 0.375
Outputs:
- block_output: bfloat16 [256, 8, 8, 128], P(None, ('rep', 'grp'), 'sub'), parts along dimension 1
- volume_grad: bfloat16 [256, 8, 8, 128], P(None, ('rep', 'grp'), 'sub'), parts along dimension 1
- first_grad: float32 [512, 256], P('rep'), parts along dimension 0
- group_grad: float32 [512, 8, 3, 3, 3], P(('rep', 'grp')), parts along dimension 0
- third_grad: float32 [512, 256], P('rep'), parts along dimension 0
There are 2 independent parts, one for each index of `rep`. A program takes and returns all parts, laid end to end along the dimension named above; an argument that names none is the same for every part. Nothing has to cross between parts.
All inputs are finite; a program needn't handle non-finite values.
Results may differ from a plain program's by a relative error of at most 0.0073.
Values may be sent and summed in bfloat16 or wider, within the bound.
No kernel may reach another device: no remote copies, remote signals or barrier semaphores. Data moves between devices by JAX's collectives and lax.ppermute only.
A program may use at most 64 MiB of HBM per device.

v0:
```python
import math

import jax
import jax.numpy as jnp
from jax import lax
from jax.sharding import PartitionSpec as P

GW = 8


def padded_2(block, sides, width):
    for axis, dim in sides:
        count = lax.axis_size(axis)
        forward = [(i, i + 1) for i in range(count - 1)]
        backward = [(target, source) for source, target in forward]
        low = lax.ppermute(
            lax.slice_in_dim(block, block.shape[dim] - width, None, axis=dim), axis, forward
        )
        high = lax.ppermute(lax.slice_in_dim(block, 0, width, axis=dim), axis, backward)
        block = jnp.concatenate([low, block, high], axis=dim)
    return block


def silu_slope(values):
    sigma = jax.nn.sigmoid(values)
    return sigma * (1.0 + values * (1.0 - sigma))


def dense_conv(source, kernel, depth_pad):
    padding = ((depth_pad, depth_pad), (0, 0), (1, 1))
    return lax.conv_general_dilated(
        source[None],
        kernel,
        (1, 1, 1),
        padding,
        dimension_numbers=("NCDHW", "OIDHW", "NCDHW"),
        preferred_element_type=jnp.float32,
    )[0]


def block_diagonal(kernel):
    rows = kernel.shape[0]
    tiled = jnp.tile(kernel, (1, rows // GW, 1, 1, 1))
    group_of = jnp.arange(rows) // GW
    mask = (group_of[:, None] == group_of[None, :]).astype(kernel.dtype)
    return tiled * mask[:, :, None, None, None]


def diagonal_blocks(dense):
    rows = dense.shape[1]
    groups = rows // GW
    shaped = dense.reshape(groups, GW, rows, *dense.shape[2:])
    group_of = jnp.arange(rows) // GW
    mask = (jnp.arange(groups)[:, None] == group_of[None, :]).astype(dense.dtype)
    picked = (shaped * mask[:, None, :, None, None, None]).sum(axis=0)
    return picked.transpose(1, 0, 2, 3, 4)


def weight_grad(padded, deltas):
    return lax.conv_general_dilated(
        padded[None],
        deltas[None],
        (1, 1, 1),
        "VALID",
        dimension_numbers=("CNDHW", "IODHW", "NCDHW"),
        preferred_element_type=jnp.float32,
    )


def per_device(volume, cotangent, first_weight, group_weight, third_weight):
    channels, depth, height, width = volume.shape
    flattened = volume.reshape(channels, -1)
    contract_lead = (((0,), (0,)), ((), ()))
    contract_tail = (((1,), (1,)), ((), ()))
    total_cells = depth * lax.axis_size("grp") * height * lax.axis_size("sub") * width
    factor = 1.0 / math.sqrt(total_cells)
    group_rows = channels // lax.axis_size("grp")
    first_pre = lax.dot_general(
        first_weight, flattened, contract_lead, preferred_element_type=jnp.float32
    )
    first_act = jax.nn.silu(first_pre).astype(jnp.bfloat16).reshape(volume.shape)
    own_kernel = lax.dynamic_slice_in_dim(
        group_weight, lax.axis_index("grp") * group_rows, group_rows, 0
    )
    dense_kernel = block_diagonal(own_kernel)
    gathered = lax.all_to_all(first_act, "grp", split_axis=0, concat_axis=1, tiled=True)
    padded_act = padded_2(gathered, (("sub", 2),), 1)
    group_pre = dense_conv(padded_act, dense_kernel, 1)
    group_act = jax.nn.silu(group_pre).astype(jnp.bfloat16)
    returned = lax.all_to_all(group_act, "grp", split_axis=1, concat_axis=0, tiled=True)
    act_flat = returned.reshape(channels, -1)
    summed = flattened.astype(jnp.float32) + lax.dot_general(
        third_weight, act_flat, contract_lead, preferred_element_type=jnp.float32
    )
    block_output = jax.nn.silu(summed).astype(jnp.bfloat16).reshape(volume.shape)
    third_delta = (cotangent.reshape(channels, -1).astype(jnp.float32) * silu_slope(summed)).astype(
        jnp.bfloat16
    )
    third_part = lax.dot_general(
        act_flat, third_delta, contract_tail, preferred_element_type=jnp.float32
    )
    third_grad = lax.psum(third_part, ("grp", "sub")) * factor
    hidden_grad = (
        jnp.dot(third_weight, third_delta, preferred_element_type=jnp.float32)
        .astype(jnp.bfloat16)
        .reshape(volume.shape)
    )
    arriving = lax.all_to_all(hidden_grad, "grp", split_axis=0, concat_axis=1, tiled=True)
    group_delta = (arriving.astype(jnp.float32) * silu_slope(group_pre)).astype(jnp.bfloat16)
    delta_rim = padded_2(group_delta, (("sub", 2),), 1)
    flipped = dense_kernel.transpose(1, 0, 2, 3, 4)[:, :, ::-1, ::-1, ::-1]
    inner_local = dense_conv(delta_rim, flipped, 1).astype(jnp.bfloat16)
    dense_grad = weight_grad(
        jnp.pad(padded_act, ((0, 0), (1, 1), (0, 0), (1, 1))), group_delta
    )
    kernel_part = diagonal_blocks(dense_grad)
    inner_grad = lax.all_to_all(inner_local, "grp", split_axis=1, concat_axis=0, tiled=True)
    group_grad = lax.psum(kernel_part, "sub") * factor
    first_delta = (
        inner_grad.reshape(channels, -1).astype(jnp.float32) * silu_slope(first_pre)
    ).astype(jnp.bfloat16)
    first_part = lax.dot_general(
        flattened, first_delta, contract_tail, preferred_element_type=jnp.float32
    )
    volume_grad = (
        (
            third_delta.astype(jnp.float32)
            + jnp.dot(first_weight, first_delta, preferred_element_type=jnp.float32)
        )
        .astype(jnp.bfloat16)
        .reshape(volume.shape)
    )
    first_grad = lax.psum(first_part, ("grp", "sub")) * factor
    return (block_output, volume_grad, first_grad, group_grad, third_grad)


def solution(mesh):
    in_specs = (
        P(None, ("rep", "grp"), "sub", None),
        P(None, ("rep", "grp"), "sub", None),
        P(),
        P(),
        P(),
    )
    out_specs = (
        P(None, ("rep", "grp"), "sub", None),
        P(None, ("rep", "grp"), "sub", None),
        P("rep", None),
        P(("rep", "grp"), None, None, None, None),
        P("rep", None),
    )
    return jax.shard_map(
        per_device, mesh=mesh, in_specs=in_specs, out_specs=out_specs, check_vma=False
    )
```

profile of v0, /device:TPU:0, one launch (start us, length us, event | category | flops | bytes accessed | tf_op | source)
XLA Modules:
  0.0 194.0 jit_solution(14904769792690059259)
XLA Ops:
  7.2 1.0 copy.70
  8.2 1.8 multiply_convert_fusion.2
  10.1 0.8 copy.71
  10.9 6.3 %all-to-all-start = ((bf16[256,1,2,128]{3,2,1,0:T(2,128)(2,1)}), bf16[256,1,2,128]{3,2,1,0:T(2,128)(2,1)S(1)}, u32[]{:S(2)}, u32[]{:S(2)}) async-start(bf16[256,1,2,128]{3,2,1,0:T(2,128)(2,1)} %copy.71), calls=%async_computation | async-start | bytes 262144 | tf_op jit(solution)/shard_map/all_to_all | solution.py:86
  17.3 6.0 %all-to-all-done = bf16[256,1,2,128]{3,2,1,0:T(2,128)(2,1)S(1)} async-done(((bf16[256,1,2,128]{3,2,1,0:T(2,128)(2,1)}), bf16[256,1,2,128]{3,2,1,0:T(2,128)(2,1)S(1)}, u32[]{:S(2)}, u32[]{:S(2)}) %all-to-all-start) | async-done | bytes 131104 | tf_op jit(solution)/shard_map/all_to_all | solution.py:86
  23.3 1.3 collective-permute-start
  24.6 1.3 collective-permute-start.1
  26.0 3.5 %collective-permute-done.1 = bf16[64,4,1,128]{3,0,1,2:T(8,128)(2,1)S(1)} collective-permute-done((bf16[64,4,1,128]{3,0,1,2:T(8,128)(2,1)S(1)}, bf16[64,4,1,128]{3,0,1,2:T(8,128)(2,1)S(1)}, u32[]{:S(2)}, u32[]{:S(2)}) %collective-permute-start.1) | collective-permute-done | bytes 65568 | tf_op jit(solution)/shard_map/ppermute | solution.py:19
  29.5 0.3 copy.107
  29.8 0.3 pad.5.clone
  30.2 0.3 copy-done.5
  30.5 1.2 add_multiply_fusion
  31.8 0.3 copy.76
  32.3 0.7 fusion.28
  33.0 3.3 %all-to-all-start.1 = ((bf16[64,4,2,128]{3,0,2,1:T(8,128)(2,1)}), bf16[64,4,2,128]{3,0,2,1:T(8,128)(2,1)S(1)}, u32[]{:S(2)}, u32[]{:S(2)}) async-start(bf16[64,4,2,128]{3,0,2,1:T(8,128)(2,1)} %fusion.28), calls=%async_computation.1 | async-start | bytes 262144 | tf_op jit(solution)/shard_map/all_to_all | solution.py:90
  36.4 0.8 copy.79
  37.2 0.3 copy.91
  37.7 0.2 pad_bitcast_fusion
  38.0 1.7 copy.93
  39.7 2.6 %all-to-all-done.1 = bf16[64,4,2,128]{3,0,2,1:T(8,128)(2,1)S(1)} async-done(((bf16[64,4,2,128]{3,0,2,1:T(8,128)(2,1)}), bf16[64,4,2,128]{3,0,2,1:T(8,128)(2,1)S(1)}, u32[]{:S(2)}, u32[]{:S(2)}) %all-to-all-start.1) | async-done | bytes 131104 | tf_op jit(solution)/shard_map/all_to_all | solution.py:90
  42.4 1.3 fusion.24
  43.9 0.8 copy.80
  44.7 3.3 %all-to-all-start.2 = ((bf16[256,1,2,128]{3,2,1,0:T(2,128)(2,1)}), bf16[256,1,2,128]{3,2,1,0:T(2,128)(2,1)S(1)}, u32[]{:S(2)}, u32[]{:S(2)}) async-start(bf16[256,1,2,128]{3,2,1,0:T(2,128)(2,1)} %copy.80), calls=%async_computation.2 | async-start | bytes 262144 | tf_op jit(solution)/shard_map/all_to_all | solution.py:108
  48.0 0.8 copy.96
  48.8 0.9 fusion.35
  49.8 4.3 %all-to-all-done.2 = bf16[256,1,2,128]{3,2,1,0:T(2,128)(2,1)S(1)} async-done(((bf16[256,1,2,128]{3,2,1,0:T(2,128)(2,1)}), bf16[256,1,2,128]{3,2,1,0:T(2,128)(2,1)S(1)}, u32[]{:S(2)}, u32[]{:S(2)}) %all-to-all-start.2) | async-done | bytes 131104 | tf_op jit(solution)/shard_map/all_to_all | solution.py:108
  54.2 2.9 %collective-permute-start.2 = (bf16[64,4,1,128]{3,0,2,1:T(8,128)(2,1)S(1)}, bf16[64,4,1,128]{3,0,2,1:T(8,128)(2,1)S(1)}, u32[]{:S(2)}, u32[]{:S(2)}) collective-permute-start(bf16[64,4,1,128]{3,0,2,1:T(8,128)(2,1)S(1)} %get-tuple-element.31), channel_id=1, source_target_pairs={{0,1},{1,2},{2,3},{4,5},{5,6},{6,7},{8,9},{9,10},{10,11},{12,13},{... | collective-permute-start | bytes 196616 | tf_op jit(solution)/shard_map/ppermute | solution.py:16
  57.1 1.3 collective-permute-start.3
  58.5 0.4 copy.94
  58.9 2.7 %collective-permute-done.3 = bf16[64,4,1,128]{3,0,2,1:T(8,128)(2,1)S(1)} collective-permute-done((bf16[64,4,1,128]{3,0,2,1:T(8,128)(2,1)S(1)}, bf16[64,4,1,128]{3,0,2,1:T(8,128)(2,1)S(1)}, u32[]{:S(2)}, u32[]{:S(2)}) %collective-permute-start.3) | collective-permute-done | bytes 65568 | tf_op jit(solution)/shard_map/ppermute | solution.py:19
  61.6 0.3 copy.108
  61.9 0.3 pad.7.clone
  62.3 2.1 %fusion.4 = bf16[4,2,8,17,64]{4,2,3,1,0:T(8,128)(2,1)S(1)} fusion(bf16[64,4,4,1,7,2]{0,4,5,2,1,3:T(8,128)(2,1)S(1)} %slice.27, bf16[64,4,4,1,8,17]{0,4,5,2,1,3:T(8,128)(2,1)S(1)} %copy.85, pred[8,17]{0,1:T(8,128)(4,1)S(1)} %copy-done.5, bf16[64,64]{0,1:T(8,128)(2,1)S(1)} %compare_convert_fusion, bf16[64,8,3,3,3]{0,1,4,3,2:T(8,128)(2,1)S(1)} %constant_dynamic-slice_fusion), kind=kOutput, calls=%fused_computation.8 | convolution fusion | flops 202055680 | bytes 482440 | tf_op jit(solution)/shard_map/conv_general_dilated | solution.py:31
  64.4 0.2 copy.86
  64.8 0.8 copy.87
  65.6 3.3 %all-to-all-start.3 = ((bf16[64,4,2,128]{3,0,2,1:T(8,128)(2,1)}), bf16[64,4,2,128]{3,0,2,1:T(8,128)(2,1)S(1)}, u32[]{:S(2)}, u32[]{:S(2)}) async-start(bf16[64,4,2,128]{3,0,2,1:T(8,128)(2,1)} %copy.87), calls=%async_computation.3 | async-start | bytes 262144 | tf_op jit(solution)/shard_map/all_to_all | solution.py:117
  68.9 0.2 all-reduce.4.cloned.1.call-start
  69.2 7.9 %fusion.3 = f32[8,64,3,3,3]{1,0,4,3,2:T(8,128)S(1)} fusion(bf16[1,64,6,4,130]{1,0,4,3,2:T(2,128)(2,1)S(1)} %copy.93, bf16[1,64,4,2,128]{1,0,4,3,2:T(2,128)(2,1)S(1)} %copy.94, f32[8,64]{1,0:T(8,128)S(1)} %fusion.40), kind=kOutput, calls=%fused_computation.7 | convolution fusion | flops 226699776 | bytes 587776 | tf_op jit(solution)/shard_map/conv_general_dilated | solution.py:60
  77.1 14.4 %psum.22 = f32[64,8,3,3,3]{0,1,4,3,2:T(8,128)S(1)} all-reduce(f32[64,8,3,3,3]{0,1,4,3,2:T(8,128)S(1)} %bitcast.154), channel_id=1, replica_groups=mesh['rep'=2,'grp'=4,'sub'=4] {'sub'}, use_global_device_ids=true, to_apply=%region_2.3 | all-reduce | flops 13824 | bytes 110592 | tf_op jit(solution)/shard_map/psum | solution.py:118
  91.5 0.2 copy.101
  91.8 0.3 reshape.178
  92.3 0.9 convolution_bitcast_fusion.1
  93.2 0.7 broadcast_multiply_fusion.2
  94.1 0.8 copy.97
  94.9 89.5 %all-reduce.4.cloned.1.call-done = (f32[256,256]{0,1:T(8,128)}, f32[256,256]{0,1:T(8,128)}) async-done(((f32[256,256]{0,1:T(8,128)}, f32[256,256]{0,1:T(8,128)}), (f32[256,256]{0,1:T(8,128)}, f32[256,256]{0,1:T(8,128)})) %all-reduce.4.cloned.1.call-update) | async-done | bytes 524304 | tf_op jit(solution)/shard_map/psum | solution.py:133
  184.4 1.1 broadcast_multiply_fusion
  185.5 0.8 copy.98
  186.3 0.8 copy.99
  (41 shorter events, 2.0 us)
Async XLA Ops:
  7.2 35.3 %copy-start = (bf16[256,256]{1,0:T(8,128)(2,1)S(1)}, bf16[256,256]{1,0:T(8,128)(2,1)}, u32[]{:S(2)}) copy-start(bf16[256,256]{1,0:T(8,128)(2,1)} %param.9) | copy-start | bytes 393220
  8.2 17.7 %copy-start.4 = (bf16[256,8,3,3,3]{0,1,4,3,2:T(8,128)(2,1)S(1)}, bf16[256,8,3,3,3]{0,1,4,3,2:T(8,128)(2,1)}, u32[]{:S(2)}) copy-start(bf16[256,8,3,3,3]{0,1,4,3,2:T(8,128)(2,1)} %param.8) | copy-start | bytes 331780
  10.9 12.4 %all-to-all-start = ((bf16[256,1,2,128]{3,2,1,0:T(2,128)(2,1)}), bf16[256,1,2,128]{3,2,1,0:T(2,128)(2,1)S(1)}, u32[]{:S(2)}, u32[]{:S(2)}) async-start(bf16[256,1,2,128]{3,2,1,0:T(2,128)(2,1)} %copy.71), calls=%async_computation | async-start | bytes 262144 | tf_op jit(solution)/shard_map/all_to_all | solution.py:86
  23.3 2.7 %collective-permute-start = (bf16[64,4,1,128]{3,0,1,2:T(8,128)(2,1)S(1)}, bf16[64,4,1,128]{3,0,1,2:T(8,128)(2,1)S(1)}, u32[]{:S(2)}, u32[]{:S(2)}) collective-permute-start(bf16[64,4,1,128]{3,0,1,2:T(8,128)(2,1)S(1)} %get-tuple-element.33), channel_id=1, source_target_pairs={{0,1},{1,2},{2,3},{4,5},{5,6},{6,7},{8,9},{9,10},{10,11},{12,13},{... | collective-permute-start | bytes 196616 | tf_op jit(solution)/shard_map/ppermute | solution.py:16
  24.6 4.9 %collective-permute-start.1 = (bf16[64,4,1,128]{3,0,1,2:T(8,128)(2,1)S(1)}, bf16[64,4,1,128]{3,0,1,2:T(8,128)(2,1)S(1)}, u32[]{:S(2)}, u32[]{:S(2)}) collective-permute-start(bf16[64,4,1,128]{3,0,1,2:T(8,128)(2,1)S(1)} %get-tuple-element.34), channel_id=1, source_target_pairs={{1,0},{2,1},{3,2},{5,4},{6,5},{7,6},{9,8},{10,9},{11,10},{13,12},{... | collective-permute-start | bytes 196616 | tf_op jit(solution)/shard_map/ppermute | solution.py:19
  29.8 0.7 copy-start.5
  32.0 4.3 %copy-start.2 = (bf16[256,1,2,128]{3,2,1,0:T(2,128)(2,1)S(1)}, bf16[256,1,2,128]{3,2,1,0:T(2,128)(2,1)}, u32[]{:S(2)}) copy-start(bf16[256,1,2,128]{3,2,1,0:T(2,128)(2,1)} %param.6) | copy-start | bytes 393220
  33.0 9.2 %all-to-all-start.1 = ((bf16[64,4,2,128]{3,0,2,1:T(8,128)(2,1)}), bf16[64,4,2,128]{3,0,2,1:T(8,128)(2,1)S(1)}, u32[]{:S(2)}, u32[]{:S(2)}) async-start(bf16[64,4,2,128]{3,0,2,1:T(8,128)(2,1)} %fusion.28), calls=%async_computation.1 | async-start | bytes 262144 | tf_op jit(solution)/shard_map/all_to_all | solution.py:90
  44.7 9.3 %all-to-all-start.2 = ((bf16[256,1,2,128]{3,2,1,0:T(2,128)(2,1)}), bf16[256,1,2,128]{3,2,1,0:T(2,128)(2,1)S(1)}, u32[]{:S(2)}, u32[]{:S(2)}) async-start(bf16[256,1,2,128]{3,2,1,0:T(2,128)(2,1)} %copy.80), calls=%async_computation.2 | async-start | bytes 262144 | tf_op jit(solution)/shard_map/all_to_all | solution.py:108
  54.2 4.7 %collective-permute-start.2 = (bf16[64,4,1,128]{3,0,2,1:T(8,128)(2,1)S(1)}, bf16[64,4,1,128]{3,0,2,1:T(8,128)(2,1)S(1)}, u32[]{:S(2)}, u32[]{:S(2)}) collective-permute-start(bf16[64,4,1,128]{3,0,2,1:T(8,128)(2,1)S(1)} %get-tuple-element.31), channel_id=1, source_target_pairs={{0,1},{1,2},{2,3},{4,5},{5,6},{6,7},{8,9},{9,10},{10,11},{12,13},{... | collective-permute-start | bytes 196616 | tf_op jit(solution)/shard_map/ppermute | solution.py:16
  57.1 4.4 %collective-permute-start.3 = (bf16[64,4,1,128]{3,0,2,1:T(8,128)(2,1)S(1)}, bf16[64,4,1,128]{3,0,2,1:T(8,128)(2,1)S(1)}, u32[]{:S(2)}, u32[]{:S(2)}) collective-permute-start(bf16[64,4,1,128]{3,0,2,1:T(8,128)(2,1)S(1)} %get-tuple-element.32), channel_id=1, source_target_pairs={{1,0},{2,1},{3,2},{5,4},{6,5},{7,6},{9,8},{10,9},{11,10},{13,12},{... | collective-permute-start | bytes 196616 | tf_op jit(solution)/shard_map/ppermute | solution.py:19
  65.6 25.9 %all-to-all-start.3 = ((bf16[64,4,2,128]{3,0,2,1:T(8,128)(2,1)}), bf16[64,4,2,128]{3,0,2,1:T(8,128)(2,1)S(1)}, u32[]{:S(2)}, u32[]{:S(2)}) async-start(bf16[64,4,2,128]{3,0,2,1:T(8,128)(2,1)} %copy.87), calls=%async_computation.3 | async-start | bytes 262144 | tf_op jit(solution)/shard_map/all_to_all | solution.py:117
  68.9 115.5 %all-reduce.4.cloned.1.call-start = ((), (), s32[]{:S(2)}) async-start(), calls=%async_computation.4 | async-start | bytes 1048576 | tf_op jit(solution)/shard_map/psum | solution.py:133
  77.1 15.0 %copy-start.1 = (f32[256,256]{0,1:T(8,128)S(1)}, f32[256,256]{0,1:T(8,128)}, u32[]{:S(2)}) copy-start(f32[256,256]{0,1:T(8,128)} %get-tuple-element.36) | copy-start | bytes 786436
  91.8 2.1 %copy-start.3 = (bf16[256,256]{1,0:T(8,128)(2,1)S(1)}, bf16[256,256]{1,0:T(8,128)(2,1)}, u32[]{:S(2)}) copy-start(bf16[256,256]{1,0:T(8,128)(2,1)} %param.7) | copy-start | bytes 393220
Sparse Core Ops, SparseCore 0:
  93.3 91.0 all-reduce.3
where the time goes:
time: 195 us; the launch traced here: 194 us
  waiting for transfers between devices  109 us (56%)
  starting transfers between devices  23.3 us (12%)
  matrix products  16.7 us (9%)
  between operations  14.5 us (7%)
  blocking collectives  14.4 us (7%)
  local copies, waits for them, and re-layouts  13.7 us (7%)
  other arithmetic  2.91 us (1%)
    psum x1, waiting for transfers between devices, per_device(): first_grad = lax.psum(first_part, ('grp', 'sub')) * factor  89.5 us
    psum x1, blocking collectives, per_device(): group_grad = lax.psum(kernel_part, 'sub') * factor  14.4 us
    conv_general_dilated x1, matrix products, weight_grad(): lax.conv_general_dilated(padded[None], deltas[None], (1, 1, 1), 'VALID',...  7.92 us
    all_to_all x1, starting transfers between devices, per_device(): lax.all_to_all(first_act, 'grp', split_axis=0, concat_axis=1, tiled=True)  6.31 us
    ppermute x2, waiting for transfers between devices, padded_2(): lax.ppermute(lax.slice_in_dim(block, 0, width, axis=dim), axis, backward)  6.11 us
    all_to_all x1, waiting for transfers between devices, per_device(): lax.all_to_all(first_act, 'grp', split_axis=0, concat_axis=1, tiled=True)  5.99 us
    unnamed x21, local copies, waits for them, and re-layouts  5.57 us
    all_to_all x1, waiting for transfers between devices, per_device(): lax.all_to_all(hidden_grad, 'grp', split_axis=0, concat_axis=1, tiled=True)  4.28 us
  transfers between devices with their start and end apart: 9, of which 6 were waited for; matrix products, arithmetic and copies ran while one was open for 8% of the time, Pallas kernels for 0%

commit v1 on v0

--- a/solution.py
+++ b/solution.py
@@ -19,6 +19,34 @@
         high = lax.ppermute(lax.slice_in_dim(block, 0, width, axis=dim), axis, backward)
         block = jnp.concatenate([low, block, high], axis=dim)
     return block
+
+
+def tree_sum(block, axes):
+    steps = []
+    for axis in axes:
+        count = lax.axis_size(axis)
+        bit = 1
+        while bit < count:
+            steps.append((axis, bit))
+            bit *= 2
+    shape = block.shape
+    pieces = block.reshape(-1)
+    kept = []
+    for axis, bit in steps:
+        pairs = [(i, i ^ bit) for i in range(lax.axis_size(axis))]
+        upper = (lax.axis_index(axis) & bit) != 0
+        half = pieces.shape[0] // 2
+        low, high = pieces[:half], pieces[half:]
+        keep = jnp.where(upper, high, low)
+        send = jnp.where(upper, low, high)
+        pieces = keep + lax.ppermute(send, axis, pairs)
+        kept.append((axis, bit, pairs, upper))
+    for axis, bit, pairs, upper in reversed(kept):
+        got = lax.ppermute(pieces, axis, pairs)
+        pieces = jnp.where(
+            upper, jnp.concatenate([got, pieces]), jnp.concatenate([pieces, got])
+        )
+    return pieces.reshape(shape)
 
 
 def silu_slope(values):
@@ -99,7 +127,7 @@
     third_part = lax.dot_general(
         act_flat, third_delta, contract_tail, preferred_element_type=jnp.float32
     )
-    third_grad = lax.psum(third_part, ("grp", "sub")) * factor
+    third_grad = tree_sum(third_part, ("sub", "grp")) * factor
     hidden_grad = (
         jnp.dot(third_weight, third_delta, preferred_element_type=jnp.float32)
         .astype(jnp.bfloat16)
@@ -115,7 +143,7 @@
     )
     kernel_part = diagonal_blocks(dense_grad)
     inner_grad = lax.all_to_all(inner_local, "grp", split_axis=1, concat_axis=0, tiled=True)
-    group_grad = lax.psum(kernel_part, "sub") * factor
+    group_grad = tree_sum(kernel_part, ("sub",)) * factor
     first_delta = (
         inner_grad.reshape(channels, -1).astype(jnp.float32) * silu_slope(first_pre)
     ).astype(jnp.bfloat16)
@@ -130,7 +158,7 @@
         .astype(jnp.bfloat16)
         .reshape(volume.shape)
     )
-    first_grad = lax.psum(first_part, ("grp", "sub")) * factor
+    first_grad = tree_sum(first_part, ("sub", "grp")) * factor
     return (block_output, volume_grad, first_grad, group_grad, third_grad)
 
 

time: 195 us -> 128 us (0.66)
  waiting for transfers between devices: 109 us -> 36.8 us
  starting transfers between devices: 23.3 us -> 46 us
  blocking collectives: 14.4 us -> 0 us
  between operations: 14.5 us -> 1.52 us
  local copies, waits for them, and re-layouts: 13.7 us -> 23.5 us
    psum x1 -> x0, waiting for transfers between devices: 89.5 us -> none  [per_device(): first_grad = lax.psum(first_part, ('grp', 'sub')) * factor]
    ppermute x0 -> x20, starting transfers between devices: none -> 24.4 us  [the longest x10 13.8 us: tree_sum(): pieces = keep + lax.ppermute(send, axis, pairs)]
    ppermute x0 -> x20, waiting for transfers between devices: none -> 18.1 us  [the longest x10 9.76 us: tree_sum(): pieces = keep + lax.ppermute(send, axis, pairs)]
    psum x1 -> x0, blocking collectives: 14.4 us -> none  [per_device(): group_grad = lax.psum(kernel_part, 'sub') * factor]
    select_n x0 -> x8, local copies, waits for them, and re-layouts: none -> 6.74 us  [the longest x4 3.44 us: tree_sum(): keep = jnp.where(upper, high, low)]
    concatenate x0 -> x16, local copies, waits for them, and re-layouts: none -> 4.45 us  [tree_sum(): jnp.concatenate([got, pieces])]
    ppermute x2, waiting for transfers between devices: 6.11 us -> 3.45 us  [padded_2(): lax.ppermute(lax.slice_in_dim(block, 0, width, axis=dim), axis, backward)]
    unnamed x21 -> x27, local copies, waits for them, and re-layouts: 5.57 us -> 4.17 us
  transfers between devices with their start and end apart: 9 -> 28, of which waited for: 6 -> 13; matrix products, arithmetic and copies ran while one was open for 8% -> 25% of each run, Pallas kernels for 0% -> 0%
where the time goes in v1:
time: 128 us; the launch traced here: 127 us
  starting transfers between devices  46 us (36%)
  waiting for transfers between devices  36.8 us (29%)
  local copies, waits for them, and re-layouts  23.5 us (18%)
  matrix products  15.3 us (12%)
  other arithmetic  3.97 us (3%)
  between operations  1.52 us (1%)
    ppermute x10, starting transfers between devices, tree_sum(): pieces = keep + lax.ppermute(send, axis, pairs)  13.8 us
    ppermute x10, starting transfers between devices, tree_sum(): got = lax.ppermute(pieces, axis, pairs)  10.6 us
    ppermute x10, waiting for transfers between devices, tree_sum(): pieces = keep + lax.ppermute(send, axis, pairs)  9.76 us
    ppermute x10, waiting for transfers between devices, tree_sum(): got = lax.ppermute(pieces, axis, pairs)  8.33 us
    conv_general_dilated x1, matrix products, weight_grad(): lax.conv_general_dilated(padded[None], deltas[None], (1, 1, 1), 'VALID',...  7.94 us
    all_to_all x1, starting transfers between devices, per_device(): lax.all_to_all(first_act, 'grp', split_axis=0, concat_axis=1, tiled=True)  6.32 us
    all_to_all x1, waiting for transfers between devices, per_device(): lax.all_to_all(first_act, 'grp', split_axis=0, concat_axis=1, tiled=True)  5.99 us
    all_to_all x1, waiting for transfers between devices, per_device(): lax.all_to_all(hidden_grad, 'grp', split_axis=0, concat_axis=1, tiled=True)  5.21 us
  transfers between devices with their start and end apart: 28, of which 13 were waited for; matrix products, arithmetic and copies ran while one was open for 25% of the time, Pallas kernels for 0%

profile of v1, /device:TPU:0, one launch (start us, length us, event | category | flops | bytes accessed | tf_op | source)
XLA Modules:
  0.0 127.2 jit_solution(13411954846457647401)
XLA Ops:
  0.6 1.0 copy.84
  1.7 1.9 %multiply_convert_fusion.2 = (bf16[256,256]{0,1:T(8,128)(2,1)S(1)}, f32[256,256]{0,1:T(8,128)}) fusion(bf16[256,256]{0,1:T(8,128)(2,1)S(1)} %bitcast.160, bf16[256,256]{1,0:T(8,128)(2,1)} %param.7), kind=kOutput, calls=%fused_computation.57 | convolution fusion | flops 33882112 | bytes 655360 | tf_op jit(solution)/shard_map/dot_general | solution.py:106
  4.4 6.3 %all-to-all-start = ((bf16[256,1,2,128]{3,2,1,0:T(2,128)(2,1)}), bf16[256,1,2,128]{3,2,1,0:T(2,128)(2,1)S(1)}, u32[]{:S(2)}, u32[]{:S(2)}) async-start(bf16[256,1,2,128]{3,2,1,0:T(2,128)(2,1)} %copy.85), calls=%async_computation | async-start | bytes 262144 | tf_op jit(solution)/shard_map/all_to_all | solution.py:114
  10.8 6.0 %all-to-all-done = bf16[256,1,2,128]{3,2,1,0:T(2,128)(2,1)S(1)} async-done(((bf16[256,1,2,128]{3,2,1,0:T(2,128)(2,1)}), bf16[256,1,2,128]{3,2,1,0:T(2,128)(2,1)S(1)}, u32[]{:S(2)}, u32[]{:S(2)}) %all-to-all-start) | async-done | bytes 131104 | tf_op jit(solution)/shard_map/all_to_all | solution.py:114
  16.8 1.3 %collective-permute-start = (bf16[64,4,1,128]{3,0,1,2:T(8,128)(2,1)S(1)}, bf16[64,4,1,128]{3,0,1,2:T(8,128)(2,1)S(1)}, u32[]{:S(2)}, u32[]{:S(2)}) collective-permute-start(bf16[64,4,1,128]{3,0,1,2:T(8,128)(2,1)S(1)} %get-tuple-element.35), channel_id=1, source_target_pairs={{0,1},{1,2},{2,3},{4,5},{5,6},{6,7},{8,9},{9,10},{10,11},{12,13},{... | collective-permute-start | bytes 196616 | tf_op jit(solution)/shard_map/ppermute | solution.py:16
  18.1 1.3 %collective-permute-start.1 = (bf16[64,4,1,128]{3,0,1,2:T(8,128)(2,1)S(1)}, bf16[64,4,1,128]{3,0,1,2:T(8,128)(2,1)S(1)}, u32[]{:S(2)}, u32[]{:S(2)}) collective-permute-start(bf16[64,4,1,128]{3,0,1,2:T(8,128)(2,1)S(1)} %get-tuple-element.36), channel_id=1, source_target_pairs={{1,0},{2,1},{3,2},{5,4},{6,5},{7,6},{9,8},{10,9},{11,10},{13,12},{... | collective-permute-start | bytes 196616 | tf_op jit(solution)/shard_map/ppermute | solution.py:19
  19.5 3.4 %collective-permute-done.1 = bf16[64,4,1,128]{3,0,1,2:T(8,128)(2,1)S(1)} collective-permute-done((bf16[64,4,1,128]{3,0,1,2:T(8,128)(2,1)S(1)}, bf16[64,4,1,128]{3,0,1,2:T(8,128)(2,1)S(1)}, u32[]{:S(2)}, u32[]{:S(2)}) %collective-permute-start.1) | collective-permute-done | bytes 65568 | tf_op jit(solution)/shard_map/ppermute | solution.py:19
  24.0 1.2 add_multiply_fusion
  26.6 3.3 %all-to-all-start.1 = ((bf16[64,4,2,128]{3,0,2,1:T(8,128)(2,1)}), bf16[64,4,2,128]{3,0,2,1:T(8,128)(2,1)S(1)}, u32[]{:S(2)}, u32[]{:S(2)}) async-start(bf16[64,4,2,128]{3,0,2,1:T(8,128)(2,1)} %fusion.30), calls=%async_computation.1 | async-start | bytes 262144 | tf_op jit(solution)/shard_map/all_to_all | solution.py:118
  31.5 1.7 %copy.109 = bf16[1,64,6,4,130]{1,0,4,3,2:T(2,128)(2,1)S(1)} copy(bf16[1,64,6,4,130]{4,1,2,3,0:T(8,128)(2,1)S(1)} %pad_bitcast_fusion) | data formatting | bytes 798720 | tf_op jit(solution)/shard_map/broadcast_in_dim | solution.py:89
  33.2 2.6 %all-to-all-done.1 = bf16[64,4,2,128]{3,0,2,1:T(8,128)(2,1)S(1)} async-done(((bf16[64,4,2,128]{3,0,2,1:T(8,128)(2,1)}), bf16[64,4,2,128]{3,0,2,1:T(8,128)(2,1)S(1)}, u32[]{:S(2)}, u32[]{:S(2)}) %all-to-all-start.1) | async-done | bytes 131104 | tf_op jit(solution)/shard_map/all_to_all | solution.py:118
  35.9 1.3 %fusion.26 = (bf16[256,256]{0,1:T(8,128)(2,1)S(1)}, bf16[256,256]{0,1:T(8,128)(2,1)S(1)}) fusion(f32[256,1,2,128]{0,3,2,1:T(8,128)} %copy.93, bf16[256,256]{1,0:T(8,128)(2,1)S(1)} %copy-done, bf16[32,8,2,128]{3,2,1,0:T(2,128)(2,1)S(1)} %bitcast.163, bf16[256,256]{0,1:T(8,128)(2,1)S(1)} %bitcast.161), kind=kOutput, calls=%fused_computation.44 | convolution fusion | flops 34406400 | bytes 917504 | tf_op jit(solution)/shard_map/dot_general | solution.py:120
  38.6 1.8 %collective-permute-start.16 = (f32[32768]{0:T(1024)S(1)}, f32[32768]{0:T(1024)S(1)}, u32[]{:S(2)}, u32[]{:S(2)}) collective-permute-start(f32[32768]{0:T(1024)S(1)} %bitcast.168), channel_id=1, source_target_pairs={{0,1},{1,0},{2,3},{3,2},{4,5},{5,4},{6,7},{7,6},{8,9},{9,8},{10,11... | collective-permute-start | bytes 393224 | tf_op jit(solution)/shard_map/ppermute | solution.py:42
  41.5 3.4 %all-to-all-start.2 = ((bf16[256,1,2,128]{3,2,1,0:T(2,128)(2,1)}), bf16[256,1,2,128]{3,2,1,0:T(2,128)(2,1)S(1)}, u32[]{:S(2)}, u32[]{:S(2)}) async-start(bf16[256,1,2,128]{3,2,1,0:T(2,128)(2,1)} %copy.94), calls=%async_computation.2 | async-start | bytes 262144 | tf_op jit(solution)/shard_map/all_to_all | solution.py:136
  44.9 1.1 collective-permute-start.17
  45.9 5.2 %all-to-all-done.2 = bf16[256,1,2,128]{3,2,1,0:T(2,128)(2,1)S(1)} async-done(((bf16[256,1,2,128]{3,2,1,0:T(2,128)(2,1)}), bf16[256,1,2,128]{3,2,1,0:T(2,128)(2,1)S(1)}, u32[]{:S(2)}, u32[]{:S(2)}) %all-to-all-start.2) | async-done | bytes 131104 | tf_op jit(solution)/shard_map/all_to_all | solution.py:136
  51.3 1.3 %collective-permute-start.2 = (bf16[64,4,1,128]{3,0,2,1:T(8,128)(2,1)S(1)}, bf16[64,4,1,128]{3,0,2,1:T(8,128)(2,1)S(1)}, u32[]{:S(2)}, u32[]{:S(2)}) collective-permute-start(bf16[64,4,1,128]{3,0,2,1:T(8,128)(2,1)S(1)} %get-tuple-element.33), channel_id=1, source_target_pairs={{0,1},{1,2},{2,3},{4,5},{5,6},{6,7},{8,9},{9,10},{10,11},{12,13},{... | collective-permute-start | bytes 196616 | tf_op jit(solution)/shard_map/ppermute | solution.py:16
  52.6 1.5 %collective-permute-start.3 = (bf16[64,4,1,128]{3,0,2,1:T(8,128)(2,1)S(1)}, bf16[64,4,1,128]{3,0,2,1:T(8,128)(2,1)S(1)}, u32[]{:S(2)}, u32[]{:S(2)}) collective-permute-start(bf16[64,4,1,128]{3,0,2,1:T(8,128)(2,1)S(1)} %get-tuple-element.34), channel_id=1, source_target_pairs={{1,0},{2,1},{3,2},{5,4},{6,5},{7,6},{9,8},{10,9},{11,10},{13,12},{... | collective-permute-start | bytes 196616 | tf_op jit(solution)/shard_map/ppermute | solution.py:19
  54.5 7.9 %fusion.3 = f32[8,64,3,3,3]{1,0,4,3,2:T(8,128)S(1)} fusion(bf16[1,64,6,4,130]{1,0,4,3,2:T(2,128)(2,1)S(1)} %copy.109, bf16[1,64,4,2,128]{1,0,4,3,2:T(2,128)(2,1)S(1)} %copy.110, f32[8,64]{1,0:T(8,128)S(1)} %fusion.43), kind=kOutput, calls=%fused_computation.7 | convolution fusion | flops 226699776 | bytes 587776 | tf_op jit(solution)/shard_map/conv_general_dilated | solution.py:88
  62.6 2.1 %copy.112 = f32[32,8,3,3,3]{4,3,2,1,0:T(4,128)S(1)} copy(f32[32,8,3,3,3]{0,1,4,3,2:T(8,128)S(1)} %get-tuple-element.37) | data formatting | bytes 55296 | tf_op jit(solution)/shard_map/jit(_where)/select_n | solution.py:41
  64.7 1.0 select_n.266
  65.7 2.6 %collective-permute-start.12 = (f32[6912]{0:T(1024)S(1)}, f32[6912]{0:T(1024)S(1)}, u32[]{:S(2)}, u32[]{:S(2)}) collective-permute-start(f32[6912]{0:T(1024)S(1)} %select_n.266), channel_id=1, source_target_pairs={{0,1},{1,0},{2,3},{3,2},{4,5},{5,4},{6,7},{7,6},{8,9},{9,8},{10,11... | collective-permute-start | bytes 82952 | tf_op jit(solution)/shard_map/ppermute | solution.py:42
  68.3 1.3 %collective-permute-start.18 = (f32[8192]{0:T(1024)S(1)}, f32[8192]{0:T(1024)S(1)}, u32[]{:S(2)}, u32[]{:S(2)}) collective-permute-start(f32[8192]{0:T(1024)S(1)} %slice_select_fusion.8), channel_id=1, source_target_pairs={{0,4},{4,0},{8,12},{12,8},{1,5},{5,1},{9,13},{13,9},{2,6},{6,2},{1... | collective-permute-start | bytes 98312 | tf_op jit(solution)/shard_map/ppermute | solution.py:42
  69.6 2.3 %copy.111 = f32[32,8,3,3,3]{4,3,2,1,0:T(4,128)S(1)} copy(f32[32,8,3,3,3]{0,1,4,3,2:T(8,128)S(1)} %get-tuple-element.38) | data formatting | bytes 55296 | tf_op jit(solution)/shard_map/jit(_where)/select_n | solution.py:40
  71.9 1.0 select_n.264
  72.9 1.7 %collective-permute-start.13 = (f32[3456]{0:T(1024)S(1)}, f32[3456]{0:T(1024)S(1)}, u32[]{:S(2)}, u32[]{:S(2)}) collective-permute-start(f32[3456]{0:T(1024)S(1)} %slice_select_fusion.11), channel_id=1, source_target_pairs={{0,2},{1,3},{2,0},{3,1},{4,6},{5,7},{6,4},{7,5},{8,10},{9,11},{10,... | collective-permute-start | bytes 41480 | tf_op jit(solution)/shard_map/ppermute | solution.py:42
  74.7 1.3 %collective-permute-start.19 = (f32[4096]{0:T(1024)S(1)}, f32[4096]{0:T(1024)S(1)}, u32[]{:S(2)}, u32[]{:S(2)}) collective-permute-start(f32[4096]{0:T(1024)S(1)} %slice_select_fusion.10), channel_id=1, source_target_pairs={{0,8},{4,12},{8,0},{12,4},{1,9},{5,13},{9,1},{13,5},{2,10},{6,14},... | collective-permute-start | bytes 49160 | tf_op jit(solution)/shard_map/ppermute | solution.py:42
  76.7 1.6 %collective-permute-start.14 = (f32[3456]{0:T(1024)S(1)}, f32[3456]{0:T(1024)S(1)}, u32[]{:S(2)}, u32[]{:S(2)}) collective-permute-start(f32[3456]{0:T(1024)S(1)} %select_add_fusion.5), channel_id=1, source_target_pairs={{0,2},{1,3},{2,0},{3,1},{4,6},{5,7},{6,4},{7,5},{8,10},{9,11},{10,... | collective-permute-start | bytes 41480 | tf_op jit(solution)/shard_map/ppermute | solution.py:45
  79.5 1.3 %collective-permute-start.20 = (f32[4096]{0:T(1024)S(1)}, f32[4096]{0:T(1024)S(1)}, u32[]{:S(2)}, u32[]{:S(2)}) collective-permute-start(f32[4096]{0:T(1024)S(1)} %select_add_fusion.4), channel_id=1, source_target_pairs={{0,8},{4,12},{8,0},{12,4},{1,9},{5,13},{9,1},{13,5},{2,10},{6,14},... | collective-permute-start | bytes 49160 | tf_op jit(solution)/shard_map/ppermute | solution.py:45
  83.0 2.1 %fusion.4 = bf16[4,2,8,17,64]{4,2,3,1,0:T(8,128)(2,1)S(1)} fusion(bf16[64,4,4,1,7,2]{0,4,5,2,1,3:T(8,128)(2,1)S(1)} %slice.113, bf16[64,4,4,1,8,17]{0,4,5,2,1,3:T(8,128)(2,1)S(1)} %copy.99, pred[8,17]{0,1:T(8,128)(4,1)S(1)} %copy-done.7, bf16[64,64]{0,1:T(8,128)(2,1)S(1)} %compare_convert_fusion, bf16[64,8,3,3,3]{0,1,4,3,2:T(8,128)(2,1)S(1)} %constant_dynamic-slice_fusion), kind=kOutput, calls=%fused_computation.8 | convolution fusion | flops 202055680 | bytes 482440 | tf_op jit(solution)/shard_map/conv_general_dilated | solution.py:59
  86.3 3.3 %all-to-all-start.3 = ((bf16[64,4,2,128]{3,0,2,1:T(8,128)(2,1)}), bf16[64,4,2,128]{3,0,2,1:T(8,128)(2,1)S(1)}, u32[]{:S(2)}, u32[]{:S(2)}) async-start(bf16[64,4,2,128]{3,0,2,1:T(8,128)(2,1)} %copy.101), calls=%async_computation.3 | async-start | bytes 262144 | tf_op jit(solution)/shard_map/all_to_all | solution.py:145
  89.6 2.0 %collective-permute-start.21 = (f32[8192]{0:T(1024)S(1)}, f32[8192]{0:T(1024)S(1)}, u32[]{:S(2)}, u32[]{:S(2)}) collective-permute-start(f32[8192]{0:T(1024)S(1)} %maximum_select_fusion.14), channel_id=1, source_target_pairs={{0,4},{4,0},{8,12},{12,8},{1,5},{5,1},{9,13},{13,9},{2,6},{6,2},{1... | collective-permute-start | bytes 98312 | tf_op jit(solution)/shard_map/ppermute | solution.py:45
  92.6 1.2 copy.117
  94.6 1.5 %all-to-all-done.3 = bf16[64,4,2,128]{3,0,2,1:T(8,128)(2,1)S(1)} async-done(((bf16[64,4,2,128]{3,0,2,1:T(8,128)(2,1)}), bf16[64,4,2,128]{3,0,2,1:T(8,128)(2,1)S(1)}, u32[]{:S(2)}, u32[]{:S(2)}) %all-to-all-start.3) | async-done | bytes 131104 | tf_op jit(solution)/shard_map/all_to_all | solution.py:145
  97.4 1.3 %collective-permute-start.22 = (f32[16384]{0:T(1024)S(1)}, f32[16384]{0:T(1024)S(1)}, u32[]{:S(2)}, u32[]{:S(2)}) collective-permute-start(f32[16384]{0:T(1024)S(1)} %maximum_select_fusion.10), channel_id=1, source_target_pairs={{0,2},{1,3},{2,0},{3,1},{4,6},{5,7},{6,4},{7,5},{8,10},{9,11},{10,... | collective-permute-start | bytes 196616 | tf_op jit(solution)/shard_map/ppermute | solution.py:45
  99.0 1.1 collective-permute-start.5
  100.1 3.3 %collective-permute-done.5 = f32[16384]{0:T(1024)S(1)} collective-permute-done((f32[16384]{0:T(1024)S(1)}, f32[16384]{0:T(1024)S(1)}, u32[]{:S(2)}, u32[]{:S(2)}) %collective-permute-start.5) | collective-permute-done | bytes 65568 | tf_op jit(solution)/shard_map/ppermute | solution.py:42
  103.4 1.7 %collective-permute-start.6 = (f32[8192]{0:T(1024)S(1)}, f32[8192]{0:T(1024)S(1)}, u32[]{:S(2)}, u32[]{:S(2)}) collective-permute-start(f32[8192]{0:T(1024)S(1)} %slice_select_fusion.9), channel_id=1, source_target_pairs={{0,4},{4,0},{8,12},{12,8},{1,5},{5,1},{9,13},{13,9},{2,6},{6,2},{1... | collective-permute-start | bytes 98312 | tf_op jit(solution)/shard_map/ppermute | solution.py:42
  105.2 2.2 %collective-permute-done.6 = f32[8192]{0:T(1024)S(1)} collective-permute-done((f32[8192]{0:T(1024)S(1)}, f32[8192]{0:T(1024)S(1)}, u32[]{:S(2)}, u32[]{:S(2)}) %collective-permute-start.6) | collective-permute-done | bytes 32800 | tf_op jit(solution)/shard_map/ppermute | solution.py:42
  107.3 1.1 collective-permute-start.7
  108.5 3.6 %collective-permute-done.7 = f32[4096]{0:T(1024)S(1)} collective-permute-done((f32[4096]{0:T(1024)S(1)}, f32[4096]{0:T(1024)S(1)}, u32[]{:S(2)}, u32[]{:S(2)}) %collective-permute-start.7) | collective-permute-done | bytes 16416 | tf_op jit(solution)/shard_map/ppermute | solution.py:42
  112.1 1.1 collective-permute-start.8
  114.2 2.5 %collective-permute-done.8 = f32[4096]{0:T(1024)S(1)} collective-permute-done((f32[4096]{0:T(1024)S(1)}, f32[4096]{0:T(1024)S(1)}, u32[]{:S(2)}, u32[]{:S(2)}) %collective-permute-start.8) | collective-permute-done | bytes 16416 | tf_op jit(solution)/shard_map/ppermute | solution.py:45
  116.7 1.6 %collective-permute-start.9 = (f32[8192]{0:T(1024)S(1)}, f32[8192]{0:T(1024)S(1)}, u32[]{:S(2)}, u32[]{:S(2)}) collective-permute-start(f32[8192]{0:T(1024)S(1)} %maximum_select_fusion.12), channel_id=1, source_target_pairs={{0,4},{4,0},{8,12},{12,8},{1,5},{5,1},{9,13},{13,9},{2,6},{6,2},{1... | collective-permute-start | bytes 98312 | tf_op jit(solution)/shard_map/ppermute | solution.py:45
  119.1 1.6 %collective-permute-done.9 = f32[8192]{0:T(1024)S(1)} collective-permute-done((f32[8192]{0:T(1024)S(1)}, f32[8192]{0:T(1024)S(1)}, u32[]{:S(2)}, u32[]{:S(2)}) %collective-permute-start.9) | collective-permute-done | bytes 32800 | tf_op jit(solution)/shard_map/ppermute | solution.py:45
  120.6 1.3 %collective-permute-start.10 = (f32[16384]{0:T(1024)S(1)}, f32[16384]{0:T(1024)S(1)}, u32[]{:S(2)}, u32[]{:S(2)}) collective-permute-start(f32[16384]{0:T(1024)S(1)} %maximum_select_fusion.8), channel_id=1, source_target_pairs={{0,2},{1,3},{2,0},{3,1},{4,6},{5,7},{6,4},{7,5},{8,10},{9,11},{10,... | collective-permute-start | bytes 196616 | tf_op jit(solution)/shard_map/ppermute | solution.py:45
  122.0 3.0 %collective-permute-done.10 = f32[16384]{0:T(1024)S(1)} collective-permute-done((f32[16384]{0:T(1024)S(1)}, f32[16384]{0:T(1024)S(1)}, u32[]{:S(2)}, u32[]{:S(2)}) %collective-permute-start.10) | collective-permute-done | bytes 65568 | tf_op jit(solution)/shard_map/ppermute | solution.py:45
  125.1 1.3 collective-permute-done.11
  (142 shorter events, 19.1 us)
Async XLA Ops:
  0.6 35.3 %copy-start = (bf16[256,256]{1,0:T(8,128)(2,1)S(1)}, bf16[256,256]{1,0:T(8,128)(2,1)}, u32[]{:S(2)}) copy-start(bf16[256,256]{1,0:T(8,128)(2,1)} %param.9) | copy-start | bytes 393220
  1.7 34.2 %copy-start.1 = (bf16[256,1,2,128]{0,3,2,1:T(8,128)(2,1)}, bf16[256,1,2,128]{0,3,2,1:T(8,128)(2,1)S(1)}, u32[]{:S(2)}) copy-start(bf16[256,1,2,128]{0,3,2,1:T(8,128)(2,1)S(1)} %copy.84) | copy-start | bytes 393220
  1.7 17.7 %copy-start.6 = (bf16[256,8,3,3,3]{0,1,4,3,2:T(8,128)(2,1)S(1)}, bf16[256,8,3,3,3]{0,1,4,3,2:T(8,128)(2,1)}, u32[]{:S(2)}) copy-start(bf16[256,8,3,3,3]{0,1,4,3,2:T(8,128)(2,1)} %param.8) | copy-start | bytes 331780
  4.4 12.4 %all-to-all-start = ((bf16[256,1,2,128]{3,2,1,0:T(2,128)(2,1)}), bf16[256,1,2,128]{3,2,1,0:T(2,128)(2,1)S(1)}, u32[]{:S(2)}, u32[]{:S(2)}) async-start(bf16[256,1,2,128]{3,2,1,0:T(2,128)(2,1)} %copy.85), calls=%async_computation | async-start | bytes 262144 | tf_op jit(solution)/shard_map/all_to_all | solution.py:114
  16.8 2.7 %collective-permute-start = (bf16[64,4,1,128]{3,0,1,2:T(8,128)(2,1)S(1)}, bf16[64,4,1,128]{3,0,1,2:T(8,128)(2,1)S(1)}, u32[]{:S(2)}, u32[]{:S(2)}) collective-permute-start(bf16[64,4,1,128]{3,0,1,2:T(8,128)(2,1)S(1)} %get-tuple-element.35), channel_id=1, source_target_pairs={{0,1},{1,2},{2,3},{4,5},{5,6},{6,7},{8,9},{9,10},{10,11},{12,13},{... | collective-permute-start | bytes 196616 | tf_op jit(solution)/shard_map/ppermute | solution.py:16
  18.1 4.9 %collective-permute-start.1 = (bf16[64,4,1,128]{3,0,1,2:T(8,128)(2,1)S(1)}, bf16[64,4,1,128]{3,0,1,2:T(8,128)(2,1)S(1)}, u32[]{:S(2)}, u32[]{:S(2)}) collective-permute-start(bf16[64,4,1,128]{3,0,1,2:T(8,128)(2,1)S(1)} %get-tuple-element.36), channel_id=1, source_target_pairs={{1,0},{2,1},{3,2},{5,4},{6,5},{7,6},{9,8},{10,9},{11,10},{13,12},{... | collective-permute-start | bytes 196616 | tf_op jit(solution)/shard_map/ppermute | solution.py:19
  23.3 0.7 copy-start.7
  25.6 4.3 %copy-start.4 = (bf16[256,1,2,128]{3,2,1,0:T(2,128)(2,1)S(1)}, bf16[256,1,2,128]{3,2,1,0:T(2,128)(2,1)}, u32[]{:S(2)}) copy-start(bf16[256,1,2,128]{3,2,1,0:T(2,128)(2,1)} %param.6) | copy-start | bytes 393220
  26.6 9.2 %all-to-all-start.1 = ((bf16[64,4,2,128]{3,0,2,1:T(8,128)(2,1)}), bf16[64,4,2,128]{3,0,2,1:T(8,128)(2,1)S(1)}, u32[]{:S(2)}, u32[]{:S(2)}) async-start(bf16[64,4,2,128]{3,0,2,1:T(8,128)(2,1)} %fusion.30), calls=%async_computation.1 | async-start | bytes 262144 | tf_op jit(solution)/shard_map/all_to_all | solution.py:118
  38.6 6.2 %collective-permute-start.16 = (f32[32768]{0:T(1024)S(1)}, f32[32768]{0:T(1024)S(1)}, u32[]{:S(2)}, u32[]{:S(2)}) collective-permute-start(f32[32768]{0:T(1024)S(1)} %bitcast.168), channel_id=1, source_target_pairs={{0,1},{1,0},{2,3},{3,2},{4,5},{5,4},{6,7},{7,6},{8,9},{9,8},{10,11... | collective-permute-start | bytes 393224 | tf_op jit(solution)/shard_map/ppermute | solution.py:42
  41.5 9.7 %all-to-all-start.2 = ((bf16[256,1,2,128]{3,2,1,0:T(2,128)(2,1)}), bf16[256,1,2,128]{3,2,1,0:T(2,128)(2,1)S(1)}, u32[]{:S(2)}, u32[]{:S(2)}) async-start(bf16[256,1,2,128]{3,2,1,0:T(2,128)(2,1)} %copy.94), calls=%async_computation.2 | async-start | bytes 262144 | tf_op jit(solution)/shard_map/all_to_all | solution.py:136
  44.9 23.4 %collective-permute-start.17 = (f32[16384]{0:T(1024)S(1)}, f32[16384]{0:T(1024)S(1)}, u32[]{:S(2)}, u32[]{:S(2)}) collective-permute-start(f32[16384]{0:T(1024)S(1)} %slice_select_fusion.6), channel_id=1, source_target_pairs={{0,2},{1,3},{2,0},{3,1},{4,6},{5,7},{6,4},{7,5},{8,10},{9,11},{10,... | collective-permute-start | bytes 196616 | tf_op jit(solution)/shard_map/ppermute | solution.py:42
  51.3 30.9 %collective-permute-start.2 = (bf16[64,4,1,128]{3,0,2,1:T(8,128)(2,1)S(1)}, bf16[64,4,1,128]{3,0,2,1:T(8,128)(2,1)S(1)}, u32[]{:S(2)}, u32[]{:S(2)}) collective-permute-start(bf16[64,4,1,128]{3,0,2,1:T(8,128)(2,1)S(1)} %get-tuple-element.33), channel_id=1, source_target_pairs={{0,1},{1,2},{2,3},{4,5},{5,6},{6,7},{8,9},{9,10},{10,11},{12,13},{... | collective-permute-start | bytes 196616 | tf_op jit(solution)/shard_map/ppermute | solution.py:16
  52.6 29.6 %collective-permute-start.3 = (bf16[64,4,1,128]{3,0,2,1:T(8,128)(2,1)S(1)}, bf16[64,4,1,128]{3,0,2,1:T(8,128)(2,1)S(1)}, u32[]{:S(2)}, u32[]{:S(2)}) collective-permute-start(bf16[64,4,1,128]{3,0,2,1:T(8,128)(2,1)S(1)} %get-tuple-element.34), channel_id=1, source_target_pairs={{1,0},{2,1},{3,2},{5,4},{6,5},{7,6},{9,8},{10,9},{11,10},{13,12},{... | collective-permute-start | bytes 196616 | tf_op jit(solution)/shard_map/ppermute | solution.py:19
  65.7 7.2 %collective-permute-start.12 = (f32[6912]{0:T(1024)S(1)}, f32[6912]{0:T(1024)S(1)}, u32[]{:S(2)}, u32[]{:S(2)}) collective-permute-start(f32[6912]{0:T(1024)S(1)} %select_n.266), channel_id=1, source_target_pairs={{0,1},{1,0},{2,3},{3,2},{4,5},{5,4},{6,7},{7,6},{8,9},{9,8},{10,11... | collective-permute-start | bytes 82952 | tf_op jit(solution)/shard_map/ppermute | solution.py:42
  68.3 6.4 %collective-permute-start.18 = (f32[8192]{0:T(1024)S(1)}, f32[8192]{0:T(1024)S(1)}, u32[]{:S(2)}, u32[]{:S(2)}) collective-permute-start(f32[8192]{0:T(1024)S(1)} %slice_select_fusion.8), channel_id=1, source_target_pairs={{0,4},{4,0},{8,12},{12,8},{1,5},{5,1},{9,13},{13,9},{2,6},{6,2},{1... | collective-permute-start | bytes 98312 | tf_op jit(solution)/shard_map/ppermute | solution.py:42
  72.9 3.8 %collective-permute-start.13 = (f32[3456]{0:T(1024)S(1)}, f32[3456]{0:T(1024)S(1)}, u32[]{:S(2)}, u32[]{:S(2)}) collective-permute-start(f32[3456]{0:T(1024)S(1)} %slice_select_fusion.11), channel_id=1, source_target_pairs={{0,2},{1,3},{2,0},{3,1},{4,6},{5,7},{6,4},{7,5},{8,10},{9,11},{10,... | collective-permute-start | bytes 41480 | tf_op jit(solution)/shard_map/ppermute | solution.py:42
  74.7 4.8 %collective-permute-start.19 = (f32[4096]{0:T(1024)S(1)}, f32[4096]{0:T(1024)S(1)}, u32[]{:S(2)}, u32[]{:S(2)}) collective-permute-start(f32[4096]{0:T(1024)S(1)} %slice_select_fusion.10), channel_id=1, source_target_pairs={{0,8},{4,12},{8,0},{12,4},{1,9},{5,13},{9,1},{13,5},{2,10},{6,14},... | collective-permute-start | bytes 49160 | tf_op jit(solution)/shard_map/ppermute | solution.py:42
  76.7 4.1 %collective-permute-start.14 = (f32[3456]{0:T(1024)S(1)}, f32[3456]{0:T(1024)S(1)}, u32[]{:S(2)}, u32[]{:S(2)}) collective-permute-start(f32[3456]{0:T(1024)S(1)} %select_add_fusion.5), channel_id=1, source_target_pairs={{0,2},{1,3},{2,0},{3,1},{4,6},{5,7},{6,4},{7,5},{8,10},{9,11},{10,... | collective-permute-start | bytes 41480 | tf_op jit(solution)/shard_map/ppermute | solution.py:45
  79.5 10.1 %collective-permute-start.20 = (f32[4096]{0:T(1024)S(1)}, f32[4096]{0:T(1024)S(1)}, u32[]{:S(2)}, u32[]{:S(2)}) collective-permute-start(f32[4096]{0:T(1024)S(1)} %select_add_fusion.4), channel_id=1, source_target_pairs={{0,8},{4,12},{8,0},{12,4},{1,9},{5,13},{9,1},{13,5},{2,10},{6,14},... | collective-permute-start | bytes 49160 | tf_op jit(solution)/shard_map/ppermute | solution.py:45
  80.9 10.8 %collective-permute-start.15 = (f32[6912]{0:T(1024)S(1)}, f32[6912]{0:T(1024)S(1)}, u32[]{:S(2)}, u32[]{:S(2)}) collective-permute-start(f32[6912]{0:T(1024)S(1)} %maximum_select_fusion.16), channel_id=1, source_target_pairs={{0,1},{1,0},{2,3},{3,2},{4,5},{5,4},{6,7},{7,6},{8,9},{9,8},{10,11... | collective-permute-start | bytes 82952 | tf_op jit(solution)/shard_map/ppermute | solution.py:45
  86.3 9.8 %all-to-all-start.3 = ((bf16[64,4,2,128]{3,0,2,1:T(8,128)(2,1)}), bf16[64,4,2,128]{3,0,2,1:T(8,128)(2,1)S(1)}, u32[]{:S(2)}, u32[]{:S(2)}) async-start(bf16[64,4,2,128]{3,0,2,1:T(8,128)(2,1)} %copy.101), calls=%async_computation.3 | async-start | bytes 262144 | tf_op jit(solution)/shard_map/all_to_all | solution.py:145
  89.6 7.7 %collective-permute-start.21 = (f32[8192]{0:T(1024)S(1)}, f32[8192]{0:T(1024)S(1)}, u32[]{:S(2)}, u32[]{:S(2)}) collective-permute-start(f32[8192]{0:T(1024)S(1)} %maximum_select_fusion.14), channel_id=1, source_target_pairs={{0,4},{4,0},{8,12},{12,8},{1,5},{5,1},{9,13},{13,9},{2,6},{6,2},{1... | collective-permute-start | bytes 98312 | tf_op jit(solution)/shard_map/ppermute | solution.py:45
  93.8 2.9 %copy-start.3 = (f32[256,256]{0,1:T(8,128)S(1)}, f32[256,256]{0,1:T(8,128)}, u32[]{:S(2)}) copy-start(f32[256,256]{0,1:T(8,128)} %get-tuple-element.40) | copy-start | bytes 786436
  94.6 2.2 %copy-start.2 = (bf16[256,1,2,128]{0,3,2,1:T(8,128)(2,1)S(1)}, bf16[256,1,2,128]{0,3,2,1:T(8,128)(2,1)}, u32[]{:S(2)}) copy-start(bf16[256,1,2,128]{0,3,2,1:T(8,128)(2,1)} %copy-done.1) | copy-start | bytes 393220
  97.3 1.6 %collective-permute-start.4 = (f32[32768]{0:T(1024)S(1)}, f32[32768]{0:T(1024)S(1)}, u32[]{:S(2)}, u32[]{:S(2)}) collective-permute-start(f32[32768]{0:T(1024)S(1)} %bitcast.167), channel_id=1, source_target_pairs={{0,1},{1,0},{2,3},{3,2},{4,5},{5,4},{6,7},{7,6},{8,9},{9,8},{10,11... | collective-permute-start | bytes 393224 | tf_op jit(solution)/shard_map/ppermute | solution.py:42
  97.4 7.7 %collective-permute-start.22 = (f32[16384]{0:T(1024)S(1)}, f32[16384]{0:T(1024)S(1)}, u32[]{:S(2)}, u32[]{:S(2)}) collective-permute-start(f32[16384]{0:T(1024)S(1)} %maximum_select_fusion.10), channel_id=1, source_target_pairs={{0,2},{1,3},{2,0},{3,1},{4,6},{5,7},{6,4},{7,5},{8,10},{9,11},{10,... | collective-permute-start | bytes 196616 | tf_op jit(solution)/shard_map/ppermute | solution.py:45
  98.7 14.4 %copy-start.5 = (bf16[256,256]{1,0:T(8,128)(2,1)S(1)}, bf16[256,256]{1,0:T(8,128)(2,1)}, u32[]{:S(2)}) copy-start(bf16[256,256]{1,0:T(8,128)(2,1)} %param.7) | copy-start | bytes 393220
  99.0 4.4 %collective-permute-start.5 = (f32[16384]{0:T(1024)S(1)}, f32[16384]{0:T(1024)S(1)}, u32[]{:S(2)}, u32[]{:S(2)}) collective-permute-start(f32[16384]{0:T(1024)S(1)} %slice_select_fusion.7), channel_id=1, source_target_pairs={{0,2},{1,3},{2,0},{3,1},{4,6},{5,7},{6,4},{7,5},{8,10},{9,11},{10,... | collective-permute-start | bytes 196616 | tf_op jit(solution)/shard_map/ppermute | solution.py:42
  103.4 4.0 %collective-permute-start.6 = (f32[8192]{0:T(1024)S(1)}, f32[8192]{0:T(1024)S(1)}, u32[]{:S(2)}, u32[]{:S(2)}) collective-permute-start(f32[8192]{0:T(1024)S(1)} %slice_select_fusion.9), channel_id=1, source_target_pairs={{0,4},{4,0},{8,12},{12,8},{1,5},{5,1},{9,13},{13,9},{2,6},{6,2},{1... | collective-permute-start | bytes 98312 | tf_op jit(solution)/shard_map/ppermute | solution.py:42
  105.1 9.1 %collective-permute-start.23 = (f32[32768]{0:T(1024)S(1)}, f32[32768]{0:T(1024)S(1)}, u32[]{:S(2)}, u32[]{:S(2)}) collective-permute-start(f32[32768]{0:T(1024)S(1)} %maximum_select_fusion.4), channel_id=1, source_target_pairs={{0,1},{1,0},{2,3},{3,2},{4,5},{5,4},{6,7},{7,6},{8,9},{9,8},{10,11... | collective-permute-start | bytes 393224 | tf_op jit(solution)/shard_map/ppermute | solution.py:45
  107.3 4.7 %collective-permute-start.7 = (f32[4096]{0:T(1024)S(1)}, f32[4096]{0:T(1024)S(1)}, u32[]{:S(2)}, u32[]{:S(2)}) collective-permute-start(f32[4096]{0:T(1024)S(1)} %slice_select_fusion.12), channel_id=1, source_target_pairs={{0,8},{4,12},{8,0},{12,4},{1,9},{5,13},{9,1},{13,5},{2,10},{6,14},... | collective-permute-start | bytes 49160 | tf_op jit(solution)/shard_map/ppermute | solution.py:42
  112.1 4.6 %collective-permute-start.8 = (f32[4096]{0:T(1024)S(1)}, f32[4096]{0:T(1024)S(1)}, u32[]{:S(2)}, u32[]{:S(2)}) collective-permute-start(f32[4096]{0:T(1024)S(1)} %select_add_fusion.6), channel_id=1, source_target_pairs={{0,8},{4,12},{8,0},{12,4},{1,9},{5,13},{9,1},{13,5},{2,10},{6,14},... | collective-permute-start | bytes 49160 | tf_op jit(solution)/shard_map/ppermute | solution.py:45
  116.7 3.9 %collective-permute-start.9 = (f32[8192]{0:T(1024)S(1)}, f32[8192]{0:T(1024)S(1)}, u32[]{:S(2)}, u32[]{:S(2)}) collective-permute-start(f32[8192]{0:T(1024)S(1)} %maximum_select_fusion.12), channel_id=1, source_target_pairs={{0,4},{4,0},{8,12},{12,8},{1,5},{5,1},{9,13},{13,9},{2,6},{6,2},{1... | collective-permute-start | bytes 98312 | tf_op jit(solution)/shard_map/ppermute | solution.py:45
  120.6 4.3 %collective-permute-start.10 = (f32[16384]{0:T(1024)S(1)}, f32[16384]{0:T(1024)S(1)}, u32[]{:S(2)}, u32[]{:S(2)}) collective-permute-start(f32[16384]{0:T(1024)S(1)} %maximum_select_fusion.8), channel_id=1, source_target_pairs={{0,2},{1,3},{2,0},{3,1},{4,6},{5,7},{6,4},{7,5},{8,10},{9,11},{10,... | collective-permute-start | bytes 196616 | tf_op jit(solution)/shard_map/ppermute | solution.py:45
  125.0 1.4 %collective-permute-start.11 = (f32[32768]{0:T(1024)S(1)}, f32[32768]{0:T(1024)S(1)}, u32[]{:S(2)}, u32[]{:S(2)}) collective-permute-start(f32[32768]{0:T(1024)S(1)} %maximum_select_fusion.2), channel_id=1, source_target_pairs={{0,1},{1,0},{2,3},{3,2},{4,5},{5,4},{6,7},{7,6},{8,9},{9,8},{10,11... | collective-permute-start | bytes 393224 | tf_op jit(solution)/shard_map/ppermute | solution.py:45

commit v2 on v0

--- a/solution.py
+++ b/solution.py
@@ -21,6 +21,51 @@
     return block
 
 
+def tree_sum(blocks):
+    order = []
+    for _, axes in blocks:
+        for axis in axes:
+            if axis not in order:
+                order.append(axis)
+    steps = []
+    for axis in order:
+        bit = 1
+        while bit < lax.axis_size(axis):
+            steps.append((axis, bit))
+            bit *= 2
+    pieces = [block.reshape(-1) for block, _ in blocks]
+    done = []
+    for axis, bit in steps:
+        pairs = [(i, i ^ bit) for i in range(lax.axis_size(axis))]
+        upper = (lax.axis_index(axis) & bit) != 0
+        members = [n for n, (_, axes) in enumerate(blocks) if axis in axes]
+        keeps, sends = [], []
+        for n in members:
+            half = pieces[n].shape[0] // 2
+            low, high = pieces[n][:half], pieces[n][half:]
+            keeps.append(jnp.where(upper, high, low))
+            sends.append(jnp.where(upper, low, high))
+        got = lax.ppermute(jnp.concatenate(sends), axis, pairs)
+        offset = 0
+        for n, keep in zip(members, keeps):
+            pieces[n] = keep + got[offset : offset + keep.shape[0]]
+            offset += keep.shape[0]
+        done.append((axis, pairs, upper, members))
+    for axis, pairs, upper, members in reversed(done):
+        got = lax.ppermute(jnp.concatenate([pieces[n] for n in members]), axis, pairs)
+        offset = 0
+        for n in members:
+            size = pieces[n].shape[0]
+            other = got[offset : offset + size]
+            offset += size
+            pieces[n] = jnp.where(
+                upper,
+                jnp.concatenate([other, pieces[n]]),
+                jnp.concatenate([pieces[n], other]),
+            )
+    return [piece.reshape(block.shape) for piece, (block, _) in zip(pieces, blocks)]
+
+
 def silu_slope(values):
     sigma = jax.nn.sigmoid(values)
     return sigma * (1.0 + values * (1.0 - sigma))
@@ -99,7 +144,6 @@
     third_part = lax.dot_general(
         act_flat, third_delta, contract_tail, preferred_element_type=jnp.float32
     )
-    third_grad = lax.psum(third_part, ("grp", "sub")) * factor
     hidden_grad = (
         jnp.dot(third_weight, third_delta, preferred_element_type=jnp.float32)
         .astype(jnp.bfloat16)
@@ -115,7 +159,6 @@
     )
     kernel_part = diagonal_blocks(dense_grad)
     inner_grad = lax.all_to_all(inner_local, "grp", split_axis=1, concat_axis=0, tiled=True)
-    group_grad = lax.psum(kernel_part, "sub") * factor
     first_delta = (
         inner_grad.reshape(channels, -1).astype(jnp.float32) * silu_slope(first_pre)
     ).astype(jnp.bfloat16)
@@ -130,7 +173,12 @@
         .astype(jnp.bfloat16)
         .reshape(volume.shape)
     )
-    first_grad = lax.psum(first_part, ("grp", "sub")) * factor
+    first_sum, third_sum, group_sum = tree_sum(
+        [(first_part, ("sub", "grp")), (third_part, ("sub", "grp")), (kernel_part, ("sub",))]
+    )
+    first_grad = first_sum * factor
+    third_grad = third_sum * factor
+    group_grad = group_sum * factor
     return (block_output, volume_grad, first_grad, group_grad, third_grad)
 
 

time: 195 us -> 123 us (0.63)
  waiting for transfers between devices: 109 us -> 38.6 us
  blocking collectives: 14.4 us -> 0 us
  local copies, waits for them, and re-layouts: 13.7 us -> 27.6 us
  between operations: 14.5 us -> 1.7 us
  starting transfers between devices: 23.3 us -> 34.7 us
    psum x1 -> x0, waiting for transfers between devices: 89.5 us -> none  [per_device(): first_grad = lax.psum(first_part, ('grp', 'sub')) * factor]
    ppermute x0 -> x8, waiting for transfers between devices: none -> 20.4 us  [the longest x4 11.4 us: tree_sum(): lax.ppermute(jnp.concatenate([pieces[n] for n in members]), axis, pairs)]
    psum x1 -> x0, blocking collectives: 14.4 us -> none  [per_device(): group_grad = lax.psum(kernel_part, 'sub') * factor]
    ppermute x0 -> x8, starting transfers between devices: none -> 10.9 us  [the longest x4 6.63 us: tree_sum(): got = lax.ppermute(jnp.concatenate(sends), axis, pairs)]
    select_n x0 -> x8, local copies, waits for them, and re-layouts: none -> 6.57 us  [the longest x4 3.29 us: tree_sum(): keeps.append(jnp.where(upper, high, low))]
    slice x0 -> x17, local copies, waits for them, and re-layouts: none -> 3.34 us  [the longest x5 3.18 us: tree_sum(): pieces[n] = keep + got[offset:offset + keep.shape[0]]]
    concatenate x0 -> x8, local copies, waits for them, and re-layouts: none -> 3.24 us  [tree_sum(): jnp.concatenate([other, pieces[n]])]
    ppermute x2, waiting for transfers between devices: 6.11 us -> 3.45 us  [padded_2(): lax.ppermute(lax.slice_in_dim(block, 0, width, axis=dim), axis, backward)]
  transfers between devices with their start and end apart: 9 -> 16, of which waited for: 6 -> 13; matrix products, arithmetic and copies ran while one was open for 8% -> 17% of each run, Pallas kernels for 0% -> 0%
where the time goes in v2:
time: 123 us; the launch traced here: 122 us
  waiting for transfers between devices  38.6 us (31%)
  starting transfers between devices  34.7 us (28%)
  local copies, waits for them, and re-layouts  27.6 us (22%)
  matrix products  15.4 us (13%)
  other arithmetic  4.26 us (3%)
  between operations  1.7 us (1%)
    ppermute x4, waiting for transfers between devices, tree_sum(): lax.ppermute(jnp.concatenate([pieces[n] for n in members]), axis, pairs)  11.4 us
    ppermute x4, waiting for transfers between devices, tree_sum(): got = lax.ppermute(jnp.concatenate(sends), axis, pairs)  8.99 us
    conv_general_dilated x1, matrix products, weight_grad(): lax.conv_general_dilated(padded[None], deltas[None], (1, 1, 1), 'VALID',...  8.32 us
    ppermute x4, starting transfers between devices, tree_sum(): got = lax.ppermute(jnp.concatenate(sends), axis, pairs)  6.63 us
    all_to_all x1, starting transfers between devices, per_device(): lax.all_to_all(first_act, 'grp', split_axis=0, concat_axis=1, tiled=True)  6.31 us
    unnamed x47, local copies, waits for them, and re-layouts  6.28 us
    all_to_all x1, waiting for transfers between devices, per_device(): lax.all_to_all(first_act, 'grp', split_axis=0, concat_axis=1, tiled=True)  5.98 us
    all_to_all x1, waiting for transfers between devices, per_device(): lax.all_to_all(hidden_grad, 'grp', split_axis=0, concat_axis=1, tiled=True)  4.43 us
  transfers between devices with their start and end apart: 16, of which 13 were waited for; matrix products, arithmetic and copies ran while one was open for 17% of the time, Pallas kernels for 0%

profile of v2, /device:TPU:0, one launch (start us, length us, event | category | flops | bytes accessed | tf_op | source)
XLA Modules:
  0.0 122.3 jit_solution(1487297698935103734)
XLA Ops:
  0.6 1.0 copy.84
  1.7 1.9 %multiply_convert_fusion.2 = (bf16[256,256]{0,1:T(8,128)(2,1)S(1)}, f32[256,256]{0,1:T(8,128)}) fusion(bf16[256,256]{0,1:T(8,128)(2,1)S(1)} %bitcast.160, bf16[256,256]{1,0:T(8,128)(2,1)} %param.7), kind=kOutput, calls=%fused_computation.59 | convolution fusion | flops 33882112 | bytes 655360 | tf_op jit(solution)/shard_map/dot_general | solution.py:123
  4.4 6.3 %all-to-all-start = ((bf16[256,1,2,128]{3,2,1,0:T(2,128)(2,1)}), bf16[256,1,2,128]{3,2,1,0:T(2,128)(2,1)S(1)}, u32[]{:S(2)}, u32[]{:S(2)}) async-start(bf16[256,1,2,128]{3,2,1,0:T(2,128)(2,1)} %copy.85), calls=%async_computation | async-start | bytes 262144 | tf_op jit(solution)/shard_map/all_to_all | solution.py:131
  10.8 6.0 %all-to-all-done = bf16[256,1,2,128]{3,2,1,0:T(2,128)(2,1)S(1)} async-done(((bf16[256,1,2,128]{3,2,1,0:T(2,128)(2,1)}), bf16[256,1,2,128]{3,2,1,0:T(2,128)(2,1)S(1)}, u32[]{:S(2)}, u32[]{:S(2)}) %all-to-all-start) | async-done | bytes 131104 | tf_op jit(solution)/shard_map/all_to_all | solution.py:131
  16.8 1.3 %collective-permute-start = (bf16[64,4,1,128]{3,0,1,2:T(8,128)(2,1)S(1)}, bf16[64,4,1,128]{3,0,1,2:T(8,128)(2,1)S(1)}, u32[]{:S(2)}, u32[]{:S(2)}) collective-permute-start(bf16[64,4,1,128]{3,0,1,2:T(8,128)(2,1)S(1)} %get-tuple-element.47), channel_id=1, source_target_pairs={{0,1},{1,2},{2,3},{4,5},{5,6},{6,7},{8,9},{9,10},{10,11},{12,13},{... | collective-permute-start | bytes 196616 | tf_op jit(solution)/shard_map/ppermute | solution.py:16
  18.1 1.3 %collective-permute-start.1 = (bf16[64,4,1,128]{3,0,1,2:T(8,128)(2,1)S(1)}, bf16[64,4,1,128]{3,0,1,2:T(8,128)(2,1)S(1)}, u32[]{:S(2)}, u32[]{:S(2)}) collective-permute-start(bf16[64,4,1,128]{3,0,1,2:T(8,128)(2,1)S(1)} %get-tuple-element.48), channel_id=1, source_target_pairs={{1,0},{2,1},{3,2},{5,4},{6,5},{7,6},{9,8},{10,9},{11,10},{13,12},{... | collective-permute-start | bytes 196616 | tf_op jit(solution)/shard_map/ppermute | solution.py:19
  19.5 3.4 %collective-permute-done.1 = bf16[64,4,1,128]{3,0,1,2:T(8,128)(2,1)S(1)} collective-permute-done((bf16[64,4,1,128]{3,0,1,2:T(8,128)(2,1)S(1)}, bf16[64,4,1,128]{3,0,1,2:T(8,128)(2,1)S(1)}, u32[]{:S(2)}, u32[]{:S(2)}) %collective-permute-start.1) | collective-permute-done | bytes 65568 | tf_op jit(solution)/shard_map/ppermute | solution.py:19
  24.0 1.2 %add_multiply_fusion = (f32[4,2,8,17,64]{4,2,3,1,0:T(8,128)S(1)}, f32[4,2,8,17,64]{4,2,3,1,0:T(8,128)S(1)}) fusion(bf16[64,64]{0,1:T(8,128)(2,1)S(1)} %compare_convert_fusion, bf16[64,8,3,3,3]{0,1,4,3,2:T(8,128)(2,1)S(1)} %constant_dynamic-slice_fusion, bf16[64,4,4,1,7,2]{0,4,5,2,1,3:T(8,128)(2,1)S(1)} %slice.265, ...), kind=kOutput, calls=%fused_computation.27 | convolution fusion | flops 202473472 | bytes 900232 | tf_op jit(solution)/shard_map/conv_general_dilated | solution.py:76
  26.6 3.3 %all-to-all-start.1 = ((bf16[64,4,2,128]{3,0,2,1:T(8,128)(2,1)}), bf16[64,4,2,128]{3,0,2,1:T(8,128)(2,1)S(1)}, u32[]{:S(2)}, u32[]{:S(2)}) async-start(bf16[64,4,2,128]{3,0,2,1:T(8,128)(2,1)} %fusion.30), calls=%async_computation.1 | async-start | bytes 262144 | tf_op jit(solution)/shard_map/all_to_all | solution.py:135
  29.9 0.8 copy.93
  31.1 0.9 copy.131
  32.2 1.7 %copy.112 = bf16[1,64,6,4,130]{1,0,4,3,2:T(2,128)(2,1)S(1)} copy(bf16[1,64,6,4,130]{4,1,2,3,0:T(8,128)(2,1)S(1)} %pad_bitcast_fusion) | data formatting | bytes 798720 | tf_op jit(solution)/shard_map/broadcast_in_dim | solution.py:106
  33.9 1.9 %all-to-all-done.1 = bf16[64,4,2,128]{3,0,2,1:T(8,128)(2,1)S(1)} async-done(((bf16[64,4,2,128]{3,0,2,1:T(8,128)(2,1)}), bf16[64,4,2,128]{3,0,2,1:T(8,128)(2,1)S(1)}, u32[]{:S(2)}, u32[]{:S(2)}) %all-to-all-start.1) | async-done | bytes 131104 | tf_op jit(solution)/shard_map/all_to_all | solution.py:135
  36.0 1.0 fusion.26
  37.4 0.8 copy.94
  38.2 3.5 %all-to-all-start.2 = ((bf16[256,1,2,128]{3,2,1,0:T(2,128)(2,1)}), bf16[256,1,2,128]{3,2,1,0:T(2,128)(2,1)S(1)}, u32[]{:S(2)}, u32[]{:S(2)}) async-start(bf16[256,1,2,128]{3,2,1,0:T(2,128)(2,1)} %copy.94), calls=%async_computation.2 | async-start | bytes 262144 | tf_op jit(solution)/shard_map/all_to_all | solution.py:152
  43.1 4.4 %all-to-all-done.2 = bf16[256,1,2,128]{3,2,1,0:T(2,128)(2,1)S(1)} async-done(((bf16[256,1,2,128]{3,2,1,0:T(2,128)(2,1)}), bf16[256,1,2,128]{3,2,1,0:T(2,128)(2,1)S(1)}, u32[]{:S(2)}, u32[]{:S(2)}) %all-to-all-start.2) | async-done | bytes 131104 | tf_op jit(solution)/shard_map/all_to_all | solution.py:152
  47.7 3.1 %collective-permute-start.2 = (bf16[64,4,1,128]{3,0,2,1:T(8,128)(2,1)S(1)}, bf16[64,4,1,128]{3,0,2,1:T(8,128)(2,1)S(1)}, u32[]{:S(2)}, u32[]{:S(2)}) collective-permute-start(bf16[64,4,1,128]{3,0,2,1:T(8,128)(2,1)S(1)} %get-tuple-element.45), channel_id=1, source_target_pairs={{0,1},{1,2},{2,3},{4,5},{5,6},{6,7},{8,9},{9,10},{10,11},{12,13},{... | collective-permute-start | bytes 196616 | tf_op jit(solution)/shard_map/ppermute | solution.py:16
  50.9 1.5 %collective-permute-start.3 = (bf16[64,4,1,128]{3,0,2,1:T(8,128)(2,1)S(1)}, bf16[64,4,1,128]{3,0,2,1:T(8,128)(2,1)S(1)}, u32[]{:S(2)}, u32[]{:S(2)}) collective-permute-start(bf16[64,4,1,128]{3,0,2,1:T(8,128)(2,1)S(1)} %get-tuple-element.46), channel_id=1, source_target_pairs={{1,0},{2,1},{3,2},{5,4},{6,5},{7,6},{9,8},{10,9},{11,10},{13,12},{... | collective-permute-start | bytes 196616 | tf_op jit(solution)/shard_map/ppermute | solution.py:19
  52.8 8.3 %fusion.3 = f32[8,64,3,3,3]{1,0,4,3,2:T(8,128)S(1)} fusion(bf16[1,64,6,4,130]{1,0,4,3,2:T(2,128)(2,1)S(1)} %copy.112, bf16[1,64,4,2,128]{1,0,4,3,2:T(2,128)(2,1)S(1)} %copy.113, f32[8,64]{1,0:T(8,128)S(1)} %fusion.48), kind=kOutput, calls=%fused_computation.7 | convolution fusion | flops 226699776 | bytes 587776 | tf_op jit(solution)/shard_map/conv_general_dilated | solution.py:105
  62.3 2.1 %fusion.4 = bf16[4,2,8,17,64]{4,2,3,1,0:T(8,128)(2,1)S(1)} fusion(bf16[64,4,4,1,7,2]{0,4,5,2,1,3:T(8,128)(2,1)S(1)} %slice.269, bf16[64,4,4,1,8,17]{0,4,5,2,1,3:T(8,128)(2,1)S(1)} %copy.99, pred[8,17]{0,1:T(8,128)(4,1)S(1)} %copy-done.17, bf16[64,64]{0,1:T(8,128)(2,1)S(1)} %copy-done.16, bf16[64,8,3,3,3]{0,1,4,3,2:T(8,128)(2,1)S(1)} %copy-done.13), kind=kOutput, calls=%fused_computation.8 | convolution fusion | flops 202055680 | bytes 482440 | tf_op jit(solution)/shard_map/conv_general_dilated | solution.py:76
  64.9 0.8 copy.101
  65.6 3.5 %all-to-all-start.3 = ((bf16[64,4,2,128]{3,0,2,1:T(8,128)(2,1)}), bf16[64,4,2,128]{3,0,2,1:T(8,128)(2,1)S(1)}, u32[]{:S(2)}, u32[]{:S(2)}) async-start(bf16[64,4,2,128]{3,0,2,1:T(8,128)(2,1)} %copy.101), calls=%async_computation.3 | async-start | bytes 262144 | tf_op jit(solution)/shard_map/all_to_all | solution.py:161
  69.3 2.1 %copy.114 = f32[32,8,3,3,3]{4,3,2,1,0:T(4,128)S(1)} copy(f32[32,8,3,3,3]{0,1,4,3,2:T(8,128)S(1)} %slice_select_fusion.6) | data formatting | bytes 55296 | tf_op jit(solution)/shard_map/jit(_where)/select_n | solution.py:47
  71.4 1.0 select_n.254
  72.4 2.5 %all-to-all-done.3 = bf16[64,4,2,128]{3,0,2,1:T(8,128)(2,1)S(1)} async-done(((bf16[64,4,2,128]{3,0,2,1:T(8,128)(2,1)}), bf16[64,4,2,128]{3,0,2,1:T(8,128)(2,1)S(1)}, u32[]{:S(2)}, u32[]{:S(2)}) %all-to-all-start.3) | async-done | bytes 131104 | tf_op jit(solution)/shard_map/all_to_all | solution.py:161
  76.4 1.3 %collective-permute-start.4 = (f32[72448]{0:T(1024)S(1)}, f32[72448]{0:T(1024)S(1)}, u32[]{:S(2)}, u32[]{:S(2)}) collective-permute-start(f32[72448]{0:T(1024)S(1)} %pad_maximum_fusion), channel_id=1, source_target_pairs={{0,1},{1,0},{2,3},{3,2},{4,5},{5,4},{6,7},{7,6},{8,9},{9,8},{10,11... | collective-permute-start | bytes 869384 | tf_op jit(solution)/shard_map/ppermute | solution.py:48
  78.1 0.8 collective-permute-done.4
  79.0 0.8 slice.250
  79.8 1.2 %copy.117 = f32[32,8,3,3,3]{0,1,4,3,2:T(8,128)S(1)} copy(f32[32,8,3,3,3]{4,3,2,1,0:T(4,128)S(1)} %slice.250) | data formatting | bytes 55296 | tf_op jit(solution)/shard_map/slice | solution.py:51
  81.2 2.1 %copy.116 = f32[32,8,3,3,3]{4,3,2,1,0:T(4,128)S(1)} copy(f32[32,8,3,3,3]{0,1,4,3,2:T(8,128)S(1)} %get-tuple-element.26) | data formatting | bytes 55296 | tf_op jit(solution)/shard_map/jit(_where)/select_n | solution.py:46
  83.3 1.0 select_n.262
  84.4 3.1 %collective-permute-start.5 = (f32[36224]{0:T(1024)S(1)}, f32[36224]{0:T(1024)S(1)}, u32[]{:S(2)}, u32[]{:S(2)}) collective-permute-start(f32[36224]{0:T(1024)S(1)} %pad_maximum_fusion.3), channel_id=1, source_target_pairs={{0,2},{1,3},{2,0},{3,1},{4,6},{5,7},{6,4},{7,5},{8,10},{9,11},{10,... | collective-permute-start | bytes 434696 | tf_op jit(solution)/shard_map/ppermute | solution.py:48
  88.2 3.4 %collective-permute-done.5 = f32[36224]{0:T(1024)S(1)} collective-permute-done((f32[36224]{0:T(1024)S(1)}, f32[36224]{0:T(1024)S(1)}, u32[]{:S(2)}, u32[]{:S(2)}) %collective-permute-start.5) | collective-permute-done | bytes 144928 | tf_op jit(solution)/shard_map/ppermute | solution.py:48
  91.6 1.3 %collective-permute-start.6 = (f32[16384]{0:T(1024)S(1)}, f32[16384]{0:T(1024)S(1)}, u32[]{:S(2)}, u32[]{:S(2)}) collective-permute-start(f32[16384]{0:T(1024)S(1)} %pad_maximum_fusion.8), channel_id=1, source_target_pairs={{0,4},{4,0},{8,12},{12,8},{1,5},{5,1},{9,13},{13,9},{2,6},{6,2},{1... | collective-permute-start | bytes 196616 | tf_op jit(solution)/shard_map/ppermute | solution.py:48
  94.0 2.0 %collective-permute-done.6 = f32[16384]{0:T(1024)S(1)} collective-permute-done((f32[16384]{0:T(1024)S(1)}, f32[16384]{0:T(1024)S(1)}, u32[]{:S(2)}, u32[]{:S(2)}) %collective-permute-start.6) | collective-permute-done | bytes 65568 | tf_op jit(solution)/shard_map/ppermute | solution.py:48
  96.0 1.0 collective-permute-start.7
  98.1 2.8 %collective-permute-done.7 = f32[8192]{0:T(1024)S(1)} collective-permute-done((f32[8192]{0:T(1024)S(1)}, f32[8192]{0:T(1024)S(1)}, u32[]{:S(2)}, u32[]{:S(2)}) %collective-permute-start.7) | collective-permute-done | bytes 32800 | tf_op jit(solution)/shard_map/ppermute | solution.py:48
  100.9 1.1 collective-permute-start.8
  102.1 3.7 %collective-permute-done.8 = f32[8192]{0:T(1024)S(1)} collective-permute-done((f32[8192]{0:T(1024)S(1)}, f32[8192]{0:T(1024)S(1)}, u32[]{:S(2)}, u32[]{:S(2)}) %collective-permute-start.8) | collective-permute-done | bytes 32800 | tf_op jit(solution)/shard_map/ppermute | solution.py:55
  105.9 1.3 %collective-permute-start.9 = (f32[16384]{0:T(1024)S(1)}, f32[16384]{0:T(1024)S(1)}, u32[]{:S(2)}, u32[]{:S(2)}) collective-permute-start(f32[16384]{0:T(1024)S(1)} %pad_maximum_fusion.6), channel_id=1, source_target_pairs={{0,4},{4,0},{8,12},{12,8},{1,5},{5,1},{9,13},{13,9},{2,6},{6,2},{1... | collective-permute-start | bytes 196616 | tf_op jit(solution)/shard_map/ppermute | solution.py:55
  107.2 3.0 %collective-permute-done.9 = f32[16384]{0:T(1024)S(1)} collective-permute-done((f32[16384]{0:T(1024)S(1)}, f32[16384]{0:T(1024)S(1)}, u32[]{:S(2)}, u32[]{:S(2)}) %collective-permute-start.9) | collective-permute-done | bytes 65568 | tf_op jit(solution)/shard_map/ppermute | solution.py:55
  110.3 1.8 %collective-permute-start.10 = (f32[36224]{0:T(1024)S(1)}, f32[36224]{0:T(1024)S(1)}, u32[]{:S(2)}, u32[]{:S(2)}) collective-permute-start(f32[36224]{0:T(1024)S(1)} %pad_maximum_fusion.4), channel_id=1, source_target_pairs={{0,2},{1,3},{2,0},{3,1},{4,6},{5,7},{6,4},{7,5},{8,10},{9,11},{10,... | collective-permute-start | bytes 434696 | tf_op jit(solution)/shard_map/ppermute | solution.py:55
  112.1 3.4 %collective-permute-done.10 = f32[36224]{0:T(1024)S(1)} collective-permute-done((f32[36224]{0:T(1024)S(1)}, f32[36224]{0:T(1024)S(1)}, u32[]{:S(2)}, u32[]{:S(2)}) %collective-permute-start.10) | collective-permute-done | bytes 144928 | tf_op jit(solution)/shard_map/ppermute | solution.py:55
  117.0 1.4 %collective-permute-done.11 = f32[72448]{0:T(1024)S(1)} collective-permute-done((f32[72448]{0:T(1024)S(1)}, f32[72448]{0:T(1024)S(1)}, u32[]{:S(2)}, u32[]{:S(2)}) %collective-permute-start.11) | collective-permute-done | bytes 289824 | tf_op jit(solution)/shard_map/ppermute | solution.py:55
  118.4 0.8 concatenate.184
  119.3 1.2 %copy.121 = f32[32,8,3,3,3]{0,1,4,3,2:T(8,128)S(1)} copy(f32[32,8,3,3,3]{4,3,2,1,0:T(4,128)S(1)} %concatenate.184) | data formatting | bytes 55296 | tf_op jit(solution)/shard_map/concatenate | solution.py:63
  121.4 0.8 fusion.22
  (152 shorter events, 15.6 us)
Async XLA Ops:
  0.6 35.3 %copy-start = (bf16[256,256]{1,0:T(8,128)(2,1)S(1)}, bf16[256,256]{1,0:T(8,128)(2,1)}, u32[]{:S(2)}) copy-start(bf16[256,256]{1,0:T(8,128)(2,1)} %param.9) | copy-start | bytes 393220
  1.7 2.7 %copy-start.3 = (bf16[256,1,2,128]{0,3,2,1:T(8,128)(2,1)}, bf16[256,1,2,128]{0,3,2,1:T(8,128)(2,1)S(1)}, u32[]{:S(2)}) copy-start(bf16[256,1,2,128]{0,3,2,1:T(8,128)(2,1)S(1)} %copy.84) | copy-start | bytes 393220
  1.7 17.7 %copy-start.14 = (bf16[256,8,3,3,3]{0,1,4,3,2:T(8,128)(2,1)S(1)}, bf16[256,8,3,3,3]{0,1,4,3,2:T(8,128)(2,1)}, u32[]{:S(2)}) copy-start(bf16[256,8,3,3,3]{0,1,4,3,2:T(8,128)(2,1)} %param.8) | copy-start | bytes 331780
  4.4 12.4 %all-to-all-start = ((bf16[256,1,2,128]{3,2,1,0:T(2,128)(2,1)}), bf16[256,1,2,128]{3,2,1,0:T(2,128)(2,1)S(1)}, u32[]{:S(2)}, u32[]{:S(2)}) async-start(bf16[256,1,2,128]{3,2,1,0:T(2,128)(2,1)} %copy.85), calls=%async_computation | async-start | bytes 262144 | tf_op jit(solution)/shard_map/all_to_all | solution.py:131
  10.8 13.0 %copy-start.15 = (bf16[64,64]{0,1:T(8,128)(2,1)}, bf16[64,64]{0,1:T(8,128)(2,1)S(1)}, u32[]{:S(2)}) copy-start(bf16[64,64]{0,1:T(8,128)(2,1)S(1)} %compare_convert_fusion) | copy-start | bytes 24580
  16.8 2.7 %collective-permute-start = (bf16[64,4,1,128]{3,0,1,2:T(8,128)(2,1)S(1)}, bf16[64,4,1,128]{3,0,1,2:T(8,128)(2,1)S(1)}, u32[]{:S(2)}, u32[]{:S(2)}) collective-permute-start(bf16[64,4,1,128]{3,0,1,2:T(8,128)(2,1)S(1)} %get-tuple-element.47), channel_id=1, source_target_pairs={{0,1},{1,2},{2,3},{4,5},{5,6},{6,7},{8,9},{9,10},{10,11},{12,13},{... | collective-permute-start | bytes 196616 | tf_op jit(solution)/shard_map/ppermute | solution.py:16
  18.1 4.9 %collective-permute-start.1 = (bf16[64,4,1,128]{3,0,1,2:T(8,128)(2,1)S(1)}, bf16[64,4,1,128]{3,0,1,2:T(8,128)(2,1)S(1)}, u32[]{:S(2)}, u32[]{:S(2)}) collective-permute-start(bf16[64,4,1,128]{3,0,1,2:T(8,128)(2,1)S(1)} %get-tuple-element.48), channel_id=1, source_target_pairs={{1,0},{2,1},{3,2},{5,4},{6,5},{7,6},{9,8},{10,9},{11,10},{13,12},{... | collective-permute-start | bytes 196616 | tf_op jit(solution)/shard_map/ppermute | solution.py:19
  19.5 4.2 %copy-start.12 = (bf16[64,8,3,3,3]{0,1,4,3,2:T(8,128)(2,1)}, bf16[64,8,3,3,3]{0,1,4,3,2:T(8,128)(2,1)S(1)}, u32[]{:S(2)}) copy-start(bf16[64,8,3,3,3]{0,1,4,3,2:T(8,128)(2,1)S(1)} %constant_dynamic-slice_fusion) | copy-start | bytes 82948
  23.3 0.7 copy-start.17
  25.6 4.3 %copy-start.9 = (bf16[256,1,2,128]{3,2,1,0:T(2,128)(2,1)S(1)}, bf16[256,1,2,128]{3,2,1,0:T(2,128)(2,1)}, u32[]{:S(2)}) copy-start(bf16[256,1,2,128]{3,2,1,0:T(2,128)(2,1)} %param.6) | copy-start | bytes 393220
  26.6 9.2 %all-to-all-start.1 = ((bf16[64,4,2,128]{3,0,2,1:T(8,128)(2,1)}), bf16[64,4,2,128]{3,0,2,1:T(8,128)(2,1)S(1)}, u32[]{:S(2)}, u32[]{:S(2)}) async-start(bf16[64,4,2,128]{3,0,2,1:T(8,128)(2,1)} %fusion.30), calls=%async_computation.1 | async-start | bytes 262144 | tf_op jit(solution)/shard_map/all_to_all | solution.py:135
  32.2 3.8 %copy-start.4 = (bf16[256,1,2,128]{0,3,2,1:T(8,128)(2,1)S(1)}, bf16[256,1,2,128]{0,3,2,1:T(8,128)(2,1)}, u32[]{:S(2)}) copy-start(bf16[256,1,2,128]{0,3,2,1:T(8,128)(2,1)} %copy-done.3) | copy-start | bytes 393220
  32.2 3.8 %copy-start.7 = (f32[256,1,2,128]{0,3,2,1:T(8,128)S(1)}, f32[256,1,2,128]{0,3,2,1:T(8,128)}, u32[]{:S(2)}) copy-start(f32[256,1,2,128]{0,3,2,1:T(8,128)} %copy.93) | copy-start | bytes 786436
  38.2 14.2 %copy-start.1 = (f32[4,2,1,128,64]{3,4,1,0,2:T(8,128)S(1)}, f32[4,2,1,128,64]{3,4,1,0,2:T(8,128)}, u32[]{:S(2)}) copy-start(f32[4,2,1,128,64]{3,4,1,0,2:T(8,128)} %copy.131) | copy-start | bytes 786436
  38.2 9.4 %all-to-all-start.2 = ((bf16[256,1,2,128]{3,2,1,0:T(2,128)(2,1)}), bf16[256,1,2,128]{3,2,1,0:T(2,128)(2,1)S(1)}, u32[]{:S(2)}, u32[]{:S(2)}) async-start(bf16[256,1,2,128]{3,2,1,0:T(2,128)(2,1)} %copy.94), calls=%async_computation.2 | async-start | bytes 262144 | tf_op jit(solution)/shard_map/all_to_all | solution.py:152
  47.7 13.4 %collective-permute-start.2 = (bf16[64,4,1,128]{3,0,2,1:T(8,128)(2,1)S(1)}, bf16[64,4,1,128]{3,0,2,1:T(8,128)(2,1)S(1)}, u32[]{:S(2)}, u32[]{:S(2)}) collective-permute-start(bf16[64,4,1,128]{3,0,2,1:T(8,128)(2,1)S(1)} %get-tuple-element.45), channel_id=1, source_target_pairs={{0,1},{1,2},{2,3},{4,5},{5,6},{6,7},{8,9},{9,10},{10,11},{12,13},{... | collective-permute-start | bytes 196616 | tf_op jit(solution)/shard_map/ppermute | solution.py:16
  50.9 10.3 %collective-permute-start.3 = (bf16[64,4,1,128]{3,0,2,1:T(8,128)(2,1)S(1)}, bf16[64,4,1,128]{3,0,2,1:T(8,128)(2,1)S(1)}, u32[]{:S(2)}, u32[]{:S(2)}) collective-permute-start(bf16[64,4,1,128]{3,0,2,1:T(8,128)(2,1)S(1)} %get-tuple-element.46), channel_id=1, source_target_pairs={{1,0},{2,1},{3,2},{5,4},{6,5},{7,6},{9,8},{10,9},{11,10},{13,12},{... | collective-permute-start | bytes 196616 | tf_op jit(solution)/shard_map/ppermute | solution.py:19
  61.5 0.8 copy-start.13
  61.5 0.8 copy-start.16
  65.6 9.3 %all-to-all-start.3 = ((bf16[64,4,2,128]{3,0,2,1:T(8,128)(2,1)}), bf16[64,4,2,128]{3,0,2,1:T(8,128)(2,1)S(1)}, u32[]{:S(2)}, u32[]{:S(2)}) async-start(bf16[64,4,2,128]{3,0,2,1:T(8,128)(2,1)} %copy.101), calls=%async_computation.3 | async-start | bytes 262144 | tf_op jit(solution)/shard_map/all_to_all | solution.py:161
  72.4 3.1 %copy-start.8 = (f32[256,256]{0,1:T(8,128)S(1)}, f32[256,256]{0,1:T(8,128)}, u32[]{:S(2)}) copy-start(f32[256,256]{0,1:T(8,128)} %get-tuple-element.58) | copy-start | bytes 786436
  72.4 3.2 %copy-start.5 = (bf16[256,1,2,128]{0,3,2,1:T(8,128)(2,1)S(1)}, bf16[256,1,2,128]{0,3,2,1:T(8,128)(2,1)}, u32[]{:S(2)}) copy-start(bf16[256,1,2,128]{0,3,2,1:T(8,128)(2,1)} %copy-done.3) | copy-start | bytes 393220
  75.5 0.9 copy-start.6
  75.7 2.0 %copy-start.2 = (f32[128,256]{0,1:T(8,128)S(1)}, f32[128,256]{0,1:T(8,128)}, u32[]{:S(2)}) copy-start(f32[128,256]{0,1:T(8,128)} %get-tuple-element.33) | copy-start | bytes 393220
  76.4 2.5 %collective-permute-start.4 = (f32[72448]{0:T(1024)S(1)}, f32[72448]{0:T(1024)S(1)}, u32[]{:S(2)}, u32[]{:S(2)}) collective-permute-start(f32[72448]{0:T(1024)S(1)} %pad_maximum_fusion), channel_id=1, source_target_pairs={{0,1},{1,0},{2,3},{3,2},{4,5},{5,4},{6,7},{7,6},{8,9},{9,8},{10,11... | collective-permute-start | bytes 869384 | tf_op jit(solution)/shard_map/ppermute | solution.py:48
  83.3 4.1 %copy-start.10 = (bf16[256,256]{0,1:T(8,128)(2,1)S(1)}, bf16[256,256]{0,1:T(8,128)(2,1)}, u32[]{:S(2)}) copy-start(bf16[256,256]{0,1:T(8,128)(2,1)} %get-tuple-element.38) | copy-start | bytes 393220
  83.3 9.7 %copy-start.11 = (bf16[256,256]{1,0:T(8,128)(2,1)S(1)}, bf16[256,256]{1,0:T(8,128)(2,1)}, u32[]{:S(2)}) copy-start(bf16[256,256]{1,0:T(8,128)(2,1)} %param.7) | copy-start | bytes 393220
  84.4 7.2 %collective-permute-start.5 = (f32[36224]{0:T(1024)S(1)}, f32[36224]{0:T(1024)S(1)}, u32[]{:S(2)}, u32[]{:S(2)}) collective-permute-start(f32[36224]{0:T(1024)S(1)} %pad_maximum_fusion.3), channel_id=1, source_target_pairs={{0,2},{1,3},{2,0},{3,1},{4,6},{5,7},{6,4},{7,5},{8,10},{9,11},{10,... | collective-permute-start | bytes 434696 | tf_op jit(solution)/shard_map/ppermute | solution.py:48
  91.6 4.3 %collective-permute-start.6 = (f32[16384]{0:T(1024)S(1)}, f32[16384]{0:T(1024)S(1)}, u32[]{:S(2)}, u32[]{:S(2)}) collective-permute-start(f32[16384]{0:T(1024)S(1)} %pad_maximum_fusion.8), channel_id=1, source_target_pairs={{0,4},{4,0},{8,12},{12,8},{1,5},{5,1},{9,13},{13,9},{2,6},{6,2},{1... | collective-permute-start | bytes 196616 | tf_op jit(solution)/shard_map/ppermute | solution.py:48
  96.0 4.9 %collective-permute-start.7 = (f32[8192]{0:T(1024)S(1)}, f32[8192]{0:T(1024)S(1)}, u32[]{:S(2)}, u32[]{:S(2)}) collective-permute-start(f32[8192]{0:T(1024)S(1)} %pad_maximum_fusion.12), channel_id=1, source_target_pairs={{0,8},{4,12},{8,0},{12,4},{1,9},{5,13},{9,1},{13,5},{2,10},{6,14},... | collective-permute-start | bytes 98312 | tf_op jit(solution)/shard_map/ppermute | solution.py:48
  100.9 4.9 %collective-permute-start.8 = (f32[8192]{0:T(1024)S(1)}, f32[8192]{0:T(1024)S(1)}, u32[]{:S(2)}, u32[]{:S(2)}) collective-permute-start(f32[8192]{0:T(1024)S(1)} %pad_maximum_fusion.10), channel_id=1, source_target_pairs={{0,8},{4,12},{8,0},{12,4},{1,9},{5,13},{9,1},{13,5},{2,10},{6,14},... | collective-permute-start | bytes 98312 | tf_op jit(solution)/shard_map/ppermute | solution.py:55
  105.9 4.3 %collective-permute-start.9 = (f32[16384]{0:T(1024)S(1)}, f32[16384]{0:T(1024)S(1)}, u32[]{:S(2)}, u32[]{:S(2)}) collective-permute-start(f32[16384]{0:T(1024)S(1)} %pad_maximum_fusion.6), channel_id=1, source_target_pairs={{0,4},{4,0},{8,12},{12,8},{1,5},{5,1},{9,13},{13,9},{2,6},{6,2},{1... | collective-permute-start | bytes 196616 | tf_op jit(solution)/shard_map/ppermute | solution.py:55
  110.3 5.2 %collective-permute-start.10 = (f32[36224]{0:T(1024)S(1)}, f32[36224]{0:T(1024)S(1)}, u32[]{:S(2)}, u32[]{:S(2)}) collective-permute-start(f32[36224]{0:T(1024)S(1)} %pad_maximum_fusion.4), channel_id=1, source_target_pairs={{0,2},{1,3},{2,0},{3,1},{4,6},{5,7},{6,4},{7,5},{8,10},{9,11},{10,... | collective-permute-start | bytes 434696 | tf_op jit(solution)/shard_map/ppermute | solution.py:55
  116.8 1.6 %collective-permute-start.11 = (f32[72448]{0:T(1024)S(1)}, f32[72448]{0:T(1024)S(1)}, u32[]{:S(2)}, u32[]{:S(2)}) collective-permute-start(f32[72448]{0:T(1024)S(1)} %pad_maximum_fusion.1), channel_id=1, source_target_pairs={{0,1},{1,0},{2,3},{3,2},{4,5},{5,4},{6,7},{7,6},{8,9},{9,8},{10,11... | collective-permute-start | bytes 869384 | tf_op jit(solution)/shard_map/ppermute | solution.py:55

commit v3 on v2

v3 whole, which is shorter than its diff:
```python
import itertools
import math

import jax
import jax.numpy as jnp
from jax import lax
from jax.sharding import PartitionSpec as P

GW = 8


def tree_sum(blocks, order):
    steps = []
    for axis in order:
        bit = lax.axis_size(axis) // 2
        while bit >= 1:
            steps.append((axis, bit))
            bit //= 2
    pieces = [block.reshape(-1) for block, _, _ in blocks]
    done = []
    for axis, bit in steps:
        pairs = [(i, i ^ bit) for i in range(lax.axis_size(axis))]
        upper = (lax.axis_index(axis) & bit) != 0
        members = [n for n, (_, axes, _) in enumerate(blocks) if axis in axes]
        keeps, sends = [], []
        for n in members:
            half = pieces[n].shape[0] // 2
            low, high = pieces[n][:half], pieces[n][half:]
            keeps.append(jnp.where(upper, high, low))
            sends.append(jnp.where(upper, low, high))
        got = lax.ppermute(jnp.concatenate(sends), axis, pairs)
        offset = 0
        for n, keep in zip(members, keeps):
            pieces[n] = keep + got[offset : offset + keep.shape[0]]
            offset += keep.shape[0]
        done.append((axis, pairs, upper))
    for axis, pairs, upper in reversed(done):
        members = [n for n, (_, _, axes) in enumerate(blocks) if axis in axes]
        if not members:
            continue
        got = lax.ppermute(jnp.concatenate([pieces[n] for n in members]), axis, pairs)
        offset = 0
        for n in members:
            size = pieces[n].shape[0]
            other = got[offset : offset + size]
            offset += size
            pieces[n] = jnp.where(
                upper,
                jnp.concatenate([other, pieces[n]]),
                jnp.concatenate([pieces[n], other]),
            )
    return pieces


def halo(block):
    for axis, dim in (("grp", 1), ("sub", 2)):
        count = lax.axis_size(axis)
        up = [(i, i + 1) for i in range(count - 1)]
        down = [(i + 1, i) for i in range(count - 1)]
        size = block.shape[dim]
        low = lax.ppermute(lax.slice_in_dim(block, size - 1, size, axis=dim), axis, up)
        high = lax.ppermute(lax.slice_in_dim(block, 0, 1, axis=dim), axis, down)
        block = jnp.concatenate([low, block, high], axis=dim)
    return jnp.pad(block, ((0, 0), (0, 0), (0, 0), (1, 1)))


def taps(ext, depth, height, width):
    channels = ext.shape[0]
    stacked = jnp.stack(
        [
            ext[:, dz : dz + depth, dy : dy + height, dx : dx + width]
            for dz, dy, dx in itertools.product(range(3), repeat=3)
        ],
        axis=1,
    )
    return stacked.reshape(channels // GW, GW * 27, depth * height * width)


def silu_slope(values):
    sigma = jax.nn.sigmoid(values)
    return sigma * (1.0 + values * (1.0 - sigma))


def per_device(volume, cotangent, first_weight, group_weight, third_weight):
    channels, depth, height, width = volume.shape
    groups = channels // GW
    flattened = volume.reshape(channels, -1)
    contract_lead = (((0,), (0,)), ((), ()))
    contract_tail = (((1,), (1,)), ((), ()))
    grouped_mm = (((2,), (1,)), ((0,), (0,)))
    grouped_nt = (((2,), (2,)), ((0,), (0,)))
    total_cells = depth * lax.axis_size("grp") * height * lax.axis_size("sub") * width
    factor = 1.0 / math.sqrt(total_cells)
    first_pre = lax.dot_general(
        first_weight, flattened, contract_lead, preferred_element_type=jnp.float32
    )
    first_act = jax.nn.silu(first_pre).astype(jnp.bfloat16).reshape(volume.shape)
    act_taps = taps(halo(first_act), depth, height, width)
    kernel = group_weight.reshape(groups, GW, GW * 27)
    group_pre = lax.dot_general(
        kernel, act_taps, grouped_mm, preferred_element_type=jnp.float32
    ).reshape(channels, -1)
    group_act = jax.nn.silu(group_pre).astype(jnp.bfloat16)
    summed = flattened.astype(jnp.float32) + lax.dot_general(
        third_weight, group_act, contract_lead, preferred_element_type=jnp.float32
    )
    block_output = jax.nn.silu(summed).astype(jnp.bfloat16).reshape(volume.shape)
    third_delta = (cotangent.reshape(channels, -1).astype(jnp.float32) * silu_slope(summed)).astype(
        jnp.bfloat16
    )
    third_part = lax.dot_general(
        group_act, third_delta, contract_tail, preferred_element_type=jnp.float32
    )
    hidden_grad = jnp.dot(third_weight, third_delta, preferred_element_type=jnp.float32).astype(
        jnp.bfloat16
    )
    group_delta = (hidden_grad.astype(jnp.float32) * silu_slope(group_pre)).astype(jnp.bfloat16)
    delta_taps = taps(halo(group_delta.reshape(volume.shape)), depth, height, width)
    flipped = (
        group_weight.reshape(groups, GW, GW, 3, 3, 3)
        .transpose(0, 2, 1, 3, 4, 5)[:, :, :, ::-1, ::-1, ::-1]
        .reshape(groups, GW, GW * 27)
    )
    inner_grad = (
        lax.dot_general(flipped, delta_taps, grouped_mm, preferred_element_type=jnp.float32)
        .reshape(channels, -1)
        .astype(jnp.bfloat16)
    )
    kernel_part = lax.dot_general(
        group_delta.reshape(groups, GW, -1), act_taps, grouped_nt, preferred_element_type=jnp.float32
    )
    first_delta = (inner_grad.astype(jnp.float32) * silu_slope(first_pre)).astype(jnp.bfloat16)
    first_part = lax.dot_general(
        flattened, first_delta, contract_tail, preferred_element_type=jnp.float32
    )
    volume_grad = (
        (
            third_delta.astype(jnp.float32)
            + jnp.dot(first_weight, first_delta, preferred_element_type=jnp.float32)
        )
        .astype(jnp.bfloat16)
        .reshape(volume.shape)
    )
    grp_count, sub_count = lax.axis_size("grp"), lax.axis_size("sub")
    kernel_laid = kernel_part.reshape(grp_count, sub_count, -1).transpose(1, 0, 2)
    first_sum, third_sum, group_sum = tree_sum(
        [
            (first_part, ("sub", "grp"), ("sub", "grp")),
            (third_part, ("sub", "grp"), ("sub", "grp")),
            (kernel_laid, ("sub", "grp"), ("sub",)),
        ],
        ("sub", "grp"),
    )
    first_grad = first_sum.reshape(first_part.shape) * factor
    third_grad = third_sum.reshape(third_part.shape) * factor
    group_grad = group_sum.reshape(channels // grp_count, GW, 3, 3, 3) * factor
    return (block_output, volume_grad, first_grad, group_grad, third_grad)


def solution(mesh):
    in_specs = (
        P(None, ("rep", "grp"), "sub", None),
        P(None, ("rep", "grp"), "sub", None),
        P(),
        P(),
        P(),
    )
    out_specs = (
        P(None, ("rep", "grp"), "sub", None),
        P(None, ("rep", "grp"), "sub", None),
        P("rep", None),
        P(("rep", "grp"), None, None, None, None),
        P("rep", None),
    )
    return jax.shard_map(
        per_device, mesh=mesh, in_specs=in_specs, out_specs=out_specs, check_vma=False
    )
```

time: 123 us -> 182 us (1.48)
  local copies, waits for them, and re-layouts: 27.6 us -> 86.9 us
  other arithmetic: 4.26 us -> 10.7 us
  matrix products: 15.4 us -> 10.9 us
  waiting for transfers between devices: 38.6 us -> 36.3 us
    unnamed x47 -> x60, local copies, waits for them, and re-layouts: 6.28 us -> 30.6 us
    reshape x2 -> x8, local copies, waits for them, and re-layouts: 1.56 us -> 24.1 us  [the longest x2 17.9 us: taps(): return stacked.reshape(channels // GW, GW * 27, depth * height * width)]
    another operation x0 -> x4, local copies, waits for them, and re-layouts: none -> 21.3 us  [taps(): jnp.stack([ext[:, dz:dz + depth, dy:dy + height, dx:dx + width] for dz, d...]
    all_to_all x4 -> x0, starting transfers between devices: 16.6 us -> none  [the longest x1 6.31 us: per_device(): lax.all_to_all(first_act, 'grp', split_axis=0, concat_axis=1, tiled=True)]
    all_to_all x4 -> x0, waiting for transfers between devices: 14.8 us -> none  [the longest x1 5.98 us: per_device(): lax.all_to_all(first_act, 'grp', split_axis=0, concat_axis=1, tiled=True)]
    ppermute x4 -> x8, starting transfers between devices: 7.19 us -> 21.9 us  [the longest x4 16.5 us: halo(): lax.ppermute(lax.slice_in_dim(block, size - 1, size, axis=dim), axis, up)]
    conv_general_dilated x3 -> x0, matrix products: 11.7 us -> none  [the longest x1 8.32 us: weight_grad(): lax.conv_general_dilated(padded[None], deltas[None], (1, 1, 1), 'VALID',...]
    dot_general x2 -> x5, matrix products: 1.2 us -> 9.09 us  [the longest x1 3.01 us: per_device(): lax.dot_general(group_delta.reshape(groups, GW, -1), act_taps, grouped_nt...]
  transfers between devices with their start and end apart: 16 -> 16, of which waited for: 13 -> 11; matrix products, arithmetic and copies ran while one was open for 17% -> 11% of each run, Pallas kernels for 0% -> 0%
where the time goes in v3:
time: 182 us; the launch traced here: 181 us
  local copies, waits for them, and re-layouts  86.9 us (48%)
  waiting for transfers between devices  36.3 us (20%)
  starting transfers between devices  34.8 us (19%)
  matrix products  10.9 us (6%)
  other arithmetic  10.7 us (6%)
    unnamed x60, local copies, waits for them, and re-layouts  30.6 us
    another operation x4, local copies, waits for them, and re-layouts, taps(): jnp.stack([ext[:, dz:dz + depth, dy:dy + height, dx:dx + width] for dz, d...  21.3 us
    reshape x2, local copies, waits for them, and re-layouts, taps(): return stacked.reshape(channels // GW, GW * 27, depth * height * width)  17.9 us
    ppermute x4, starting transfers between devices, halo(): lax.ppermute(lax.slice_in_dim(block, size - 1, size, axis=dim), axis, up)  16.5 us
    ppermute x4, waiting for transfers between devices, tree_sum(): got = lax.ppermute(jnp.concatenate(sends), axis, pairs)  16.4 us
    ppermute x4, waiting for transfers between devices, tree_sum(): lax.ppermute(jnp.concatenate([pieces[n] for n in members]), axis, pairs)  14.1 us
    ppermute x4, starting transfers between devices, tree_sum(): got = lax.ppermute(jnp.concatenate(sends), axis, pairs)  8.36 us
    unnamed x12, other arithmetic  7.85 us
  transfers between devices with their start and end apart: 16, of which 11 were waited for; matrix products, arithmetic and copies ran while one was open for 11% of the time, Pallas kernels for 0%

profile of v3, /device:TPU:0, one launch (start us, length us, event | category | flops | bytes accessed | tf_op | source)
XLA Modules:
  0.0 181.1 jit_solution(5077296260788543440)
XLA Ops:
  0.7 1.1 copy.45
  1.7 1.1 multiply_convert_fusion.3
  2.9 1.3 collective-permute-start.1
  4.2 5.6 %collective-permute-start = (bf16[256,1,2,128]{0,3,2,1:T(8,128)(2,1)S(1)}, bf16[256,1,2,128]{0,3,2,1:T(8,128)(2,1)S(1)}, u32[]{:S(2)}, u32[]{:S(2)}) collective-permute-start(bf16[256,1,2,128]{0,3,2,1:T(8,128)(2,1)S(1)} %bitcast.289), channel_id=1, source_target_pairs={{0,4},{4,8},{8,12},{1,5},{5,9},{9,13},{2,6},{6,10},{10,14},{3,7},{... | collective-permute-start | bytes 393224 | tf_op jit(solution)/shard_map/ppermute | solution.py:61
  9.7 1.5 collective-permute-done.1
  11.3 1.2 collective-permute-done
  12.5 0.8 fusion.84
  13.3 1.3 collective-permute-start.2
  14.6 1.3 collective-permute-start.3
  15.9 1.0 copy.47
  16.9 2.0 %reshape.195 = bf16[32,8,8,3,3,3]{1,0,2,5,4,3:T(8,128)(2,1)S(1)} reshape(bf16[256,8,3,3,3]{0,1,4,3,2:T(8,128)(2,1)S(1)} %copy-done.2) | data formatting | bytes 221184 | tf_op jit(solution)/shard_map/reshape | solution.py:120
  18.9 1.0 copy.51
  20.0 3.3 %reshape.190 = bf16[32,8,216]{1,0,2:T(8,128)(2,1)} reshape(bf16[256,8,3,3,3]{0,4,3,2,1:T(4,128)(2,1)S(1)} %copy.47) | data formatting | bytes 221184 | tf_op jit(solution)/shard_map/reshape | solution.py:99
  23.3 1.6 rev.3
  24.8 2.3 %copy.54 = bf16[32,8,8,3,3,3]{0,1,5,4,3,2:T(8,128)(2,1)S(1)} copy(bf16[32,8,8,3,3,3]{2,0,1,5,4,3:T(8,128)(2,1)} %rev.3) | data formatting | bytes 221184 | tf_op jit(solution)/shard_map/rev | solution.py:120
  33.0 0.7 fusion.67
  45.7 10.0 %copy.46 = bf16[256,27,1,2,128]{4,3,1,0,2:T(2,128)(2,1)} copy(bf16[256,27,1,2,128]{0,4,3,2,1:T(8,128)(2,1)} %fusion.49) | data formatting | bytes 7077888 | tf_op jit(solution)/shard_map/stack | solution.py:69
  55.7 9.0 %reshape.189 = bf16[32,216,256]{2,1,0:T(8,128)(2,1)} reshape(bf16[256,27,1,2,128]{4,3,1,0,2:T(2,128)(2,1)} %copy.46) | data formatting | bytes 7077888 | tf_op jit(solution)/shard_map/reshape | solution.py:76
  64.7 3.0 %fusion.5 = f32[256,256]{1,0:T(8,128)S(1)} fusion(bf16[32,216,256]{2,1,0:T(8,128)(2,1)} %reshape.189, bf16[32,8,216]{1,0,2:T(8,128)(2,1)S(1)} %copy-done.1), kind=kOutput, calls=%fused_computation.10 | convolution fusion | flops 28311552 | bytes 3911680 | tf_op jit(solution)/shard_map/dot_general | solution.py:100
  68.5 1.3 collective-permute-start.5
  69.8 5.0 %collective-permute-start.4 = (bf16[256,1,2,128]{0,3,2,1:T(8,128)(2,1)S(1)}, bf16[256,1,2,128]{0,3,2,1:T(8,128)(2,1)S(1)}, u32[]{:S(2)}, u32[]{:S(2)}) collective-permute-start(bf16[256,1,2,128]{0,3,2,1:T(8,128)(2,1)S(1)} %bitcast.278), channel_id=1, source_target_pairs={{0,4},{4,8},{8,12},{1,5},{5,9},{9,13},{2,6},{6,10},{10,14},{3,7},{... | collective-permute-start | bytes 393224 | tf_op jit(solution)/shard_map/ppermute | solution.py:61
  74.8 3.0 %fusion.75 = f32[32,8,216]{2,1,0:T(8,128)S(1)} fusion(bf16[32,216,256]{2,1,0:T(8,128)(2,1)} %reshape.189, bf16[256,256]{1,0:T(8,128)(2,1)S(1)} %copy.62), kind=kOutput, calls=%fused_computation.165 | convolution fusion | flops 28311552 | bytes 3891200 | tf_op jit(solution)/shard_map/dot_general | solution.py:129
  78.6 4.6 %collective-permute-start.6 = (bf16[256,3,1,128]{0,3,2,1:T(8,128)(2,1)S(1)}, bf16[256,3,1,128]{0,3,2,1:T(8,128)(2,1)S(1)}, u32[]{:S(2)}, u32[]{:S(2)}) collective-permute-start(bf16[256,3,1,128]{0,3,2,1:T(8,128)(2,1)S(1)} %get-tuple-element.20), channel_id=1, source_target_pairs={{0,1},{1,2},{2,3},{4,5},{5,6},{6,7},{8,9},{9,10},{10,11},{12,13},{... | collective-permute-start | bytes 589832 | tf_op jit(solution)/shard_map/ppermute | solution.py:61
  83.3 1.5 collective-permute-start.7
  85.0 3.1 %collective-permute-done.7 = bf16[256,3,1,128]{0,3,2,1:T(8,128)(2,1)S(1)} collective-permute-done((bf16[256,3,1,128]{0,3,2,1:T(8,128)(2,1)S(1)}, bf16[256,3,1,128]{0,3,2,1:T(8,128)(2,1)S(1)}, u32[]{:S(2)}, u32[]{:S(2)}) %collective-permute-start.7) | collective-permute-done | bytes 196640 | tf_op jit(solution)/shard_map/ppermute | solution.py:62
  93.6 0.7 fusion.41
  106.3 10.0 %copy.53 = bf16[256,27,1,2,128]{4,3,1,0,2:T(2,128)(2,1)} copy(bf16[256,27,1,2,128]{0,4,3,2,1:T(8,128)(2,1)} %fusion.23) | data formatting | bytes 7077888 | tf_op jit(solution)/shard_map/stack | solution.py:69
  116.3 8.9 %reshape.194 = bf16[32,216,256]{2,1,0:T(8,128)(2,1)} reshape(bf16[256,27,1,2,128]{4,3,1,0,2:T(2,128)(2,1)} %copy.53) | data formatting | bytes 7077888 | tf_op jit(solution)/shard_map/reshape | solution.py:76
  125.2 2.6 %fusion.14 = f32[256,256]{1,0:T(8,128)S(1)} fusion(bf16[32,216,256]{2,1,0:T(8,128)(2,1)} %reshape.194, bf16[32,8,216]{2,1,0:T(8,128)(2,1)S(1)} %copy.55), kind=kOutput, calls=%fused_computation.19 | convolution fusion | flops 28442624 | bytes 3911680 | tf_op jit(solution)/shard_map/dot_general | solution.py:125
  128.5 3.9 %collective-permute-start.8 = (f32[93184]{0:T(1024)S(1)}, f32[93184]{0:T(1024)S(1)}, u32[]{:S(2)}, u32[]{:S(2)}) collective-permute-start(f32[93184]{0:T(1024)S(1)} %pad_maximum_fusion.2), channel_id=1, source_target_pairs={{0,2},{1,3},{2,0},{3,1},{4,6},{5,7},{6,4},{7,5},{8,10},{9,11},{10,... | collective-permute-start | bytes 1118216 | tf_op jit(solution)/shard_map/ppermute | solution.py:31
  132.9 8.2 %collective-permute-done.8 = f32[93184]{0:T(1024)S(1)} collective-permute-done((f32[93184]{0:T(1024)S(1)}, f32[93184]{0:T(1024)S(1)}, u32[]{:S(2)}, u32[]{:S(2)}) %collective-permute-start.8) | collective-permute-done | bytes 372768 | tf_op jit(solution)/shard_map/ppermute | solution.py:31
  141.3 0.8 collective-permute-start.9
  142.0 1.1 collective-permute-done.9
  143.2 3.1 %collective-permute-start.10 = (f32[23296]{0:T(1024)S(1)}, f32[23296]{0:T(1024)S(1)}, u32[]{:S(2)}, u32[]{:S(2)}) collective-permute-start(f32[23296]{0:T(1024)S(1)} %pad_maximum_fusion.18), channel_id=1, source_target_pairs={{0,8},{4,12},{8,0},{12,4},{1,9},{5,13},{9,1},{13,5},{2,10},{6,14},... | collective-permute-start | bytes 279560 | tf_op jit(solution)/shard_map/ppermute | solution.py:31
  146.3 0.8 copy.71
  147.1 4.5 %collective-permute-done.10 = f32[23296]{0:T(1024)S(1)} collective-permute-done((f32[23296]{0:T(1024)S(1)}, f32[23296]{0:T(1024)S(1)}, u32[]{:S(2)}, u32[]{:S(2)}) %collective-permute-start.10) | collective-permute-done | bytes 93216 | tf_op jit(solution)/shard_map/ppermute | solution.py:31
  152.4 0.8 copy.72
  153.2 2.6 %collective-permute-done.11 = f32[11648]{0:T(1024)S(1)} collective-permute-done((f32[11648]{0:T(1024)S(1)}, f32[11648]{0:T(1024)S(1)}, u32[]{:S(2)}, u32[]{:S(2)}) %collective-permute-start.11) | collective-permute-done | bytes 46624 | tf_op jit(solution)/shard_map/ppermute | solution.py:31
  157.5 2.3 %collective-permute-done.12 = f32[8192]{0:T(1024)S(1)} collective-permute-done((f32[8192]{0:T(1024)S(1)}, f32[8192]{0:T(1024)S(1)}, u32[]{:S(2)}, u32[]{:S(2)}) %collective-permute-start.12) | collective-permute-done | bytes 32800 | tf_op jit(solution)/shard_map/ppermute | solution.py:41
  159.9 1.9 %collective-permute-start.13 = (f32[16384]{0:T(1024)S(1)}, f32[16384]{0:T(1024)S(1)}, u32[]{:S(2)}, u32[]{:S(2)}) collective-permute-start(f32[16384]{0:T(1024)S(1)} %pad_maximum_fusion.20), channel_id=1, source_target_pairs={{0,8},{4,12},{8,0},{12,4},{1,9},{5,13},{9,1},{13,5},{2,10},{6,14},... | collective-permute-start | bytes 196616 | tf_op jit(solution)/shard_map/ppermute | solution.py:41
  161.8 4.0 %collective-permute-done.13 = f32[16384]{0:T(1024)S(1)} collective-permute-done((f32[16384]{0:T(1024)S(1)}, f32[16384]{0:T(1024)S(1)}, u32[]{:S(2)}, u32[]{:S(2)}) %collective-permute-start.13) | collective-permute-done | bytes 65568 | tf_op jit(solution)/shard_map/ppermute | solution.py:41
  166.0 1.3 collective-permute-done.14
  168.0 2.0 %collective-permute-start.15 = (f32[72448]{0:T(1024)S(1)}, f32[72448]{0:T(1024)S(1)}, u32[]{:S(2)}, u32[]{:S(2)}) collective-permute-start(f32[72448]{0:T(1024)S(1)} %pad_maximum_fusion.3), channel_id=1, source_target_pairs={{0,2},{1,3},{2,0},{3,1},{4,6},{5,7},{6,4},{7,5},{8,10},{9,11},{10,... | collective-permute-start | bytes 869384 | tf_op jit(solution)/shard_map/ppermute | solution.py:41
  170.8 6.5 %collective-permute-done.15 = f32[72448]{0:T(1024)S(1)} collective-permute-done((f32[72448]{0:T(1024)S(1)}, f32[72448]{0:T(1024)S(1)}, u32[]{:S(2)}, u32[]{:S(2)}) %collective-permute-start.15) | collective-permute-done | bytes 289824 | tf_op jit(solution)/shard_map/ppermute | solution.py:41
  177.4 0.8 concatenate.216
  178.2 1.2 copy.69
  179.5 0.8 fusion.77
  180.2 0.8 fusion.20
  (161 shorter events, 42.5 us)
Async XLA Ops:
  0.6 67.2 %copy-start = (bf16[256,256]{1,0:T(8,128)(2,1)S(1)}, bf16[256,256]{1,0:T(8,128)(2,1)}, u32[]{:S(2)}) copy-start(bf16[256,256]{1,0:T(8,128)(2,1)} %param.9) | copy-start | bytes 393220
  0.6 16.2 %copy-start.2 = (bf16[256,8,3,3,3]{0,1,4,3,2:T(8,128)(2,1)S(1)}, bf16[256,8,3,3,3]{0,1,4,3,2:T(8,128)(2,1)}, u32[]{:S(2)}) copy-start(bf16[256,8,3,3,3]{0,1,4,3,2:T(8,128)(2,1)} %param.8) | copy-start | bytes 331780
  2.9 8.4 %collective-permute-start.1 = (bf16[256,1,2,128]{0,3,2,1:T(8,128)(2,1)S(1)}, bf16[256,1,2,128]{0,3,2,1:T(8,128)(2,1)S(1)}, u32[]{:S(2)}, u32[]{:S(2)}) collective-permute-start(bf16[256,1,2,128]{0,3,2,1:T(8,128)(2,1)S(1)} %bitcast.288), channel_id=1, source_target_pairs={{4,0},{8,4},{12,8},{5,1},{9,5},{13,9},{6,2},{10,6},{14,10},{7,3},{... | collective-permute-start | bytes 393224 | tf_op jit(solution)/shard_map/ppermute | solution.py:62
  4.2 8.3 %collective-permute-start = (bf16[256,1,2,128]{0,3,2,1:T(8,128)(2,1)S(1)}, bf16[256,1,2,128]{0,3,2,1:T(8,128)(2,1)S(1)}, u32[]{:S(2)}, u32[]{:S(2)}) collective-permute-start(bf16[256,1,2,128]{0,3,2,1:T(8,128)(2,1)S(1)} %bitcast.289), channel_id=1, source_target_pairs={{0,4},{4,8},{8,12},{1,5},{5,9},{9,13},{2,6},{6,10},{10,14},{3,7},{... | collective-permute-start | bytes 393224 | tf_op jit(solution)/shard_map/ppermute | solution.py:61
  13.3 14.2 %collective-permute-start.2 = (bf16[256,3,1,128]{0,3,2,1:T(8,128)(2,1)}, bf16[256,3,1,128]{0,3,2,1:T(8,128)(2,1)S(1)}, u32[]{:S(2)}, u32[]{:S(2)}) collective-permute-start(bf16[256,3,1,128]{0,3,2,1:T(8,128)(2,1)} %get-tuple-element.22), channel_id=1, source_target_pairs={{0,1},{1,2},{2,3},{4,5},{5,6},{6,7},{8,9},{9,10},{10,11},{12,13},{... | collective-permute-start | bytes 589832 | tf_op jit(solution)/shard_map/ppermute | solution.py:61
  14.6 12.9 %collective-permute-start.3 = (bf16[256,3,1,128]{0,3,2,1:T(8,128)(2,1)}, bf16[256,3,1,128]{0,3,2,1:T(8,128)(2,1)S(1)}, u32[]{:S(2)}, u32[]{:S(2)}) collective-permute-start(bf16[256,3,1,128]{0,3,2,1:T(8,128)(2,1)} %get-tuple-element.23), channel_id=1, source_target_pairs={{1,0},{2,1},{3,2},{5,4},{6,5},{7,6},{9,8},{10,9},{11,10},{13,12},{... | collective-permute-start | bytes 589832 | tf_op jit(solution)/shard_map/ppermute | solution.py:62
  55.7 9.0 %copy-start.1 = (bf16[32,8,216]{1,0,2:T(8,128)(2,1)S(1)}, bf16[32,8,216]{1,0,2:T(8,128)(2,1)}, u32[]{:S(2)}) copy-start(bf16[32,8,216]{1,0,2:T(8,128)(2,1)} %reshape.190) | copy-start | bytes 331780
  68.1 10.1 %copy-start.4 = (bf16[256,256]{0,1:T(8,128)(2,1)}, bf16[256,256]{0,1:T(8,128)(2,1)S(1)}, u32[]{:S(2)}) copy-start(bf16[256,256]{0,1:T(8,128)(2,1)S(1)} %get-tuple-element.32) | copy-start | bytes 393220
  68.5 10.0 %collective-permute-start.5 = (bf16[256,1,2,128]{0,3,2,1:T(8,128)(2,1)S(1)}, bf16[256,1,2,128]{0,3,2,1:T(8,128)(2,1)S(1)}, u32[]{:S(2)}, u32[]{:S(2)}) collective-permute-start(bf16[256,1,2,128]{0,3,2,1:T(8,128)(2,1)S(1)} %bitcast.277), channel_id=1, source_target_pairs={{4,0},{8,4},{12,8},{5,1},{9,5},{13,9},{6,2},{10,6},{14,10},{7,3},{... | collective-permute-start | bytes 393224 | tf_op jit(solution)/shard_map/ppermute | solution.py:62
  69.8 8.7 %collective-permute-start.4 = (bf16[256,1,2,128]{0,3,2,1:T(8,128)(2,1)S(1)}, bf16[256,1,2,128]{0,3,2,1:T(8,128)(2,1)S(1)}, u32[]{:S(2)}, u32[]{:S(2)}) collective-permute-start(bf16[256,1,2,128]{0,3,2,1:T(8,128)(2,1)S(1)} %bitcast.278), channel_id=1, source_target_pairs={{0,4},{4,8},{8,12},{1,5},{5,9},{9,13},{2,6},{6,10},{10,14},{3,7},{... | collective-permute-start | bytes 393224 | tf_op jit(solution)/shard_map/ppermute | solution.py:61
  78.6 6.4 %collective-permute-start.6 = (bf16[256,3,1,128]{0,3,2,1:T(8,128)(2,1)S(1)}, bf16[256,3,1,128]{0,3,2,1:T(8,128)(2,1)S(1)}, u32[]{:S(2)}, u32[]{:S(2)}) collective-permute-start(bf16[256,3,1,128]{0,3,2,1:T(8,128)(2,1)S(1)} %get-tuple-element.20), channel_id=1, source_target_pairs={{0,1},{1,2},{2,3},{4,5},{5,6},{6,7},{8,9},{9,10},{10,11},{12,13},{... | collective-permute-start | bytes 589832 | tf_op jit(solution)/shard_map/ppermute | solution.py:61
  83.3 4.8 %collective-permute-start.7 = (bf16[256,3,1,128]{0,3,2,1:T(8,128)(2,1)S(1)}, bf16[256,3,1,128]{0,3,2,1:T(8,128)(2,1)S(1)}, u32[]{:S(2)}, u32[]{:S(2)}) collective-permute-start(bf16[256,3,1,128]{0,3,2,1:T(8,128)(2,1)S(1)} %get-tuple-element.21), channel_id=1, source_target_pairs={{1,0},{2,1},{3,2},{5,4},{6,5},{7,6},{9,8},{10,9},{11,10},{13,12},{... | collective-permute-start | bytes 589832 | tf_op jit(solution)/shard_map/ppermute | solution.py:62
  128.3 23.9 %copy-start.3 = (bf16[256,256]{1,0:T(8,128)(2,1)S(1)}, bf16[256,256]{1,0:T(8,128)(2,1)}, u32[]{:S(2)}) copy-start(bf16[256,256]{1,0:T(8,128)(2,1)} %param.7) | copy-start | bytes 393220
  128.3 23.9 %copy-start.5 = (bf16[256,256]{0,1:T(8,128)(2,1)S(1)}, bf16[256,256]{0,1:T(8,128)(2,1)}, u32[]{:S(2)}) copy-start(bf16[256,256]{0,1:T(8,128)(2,1)} %copy-done.4) | copy-start | bytes 393220
  128.5 12.6 %collective-permute-start.8 = (f32[93184]{0:T(1024)S(1)}, f32[93184]{0:T(1024)S(1)}, u32[]{:S(2)}, u32[]{:S(2)}) collective-permute-start(f32[93184]{0:T(1024)S(1)} %pad_maximum_fusion.2), channel_id=1, source_target_pairs={{0,2},{1,3},{2,0},{3,1},{4,6},{5,7},{6,4},{7,5},{8,10},{9,11},{10,... | collective-permute-start | bytes 1118216 | tf_op jit(solution)/shard_map/ppermute | solution.py:31
  141.3 1.8 %collective-permute-start.9 = (f32[46592]{0:T(1024)S(1)}, f32[46592]{0:T(1024)S(1)}, u32[]{:S(2)}, u32[]{:S(2)}) collective-permute-start(f32[46592]{0:T(1024)S(1)} %pad_maximum_fusion.4), channel_id=1, source_target_pairs={{0,1},{1,0},{2,3},{3,2},{4,5},{5,4},{6,7},{7,6},{8,9},{9,8},{10,11... | collective-permute-start | bytes 559112 | tf_op jit(solution)/shard_map/ppermute | solution.py:31
  143.2 8.4 %collective-permute-start.10 = (f32[23296]{0:T(1024)S(1)}, f32[23296]{0:T(1024)S(1)}, u32[]{:S(2)}, u32[]{:S(2)}) collective-permute-start(f32[23296]{0:T(1024)S(1)} %pad_maximum_fusion.18), channel_id=1, source_target_pairs={{0,8},{4,12},{8,0},{12,4},{1,9},{5,13},{9,1},{13,5},{2,10},{6,14},... | collective-permute-start | bytes 279560 | tf_op jit(solution)/shard_map/ppermute | solution.py:31
  151.6 4.2 %collective-permute-start.11 = (f32[11648]{0:T(1024)S(1)}, f32[11648]{0:T(1024)S(1)}, u32[]{:S(2)}, u32[]{:S(2)}) collective-permute-start(f32[11648]{0:T(1024)S(1)} %pad_maximum_fusion.22), channel_id=1, source_target_pairs={{0,4},{4,0},{8,12},{12,8},{1,5},{5,1},{9,13},{13,9},{2,6},{6,2},{1... | collective-permute-start | bytes 139784 | tf_op jit(solution)/shard_map/ppermute | solution.py:31
  155.8 4.0 %collective-permute-start.12 = (f32[8192]{0:T(1024)S(1)}, f32[8192]{0:T(1024)S(1)}, u32[]{:S(2)}, u32[]{:S(2)}) collective-permute-start(f32[8192]{0:T(1024)S(1)} %pad_maximum_fusion.24), channel_id=1, source_target_pairs={{0,4},{4,0},{8,12},{12,8},{1,5},{5,1},{9,13},{13,9},{2,6},{6,2},{1... | collective-permute-start | bytes 98312 | tf_op jit(solution)/shard_map/ppermute | solution.py:41
  159.9 5.9 %collective-permute-start.13 = (f32[16384]{0:T(1024)S(1)}, f32[16384]{0:T(1024)S(1)}, u32[]{:S(2)}, u32[]{:S(2)}) collective-permute-start(f32[16384]{0:T(1024)S(1)} %pad_maximum_fusion.20), channel_id=1, source_target_pairs={{0,8},{4,12},{8,0},{12,4},{1,9},{5,13},{9,1},{13,5},{2,10},{6,14},... | collective-permute-start | bytes 196616 | tf_op jit(solution)/shard_map/ppermute | solution.py:41
  165.9 1.4 collective-permute-start.14
  168.0 9.2 %collective-permute-start.15 = (f32[72448]{0:T(1024)S(1)}, f32[72448]{0:T(1024)S(1)}, u32[]{:S(2)}, u32[]{:S(2)}) collective-permute-start(f32[72448]{0:T(1024)S(1)} %pad_maximum_fusion.3), channel_id=1, source_target_pairs={{0,2},{1,3},{2,0},{3,1},{4,6},{5,7},{6,4},{7,5},{8,10},{9,11},{10,... | collective-permute-start | bytes 869384 | tf_op jit(solution)/shard_map/ppermute | solution.py:41

commit v4 on v3

--- a/solution.py
+++ b/solution.py
@@ -1,12 +1,117 @@
+import functools
 import itertools
 import math
 
 import jax
 import jax.numpy as jnp
 from jax import lax
+from jax.experimental import pallas as pl
+from jax.experimental.pallas import tpu as pltpu
 from jax.sharding import PartitionSpec as P
 
 GW = 8
+LANES = 128
+TAPS_PER_BLOCK = 16
+
+
+def shift_lanes(block, offset):
+    lane = lax.broadcasted_iota(jnp.int32, block.shape, 1)
+    rolled = pltpu.roll(block, (-offset) % LANES, 1)
+    edge = LANES - 1 if offset > 0 else 0
+    return jnp.where(lane == edge, jnp.zeros_like(rolled), rolled)
+
+
+def conv_body(ext_ref, w_ref, out_ref):
+    height, channels = out_ref.shape[0], out_ref.shape[1]
+    for y in range(height):
+        parts = None
+        for dz, dy in itertools.product(range(3), repeat=2):
+            product = jnp.dot(
+                w_ref[dz * 3 + dy], ext_ref[dz, y + dy], preferred_element_type=jnp.float32
+            )
+            parts = product if parts is None else parts + product
+        out_ref[y] = (
+            parts[channels : 2 * channels]
+            + shift_lanes(parts[:channels], -1)
+            + shift_lanes(parts[2 * channels :], 1)
+        )
+
+
+def conv_call(ext, weights):
+    _, rows, channels, width = ext.shape
+    height = rows - 2
+    return pl.pallas_call(
+        conv_body,
+        out_shape=jax.ShapeDtypeStruct((height, channels, width), jnp.float32),
+        in_specs=[pl.BlockSpec(memory_space=pltpu.VMEM)] * 2,
+        out_specs=pl.BlockSpec(memory_space=pltpu.VMEM),
+        cost_estimate=pl.CostEstimate(
+            flops=2 * 27 * channels * channels * height * width,
+            transcendentals=0,
+            bytes_accessed=ext.size * 2 + weights.size * 2 + height * channels * width * 4,
+        ),
+    )(ext, weights)
+
+
+def wgrad_body(act_ref, delta_ref, mask_ref, sel_ref, out_ref):
+    height, channels = delta_ref.shape[0], delta_ref.shape[1]
+    stacked = []
+    for y in range(height):
+        row = delta_ref[y].astype(jnp.float32)
+        stacked.append(
+            jnp.concatenate([shift_lanes(row, 1), row, shift_lanes(row, -1)], axis=0).astype(
+                jnp.bfloat16
+            )
+        )
+    mask = mask_ref[...]
+    totals = [jnp.zeros((channels, LANES), jnp.float32) for _ in range(out_ref.shape[0])]
+    for dz, dy in itertools.product(range(3), repeat=2):
+        grads = None
+        for y in range(height):
+            term = lax.dot_general(
+                stacked[y],
+                act_ref[dz, y + dy],
+                (((1,), (1,)), ((), ())),
+                preferred_element_type=jnp.float32,
+            )
+            grads = term if grads is None else grads + term
+        for dx in range(3):
+            tap = dz * 9 + dy * 3 + dx
+            picked = grads[dx * channels : (dx + 1) * channels] * mask
+            folded = picked[:, :LANES]
+            for start in range(LANES, channels, LANES):
+                folded = folded + picked[:, start : start + LANES]
+            high = folded.astype(jnp.bfloat16)
+            low = (folded - high.astype(jnp.float32)).astype(jnp.bfloat16)
+            sel = sel_ref[tap % TAPS_PER_BLOCK]
+            totals[tap // TAPS_PER_BLOCK] += jnp.dot(
+                high, sel, preferred_element_type=jnp.float32
+            ) + jnp.dot(low, sel, preferred_element_type=jnp.float32)
+    for n, total in enumerate(totals):
+        out_ref[n] = total
+
+
+def wgrad_call(act_ext, delta):
+    height, channels, width = delta.shape
+    blocks = -(-27 // TAPS_PER_BLOCK)
+    group_of = jnp.arange(channels) // GW
+    mask = (group_of[:, None] == group_of[None, :]).astype(jnp.float32)
+    lane = jnp.arange(LANES)
+    sel = (
+        lane[None, None, :] == jnp.arange(TAPS_PER_BLOCK)[:, None, None] * GW + (lane % GW)[None, :, None]
+    ).astype(jnp.bfloat16)
+    out = pl.pallas_call(
+        wgrad_body,
+        out_shape=jax.ShapeDtypeStruct((blocks, channels, LANES), jnp.float32),
+        in_specs=[pl.BlockSpec(memory_space=pltpu.VMEM)] * 4,
+        out_specs=pl.BlockSpec(memory_space=pltpu.VMEM),
+        cost_estimate=pl.CostEstimate(
+            flops=2 * 27 * channels * channels * height * width + 4 * 27 * channels * LANES * LANES,
+            transcendentals=0,
+            bytes_accessed=act_ext.size * 2 + delta.size * 2 + blocks * channels * LANES * 4,
+        ),
+    )(act_ext, delta, mask, sel)
+    return out.transpose(1, 0, 2).reshape(channels, blocks * LANES)[:, : 27 * GW]
 
 
 def tree_sum(blocks, order):
@@ -53,7 +158,7 @@
 
 
 def halo(block):
-    for axis, dim in (("grp", 1), ("sub", 2)):
+    for axis, dim in (("grp", 0), ("sub", 1)):
         count = lax.axis_size(axis)
         up = [(i, i + 1) for i in range(count - 1)]
         down = [(i + 1, i) for i in range(count - 1)]
@@ -61,19 +166,7 @@
         low = lax.ppermute(lax.slice_in_dim(block, size - 1, size, axis=dim), axis, up)
         high = lax.ppermute(lax.slice_in_dim(block, 0, 1, axis=dim), axis, down)
         block = jnp.concatenate([low, block, high], axis=dim)
-    return jnp.pad(block, ((0, 0), (0, 0), (0, 0), (1, 1)))
-
-
-def taps(ext, depth, height, width):
-    channels = ext.shape[0]
-    stacked = jnp.stack(
-        [
-            ext[:, dz : dz + depth, dy : dy + height, dx : dx + width]
-            for dz, dy, dx in itertools.product(range(3), repeat=3)
-        ],
-        axis=1,
-    )
-    return stacked.reshape(channels // GW, GW * 27, depth * height * width)
+    return block
 
 
 def silu_slope(values):
@@ -81,54 +174,59 @@
     return sigma * (1.0 + values * (1.0 - sigma))
 
 
+def conv_weights(group_weight):
+    channels = group_weight.shape[0]
+    tiled = jnp.tile(group_weight, (1, channels // GW, 1, 1, 1))
+    group_of = jnp.arange(channels) // GW
+    mask = (group_of[:, None] == group_of[None, :]).astype(group_weight.dtype)
+    dense = tiled * mask[:, :, None, None, None]
+    forward = dense.transpose(2, 3, 4, 0, 1).reshape(9, 3 * channels, channels)
+    backward = dense[:, :, ::-1, ::-1, ::-1].transpose(2, 3, 4, 1, 0).reshape(9, 3 * channels, channels)
+    return forward, backward
+
+
 def per_device(volume, cotangent, first_weight, group_weight, third_weight):
     channels, depth, height, width = volume.shape
-    groups = channels // GW
     flattened = volume.reshape(channels, -1)
     contract_lead = (((0,), (0,)), ((), ()))
     contract_tail = (((1,), (1,)), ((), ()))
-    grouped_mm = (((2,), (1,)), ((0,), (0,)))
-    grouped_nt = (((2,), (2,)), ((0,), (0,)))
     total_cells = depth * lax.axis_size("grp") * height * lax.axis_size("sub") * width
     factor = 1.0 / math.sqrt(total_cells)
+
+    def to_rows(block):
+        return block.reshape(channels, depth, height, width).transpose(1, 2, 0, 3)
+
+    def from_rows(block):
+        return block.transpose(1, 0, 2).reshape(channels, -1)
+
+    forward_kernel, backward_kernel = conv_weights(group_weight)
     first_pre = lax.dot_general(
         first_weight, flattened, contract_lead, preferred_element_type=jnp.float32
     )
-    first_act = jax.nn.silu(first_pre).astype(jnp.bfloat16).reshape(volume.shape)
-    act_taps = taps(halo(first_act), depth, height, width)
-    kernel = group_weight.reshape(groups, GW, GW * 27)
-    group_pre = lax.dot_general(
-        kernel, act_taps, grouped_mm, preferred_element_type=jnp.float32
-    ).reshape(channels, -1)
+    first_act = jax.nn.silu(first_pre).astype(jnp.bfloat16)
+    act_ext = halo(to_rows(first_act))
+    group_pre = conv_call(act_ext, forward_kernel)
     group_act = jax.nn.silu(group_pre).astype(jnp.bfloat16)
+    act_flat = from_rows(group_act)
     summed = flattened.astype(jnp.float32) + lax.dot_general(
-        third_weight, group_act, contract_lead, preferred_element_type=jnp.float32
+        third_weight, act_flat, contract_lead, preferred_element_type=jnp.float32
     )
     block_output = jax.nn.silu(summed).astype(jnp.bfloat16).reshape(volume.shape)
     third_delta = (cotangent.reshape(channels, -1).astype(jnp.float32) * silu_slope(summed)).astype(
         jnp.bfloat16
     )
     third_part = lax.dot_general(
-        group_act, third_delta, contract_tail, preferred_element_type=jnp.float32
+        act_flat, third_delta, contract_tail, preferred_element_type=jnp.float32
     )
     hidden_grad = jnp.dot(third_weight, third_delta, preferred_element_type=jnp.float32).astype(
         jnp.bfloat16
     )
-    group_delta = (hidden_grad.astype(jnp.float32) * silu_slope(group_pre)).astype(jnp.bfloat16)
-    delta_taps = taps(halo(group_delta.reshape(volume.shape)), depth, height, width)
-    flipped = (
-        group_weight.reshape(groups, GW, GW, 3, 3, 3)
-        .transpose(0, 2, 1, 3, 4, 5)[:, :, :, ::-1, ::-1, ::-1]
-        .reshape(groups, GW, GW * 27)
-    )
-    inner_grad = (
-        lax.dot_general(flipped, delta_taps, grouped_mm, preferred_element_type=jnp.float32)
-        .reshape(channels, -1)
-        .astype(jnp.bfloat16)
-    )
-    kernel_part = lax.dot_general(
-        group_delta.reshape(groups, GW, -1), act_taps, grouped_nt, preferred_element_type=jnp.float32
-    )
+    group_delta = (
+        to_rows(hidden_grad)[0].astype(jnp.float32) * silu_slope(group_pre)
+    ).astype(jnp.bfloat16)
+    delta_ext = halo(group_delta[None])
+    inner_grad = from_rows(conv_call(delta_ext, backward_kernel).astype(jnp.bfloat16))
+    kernel_part = wgrad_call(act_ext, group_delta)
     first_delta = (inner_grad.astype(jnp.float32) * silu_slope(first_pre)).astype(jnp.bfloat16)
     first_part = lax.dot_general(
         flattened, first_delta, contract_tail, preferred_element_type=jnp.float32
@@ -153,7 +251,10 @@
     )
     first_grad = first_sum.reshape(first_part.shape) * factor
     third_grad = third_sum.reshape(third_part.shape) * factor
-    group_grad = group_sum.reshape(channels // grp_count, GW, 3, 3, 3) * factor
+    own_rows = channels // grp_count
+    group_grad = (
+        group_sum.reshape(own_rows, 27, GW).transpose(0, 2, 1).reshape(own_rows, GW, 3, 3, 3) * factor
+    )
     return (block_output, volume_grad, first_grad, group_grad, third_grad)
 
 

time: 182 us -> 121 us (0.66)
  local copies, waits for them, and re-layouts: 86.9 us -> 17.2 us
  Pallas kernels: 0 us -> 15.6 us
  matrix products: 10.9 us -> 2.29 us
  other arithmetic: 10.7 us -> 13.9 us
  waiting for transfers between devices: 36.3 us -> 34.4 us
    unnamed x60 -> x19, local copies, waits for them, and re-layouts: 30.6 us -> 2.91 us
    reshape x6 -> x1, local copies, waits for them, and re-layouts: 23.8 us -> 0.12 us  [to_rows(): return block.reshape(channels, depth, height, width).transpose(1, 2, 0, 3)]
    another operation x4 -> x0, local copies, waits for them, and re-layouts: 21.3 us -> none  [taps(): jnp.stack([ext[:, dz:dz + depth, dy:dy + height, dx:dx + width] for dz, d...]
    pallas_call x0 -> x3, Pallas kernels: none -> 15.6 us  [the longest x2 10 us: conv_call(): pl.pallas_call(conv_body, out_shape=jax.ShapeDtypeStruct((height, channel...]
    dot_general x5 -> x2, matrix products: 9.09 us -> 0.51 us  [the longest x1 0.28 us: per_device(): lax.dot_general(third_weight, act_flat, contract_lead, preferred_element_...]
    unnamed x12 -> x0, other arithmetic: 7.85 us -> none
    transpose x0 -> x3, local copies, waits for them, and re-layouts: none -> 7.29 us  [the longest x1 6.06 us: conv_weights(): forward = dense.transpose(2, 3, 4, 0, 1).reshape(9, 3 * channels, channels)]
    mul x1 -> x3, other arithmetic: 0.78 us -> 4.99 us  [the longest x1 4.21 us: conv_weights(): dense = tiled * mask[:, :, None, None, None]]
  transfers between devices with their start and end apart: 16 -> 16, of which waited for: 11 -> 10; matrix products, arithmetic and copies ran while one was open for 11% -> 18% of each run, Pallas kernels for 0% -> 5%
where the time goes in v4:
time: 121 us
  starting transfers between devices  36 us (30%)
  waiting for transfers between devices  34.4 us (28%)
  local copies, waits for them, and re-layouts  17.2 us (14%)
  Pallas kernels  15.6 us (13%)
  other arithmetic  13.9 us (11%)
  matrix products  2.29 us (2%)
  between operations  1.44 us (1%)
    ppermute x4, starting transfers between devices, halo(): lax.ppermute(lax.slice_in_dim(block, size - 1, size, axis=dim), axis, up)  16.7 us
    ppermute x4, waiting for transfers between devices, tree_sum(): got = lax.ppermute(jnp.concatenate(sends), axis, pairs)  16.1 us
    ppermute x4, waiting for transfers between devices, tree_sum(): lax.ppermute(jnp.concatenate([pieces[n] for n in members]), axis, pairs)  14.3 us
    pallas_call x2, Pallas kernels, conv_call(): pl.pallas_call(conv_body, out_shape=jax.ShapeDtypeStruct((height, channel...  10 us
    ppermute x4, starting transfers between devices, tree_sum(): got = lax.ppermute(jnp.concatenate(sends), axis, pairs)  8.85 us
    transpose x1, local copies, waits for them, and re-layouts, conv_weights(): forward = dense.transpose(2, 3, 4, 0, 1).reshape(9, 3 * channels, channels)  6.06 us
    pallas_call x1, Pallas kernels, wgrad_call(): pl.pallas_call(wgrad_body, out_shape=jax.ShapeDtypeStruct((blocks, channe...  5.6 us
    ppermute x4, starting transfers between devices, halo(): high = lax.ppermute(lax.slice_in_dim(block, 0, 1, axis=dim), axis, down)  5.35 us
  transfers between devices with their start and end apart: 16, of which 10 were waited for; matrix products, arithmetic and copies ran while one was open for 18% of the time, Pallas kernels for 5%

profile of v4, /device:TPU:0, one launch (start us, length us, event | category | flops | bytes accessed | tf_op | source)
XLA Modules:
  0.0 120.8 jit_solution(1453833994628266518)
XLA Ops:
  0.6 1.0 copy.58
  1.7 1.1 multiply_convert_fusion.2
  3.0 4.9 %collective-permute-start = (bf16[1,2,256,128]{3,2,1,0:T(8,128)(2,1)S(1)}, bf16[1,2,256,128]{3,2,1,0:T(8,128)(2,1)S(1)}, u32[]{:S(2)}, u32[]{:S(2)}) collective-permute-start(bf16[1,2,256,128]{3,2,1,0:T(8,128)(2,1)S(1)} %bitcast.82), channel_id=1, source_target_pairs={{0,4},{4,8},{8,12},{1,5},{5,9},{9,13},{2,6},{6,10},{10,14},{3,7},{... | collective-permute-start | bytes 393224 | tf_op jit(solution)/shard_map/ppermute | solution.py:166
  7.9 1.3 %collective-permute-start.1 = (bf16[1,2,256,128]{3,2,1,0:T(8,128)(2,1)S(1)}, bf16[1,2,256,128]{3,2,1,0:T(8,128)(2,1)S(1)}, u32[]{:S(2)}, u32[]{:S(2)}) collective-permute-start(bf16[1,2,256,128]{3,2,1,0:T(8,128)(2,1)S(1)} %bitcast.83), channel_id=1, source_target_pairs={{4,0},{8,4},{12,8},{5,1},{9,5},{13,9},{6,2},{10,6},{14,10},{7,3},{... | collective-permute-start | bytes 393224 | tf_op jit(solution)/shard_map/ppermute | solution.py:167
  9.2 0.8 compare_convert_fusion
  10.2 4.2 %bitcast_multiply_fusion = (bf16[256,256,3,3,3]{0,1,4,3,2:T(8,128)(2,1)}, bf16[3,3,3,256,256]{3,4,2,1,0:T(8,128)(2,1)}) fusion(bf16[256,256]{0,1:T(8,128)(2,1)S(1)} %copy.60, bf16[256,8,3,3,3]{0,1,4,3,2:T(8,128)(2,1)} %param.8), kind=kLoop, calls=%fused_computation | loop fusion | flops 1769472 | bytes 7319552 | tf_op jit(solution)/shard_map/mul | solution.py:182
  14.4 6.1 %copy.61 = bf16[3,3,3,256,256]{4,3,2,1,0:T(8,128)(2,1)} copy(bf16[3,3,3,256,256]{3,4,2,1,0:T(8,128)(2,1)} %get-tuple-element.40) | data formatting | bytes 7077888 | tf_op jit(solution)/shard_map/transpose | solution.py:183
  20.6 4.1 %rev.3 = bf16[256,256,3,3,3]{0,1,4,3,2:T(8,128)(2,1)} reverse(bf16[256,256,3,3,3]{0,1,4,3,2:T(8,128)(2,1)} %get-tuple-element.39), dimensions={2,3,4} | reverse | bytes 7077888 | tf_op jit(solution)/shard_map/rev | solution.py:184
  24.8 1.5 %collective-permute-start.2 = (bf16[3,1,256,128]{3,2,1,0:T(8,128)(2,1)S(1)}, bf16[3,1,256,128]{3,2,1,0:T(8,128)(2,1)S(1)}, u32[]{:S(2)}, u32[]{:S(2)}) collective-permute-start(bf16[3,1,256,128]{3,2,1,0:T(8,128)(2,1)S(1)} %get-tuple-element.27), channel_id=1, source_target_pairs={{0,1},{1,2},{2,3},{4,5},{5,6},{6,7},{8,9},{9,10},{10,11},{12,13},{... | collective-permute-start | bytes 589832 | tf_op jit(solution)/shard_map/ppermute | solution.py:166
  26.3 1.3 %collective-permute-start.3 = (bf16[3,1,256,128]{3,2,1,0:T(8,128)(2,1)S(1)}, bf16[3,1,256,128]{3,2,1,0:T(8,128)(2,1)S(1)}, u32[]{:S(2)}, u32[]{:S(2)}) collective-permute-start(bf16[3,1,256,128]{3,2,1,0:T(8,128)(2,1)S(1)} %get-tuple-element.28), channel_id=1, source_target_pairs={{1,0},{2,1},{3,2},{5,4},{6,5},{7,6},{9,8},{10,9},{11,10},{13,12},{... | collective-permute-start | bytes 589832 | tf_op jit(solution)/shard_map/ppermute | solution.py:167
  27.6 1.2 fusion.5.sel_ref
  28.8 2.4 %collective-permute-done.3 = bf16[3,1,256,128]{3,2,1,0:T(8,128)(2,1)S(1)} collective-permute-done((bf16[3,1,256,128]{3,2,1,0:T(8,128)(2,1)S(1)}, bf16[3,1,256,128]{3,2,1,0:T(8,128)(2,1)S(1)}, u32[]{:S(2)}, u32[]{:S(2)}) %collective-permute-start.3) | collective-permute-done | bytes 196640 | tf_op jit(solution)/shard_map/ppermute | solution.py:167
  31.2 1.0 pad_maximum_fusion.ext_ref.act_ref
  32.2 5.0 %shard_map.92 = f32[2,256,128]{2,1,0:T(8,128)} custom-call(bf16[3,4,256,128]{3,2,1,0:T(8,128)(2,1)} %pad_maximum_fusion.ext_ref.act_ref, bf16[9,768,256]{2,1,0:T(8,128)(2,1)} %bitcast.77), custom_call_target="tpu_custom_call" | custom-call | flops 905969664 | bytes 4587520 | tf_op jit(solution)/shard_map/pallas_call | solution.py:43
  37.2 1.1 fusion.11
  38.5 0.3 fusion.10
  39.3 4.6 %collective-permute-start.4 = (bf16[1,2,256,128]{3,2,1,0:T(8,128)(2,1)S(1)}, bf16[1,2,256,128]{3,2,1,0:T(8,128)(2,1)S(1)}, u32[]{:S(2)}, u32[]{:S(2)}) collective-permute-start(bf16[1,2,256,128]{3,2,1,0:T(8,128)(2,1)S(1)} %bitcast.78), channel_id=1, source_target_pairs={{0,4},{4,8},{8,12},{1,5},{5,9},{9,13},{2,6},{6,10},{10,14},{3,7},{... | collective-permute-start | bytes 393224 | tf_op jit(solution)/shard_map/ppermute | solution.py:166
  43.8 1.3 %collective-permute-start.5 = (bf16[1,2,256,128]{3,2,1,0:T(8,128)(2,1)S(1)}, bf16[1,2,256,128]{3,2,1,0:T(8,128)(2,1)S(1)}, u32[]{:S(2)}, u32[]{:S(2)}) collective-permute-start(bf16[1,2,256,128]{3,2,1,0:T(8,128)(2,1)S(1)} %bitcast.79), channel_id=1, source_target_pairs={{4,0},{8,4},{12,8},{5,1},{9,5},{13,9},{6,2},{10,6},{14,10},{7,3},{... | collective-permute-start | bytes 393224 | tf_op jit(solution)/shard_map/ppermute | solution.py:167
  45.1 5.6 %shard_map.94 = f32[2,256,128]{2,1,0:T(8,128)} custom-call(bf16[3,4,256,128]{3,2,1,0:T(8,128)(2,1)} %pad_maximum_fusion.ext_ref.act_ref, bf16[2,256,128]{2,1,0:T(8,128)(2,1)} %copy-done.2, f32[256,256]{1,0:T(8,128)} %get-tuple-element.55.mask_ref, bf16[16,128,128]{2,1,0:T(8,128)(2,1)} %fusion.5.sel_ref), custom_call_target="tpu_custom_call" | custom-call | flops 1358954496 | bytes 1179648 | tf_op jit(solution)/shard_map/pallas_call | solution.py:103
  50.7 1.1 copy.71
  52.0 0.3 reshape.292
  52.7 1.0 pad_maximum_fusion.3
  53.7 5.8 %collective-permute-start.6 = (bf16[3,1,256,128]{3,2,1,0:T(8,128)(2,1)S(1)}, bf16[3,1,256,128]{3,2,1,0:T(8,128)(2,1)S(1)}, u32[]{:S(2)}, u32[]{:S(2)}) collective-permute-start(bf16[3,1,256,128]{3,2,1,0:T(8,128)(2,1)S(1)} %get-tuple-element.25), channel_id=1, source_target_pairs={{0,1},{1,2},{2,3},{4,5},{5,6},{6,7},{8,9},{9,10},{10,11},{12,13},{... | collective-permute-start | bytes 589832 | tf_op jit(solution)/shard_map/ppermute | solution.py:166
  59.5 1.5 %collective-permute-start.7 = (bf16[3,1,256,128]{3,2,1,0:T(8,128)(2,1)S(1)}, bf16[3,1,256,128]{3,2,1,0:T(8,128)(2,1)S(1)}, u32[]{:S(2)}, u32[]{:S(2)}) collective-permute-start(bf16[3,1,256,128]{3,2,1,0:T(8,128)(2,1)S(1)} %get-tuple-element.26), channel_id=1, source_target_pairs={{1,0},{2,1},{3,2},{5,4},{6,5},{7,6},{9,8},{10,9},{11,10},{13,12},{... | collective-permute-start | bytes 589832 | tf_op jit(solution)/shard_map/ppermute | solution.py:167
  61.2 1.6 %collective-permute-done.7 = bf16[3,1,256,128]{3,2,1,0:T(8,128)(2,1)S(1)} collective-permute-done((bf16[3,1,256,128]{3,2,1,0:T(8,128)(2,1)S(1)}, bf16[3,1,256,128]{3,2,1,0:T(8,128)(2,1)S(1)}, u32[]{:S(2)}, u32[]{:S(2)}) %collective-permute-start.7) | collective-permute-done | bytes 196640 | tf_op jit(solution)/shard_map/ppermute | solution.py:167
  62.9 1.0 pad_maximum_fusion.1.ext_ref
  63.8 5.0 %shard_map.93 = f32[2,256,128]{2,1,0:T(8,128)} custom-call(bf16[3,4,256,128]{3,2,1,0:T(8,128)(2,1)} %pad_maximum_fusion.1.ext_ref, bf16[9,768,256]{2,1,0:T(8,128)(2,1)} %bitcast.76), custom_call_target="tpu_custom_call" | custom-call | flops 905969664 | bytes 4587520 | tf_op jit(solution)/shard_map/pallas_call | solution.py:43
  68.9 1.0 convert_bitcast_fusion
  70.6 3.6 %collective-permute-start.8 = (f32[93184]{0:T(1024)S(1)}, f32[93184]{0:T(1024)S(1)}, u32[]{:S(2)}, u32[]{:S(2)}) collective-permute-start(f32[93184]{0:T(1024)S(1)} %pad_maximum_fusion.4), channel_id=1, source_target_pairs={{0,2},{1,3},{2,0},{3,1},{4,6},{5,7},{6,4},{7,5},{8,10},{9,11},{10,... | collective-permute-start | bytes 1118216 | tf_op jit(solution)/shard_map/ppermute | solution.py:136
  74.6 8.2 %collective-permute-done.8 = f32[93184]{0:T(1024)S(1)} collective-permute-done((f32[93184]{0:T(1024)S(1)}, f32[93184]{0:T(1024)S(1)}, u32[]{:S(2)}, u32[]{:S(2)}) %collective-permute-start.8) | collective-permute-done | bytes 372768 | tf_op jit(solution)/shard_map/ppermute | solution.py:136
  82.9 0.8 collective-permute-start.9
  83.7 1.1 collective-permute-done.9
  84.8 3.7 %collective-permute-start.10 = (f32[23296]{0:T(1024)S(1)}, f32[23296]{0:T(1024)S(1)}, u32[]{:S(2)}, u32[]{:S(2)}) collective-permute-start(f32[23296]{0:T(1024)S(1)} %pad_maximum_fusion.8), channel_id=1, source_target_pairs={{0,8},{4,12},{8,0},{12,4},{1,9},{5,13},{9,1},{13,5},{2,10},{6,14},... | collective-permute-start | bytes 279560 | tf_op jit(solution)/shard_map/ppermute | solution.py:136
  88.6 0.8 copy.82
  89.3 4.5 %collective-permute-done.10 = f32[23296]{0:T(1024)S(1)} collective-permute-done((f32[23296]{0:T(1024)S(1)}, f32[23296]{0:T(1024)S(1)}, u32[]{:S(2)}, u32[]{:S(2)}) %collective-permute-start.10) | collective-permute-done | bytes 93216 | tf_op jit(solution)/shard_map/ppermute | solution.py:136
  93.9 0.8 collective-permute-start.11
  94.9 0.8 copy.83
  95.7 2.3 %collective-permute-done.11 = f32[11648]{0:T(1024)S(1)} collective-permute-done((f32[11648]{0:T(1024)S(1)}, f32[11648]{0:T(1024)S(1)}, u32[]{:S(2)}, u32[]{:S(2)}) %collective-permute-start.11) | collective-permute-done | bytes 46624 | tf_op jit(solution)/shard_map/ppermute | solution.py:136
  98.1 0.8 collective-permute-start.12
  99.2 2.8 %collective-permute-done.12 = f32[8192]{0:T(1024)S(1)} collective-permute-done((f32[8192]{0:T(1024)S(1)}, f32[8192]{0:T(1024)S(1)}, u32[]{:S(2)}, u32[]{:S(2)}) %collective-permute-start.12) | collective-permute-done | bytes 32800 | tf_op jit(solution)/shard_map/ppermute | solution.py:146
  102.1 2.1 %collective-permute-start.13 = (f32[16384]{0:T(1024)S(1)}, f32[16384]{0:T(1024)S(1)}, u32[]{:S(2)}, u32[]{:S(2)}) collective-permute-start(f32[16384]{0:T(1024)S(1)} %pad_maximum_fusion.10), channel_id=1, source_target_pairs={{0,8},{4,12},{8,0},{12,4},{1,9},{5,13},{9,1},{13,5},{2,10},{6,14},... | collective-permute-start | bytes 196616 | tf_op jit(solution)/shard_map/ppermute | solution.py:146
  104.3 3.1 %collective-permute-done.13 = f32[16384]{0:T(1024)S(1)} collective-permute-done((f32[16384]{0:T(1024)S(1)}, f32[16384]{0:T(1024)S(1)}, u32[]{:S(2)}, u32[]{:S(2)}) %collective-permute-start.13) | collective-permute-done | bytes 65568 | tf_op jit(solution)/shard_map/ppermute | solution.py:146
  107.6 1.3 %collective-permute-done.14 = f32[36224]{0:T(1024)S(1)} collective-permute-done((f32[36224]{0:T(1024)S(1)}, f32[36224]{0:T(1024)S(1)}, u32[]{:S(2)}, u32[]{:S(2)}) %collective-permute-start.14) | collective-permute-done | bytes 144928 | tf_op jit(solution)/shard_map/ppermute | solution.py:146
  109.4 2.0 %collective-permute-start.15 = (f32[72448]{0:T(1024)S(1)}, f32[72448]{0:T(1024)S(1)}, u32[]{:S(2)}, u32[]{:S(2)}) collective-permute-start(f32[72448]{0:T(1024)S(1)} %pad_maximum_fusion.5), channel_id=1, source_target_pairs={{0,2},{1,3},{2,0},{3,1},{4,6},{5,7},{6,4},{7,5},{8,10},{9,11},{10,... | collective-permute-start | bytes 869384 | tf_op jit(solution)/shard_map/ppermute | solution.py:146
  111.5 7.1 %collective-permute-done.15 = f32[72448]{0:T(1024)S(1)} collective-permute-done((f32[72448]{0:T(1024)S(1)}, f32[72448]{0:T(1024)S(1)}, u32[]{:S(2)}, u32[]{:S(2)}) %collective-permute-start.15) | collective-permute-done | bytes 289824 | tf_op jit(solution)/shard_map/ppermute | solution.py:146
  118.8 0.3 copy.80
  119.2 0.8 fusion.12
  119.9 0.8 fusion.6
  (115 shorter events, 4.7 us)
Async XLA Ops:
  0.6 37.8 %copy-start = (bf16[256,256]{1,0:T(8,128)(2,1)S(1)}, bf16[256,256]{1,0:T(8,128)(2,1)}, u32[]{:S(2)}) copy-start(bf16[256,256]{1,0:T(8,128)(2,1)} %param.9) | copy-start | bytes 393220
  3.0 21.8 %collective-permute-start = (bf16[1,2,256,128]{3,2,1,0:T(8,128)(2,1)S(1)}, bf16[1,2,256,128]{3,2,1,0:T(8,128)(2,1)S(1)}, u32[]{:S(2)}, u32[]{:S(2)}) collective-permute-start(bf16[1,2,256,128]{3,2,1,0:T(8,128)(2,1)S(1)} %bitcast.82), channel_id=1, source_target_pairs={{0,4},{4,8},{8,12},{1,5},{5,9},{9,13},{2,6},{6,10},{10,14},{3,7},{... | collective-permute-start | bytes 393224 | tf_op jit(solution)/shard_map/ppermute | solution.py:166
  7.9 16.8 %collective-permute-start.1 = (bf16[1,2,256,128]{3,2,1,0:T(8,128)(2,1)S(1)}, bf16[1,2,256,128]{3,2,1,0:T(8,128)(2,1)S(1)}, u32[]{:S(2)}, u32[]{:S(2)}) collective-permute-start(bf16[1,2,256,128]{3,2,1,0:T(8,128)(2,1)S(1)} %bitcast.83), channel_id=1, source_target_pairs={{4,0},{8,4},{12,8},{5,1},{9,5},{13,9},{6,2},{10,6},{14,10},{7,3},{... | collective-permute-start | bytes 393224 | tf_op jit(solution)/shard_map/ppermute | solution.py:167
  14.4 6.1 %copy-start.4 = (bf16[256,1,2,128]{3,2,1,0:T(2,128)(2,1)S(1)}, bf16[256,1,2,128]{3,2,1,0:T(2,128)(2,1)}, u32[]{:S(2)}) copy-start(bf16[256,1,2,128]{3,2,1,0:T(2,128)(2,1)} %param.6) | copy-start | bytes 393220
  24.8 4.0 %collective-permute-start.2 = (bf16[3,1,256,128]{3,2,1,0:T(8,128)(2,1)S(1)}, bf16[3,1,256,128]{3,2,1,0:T(8,128)(2,1)S(1)}, u32[]{:S(2)}, u32[]{:S(2)}) collective-permute-start(bf16[3,1,256,128]{3,2,1,0:T(8,128)(2,1)S(1)} %get-tuple-element.27), channel_id=1, source_target_pairs={{0,1},{1,2},{2,3},{4,5},{5,6},{6,7},{8,9},{9,10},{10,11},{12,13},{... | collective-permute-start | bytes 589832 | tf_op jit(solution)/shard_map/ppermute | solution.py:166
  26.3 4.9 %collective-permute-start.3 = (bf16[3,1,256,128]{3,2,1,0:T(8,128)(2,1)S(1)}, bf16[3,1,256,128]{3,2,1,0:T(8,128)(2,1)S(1)}, u32[]{:S(2)}, u32[]{:S(2)}) collective-permute-start(bf16[3,1,256,128]{3,2,1,0:T(8,128)(2,1)S(1)} %get-tuple-element.28), channel_id=1, source_target_pairs={{1,0},{2,1},{3,2},{5,4},{6,5},{7,6},{9,8},{10,9},{11,10},{13,12},{... | collective-permute-start | bytes 589832 | tf_op jit(solution)/shard_map/ppermute | solution.py:167
  37.2 1.9 %copy-start.1 = (f32[2,256,128]{2,1,0:T(8,128)S(1)}, f32[2,256,128]{2,1,0:T(8,128)}, u32[]{:S(2)}) copy-start(f32[2,256,128]{2,1,0:T(8,128)} %shard_map.92) | copy-start | bytes 786436
  39.2 5.9 %copy-start.2 = (bf16[2,256,128]{2,1,0:T(8,128)(2,1)}, bf16[2,256,128]{2,1,0:T(8,128)(2,1)S(1)}, u32[]{:S(2)}) copy-start(bf16[2,256,128]{2,1,0:T(8,128)(2,1)S(1)} %fusion.8.delta_ref) | copy-start | bytes 393220
  39.3 13.5 %collective-permute-start.4 = (bf16[1,2,256,128]{3,2,1,0:T(8,128)(2,1)S(1)}, bf16[1,2,256,128]{3,2,1,0:T(8,128)(2,1)S(1)}, u32[]{:S(2)}, u32[]{:S(2)}) collective-permute-start(bf16[1,2,256,128]{3,2,1,0:T(8,128)(2,1)S(1)} %bitcast.78), channel_id=1, source_target_pairs={{0,4},{4,8},{8,12},{1,5},{5,9},{9,13},{2,6},{6,10},{10,14},{3,7},{... | collective-permute-start | bytes 393224 | tf_op jit(solution)/shard_map/ppermute | solution.py:166
  43.8 8.9 %collective-permute-start.5 = (bf16[1,2,256,128]{3,2,1,0:T(8,128)(2,1)S(1)}, bf16[1,2,256,128]{3,2,1,0:T(8,128)(2,1)S(1)}, u32[]{:S(2)}, u32[]{:S(2)}) collective-permute-start(bf16[1,2,256,128]{3,2,1,0:T(8,128)(2,1)S(1)} %bitcast.79), channel_id=1, source_target_pairs={{4,0},{8,4},{12,8},{5,1},{9,5},{13,9},{6,2},{10,6},{14,10},{7,3},{... | collective-permute-start | bytes 393224 | tf_op jit(solution)/shard_map/ppermute | solution.py:167
  50.7 12.1 %copy-start.3 = (bf16[2,256,128]{2,1,0:T(8,128)(2,1)S(1)}, bf16[2,256,128]{2,1,0:T(8,128)(2,1)}, u32[]{:S(2)}) copy-start(bf16[2,256,128]{2,1,0:T(8,128)(2,1)} %copy-done.2) | copy-start | bytes 393220
  53.7 7.5 %collective-permute-start.6 = (bf16[3,1,256,128]{3,2,1,0:T(8,128)(2,1)S(1)}, bf16[3,1,256,128]{3,2,1,0:T(8,128)(2,1)S(1)}, u32[]{:S(2)}, u32[]{:S(2)}) collective-permute-start(bf16[3,1,256,128]{3,2,1,0:T(8,128)(2,1)S(1)} %get-tuple-element.25), channel_id=1, source_target_pairs={{0,1},{1,2},{2,3},{4,5},{5,6},{6,7},{8,9},{9,10},{10,11},{12,13},{... | collective-permute-start | bytes 589832 | tf_op jit(solution)/shard_map/ppermute | solution.py:166
  59.5 3.3 %collective-permute-start.7 = (bf16[3,1,256,128]{3,2,1,0:T(8,128)(2,1)S(1)}, bf16[3,1,256,128]{3,2,1,0:T(8,128)(2,1)S(1)}, u32[]{:S(2)}, u32[]{:S(2)}) collective-permute-start(bf16[3,1,256,128]{3,2,1,0:T(8,128)(2,1)S(1)} %get-tuple-element.26), channel_id=1, source_target_pairs={{1,0},{2,1},{3,2},{5,4},{6,5},{7,6},{9,8},{10,9},{11,10},{13,12},{... | collective-permute-start | bytes 589832 | tf_op jit(solution)/shard_map/ppermute | solution.py:167
  70.3 24.4 %copy-start.5 = (bf16[256,256]{1,0:T(8,128)(2,1)S(1)}, bf16[256,256]{1,0:T(8,128)(2,1)}, u32[]{:S(2)}) copy-start(bf16[256,256]{1,0:T(8,128)(2,1)} %param.7) | copy-start | bytes 393220
  70.6 12.2 %collective-permute-start.8 = (f32[93184]{0:T(1024)S(1)}, f32[93184]{0:T(1024)S(1)}, u32[]{:S(2)}, u32[]{:S(2)}) collective-permute-start(f32[93184]{0:T(1024)S(1)} %pad_maximum_fusion.4), channel_id=1, source_target_pairs={{0,2},{1,3},{2,0},{3,1},{4,6},{5,7},{6,4},{7,5},{8,10},{9,11},{10,... | collective-permute-start | bytes 1118216 | tf_op jit(solution)/shard_map/ppermute | solution.py:136
  82.9 1.8 %collective-permute-start.9 = (f32[46592]{0:T(1024)S(1)}, f32[46592]{0:T(1024)S(1)}, u32[]{:S(2)}, u32[]{:S(2)}) collective-permute-start(f32[46592]{0:T(1024)S(1)} %pad_maximum_fusion.6), channel_id=1, source_target_pairs={{0,1},{1,0},{2,3},{3,2},{4,5},{5,4},{6,7},{7,6},{8,9},{9,8},{10,11... | collective-permute-start | bytes 559112 | tf_op jit(solution)/shard_map/ppermute | solution.py:136
  84.8 9.0 %collective-permute-start.10 = (f32[23296]{0:T(1024)S(1)}, f32[23296]{0:T(1024)S(1)}, u32[]{:S(2)}, u32[]{:S(2)}) collective-permute-start(f32[23296]{0:T(1024)S(1)} %pad_maximum_fusion.8), channel_id=1, source_target_pairs={{0,8},{4,12},{8,0},{12,4},{1,9},{5,13},{9,1},{13,5},{2,10},{6,14},... | collective-permute-start | bytes 279560 | tf_op jit(solution)/shard_map/ppermute | solution.py:136
  93.9 4.2 %collective-permute-start.11 = (f32[11648]{0:T(1024)S(1)}, f32[11648]{0:T(1024)S(1)}, u32[]{:S(2)}, u32[]{:S(2)}) collective-permute-start(f32[11648]{0:T(1024)S(1)} %pad_maximum_fusion.12), channel_id=1, source_target_pairs={{0,4},{4,0},{8,12},{12,8},{1,5},{5,1},{9,13},{13,9},{2,6},{6,2},{1... | collective-permute-start | bytes 139784 | tf_op jit(solution)/shard_map/ppermute | solution.py:136
  98.1 4.0 %collective-permute-start.12 = (f32[8192]{0:T(1024)S(1)}, f32[8192]{0:T(1024)S(1)}, u32[]{:S(2)}, u32[]{:S(2)}) collective-permute-start(f32[8192]{0:T(1024)S(1)} %pad_maximum_fusion.14), channel_id=1, source_target_pairs={{0,4},{4,0},{8,12},{12,8},{1,5},{5,1},{9,13},{13,9},{2,6},{6,2},{1... | collective-permute-start | bytes 98312 | tf_op jit(solution)/shard_map/ppermute | solution.py:146
  102.1 5.2 %collective-permute-start.13 = (f32[16384]{0:T(1024)S(1)}, f32[16384]{0:T(1024)S(1)}, u32[]{:S(2)}, u32[]{:S(2)}) collective-permute-start(f32[16384]{0:T(1024)S(1)} %pad_maximum_fusion.10), channel_id=1, source_target_pairs={{0,8},{4,12},{8,0},{12,4},{1,9},{5,13},{9,1},{13,5},{2,10},{6,14},... | collective-permute-start | bytes 196616 | tf_op jit(solution)/shard_map/ppermute | solution.py:146
  107.4 1.4 %collective-permute-start.14 = (f32[36224]{0:T(1024)S(1)}, f32[36224]{0:T(1024)S(1)}, u32[]{:S(2)}, u32[]{:S(2)}) collective-permute-start(f32[36224]{0:T(1024)S(1)} %pad_maximum_fusion.7), channel_id=1, source_target_pairs={{0,1},{1,0},{2,3},{3,2},{4,5},{5,4},{6,7},{7,6},{8,9},{9,8},{10,11... | collective-permute-start | bytes 434696 | tf_op jit(solution)/shard_map/ppermute | solution.py:146
  109.4 9.2 %collective-permute-start.15 = (f32[72448]{0:T(1024)S(1)}, f32[72448]{0:T(1024)S(1)}, u32[]{:S(2)}, u32[]{:S(2)}) collective-permute-start(f32[72448]{0:T(1024)S(1)} %pad_maximum_fusion.5), channel_id=1, source_target_pairs={{0,2},{1,3},{2,0},{3,1},{4,6},{5,7},{6,4},{7,5},{8,10},{9,11},{10,... | collective-permute-start | bytes 869384 | tf_op jit(solution)/shard_map/ppermute | solution.py:146

commit v5 on v4

--- a/solution.py
+++ b/solution.py
@@ -116,11 +116,13 @@
 
 def tree_sum(blocks, order):
     steps = []
-    for axis in order:
-        bit = lax.axis_size(axis) // 2
-        while bit >= 1:
-            steps.append((axis, bit))
-            bit //= 2
+    for axis, rising in order:
+        bits = []
+        bit = 1
+        while bit < lax.axis_size(axis):
+            bits.append(bit)
+            bit *= 2
+        steps += [(axis, bit) for bit in (bits if rising else bits[::-1])]
     pieces = [block.reshape(-1) for block, _, _ in blocks]
     done = []
     for axis, bit in steps:
@@ -176,13 +178,22 @@
 
 def conv_weights(group_weight):
     channels = group_weight.shape[0]
-    tiled = jnp.tile(group_weight, (1, channels // GW, 1, 1, 1))
     group_of = jnp.arange(channels) // GW
     mask = (group_of[:, None] == group_of[None, :]).astype(group_weight.dtype)
-    dense = tiled * mask[:, :, None, None, None]
-    forward = dense.transpose(2, 3, 4, 0, 1).reshape(9, 3 * channels, channels)
-    backward = dense[:, :, ::-1, ::-1, ::-1].transpose(2, 3, 4, 1, 0).reshape(9, 3 * channels, channels)
+    compact = group_weight.reshape(channels, GW, 27)
+    forward = jnp.broadcast_to(
+        compact.transpose(2, 0, 1)[:, :, None, :], (27, channels, channels // GW, GW)
+    ).reshape(27, channels, channels)
+    backward = jnp.broadcast_to(
+        compact[:, :, ::-1].transpose(2, 1, 0)[:, None, :, :], (27, channels // GW, GW, channels)
+    ).reshape(27, channels, channels)
+    forward = (forward * mask).reshape(9, 3 * channels, channels)
+    backward = (backward * mask).reshape(9, 3 * channels, channels)
     return forward, backward
+
+
+def rounded(values):
+    return lax.reduce_precision(values, exponent_bits=8, mantissa_bits=7).astype(jnp.bfloat16)
 
 
 def per_device(volume, cotangent, first_weight, group_weight, third_weight):
@@ -203,31 +214,25 @@
     first_pre = lax.dot_general(
         first_weight, flattened, contract_lead, preferred_element_type=jnp.float32
     )
-    first_act = jax.nn.silu(first_pre).astype(jnp.bfloat16)
+    first_act = rounded(jax.nn.silu(first_pre))
     act_ext = halo(to_rows(first_act))
     group_pre = conv_call(act_ext, forward_kernel)
-    group_act = jax.nn.silu(group_pre).astype(jnp.bfloat16)
+    group_act = rounded(jax.nn.silu(group_pre))
     act_flat = from_rows(group_act)
     summed = flattened.astype(jnp.float32) + lax.dot_general(
         third_weight, act_flat, contract_lead, preferred_element_type=jnp.float32
     )
     block_output = jax.nn.silu(summed).astype(jnp.bfloat16).reshape(volume.shape)
-    third_delta = (cotangent.reshape(channels, -1).astype(jnp.float32) * silu_slope(summed)).astype(
-        jnp.bfloat16
-    )
+    third_delta = rounded(cotangent.reshape(channels, -1).astype(jnp.float32) * silu_slope(summed))
     third_part = lax.dot_general(
         act_flat, third_delta, contract_tail, preferred_element_type=jnp.float32
     )
-    hidden_grad = jnp.dot(third_weight, third_delta, preferred_element_type=jnp.float32).astype(
-        jnp.bfloat16
-    )
-    group_delta = (
-        to_rows(hidden_grad)[0].astype(jnp.float32) * silu_slope(group_pre)
-    ).astype(jnp.bfloat16)
+    hidden_grad = rounded(jnp.dot(third_weight, third_delta, preferred_element_type=jnp.float32))
+    group_delta = rounded(to_rows(hidden_grad)[0].astype(jnp.float32) * silu_slope(group_pre))
     delta_ext = halo(group_delta[None])
-    inner_grad = from_rows(conv_call(delta_ext, backward_kernel).astype(jnp.bfloat16))
+    inner_grad = from_rows(rounded(conv_call(delta_ext, backward_kernel)))
     kernel_part = wgrad_call(act_ext, group_delta)
-    first_delta = (inner_grad.astype(jnp.float32) * silu_slope(first_pre)).astype(jnp.bfloat16)
+    first_delta = rounded(inner_grad.astype(jnp.float32) * silu_slope(first_pre))
     first_part = lax.dot_general(
         flattened, first_delta, contract_tail, preferred_element_type=jnp.float32
     )
@@ -247,7 +252,7 @@
             (third_part, ("sub", "grp"), ("sub", "grp")),
             (kernel_laid, ("sub", "grp"), ("sub",)),
         ],
-        ("sub", "grp"),
+        (("sub", True), ("grp", False)),
     )
     first_grad = first_sum.reshape(first_part.shape) * factor
     third_grad = third_sum.reshape(third_part.shape) * factor

time: 121 us -> 128 us (1.058)
  local copies, waits for them, and re-layouts: 17.2 us -> 29.6 us
  waiting for transfers between devices: 34.4 us -> 31.2 us
  starting transfers between devices: 36 us -> 33.5 us
    reshape x0 -> x2, local copies, waits for them, and re-layouts: none -> 17.2 us  [conv_weights(): forward = jnp.broadcast_to(compact.transpose(2, 0, 1)[:, :, None, :], (27...]
    transpose x1 -> x2, local copies, waits for them, and re-layouts: 6.06 us -> 0.93 us  [the longest x1 0.92 us: conv_weights(): compact.transpose(2, 0, 1)[:, :, None, :]]
    rev x1 -> x0, local copies, waits for them, and re-layouts: 4.11 us -> none  [conv_weights(): dense[:, :, ::-1, ::-1, ::-1].transpose(2, 3, 4, 1, 0)]
    broadcast_in_dim x0 -> x2, local copies, waits for them, and re-layouts: none -> 2.85 us  [the longest x1 2.62 us: conv_weights(): jnp.broadcast_to(compact.transpose(2, 0, 1)[:, :, None, :], (27, channels...]
    ppermute x4, waiting for transfers between devices: 16.1 us -> 13.9 us  [tree_sum(): got = lax.ppermute(jnp.concatenate(sends), axis, pairs)]
    ppermute x4, starting transfers between devices: 5.02 us -> 2.95 us  [tree_sum(): lax.ppermute(jnp.concatenate([pieces[n] for n in members]), axis, pairs)]
    unnamed x19 -> x23, local copies, waits for them, and re-layouts: 2.91 us -> 4.28 us
  transfers between devices with their start and end apart: 16 -> 16, of which waited for: 10 -> 10; matrix products, arithmetic and copies ran while one was open for 18% -> 25% of each run, Pallas kernels for 5% -> 4%
where the time goes in v5:
time: 128 us; the launch traced here: 127 us
  starting transfers between devices  33.5 us (26%)
  waiting for transfers between devices  31.2 us (24%)
  local copies, waits for them, and re-layouts  29.6 us (23%)
  Pallas kernels  15.6 us (12%)
  other arithmetic  13.1 us (10%)
  matrix products  2.3 us (2%)
  between operations  1.49 us (1%)
    reshape x2, local copies, waits for them, and re-layouts, conv_weights(): forward = jnp.broadcast_to(compact.transpose(2, 0, 1)[:, :, None, :], (27...  17.2 us
    ppermute x4, starting transfers between devices, halo(): lax.ppermute(lax.slice_in_dim(block, size - 1, size, axis=dim), axis, up)  16.8 us
    ppermute x4, waiting for transfers between devices, tree_sum(): got = lax.ppermute(jnp.concatenate(sends), axis, pairs)  13.9 us
    ppermute x4, waiting for transfers between devices, tree_sum(): lax.ppermute(jnp.concatenate([pieces[n] for n in members]), axis, pairs)  13.2 us
    pallas_call x2, Pallas kernels, conv_call(): pl.pallas_call(conv_body, out_shape=jax.ShapeDtypeStruct((height, channel...  10 us
    ppermute x4, starting transfers between devices, tree_sum(): got = lax.ppermute(jnp.concatenate(sends), axis, pairs)  8.43 us
    pallas_call x1, Pallas kernels, wgrad_call(): pl.pallas_call(wgrad_body, out_shape=jax.ShapeDtypeStruct((blocks, channe...  5.6 us
    ppermute x4, starting transfers between devices, halo(): high = lax.ppermute(lax.slice_in_dim(block, 0, 1, axis=dim), axis, down)  5.35 us
  transfers between devices with their start and end apart: 16, of which 10 were waited for; matrix products, arithmetic and copies ran while one was open for 25% of the time, Pallas kernels for 4%

profile of v5, /device:TPU:0, one launch (start us, length us, event | category | flops | bytes accessed | tf_op | source)
XLA Modules:
  0.0 126.8 jit_solution(4598857583783470896)
XLA Ops:
  0.6 1.0 copy.57
  1.7 1.1 reduce-precision_convert_fusion.2
  3.0 4.9 %collective-permute-start = (bf16[1,2,256,128]{3,2,1,0:T(8,128)(2,1)S(1)}, bf16[1,2,256,128]{3,2,1,0:T(8,128)(2,1)S(1)}, u32[]{:S(2)}, u32[]{:S(2)}) collective-permute-start(bf16[1,2,256,128]{3,2,1,0:T(8,128)(2,1)S(1)} %bitcast.90), channel_id=1, source_target_pairs={{0,4},{4,8},{8,12},{1,5},{5,9},{9,13},{2,6},{6,10},{10,14},{3,7},{... | collective-permute-start | bytes 393224 | tf_op jit(solution)/shard_map/ppermute | solution.py:168
  7.9 1.3 %collective-permute-start.1 = (bf16[1,2,256,128]{3,2,1,0:T(8,128)(2,1)S(1)}, bf16[1,2,256,128]{3,2,1,0:T(8,128)(2,1)S(1)}, u32[]{:S(2)}, u32[]{:S(2)}) collective-permute-start(bf16[1,2,256,128]{3,2,1,0:T(8,128)(2,1)S(1)} %bitcast.91), channel_id=1, source_target_pairs={{4,0},{8,4},{12,8},{5,1},{9,5},{13,9},{6,2},{10,6},{14,10},{7,3},{... | collective-permute-start | bytes 393224 | tf_op jit(solution)/shard_map/ppermute | solution.py:169
  9.2 0.8 compare_convert_fusion
  10.1 0.9 copy.59
  11.0 2.6 %broadcast_in_dim.6 = bf16[27,256,32,8]{1,0,3,2:T(8,128)(2,1)} broadcast(bf16[27,256,8]{1,0,2:T(8,128)(2,1)S(1)} %copy.59), dimensions={0,1,3} | broadcast | bytes 3649536 | tf_op jit(solution)/shard_map/broadcast_in_dim | solution.py:184
  13.6 8.6 %reshape.294 = bf16[9,768,256]{1,0,2:T(8,128)(2,1)} reshape(bf16[27,256,32,8]{1,0,3,2:T(8,128)(2,1)} %broadcast_in_dim.6) | data formatting | bytes 7077888 | tf_op jit(solution)/shard_map/reshape | solution.py:186
  22.2 8.6 %copy.60 = bf16[9,768,256]{2,1,0:T(8,128)(2,1)} copy(bf16[9,768,256]{1,0,2:T(8,128)(2,1)} %reshape.294) | data formatting | bytes 7077888 | tf_op jit(solution)/shard_map/reshape | solution.py:186
  30.9 0.4 mul.87
  31.6 1.4 %copy-done.1 = bf16[9,768,256]{2,1,0:T(8,128)(2,1)S(1)} copy-done((bf16[9,768,256]{2,1,0:T(8,128)(2,1)S(1)}, bf16[9,768,256]{2,1,0:T(8,128)(2,1)}, u32[]{:S(2)}) %copy-start.1) | copy-done | bytes 3538968
  32.9 3.4 %bitcast_multiply_fusion = (bf16[9,768,256]{2,1,0:T(8,128)(2,1)}, bf16[9,768,256]{2,1,0:T(8,128)(2,1)}) fusion(bf16[9,768,256]{2,1,0:T(8,128)(2,1)S(1)} %bitcast.85, bf16[9,768,256]{2,1,0:T(8,128)(2,1)S(1)} %copy-done.1, bf16[9,768,256]{2,1,0:T(8,128)(2,1)S(1)} %bitcast.84), kind=kLoop, calls=%fused_computation | loop fusion | flops 3538944 | bytes 17694720 | tf_op jit(solution)/shard_map/mul | solution.py:191
  36.5 1.5 %collective-permute-start.2 = (bf16[3,1,256,128]{3,2,1,0:T(8,128)(2,1)S(1)}, bf16[3,1,256,128]{3,2,1,0:T(8,128)(2,1)S(1)}, u32[]{:S(2)}, u32[]{:S(2)}) collective-permute-start(bf16[3,1,256,128]{3,2,1,0:T(8,128)(2,1)S(1)} %get-tuple-element.29), channel_id=1, source_target_pairs={{0,1},{1,2},{2,3},{4,5},{5,6},{6,7},{8,9},{9,10},{10,11},{12,13},{... | collective-permute-start | bytes 589832 | tf_op jit(solution)/shard_map/ppermute | solution.py:168
  38.0 1.3 %collective-permute-start.3 = (bf16[3,1,256,128]{3,2,1,0:T(8,128)(2,1)S(1)}, bf16[3,1,256,128]{3,2,1,0:T(8,128)(2,1)S(1)}, u32[]{:S(2)}, u32[]{:S(2)}) collective-permute-start(bf16[3,1,256,128]{3,2,1,0:T(8,128)(2,1)S(1)} %get-tuple-element.30), channel_id=1, source_target_pairs={{1,0},{2,1},{3,2},{5,4},{6,5},{7,6},{9,8},{10,9},{11,10},{13,12},{... | collective-permute-start | bytes 589832 | tf_op jit(solution)/shard_map/ppermute | solution.py:169
  39.3 1.2 fusion.5.sel_ref
  40.5 2.4 %collective-permute-done.3 = bf16[3,1,256,128]{3,2,1,0:T(8,128)(2,1)S(1)} collective-permute-done((bf16[3,1,256,128]{3,2,1,0:T(8,128)(2,1)S(1)}, bf16[3,1,256,128]{3,2,1,0:T(8,128)(2,1)S(1)}, u32[]{:S(2)}, u32[]{:S(2)}) %collective-permute-start.3) | collective-permute-done | bytes 196640 | tf_op jit(solution)/shard_map/ppermute | solution.py:169
  42.9 1.0 pad_maximum_fusion.ext_ref.act_ref
  43.9 5.0 %shard_map.92 = f32[2,256,128]{2,1,0:T(8,128)} custom-call(bf16[3,4,256,128]{3,2,1,0:T(8,128)(2,1)} %pad_maximum_fusion.ext_ref.act_ref, bf16[9,768,256]{2,1,0:T(8,128)(2,1)} %get-tuple-element.26.w_ref), custom_call_target="tpu_custom_call" | custom-call | flops 905969664 | bytes 4587520 | tf_op jit(solution)/shard_map/pallas_call | solution.py:43
  49.0 1.1 fusion.14
  51.0 4.6 %collective-permute-start.4 = (bf16[1,2,256,128]{3,2,1,0:T(8,128)(2,1)S(1)}, bf16[1,2,256,128]{3,2,1,0:T(8,128)(2,1)S(1)}, u32[]{:S(2)}, u32[]{:S(2)}) collective-permute-start(bf16[1,2,256,128]{3,2,1,0:T(8,128)(2,1)S(1)} %bitcast.86), channel_id=1, source_target_pairs={{0,4},{4,8},{8,12},{1,5},{5,9},{9,13},{2,6},{6,10},{10,14},{3,7},{... | collective-permute-start | bytes 393224 | tf_op jit(solution)/shard_map/ppermute | solution.py:168
  55.5 1.3 %collective-permute-start.5 = (bf16[1,2,256,128]{3,2,1,0:T(8,128)(2,1)S(1)}, bf16[1,2,256,128]{3,2,1,0:T(8,128)(2,1)S(1)}, u32[]{:S(2)}, u32[]{:S(2)}) collective-permute-start(bf16[1,2,256,128]{3,2,1,0:T(8,128)(2,1)S(1)} %bitcast.87), channel_id=1, source_target_pairs={{4,0},{8,4},{12,8},{5,1},{9,5},{13,9},{6,2},{10,6},{14,10},{7,3},{... | collective-permute-start | bytes 393224 | tf_op jit(solution)/shard_map/ppermute | solution.py:169
  56.9 5.6 %shard_map.94 = f32[2,256,128]{2,1,0:T(8,128)} custom-call(bf16[3,4,256,128]{3,2,1,0:T(8,128)(2,1)} %pad_maximum_fusion.ext_ref.act_ref, bf16[2,256,128]{2,1,0:T(8,128)(2,1)} %copy-done.3, f32[256,256]{1,0:T(8,128)} %get-tuple-element.55.mask_ref, bf16[16,128,128]{2,1,0:T(8,128)(2,1)} %fusion.5.sel_ref), custom_call_target="tpu_custom_call" | custom-call | flops 1358954496 | bytes 1179648 | tf_op jit(solution)/shard_map/pallas_call | solution.py:103
  62.5 1.1 copy.70
  63.7 0.3 reshape.300
  64.5 1.0 pad_maximum_fusion.3
  65.4 5.8 %collective-permute-start.6 = (bf16[3,1,256,128]{3,2,1,0:T(8,128)(2,1)S(1)}, bf16[3,1,256,128]{3,2,1,0:T(8,128)(2,1)S(1)}, u32[]{:S(2)}, u32[]{:S(2)}) collective-permute-start(bf16[3,1,256,128]{3,2,1,0:T(8,128)(2,1)S(1)} %get-tuple-element.27), channel_id=1, source_target_pairs={{0,1},{1,2},{2,3},{4,5},{5,6},{6,7},{8,9},{9,10},{10,11},{12,13},{... | collective-permute-start | bytes 589832 | tf_op jit(solution)/shard_map/ppermute | solution.py:168
  71.2 1.5 %collective-permute-start.7 = (bf16[3,1,256,128]{3,2,1,0:T(8,128)(2,1)S(1)}, bf16[3,1,256,128]{3,2,1,0:T(8,128)(2,1)S(1)}, u32[]{:S(2)}, u32[]{:S(2)}) collective-permute-start(bf16[3,1,256,128]{3,2,1,0:T(8,128)(2,1)S(1)} %get-tuple-element.28), channel_id=1, source_target_pairs={{1,0},{2,1},{3,2},{5,4},{6,5},{7,6},{9,8},{10,9},{11,10},{13,12},{... | collective-permute-start | bytes 589832 | tf_op jit(solution)/shard_map/ppermute | solution.py:169
  72.9 1.6 %collective-permute-done.7 = bf16[3,1,256,128]{3,2,1,0:T(8,128)(2,1)S(1)} collective-permute-done((bf16[3,1,256,128]{3,2,1,0:T(8,128)(2,1)S(1)}, bf16[3,1,256,128]{3,2,1,0:T(8,128)(2,1)S(1)}, u32[]{:S(2)}, u32[]{:S(2)}) %collective-permute-start.7) | collective-permute-done | bytes 196640 | tf_op jit(solution)/shard_map/ppermute | solution.py:169
  74.6 1.0 pad_maximum_fusion.1.ext_ref
  75.6 5.0 %shard_map.93 = f32[2,256,128]{2,1,0:T(8,128)} custom-call(bf16[3,4,256,128]{3,2,1,0:T(8,128)(2,1)} %pad_maximum_fusion.1.ext_ref, bf16[9,768,256]{2,1,0:T(8,128)(2,1)} %get-tuple-element.25.w_ref), custom_call_target="tpu_custom_call" | custom-call | flops 905969664 | bytes 4587520 | tf_op jit(solution)/shard_map/pallas_call | solution.py:43
  80.6 1.0 convert_bitcast_fusion
  82.3 3.8 %collective-permute-start.8 = (f32[93184]{0:T(1024)S(1)}, f32[93184]{0:T(1024)S(1)}, u32[]{:S(2)}, u32[]{:S(2)}) collective-permute-start(f32[93184]{0:T(1024)S(1)} %pad_maximum_fusion.4), channel_id=1, source_target_pairs={{0,1},{1,0},{2,3},{3,2},{4,5},{5,4},{6,7},{7,6},{8,9},{9,8},{10,11... | collective-permute-start | bytes 1118216 | tf_op jit(solution)/shard_map/ppermute | solution.py:138
  86.6 0.9 collective-permute-done.8
  87.7 6.9 %collective-permute-done.9 = f32[46592]{0:T(1024)S(1)} collective-permute-done((f32[46592]{0:T(1024)S(1)}, f32[46592]{0:T(1024)S(1)}, u32[]{:S(2)}, u32[]{:S(2)}) %collective-permute-start.9) | collective-permute-done | bytes 186400 | tf_op jit(solution)/shard_map/ppermute | solution.py:138
  94.8 3.7 %collective-permute-start.10 = (f32[23296]{0:T(1024)S(1)}, f32[23296]{0:T(1024)S(1)}, u32[]{:S(2)}, u32[]{:S(2)}) collective-permute-start(f32[23296]{0:T(1024)S(1)} %pad_maximum_fusion.8), channel_id=1, source_target_pairs={{0,8},{4,12},{8,0},{12,4},{1,9},{5,13},{9,1},{13,5},{2,10},{6,14},... | collective-permute-start | bytes 279560 | tf_op jit(solution)/shard_map/ppermute | solution.py:138
  98.5 0.8 copy.81
  99.2 3.7 %collective-permute-done.10 = f32[23296]{0:T(1024)S(1)} collective-permute-done((f32[23296]{0:T(1024)S(1)}, f32[23296]{0:T(1024)S(1)}, u32[]{:S(2)}, u32[]{:S(2)}) %collective-permute-start.10) | collective-permute-done | bytes 93216 | tf_op jit(solution)/shard_map/ppermute | solution.py:138
  103.1 0.7 collective-permute-start.11
  104.0 0.8 copy.82
  104.8 2.4 %collective-permute-done.11 = f32[11648]{0:T(1024)S(1)} collective-permute-done((f32[11648]{0:T(1024)S(1)}, f32[11648]{0:T(1024)S(1)}, u32[]{:S(2)}, u32[]{:S(2)}) %collective-permute-start.11) | collective-permute-done | bytes 46624 | tf_op jit(solution)/shard_map/ppermute | solution.py:138
  107.2 0.7 collective-permute-start.12
  108.3 2.9 %collective-permute-done.12 = f32[8192]{0:T(1024)S(1)} collective-permute-done((f32[8192]{0:T(1024)S(1)}, f32[8192]{0:T(1024)S(1)}, u32[]{:S(2)}, u32[]{:S(2)}) %collective-permute-start.12) | collective-permute-done | bytes 32800 | tf_op jit(solution)/shard_map/ppermute | solution.py:148
  111.3 2.1 %collective-permute-start.13 = (f32[16384]{0:T(1024)S(1)}, f32[16384]{0:T(1024)S(1)}, u32[]{:S(2)}, u32[]{:S(2)}) collective-permute-start(f32[16384]{0:T(1024)S(1)} %pad_maximum_fusion.10), channel_id=1, source_target_pairs={{0,8},{4,12},{8,0},{12,4},{1,9},{5,13},{9,1},{13,5},{2,10},{6,14},... | collective-permute-start | bytes 196616 | tf_op jit(solution)/shard_map/ppermute | solution.py:148
  113.4 3.8 %collective-permute-done.13 = f32[16384]{0:T(1024)S(1)} collective-permute-done((f32[16384]{0:T(1024)S(1)}, f32[16384]{0:T(1024)S(1)}, u32[]{:S(2)}, u32[]{:S(2)}) %collective-permute-start.13) | collective-permute-done | bytes 65568 | tf_op jit(solution)/shard_map/ppermute | solution.py:148
  117.4 5.1 %collective-permute-done.14 = f32[36224]{0:T(1024)S(1)} collective-permute-done((f32[36224]{0:T(1024)S(1)}, f32[36224]{0:T(1024)S(1)}, u32[]{:S(2)}, u32[]{:S(2)}) %collective-permute-start.14) | collective-permute-done | bytes 144928 | tf_op jit(solution)/shard_map/ppermute | solution.py:148
  123.2 1.4 %collective-permute-done.15 = f32[72448]{0:T(1024)S(1)} collective-permute-done((f32[72448]{0:T(1024)S(1)}, f32[72448]{0:T(1024)S(1)}, u32[]{:S(2)}, u32[]{:S(2)}) %collective-permute-start.15) | collective-permute-done | bytes 289824 | tf_op jit(solution)/shard_map/ppermute | solution.py:148
  125.2 0.8 fusion.15
  126.0 0.8 fusion.6
  (123 shorter events, 5.6 us)
Async XLA Ops:
  0.6 49.5 %copy-start = (bf16[256,256]{1,0:T(8,128)(2,1)S(1)}, bf16[256,256]{1,0:T(8,128)(2,1)}, u32[]{:S(2)}) copy-start(bf16[256,256]{1,0:T(8,128)(2,1)} %param.9) | copy-start | bytes 393220
  3.0 33.5 %collective-permute-start = (bf16[1,2,256,128]{3,2,1,0:T(8,128)(2,1)S(1)}, bf16[1,2,256,128]{3,2,1,0:T(8,128)(2,1)S(1)}, u32[]{:S(2)}, u32[]{:S(2)}) collective-permute-start(bf16[1,2,256,128]{3,2,1,0:T(8,128)(2,1)S(1)} %bitcast.90), channel_id=1, source_target_pairs={{0,4},{4,8},{8,12},{1,5},{5,9},{9,13},{2,6},{6,10},{10,14},{3,7},{... | collective-permute-start | bytes 393224 | tf_op jit(solution)/shard_map/ppermute | solution.py:168
  7.9 28.5 %collective-permute-start.1 = (bf16[1,2,256,128]{3,2,1,0:T(8,128)(2,1)S(1)}, bf16[1,2,256,128]{3,2,1,0:T(8,128)(2,1)S(1)}, u32[]{:S(2)}, u32[]{:S(2)}) collective-permute-start(bf16[1,2,256,128]{3,2,1,0:T(8,128)(2,1)S(1)} %bitcast.91), channel_id=1, source_target_pairs={{4,0},{8,4},{12,8},{5,1},{9,5},{13,9},{6,2},{10,6},{14,10},{7,3},{... | collective-permute-start | bytes 393224 | tf_op jit(solution)/shard_map/ppermute | solution.py:169
  22.2 8.6 %copy-start.5 = (bf16[256,8,3,3,3]{0,1,4,3,2:T(8,128)(2,1)S(1)}, bf16[256,8,3,3,3]{0,1,4,3,2:T(8,128)(2,1)}, u32[]{:S(2)}) copy-start(bf16[256,8,3,3,3]{0,1,4,3,2:T(8,128)(2,1)} %param.8) | copy-start | bytes 331780
  22.2 8.6 %copy-start.6 = (bf16[256,1,2,128]{3,2,1,0:T(2,128)(2,1)S(1)}, bf16[256,1,2,128]{3,2,1,0:T(2,128)(2,1)}, u32[]{:S(2)}) copy-start(bf16[256,1,2,128]{3,2,1,0:T(2,128)(2,1)} %param.6) | copy-start | bytes 393220
  30.9 2.0 %copy-start.1 = (bf16[9,768,256]{2,1,0:T(8,128)(2,1)S(1)}, bf16[9,768,256]{2,1,0:T(8,128)(2,1)}, u32[]{:S(2)}) copy-start(bf16[9,768,256]{2,1,0:T(8,128)(2,1)} %copy.60) | copy-start | bytes 10616836
  36.5 4.0 %collective-permute-start.2 = (bf16[3,1,256,128]{3,2,1,0:T(8,128)(2,1)S(1)}, bf16[3,1,256,128]{3,2,1,0:T(8,128)(2,1)S(1)}, u32[]{:S(2)}, u32[]{:S(2)}) collective-permute-start(bf16[3,1,256,128]{3,2,1,0:T(8,128)(2,1)S(1)} %get-tuple-element.29), channel_id=1, source_target_pairs={{0,1},{1,2},{2,3},{4,5},{5,6},{6,7},{8,9},{9,10},{10,11},{12,13},{... | collective-permute-start | bytes 589832 | tf_op jit(solution)/shard_map/ppermute | solution.py:168
  38.0 4.9 %collective-permute-start.3 = (bf16[3,1,256,128]{3,2,1,0:T(8,128)(2,1)S(1)}, bf16[3,1,256,128]{3,2,1,0:T(8,128)(2,1)S(1)}, u32[]{:S(2)}, u32[]{:S(2)}) collective-permute-start(bf16[3,1,256,128]{3,2,1,0:T(8,128)(2,1)S(1)} %get-tuple-element.30), channel_id=1, source_target_pairs={{1,0},{2,1},{3,2},{5,4},{6,5},{7,6},{9,8},{10,9},{11,10},{13,12},{... | collective-permute-start | bytes 589832 | tf_op jit(solution)/shard_map/ppermute | solution.py:169
  48.9 1.9 %copy-start.2 = (f32[2,256,128]{2,1,0:T(8,128)S(1)}, f32[2,256,128]{2,1,0:T(8,128)}, u32[]{:S(2)}) copy-start(f32[2,256,128]{2,1,0:T(8,128)} %shard_map.92) | copy-start | bytes 786436
  51.0 5.9 %copy-start.3 = (bf16[2,256,128]{2,1,0:T(8,128)(2,1)}, bf16[2,256,128]{2,1,0:T(8,128)(2,1)S(1)}, u32[]{:S(2)}) copy-start(bf16[2,256,128]{2,1,0:T(8,128)(2,1)S(1)} %fusion.9.delta_ref) | copy-start | bytes 393220
  51.0 13.5 %collective-permute-start.4 = (bf16[1,2,256,128]{3,2,1,0:T(8,128)(2,1)S(1)}, bf16[1,2,256,128]{3,2,1,0:T(8,128)(2,1)S(1)}, u32[]{:S(2)}, u32[]{:S(2)}) collective-permute-start(bf16[1,2,256,128]{3,2,1,0:T(8,128)(2,1)S(1)} %bitcast.86), channel_id=1, source_target_pairs={{0,4},{4,8},{8,12},{1,5},{5,9},{9,13},{2,6},{6,10},{10,14},{3,7},{... | collective-permute-start | bytes 393224 | tf_op jit(solution)/shard_map/ppermute | solution.py:168
  55.5 8.9 %collective-permute-start.5 = (bf16[1,2,256,128]{3,2,1,0:T(8,128)(2,1)S(1)}, bf16[1,2,256,128]{3,2,1,0:T(8,128)(2,1)S(1)}, u32[]{:S(2)}, u32[]{:S(2)}) collective-permute-start(bf16[1,2,256,128]{3,2,1,0:T(8,128)(2,1)S(1)} %bitcast.87), channel_id=1, source_target_pairs={{4,0},{8,4},{12,8},{5,1},{9,5},{13,9},{6,2},{10,6},{14,10},{7,3},{... | collective-permute-start | bytes 393224 | tf_op jit(solution)/shard_map/ppermute | solution.py:169
  62.5 12.1 %copy-start.4 = (bf16[2,256,128]{2,1,0:T(8,128)(2,1)S(1)}, bf16[2,256,128]{2,1,0:T(8,128)(2,1)}, u32[]{:S(2)}) copy-start(bf16[2,256,128]{2,1,0:T(8,128)(2,1)} %copy-done.3) | copy-start | bytes 393220
  65.4 7.5 %collective-permute-start.6 = (bf16[3,1,256,128]{3,2,1,0:T(8,128)(2,1)S(1)}, bf16[3,1,256,128]{3,2,1,0:T(8,128)(2,1)S(1)}, u32[]{:S(2)}, u32[]{:S(2)}) collective-permute-start(bf16[3,1,256,128]{3,2,1,0:T(8,128)(2,1)S(1)} %get-tuple-element.27), channel_id=1, source_target_pairs={{0,1},{1,2},{2,3},{4,5},{5,6},{6,7},{8,9},{9,10},{10,11},{12,13},{... | collective-permute-start | bytes 589832 | tf_op jit(solution)/shard_map/ppermute | solution.py:168
  71.2 3.3 %collective-permute-start.7 = (bf16[3,1,256,128]{3,2,1,0:T(8,128)(2,1)S(1)}, bf16[3,1,256,128]{3,2,1,0:T(8,128)(2,1)S(1)}, u32[]{:S(2)}, u32[]{:S(2)}) collective-permute-start(bf16[3,1,256,128]{3,2,1,0:T(8,128)(2,1)S(1)} %get-tuple-element.28), channel_id=1, source_target_pairs={{1,0},{2,1},{3,2},{5,4},{6,5},{7,6},{9,8},{10,9},{11,10},{13,12},{... | collective-permute-start | bytes 589832 | tf_op jit(solution)/shard_map/ppermute | solution.py:169
  82.1 21.7 %copy-start.7 = (bf16[256,256]{1,0:T(8,128)(2,1)S(1)}, bf16[256,256]{1,0:T(8,128)(2,1)}, u32[]{:S(2)}) copy-start(bf16[256,256]{1,0:T(8,128)(2,1)} %param.7) | copy-start | bytes 393220
  82.3 5.2 %collective-permute-start.8 = (f32[93184]{0:T(1024)S(1)}, f32[93184]{0:T(1024)S(1)}, u32[]{:S(2)}, u32[]{:S(2)}) collective-permute-start(f32[93184]{0:T(1024)S(1)} %pad_maximum_fusion.4), channel_id=1, source_target_pairs={{0,1},{1,0},{2,3},{3,2},{4,5},{5,4},{6,7},{7,6},{8,9},{9,8},{10,11... | collective-permute-start | bytes 1118216 | tf_op jit(solution)/shard_map/ppermute | solution.py:138
  87.6 7.1 %collective-permute-start.9 = (f32[46592]{0:T(1024)S(1)}, f32[46592]{0:T(1024)S(1)}, u32[]{:S(2)}, u32[]{:S(2)}) collective-permute-start(f32[46592]{0:T(1024)S(1)} %pad_maximum_fusion.6), channel_id=1, source_target_pairs={{0,2},{1,3},{2,0},{3,1},{4,6},{5,7},{6,4},{7,5},{8,10},{9,11},{10,... | collective-permute-start | bytes 559112 | tf_op jit(solution)/shard_map/ppermute | solution.py:138
  94.8 8.2 %collective-permute-start.10 = (f32[23296]{0:T(1024)S(1)}, f32[23296]{0:T(1024)S(1)}, u32[]{:S(2)}, u32[]{:S(2)}) collective-permute-start(f32[23296]{0:T(1024)S(1)} %pad_maximum_fusion.8), channel_id=1, source_target_pairs={{0,8},{4,12},{8,0},{12,4},{1,9},{5,13},{9,1},{13,5},{2,10},{6,14},... | collective-permute-start | bytes 279560 | tf_op jit(solution)/shard_map/ppermute | solution.py:138
  103.1 4.2 %collective-permute-start.11 = (f32[11648]{0:T(1024)S(1)}, f32[11648]{0:T(1024)S(1)}, u32[]{:S(2)}, u32[]{:S(2)}) collective-permute-start(f32[11648]{0:T(1024)S(1)} %pad_maximum_fusion.12), channel_id=1, source_target_pairs={{0,4},{4,0},{8,12},{12,8},{1,5},{5,1},{9,13},{13,9},{2,6},{6,2},{1... | collective-permute-start | bytes 139784 | tf_op jit(solution)/shard_map/ppermute | solution.py:138
  107.2 4.0 %collective-permute-start.12 = (f32[8192]{0:T(1024)S(1)}, f32[8192]{0:T(1024)S(1)}, u32[]{:S(2)}, u32[]{:S(2)}) collective-permute-start(f32[8192]{0:T(1024)S(1)} %pad_maximum_fusion.14), channel_id=1, source_target_pairs={{0,4},{4,0},{8,12},{12,8},{1,5},{5,1},{9,13},{13,9},{2,6},{6,2},{1... | collective-permute-start | bytes 98312 | tf_op jit(solution)/shard_map/ppermute | solution.py:148
  111.3 5.9 %collective-permute-start.13 = (f32[16384]{0:T(1024)S(1)}, f32[16384]{0:T(1024)S(1)}, u32[]{:S(2)}, u32[]{:S(2)}) collective-permute-start(f32[16384]{0:T(1024)S(1)} %pad_maximum_fusion.10), channel_id=1, source_target_pairs={{0,8},{4,12},{8,0},{12,4},{1,9},{5,13},{9,1},{13,5},{2,10},{6,14},... | collective-permute-start | bytes 196616 | tf_op jit(solution)/shard_map/ppermute | solution.py:148
  117.3 5.2 %collective-permute-start.14 = (f32[36224]{0:T(1024)S(1)}, f32[36224]{0:T(1024)S(1)}, u32[]{:S(2)}, u32[]{:S(2)}) collective-permute-start(f32[36224]{0:T(1024)S(1)} %pad_maximum_fusion.7), channel_id=1, source_target_pairs={{0,2},{1,3},{2,0},{3,1},{4,6},{5,7},{6,4},{7,5},{8,10},{9,11},{10,... | collective-permute-start | bytes 434696 | tf_op jit(solution)/shard_map/ppermute | solution.py:148
  123.0 1.6 %collective-permute-start.15 = (f32[72448]{0:T(1024)S(1)}, f32[72448]{0:T(1024)S(1)}, u32[]{:S(2)}, u32[]{:S(2)}) collective-permute-start(f32[72448]{0:T(1024)S(1)} %pad_maximum_fusion.5), channel_id=1, source_target_pairs={{0,1},{1,0},{2,3},{3,2},{4,5},{5,4},{6,7},{7,6},{8,9},{9,8},{10,11... | collective-permute-start | bytes 869384 | tf_op jit(solution)/shard_map/ppermute | solution.py:148

commit v6 on v5

--- a/solution.py
+++ b/solution.py
@@ -114,49 +114,20 @@
     return out.transpose(1, 0, 2).reshape(channels, blocks * LANES)[:, : 27 * GW]
 
 
-def tree_sum(blocks, order):
-    steps = []
-    for axis, rising in order:
-        bits = []
-        bit = 1
+def all_sum(flat):
+    first = [(i, i ^ 1) for i in range(lax.axis_size("sub"))]
+    upper = (lax.axis_index("sub") & 1) != 0
+    half = flat.shape[0] // 2
+    low, high = flat[:half], flat[half:]
+    piece = jnp.where(upper, high, low) + lax.ppermute(jnp.where(upper, low, high), "sub", first)
+    for axis, start in (("sub", 2), ("grp", 1)):
+        bit = start
         while bit < lax.axis_size(axis):
-            bits.append(bit)
+            pairs = [(i, i ^ bit) for i in range(lax.axis_size(axis))]
+            piece = piece + lax.ppermute(piece, axis, pairs)
             bit *= 2
-        steps += [(axis, bit) for bit in (bits if rising else bits[::-1])]
-    pieces = [block.reshape(-1) for block, _, _ in blocks]
-    done = []
-    for axis, bit in steps:
-        pairs = [(i, i ^ bit) for i in range(lax.axis_size(axis))]
-        upper = (lax.axis_index(axis) & bit) != 0
-        members = [n for n, (_, axes, _) in enumerate(blocks) if axis in axes]
-        keeps, sends = [], []
-        for n in members:
-            half = pieces[n].shape[0] // 2
-            low, high = pieces[n][:half], pieces[n][half:]
-            keeps.append(jnp.where(upper, high, low))
-            sends.append(jnp.where(upper, low, high))
-        got = lax.ppermute(jnp.concatenate(sends), axis, pairs)
-        offset = 0
-        for n, keep in zip(members, keeps):
-            pieces[n] = keep + got[offset : offset + keep.shape[0]]
-            offset += keep.shape[0]
-        done.append((axis, pairs, upper))
-    for axis, pairs, upper in reversed(done):
-        members = [n for n, (_, _, axes) in enumerate(blocks) if axis in axes]
-        if not members:
-            continue
-        got = lax.ppermute(jnp.concatenate([pieces[n] for n in members]), axis, pairs)
-        offset = 0
-        for n in members:
-            size = pieces[n].shape[0]
-            other = got[offset : offset + size]
-            offset += size
-            pieces[n] = jnp.where(
-                upper,
-                jnp.concatenate([other, pieces[n]]),
-                jnp.concatenate([pieces[n], other]),
-            )
-    return pieces
+    other = lax.ppermute(piece, "sub", first)
+    return jnp.where(upper, jnp.concatenate([other, piece]), jnp.concatenate([piece, other]))
 
 
 def halo(block):
@@ -179,16 +150,13 @@
 def conv_weights(group_weight):
     channels = group_weight.shape[0]
     group_of = jnp.arange(channels) // GW
-    mask = (group_of[:, None] == group_of[None, :]).astype(group_weight.dtype)
-    compact = group_weight.reshape(channels, GW, 27)
-    forward = jnp.broadcast_to(
-        compact.transpose(2, 0, 1)[:, :, None, :], (27, channels, channels // GW, GW)
-    ).reshape(27, channels, channels)
-    backward = jnp.broadcast_to(
-        compact[:, :, ::-1].transpose(2, 1, 0)[:, None, :, :], (27, channels // GW, GW, channels)
-    ).reshape(27, channels, channels)
-    forward = (forward * mask).reshape(9, 3 * channels, channels)
-    backward = (backward * mask).reshape(9, 3 * channels, channels)
+    mask = (group_of[:, None] == group_of[None, :]).astype(jnp.float32)
+    spread = (jnp.arange(GW)[:, None] == jnp.arange(channels)[None, :] % GW).astype(jnp.float32)
+    compact = group_weight.reshape(channels, GW, 27).astype(jnp.float32)
+    forward = jnp.einsum("ojt,ji->toi", compact, spread)
+    backward = jnp.einsum("ji,ojt->tio", spread, compact[:, :, ::-1])
+    forward = (forward * mask).astype(group_weight.dtype).reshape(9, 3 * channels, channels)
+    backward = (backward * mask).astype(group_weight.dtype).reshape(9, 3 * channels, channels)
     return forward, backward
 
 
@@ -244,22 +212,17 @@
         .astype(jnp.bfloat16)
         .reshape(volume.shape)
     )
-    grp_count, sub_count = lax.axis_size("grp"), lax.axis_size("sub")
-    kernel_laid = kernel_part.reshape(grp_count, sub_count, -1).transpose(1, 0, 2)
-    first_sum, third_sum, group_sum = tree_sum(
-        [
-            (first_part, ("sub", "grp"), ("sub", "grp")),
-            (third_part, ("sub", "grp"), ("sub", "grp")),
-            (kernel_laid, ("sub", "grp"), ("sub",)),
-        ],
-        (("sub", True), ("grp", False)),
-    )
-    first_grad = first_sum.reshape(first_part.shape) * factor
-    third_grad = third_sum.reshape(third_part.shape) * factor
-    own_rows = channels // grp_count
-    group_grad = (
-        group_sum.reshape(own_rows, 27, GW).transpose(0, 2, 1).reshape(own_rows, GW, 3, 3, 3) * factor
-    )
+    total = all_sum(
+        jnp.concatenate([first_part.reshape(-1), third_part.reshape(-1), kernel_part.reshape(-1)])
+    )
+    square = first_part.size
+    first_grad = total[:square].reshape(first_part.shape) * factor
+    third_grad = total[square : 2 * square].reshape(third_part.shape) * factor
+    own_rows = channels // lax.axis_size("grp")
+    own = lax.dynamic_slice_in_dim(
+        total[2 * square :].reshape(channels, -1), lax.axis_index("grp") * own_rows, own_rows, 0
+    )
+    group_grad = own.reshape(own_rows, 27, GW).transpose(0, 2, 1).reshape(own_rows, GW, 3, 3, 3) * factor
     return (block_output, volume_grad, first_grad, group_grad, third_grad)
 
 

time: 128 us -> 112 us (0.88)
  local copies, waits for them, and re-layouts: 29.6 us -> 6.53 us
  matrix products: 2.3 us -> 9.16 us
  waiting for transfers between devices: 31.2 us -> 37.9 us
  other arithmetic: 13.1 us -> 7.83 us
    reshape x3 -> x2, local copies, waits for them, and re-layouts: 17.5 us -> 0.63 us  [the longest x1 0.35 us: per_device(): total[2 * square:].reshape(channels, -1)]
    ppermute x8 -> x5, waiting for transfers between devices: 27.2 us -> 35.6 us  [the longest x3 34.3 us: all_sum(): piece = piece + lax.ppermute(piece, axis, pairs)]
    dot_general x0 -> x2, matrix products: none -> 6.86 us  [the longest x1 3.95 us: conv_weights(): forward = jnp.einsum('ojt,ji->toi', compact, spread)]
    mul x3 -> x2, other arithmetic: 5.05 us -> 0.84 us  [the longest x1 0.83 us: per_device(): third_grad = total[square:2 * square].reshape(third_part.shape) * factor]
    ppermute x4, waiting for transfers between devices: 4.03 us -> 0.01 us  [halo(): high = lax.ppermute(lax.slice_in_dim(block, 0, 1, axis=dim), axis, down)]
    broadcast_in_dim x2 -> x0, local copies, waits for them, and re-layouts: 2.85 us -> none  [the longest x1 2.62 us: conv_weights(): jnp.broadcast_to(compact.transpose(2, 0, 1)[:, :, None, :], (27, channels...]
    ppermute x4, waiting for transfers between devices: 0.01 us -> 2.31 us  [halo(): lax.ppermute(lax.slice_in_dim(block, size - 1, size, axis=dim), axis, up)]
    ppermute x8 -> x5, starting transfers between devices: 11.4 us -> 9.9 us  [the longest x3 6.16 us: all_sum(): piece = piece + lax.ppermute(piece, axis, pairs)]
  transfers between devices with their start and end apart: 16 -> 13, of which waited for: 10 -> 6; matrix products, arithmetic and copies ran while one was open for 25% -> 11% of each run, Pallas kernels for 4% -> 5%
where the time goes in v6:
time: 112 us; the launch traced here: 111 us
  waiting for transfers between devices  37.9 us (34%)
  starting transfers between devices  32.9 us (29%)
  Pallas kernels  15.6 us (14%)
  matrix products  9.16 us (8%)
  other arithmetic  7.83 us (7%)
  local copies, waits for them, and re-layouts  6.53 us (6%)
    ppermute x3, waiting for transfers between devices, all_sum(): piece = piece + lax.ppermute(piece, axis, pairs)  34.3 us
    ppermute x4, starting transfers between devices, halo(): lax.ppermute(lax.slice_in_dim(block, size - 1, size, axis=dim), axis, up)  17.8 us
    pallas_call x2, Pallas kernels, conv_call(): pl.pallas_call(conv_body, out_shape=jax.ShapeDtypeStruct((height, channel...  10 us
    ppermute x3, starting transfers between devices, all_sum(): piece = piece + lax.ppermute(piece, axis, pairs)  6.16 us
    pallas_call x1, Pallas kernels, wgrad_call(): pl.pallas_call(wgrad_body, out_shape=jax.ShapeDtypeStruct((blocks, channe...  5.6 us
    ppermute x4, starting transfers between devices, halo(): high = lax.ppermute(lax.slice_in_dim(block, 0, 1, axis=dim), axis, down)  5.17 us
    dot_general x1, matrix products, conv_weights(): forward = jnp.einsum('ojt,ji->toi', compact, spread)  3.95 us
    ppermute x1, starting transfers between devices, all_sum(): lax.ppermute(jnp.where(upper, low, high), 'sub', first)  3.66 us
  transfers between devices with their start and end apart: 13, of which 6 were waited for; matrix products, arithmetic and copies ran while one was open for 11% of the time, Pallas kernels for 5%

profile of v6, /device:TPU:0, one launch (start us, length us, event | category | flops | bytes accessed | tf_op | source)
XLA Modules:
  0.0 111.1 jit_solution(12192846264449130335)
XLA Ops:
  0.7 1.1 copy.26
  1.7 1.1 %reduce-precision_convert_fusion.2 = (bf16[256,256]{0,1:T(8,128)(2,1)S(1)}, f32[256,256]{0,1:T(8,128)S(1)}) fusion(bf16[256,256]{0,1:T(8,128)(2,1)S(1)} %bitcast.101, bf16[256,256]{1,0:T(8,128)(2,1)} %param.7), kind=kOutput, calls=%fused_computation.40 | convolution fusion | flops 33947648 | bytes 655360 | tf_op jit(solution)/shard_map/dot_general | solution.py:182
  3.0 1.3 %collective-permute-start.1 = (bf16[1,2,256,128]{3,2,1,0:T(8,128)(2,1)S(1)}, bf16[1,2,256,128]{3,2,1,0:T(8,128)(2,1)S(1)}, u32[]{:S(2)}, u32[]{:S(2)}) collective-permute-start(bf16[1,2,256,128]{3,2,1,0:T(8,128)(2,1)S(1)} %bitcast.94), channel_id=1, source_target_pairs={{4,0},{8,4},{12,8},{5,1},{9,5},{13,9},{6,2},{10,6},{14,10},{7,3},{... | collective-permute-start | bytes 393224 | tf_op jit(solution)/shard_map/ppermute | solution.py:140
  4.3 5.6 %collective-permute-start = (bf16[1,2,256,128]{3,2,1,0:T(8,128)(2,1)S(1)}, bf16[1,2,256,128]{3,2,1,0:T(8,128)(2,1)S(1)}, u32[]{:S(2)}, u32[]{:S(2)}) collective-permute-start(bf16[1,2,256,128]{3,2,1,0:T(8,128)(2,1)S(1)} %bitcast.95), channel_id=1, source_target_pairs={{0,4},{4,8},{8,12},{1,5},{5,9},{9,13},{2,6},{6,10},{10,14},{3,7},{... | collective-permute-start | bytes 393224 | tf_op jit(solution)/shard_map/ppermute | solution.py:139
  10.0 4.0 %fusion = bf16[27,256,256]{2,1,0:T(8,128)(2,1)} fusion(f32[256,256]{1,0:T(8,128)S(1)} %compare_convert_fusion.mask_ref, bf16[256,8,27]{0,1,2:T(8,128)(2,1)} %bitcast.107, s32[256]{0:T(256)S(1)} %and_select_fusion.2), kind=kOutput, calls=%fused_computation.1 | convolution fusion | flops 31852544 | bytes 3912704 | tf_op jit(solution)/shard_map/ojt,ji->toi/dot_general | solution.py:156
  14.0 2.9 %multiply_convert_fusion = bf16[256,256,27]{1,0,2:T(8,128)(2,1)} fusion(f32[256,256]{1,0:T(8,128)S(1)} %compare_convert_fusion.mask_ref, bf16[256,8,27]{0,1,2:T(8,128)(2,1)S(1)} %bitcast.108, s32[256]{0:T(256)S(1)} %and_select_fusion.2), kind=kOutput, calls=%fused_computation.2 | convolution fusion | flops 31907840 | bytes 3912704 | tf_op jit(solution)/shard_map/ji,ojt->tio/dot_general | solution.py:157
  17.1 1.3 %collective-permute-start.3 = (bf16[3,1,256,128]{3,2,1,0:T(8,128)(2,1)S(1)}, bf16[3,1,256,128]{3,2,1,0:T(8,128)(2,1)S(1)}, u32[]{:S(2)}, u32[]{:S(2)}) collective-permute-start(bf16[3,1,256,128]{3,2,1,0:T(8,128)(2,1)S(1)} %get-tuple-element.25), channel_id=1, source_target_pairs={{1,0},{2,1},{3,2},{5,4},{6,5},{7,6},{9,8},{10,9},{11,10},{13,12},{... | collective-permute-start | bytes 589832 | tf_op jit(solution)/shard_map/ppermute | solution.py:140
  18.4 3.0 %collective-permute-start.2 = (bf16[3,1,256,128]{3,2,1,0:T(8,128)(2,1)S(1)}, bf16[3,1,256,128]{3,2,1,0:T(8,128)(2,1)S(1)}, u32[]{:S(2)}, u32[]{:S(2)}) collective-permute-start(bf16[3,1,256,128]{3,2,1,0:T(8,128)(2,1)S(1)} %get-tuple-element.24), channel_id=1, source_target_pairs={{0,1},{1,2},{2,3},{4,5},{5,6},{6,7},{8,9},{9,10},{10,11},{12,13},{... | collective-permute-start | bytes 589832 | tf_op jit(solution)/shard_map/ppermute | solution.py:139
  21.6 1.0 collective-permute-done.2
  22.5 1.0 pad_maximum_fusion.ext_ref.act_ref
  23.5 5.0 %shard_map.92 = f32[2,256,128]{2,1,0:T(8,128)} custom-call(bf16[3,4,256,128]{3,2,1,0:T(8,128)(2,1)} %pad_maximum_fusion.ext_ref.act_ref, bf16[9,768,256]{2,1,0:T(8,128)(2,1)} %bitcast.85), custom_call_target="tpu_custom_call" | custom-call | flops 905969664 | bytes 4587520 | tf_op jit(solution)/shard_map/pallas_call | solution.py:43
  28.5 1.1 fusion.16
  29.8 0.3 fusion.12
  30.1 0.2 fusion.5
  30.3 0.1 copy.30
  30.6 1.3 %collective-permute-start.5 = (bf16[1,2,256,128]{3,2,1,0:T(8,128)(2,1)S(1)}, bf16[1,2,256,128]{3,2,1,0:T(8,128)(2,1)S(1)}, u32[]{:S(2)}, u32[]{:S(2)}) collective-permute-start(bf16[1,2,256,128]{3,2,1,0:T(8,128)(2,1)S(1)} %bitcast.90), channel_id=1, source_target_pairs={{4,0},{8,4},{12,8},{5,1},{9,5},{13,9},{6,2},{10,6},{14,10},{7,3},{... | collective-permute-start | bytes 393224 | tf_op jit(solution)/shard_map/ppermute | solution.py:140
  31.9 4.6 %collective-permute-start.4 = (bf16[1,2,256,128]{3,2,1,0:T(8,128)(2,1)S(1)}, bf16[1,2,256,128]{3,2,1,0:T(8,128)(2,1)S(1)}, u32[]{:S(2)}, u32[]{:S(2)}) collective-permute-start(bf16[1,2,256,128]{3,2,1,0:T(8,128)(2,1)S(1)} %bitcast.91), channel_id=1, source_target_pairs={{0,4},{4,8},{8,12},{1,5},{5,9},{9,13},{2,6},{6,10},{10,14},{3,7},{... | collective-permute-start | bytes 393224 | tf_op jit(solution)/shard_map/ppermute | solution.py:139
  36.4 1.1 %fusion.6.sel_ref = bf16[16,128,128]{2,1,0:T(8,128)(2,1)} fusion(s32[16,128]{1,0:T(8,128)S(1)} %broadcast_add_fusion), kind=kLoop, calls=%fused_computation.14 | loop fusion | flops 524288 | bytes 532480 | tf_op jit(solution)/shard_map/convert_element_type | solution.py:102
  37.6 1.3 %collective-permute-done.4 = bf16[1,2,256,128]{3,2,1,0:T(8,128)(2,1)S(1)} collective-permute-done((bf16[1,2,256,128]{3,2,1,0:T(8,128)(2,1)S(1)}, bf16[1,2,256,128]{3,2,1,0:T(8,128)(2,1)S(1)}, u32[]{:S(2)}, u32[]{:S(2)}) %collective-permute-start.4) | collective-permute-done | bytes 131104 | tf_op jit(solution)/shard_map/ppermute | solution.py:139
  39.0 1.3 %collective-permute-start.7 = (bf16[3,1,256,128]{3,2,1,0:T(8,128)(2,1)S(1)}, bf16[3,1,256,128]{3,2,1,0:T(8,128)(2,1)S(1)}, u32[]{:S(2)}, u32[]{:S(2)}) collective-permute-start(bf16[3,1,256,128]{3,2,1,0:T(8,128)(2,1)S(1)} %get-tuple-element.23), channel_id=1, source_target_pairs={{1,0},{2,1},{3,2},{5,4},{6,5},{7,6},{9,8},{10,9},{11,10},{13,12},{... | collective-permute-start | bytes 589832 | tf_op jit(solution)/shard_map/ppermute | solution.py:140
  40.3 4.7 %collective-permute-start.6 = (bf16[3,1,256,128]{3,2,1,0:T(8,128)(2,1)S(1)}, bf16[3,1,256,128]{3,2,1,0:T(8,128)(2,1)S(1)}, u32[]{:S(2)}, u32[]{:S(2)}) collective-permute-start(bf16[3,1,256,128]{3,2,1,0:T(8,128)(2,1)S(1)} %get-tuple-element.22), channel_id=1, source_target_pairs={{0,1},{1,2},{2,3},{4,5},{5,6},{6,7},{8,9},{9,10},{10,11},{12,13},{... | collective-permute-start | bytes 589832 | tf_op jit(solution)/shard_map/ppermute | solution.py:139
  45.0 5.6 %shard_map.94 = f32[2,256,128]{2,1,0:T(8,128)} custom-call(bf16[3,4,256,128]{3,2,1,0:T(8,128)(2,1)} %pad_maximum_fusion.ext_ref.act_ref, bf16[2,256,128]{2,1,0:T(8,128)(2,1)} %copy-done.3, f32[256,256]{1,0:T(8,128)} %copy-done.1, bf16[16,128,128]{2,1,0:T(8,128)(2,1)} %fusion.6.sel_ref), custom_call_target="tpu_custom_call" | custom-call | flops 1358954496 | bytes 1179648 | tf_op jit(solution)/shard_map/pallas_call | solution.py:103
  50.6 1.1 copy.32
  51.7 0.1 copy.33
  51.9 0.3 reshape.203
  52.1 0.2 convolution_bitcast_fusion.1
  52.4 0.1 copy.38
  52.5 1.9 %pad_maximum_fusion.1.ext_ref = bf16[3,4,256,128]{3,2,1,0:T(8,128)(2,1)} fusion(bf16[3,1,256,128]{3,2,1,0:T(8,128)(2,1)S(1)} %collective-permute-done.7, bf16[1,2,256,128]{3,2,1,0:T(8,128)(2,1)S(1)} %collective-permute-done.5, bf16[1,2,256,128]{3,2,1,0:T(8,128)(2,1)} %bitcast.93, bf16[1,2,256,128]{3,2,1,0:T(8,128)(2,1)S(1)} %collective-permute-done.4, ...), kind=kLoop, calls=%fused_computation.16 | loop fusion | flops 1572864 | bytes 1572864 | tf_op jit(solution)/shard_map/concatenate | solution.py:141
  54.4 5.0 %shard_map.93 = f32[2,256,128]{2,1,0:T(8,128)} custom-call(bf16[3,4,256,128]{3,2,1,0:T(8,128)(2,1)} %pad_maximum_fusion.1.ext_ref, bf16[9,768,256]{2,1,0:T(8,128)(2,1)} %bitcast.84), custom_call_target="tpu_custom_call" | custom-call | flops 905969664 | bytes 4587520 | tf_op jit(solution)/shard_map/pallas_call | solution.py:43
  59.4 1.0 convert_bitcast_fusion
  60.4 0.1 copy.31
  60.7 0.2 convolution_bitcast_fusion
  60.9 0.1 copy.34
  61.0 0.1 copy.39
  61.3 3.7 %collective-permute-start.8 = (f32[93184]{0:T(1024)S(1)}, f32[93184]{0:T(1024)S(1)}, u32[]{:S(2)}, u32[]{:S(2)}) collective-permute-start(f32[93184]{0:T(1024)S(1)} %fusion.13), channel_id=1, source_target_pairs={{0,1},{1,0},{2,3},{3,2},{4,5},{5,4},{6,7},{7,6},{8,9},{9,8},{10,11... | collective-permute-start | bytes 1118216 | tf_op jit(solution)/shard_map/ppermute | solution.py:122
  64.9 1.3 %collective-permute-done.8 = f32[93184]{0:T(1024)S(1)} collective-permute-done((f32[93184]{0:T(1024)S(1)}, f32[93184]{0:T(1024)S(1)}, u32[]{:S(2)}, u32[]{:S(2)}) %collective-permute-start.8) | collective-permute-done | bytes 372768 | tf_op jit(solution)/shard_map/ppermute | solution.py:122
  66.3 0.8 collective-permute-start.9
  67.1 10.2 %collective-permute-done.9 = f32[93184]{0:T(1024)S(1)} collective-permute-done((f32[93184]{0:T(1024)S(1)}, f32[93184]{0:T(1024)S(1)}, u32[]{:S(2)}, u32[]{:S(2)}) %collective-permute-start.9) | collective-permute-done | bytes 372768 | tf_op jit(solution)/shard_map/ppermute | solution.py:127
  77.4 2.5 %collective-permute-start.10 = (f32[93184]{0:T(1024)S(1)}, f32[93184]{0:T(1024)S(1)}, u32[]{:S(2)}, u32[]{:S(2)}) collective-permute-start(f32[93184]{0:T(1024)S(1)} %add.108), channel_id=1, source_target_pairs={{0,4},{4,0},{8,12},{12,8},{1,5},{5,1},{9,13},{13,9},{2,6},{6,2},{1... | collective-permute-start | bytes 1118216 | tf_op jit(solution)/shard_map/ppermute | solution.py:127
  79.9 8.4 %collective-permute-done.10 = f32[93184]{0:T(1024)S(1)} collective-permute-done((f32[93184]{0:T(1024)S(1)}, f32[93184]{0:T(1024)S(1)}, u32[]{:S(2)}, u32[]{:S(2)}) %collective-permute-start.10) | collective-permute-done | bytes 372768 | tf_op jit(solution)/shard_map/ppermute | solution.py:127
  88.3 2.8 %collective-permute-start.11 = (f32[93184]{0:T(1024)S(1)}, f32[93184]{0:T(1024)S(1)}, u32[]{:S(2)}, u32[]{:S(2)}) collective-permute-start(f32[93184]{0:T(1024)S(1)} %add.109), channel_id=1, source_target_pairs={{0,8},{4,12},{8,0},{12,4},{1,9},{5,13},{9,1},{13,5},{2,10},{6,14},... | collective-permute-start | bytes 1118216 | tf_op jit(solution)/shard_map/ppermute | solution.py:127
  91.2 15.7 %collective-permute-done.11 = f32[93184]{0:T(1024)S(1)} collective-permute-done((f32[93184]{0:T(1024)S(1)}, f32[93184]{0:T(1024)S(1)}, u32[]{:S(2)}, u32[]{:S(2)}) %collective-permute-start.11) | collective-permute-done | bytes 372768 | tf_op jit(solution)/shard_map/ppermute | solution.py:127
  107.0 0.8 copy.36
  107.7 0.2 fusion.3
  108.0 0.8 copy.37
  109.1 0.8 slice_multiply_fusion
  109.9 0.4 reshape.205
  110.3 0.7 copy.35
  (48 shorter events, 1.7 us)
Async XLA Ops:
  0.6 29.1 %copy-start = (bf16[256,256]{1,0:T(8,128)(2,1)S(1)}, bf16[256,256]{1,0:T(8,128)(2,1)}, u32[]{:S(2)}) copy-start(bf16[256,256]{1,0:T(8,128)(2,1)} %param.9) | copy-start | bytes 393220
  0.6 13.3 %copy-start.4 = (bf16[256,8,3,3,3]{0,1,4,3,2:T(8,128)(2,1)S(1)}, bf16[256,8,3,3,3]{0,1,4,3,2:T(8,128)(2,1)}, u32[]{:S(2)}) copy-start(bf16[256,8,3,3,3]{0,1,4,3,2:T(8,128)(2,1)} %param.8) | copy-start | bytes 331780
  3.0 14.0 %collective-permute-start.1 = (bf16[1,2,256,128]{3,2,1,0:T(8,128)(2,1)S(1)}, bf16[1,2,256,128]{3,2,1,0:T(8,128)(2,1)S(1)}, u32[]{:S(2)}, u32[]{:S(2)}) collective-permute-start(bf16[1,2,256,128]{3,2,1,0:T(8,128)(2,1)S(1)} %bitcast.94), channel_id=1, source_target_pairs={{4,0},{8,4},{12,8},{5,1},{9,5},{13,9},{6,2},{10,6},{14,10},{7,3},{... | collective-permute-start | bytes 393224 | tf_op jit(solution)/shard_map/ppermute | solution.py:140
  4.3 12.7 %collective-permute-start = (bf16[1,2,256,128]{3,2,1,0:T(8,128)(2,1)S(1)}, bf16[1,2,256,128]{3,2,1,0:T(8,128)(2,1)S(1)}, u32[]{:S(2)}, u32[]{:S(2)}) collective-permute-start(bf16[1,2,256,128]{3,2,1,0:T(8,128)(2,1)S(1)} %bitcast.95), channel_id=1, source_target_pairs={{0,4},{4,8},{8,12},{1,5},{5,9},{9,13},{2,6},{6,10},{10,14},{3,7},{... | collective-permute-start | bytes 393224 | tf_op jit(solution)/shard_map/ppermute | solution.py:139
  10.0 6.9 %copy-start.1 = (f32[256,256]{1,0:T(8,128)}, f32[256,256]{1,0:T(8,128)S(1)}, u32[]{:S(2)}) copy-start(f32[256,256]{1,0:T(8,128)S(1)} %compare_convert_fusion.mask_ref) | copy-start | bytes 786436
  10.0 6.9 %copy-start.5 = (bf16[256,1,2,128]{3,2,1,0:T(2,128)(2,1)S(1)}, bf16[256,1,2,128]{3,2,1,0:T(2,128)(2,1)}, u32[]{:S(2)}) copy-start(bf16[256,1,2,128]{3,2,1,0:T(2,128)(2,1)} %param.6) | copy-start | bytes 393220
  17.1 4.4 %collective-permute-start.3 = (bf16[3,1,256,128]{3,2,1,0:T(8,128)(2,1)S(1)}, bf16[3,1,256,128]{3,2,1,0:T(8,128)(2,1)S(1)}, u32[]{:S(2)}, u32[]{:S(2)}) collective-permute-start(bf16[3,1,256,128]{3,2,1,0:T(8,128)(2,1)S(1)} %get-tuple-element.25), channel_id=1, source_target_pairs={{1,0},{2,1},{3,2},{5,4},{6,5},{7,6},{9,8},{10,9},{11,10},{13,12},{... | collective-permute-start | bytes 589832 | tf_op jit(solution)/shard_map/ppermute | solution.py:140
  18.4 4.1 %collective-permute-start.2 = (bf16[3,1,256,128]{3,2,1,0:T(8,128)(2,1)S(1)}, bf16[3,1,256,128]{3,2,1,0:T(8,128)(2,1)S(1)}, u32[]{:S(2)}, u32[]{:S(2)}) collective-permute-start(bf16[3,1,256,128]{3,2,1,0:T(8,128)(2,1)S(1)} %get-tuple-element.24), channel_id=1, source_target_pairs={{0,1},{1,2},{2,3},{4,5},{5,6},{6,7},{8,9},{9,10},{10,11},{12,13},{... | collective-permute-start | bytes 589832 | tf_op jit(solution)/shard_map/ppermute | solution.py:139
  28.5 1.9 %copy-start.2 = (f32[2,256,128]{2,1,0:T(8,128)S(1)}, f32[2,256,128]{2,1,0:T(8,128)}, u32[]{:S(2)}) copy-start(f32[2,256,128]{2,1,0:T(8,128)} %shard_map.92) | copy-start | bytes 786436
  30.6 14.4 %copy-start.3 = (bf16[2,256,128]{2,1,0:T(8,128)(2,1)}, bf16[2,256,128]{2,1,0:T(8,128)(2,1)S(1)}, u32[]{:S(2)}) copy-start(bf16[2,256,128]{2,1,0:T(8,128)(2,1)S(1)} %fusion.8.delta_ref) | copy-start | bytes 393220
  30.6 7.0 %collective-permute-start.5 = (bf16[1,2,256,128]{3,2,1,0:T(8,128)(2,1)S(1)}, bf16[1,2,256,128]{3,2,1,0:T(8,128)(2,1)S(1)}, u32[]{:S(2)}, u32[]{:S(2)}) collective-permute-start(bf16[1,2,256,128]{3,2,1,0:T(8,128)(2,1)S(1)} %bitcast.90), channel_id=1, source_target_pairs={{4,0},{8,4},{12,8},{5,1},{9,5},{13,9},{6,2},{10,6},{14,10},{7,3},{... | collective-permute-start | bytes 393224 | tf_op jit(solution)/shard_map/ppermute | solution.py:140
  31.9 7.1 %collective-permute-start.4 = (bf16[1,2,256,128]{3,2,1,0:T(8,128)(2,1)S(1)}, bf16[1,2,256,128]{3,2,1,0:T(8,128)(2,1)S(1)}, u32[]{:S(2)}, u32[]{:S(2)}) collective-permute-start(bf16[1,2,256,128]{3,2,1,0:T(8,128)(2,1)S(1)} %bitcast.91), channel_id=1, source_target_pairs={{0,4},{4,8},{8,12},{1,5},{5,9},{9,13},{2,6},{6,10},{10,14},{3,7},{... | collective-permute-start | bytes 393224 | tf_op jit(solution)/shard_map/ppermute | solution.py:139
  39.0 13.5 %collective-permute-start.7 = (bf16[3,1,256,128]{3,2,1,0:T(8,128)(2,1)S(1)}, bf16[3,1,256,128]{3,2,1,0:T(8,128)(2,1)S(1)}, u32[]{:S(2)}, u32[]{:S(2)}) collective-permute-start(bf16[3,1,256,128]{3,2,1,0:T(8,128)(2,1)S(1)} %get-tuple-element.23), channel_id=1, source_target_pairs={{1,0},{2,1},{3,2},{5,4},{6,5},{7,6},{9,8},{10,9},{11,10},{13,12},{... | collective-permute-start | bytes 589832 | tf_op jit(solution)/shard_map/ppermute | solution.py:140
  40.3 12.2 %collective-permute-start.6 = (bf16[3,1,256,128]{3,2,1,0:T(8,128)(2,1)S(1)}, bf16[3,1,256,128]{3,2,1,0:T(8,128)(2,1)S(1)}, u32[]{:S(2)}, u32[]{:S(2)}) collective-permute-start(bf16[3,1,256,128]{3,2,1,0:T(8,128)(2,1)S(1)} %get-tuple-element.22), channel_id=1, source_target_pairs={{0,1},{1,2},{2,3},{4,5},{5,6},{6,7},{8,9},{9,10},{10,11},{12,13},{... | collective-permute-start | bytes 589832 | tf_op jit(solution)/shard_map/ppermute | solution.py:139
  60.9 46.8 %copy-start.6 = (bf16[256,256]{1,0:T(8,128)(2,1)S(1)}, bf16[256,256]{1,0:T(8,128)(2,1)}, u32[]{:S(2)}) copy-start(bf16[256,256]{1,0:T(8,128)(2,1)} %param.7) | copy-start | bytes 393220
  61.3 5.0 %collective-permute-start.8 = (f32[93184]{0:T(1024)S(1)}, f32[93184]{0:T(1024)S(1)}, u32[]{:S(2)}, u32[]{:S(2)}) collective-permute-start(f32[93184]{0:T(1024)S(1)} %fusion.13), channel_id=1, source_target_pairs={{0,1},{1,0},{2,3},{3,2},{4,5},{5,4},{6,7},{7,6},{8,9},{9,8},{10,11... | collective-permute-start | bytes 1118216 | tf_op jit(solution)/shard_map/ppermute | solution.py:122
  66.3 11.0 %collective-permute-start.9 = (f32[93184]{0:T(1024)S(1)}, f32[93184]{0:T(1024)S(1)}, u32[]{:S(2)}, u32[]{:S(2)}) collective-permute-start(f32[93184]{0:T(1024)S(1)} %select_add_fusion), channel_id=1, source_target_pairs={{0,2},{1,3},{2,0},{3,1},{4,6},{5,7},{6,4},{7,5},{8,10},{9,11},{10,... | collective-permute-start | bytes 1118216 | tf_op jit(solution)/shard_map/ppermute | solution.py:127
  77.4 10.9 %collective-permute-start.10 = (f32[93184]{0:T(1024)S(1)}, f32[93184]{0:T(1024)S(1)}, u32[]{:S(2)}, u32[]{:S(2)}) collective-permute-start(f32[93184]{0:T(1024)S(1)} %add.108), channel_id=1, source_target_pairs={{0,4},{4,0},{8,12},{12,8},{1,5},{5,1},{9,13},{13,9},{2,6},{6,2},{1... | collective-permute-start | bytes 1118216 | tf_op jit(solution)/shard_map/ppermute | solution.py:127
  88.3 18.5 %collective-permute-start.11 = (f32[93184]{0:T(1024)S(1)}, f32[93184]{0:T(1024)S(1)}, u32[]{:S(2)}, u32[]{:S(2)}) collective-permute-start(f32[93184]{0:T(1024)S(1)} %add.109), channel_id=1, source_target_pairs={{0,8},{4,12},{8,0},{12,4},{1,9},{5,13},{9,1},{13,5},{2,10},{6,14},... | collective-permute-start | bytes 1118216 | tf_op jit(solution)/shard_map/ppermute | solution.py:127
  106.9 2.0 %collective-permute-start.12 = (f32[93184]{0:T(1024)S(1)}, f32[93184]{0:T(1024)S(1)}, u32[]{:S(2)}, u32[]{:S(2)}) collective-permute-start(f32[93184]{0:T(1024)S(1)} %add.110), channel_id=1, source_target_pairs={{0,1},{1,0},{2,3},{3,2},{4,5},{5,4},{6,7},{7,6},{8,9},{9,8},{10,11... | collective-permute-start | bytes 1118216 | tf_op jit(solution)/shard_map/ppermute | solution.py:129

commit v7 on v5

--- a/solution.py
+++ b/solution.py
@@ -179,16 +179,13 @@
 def conv_weights(group_weight):
     channels = group_weight.shape[0]
     group_of = jnp.arange(channels) // GW
-    mask = (group_of[:, None] == group_of[None, :]).astype(group_weight.dtype)
-    compact = group_weight.reshape(channels, GW, 27)
-    forward = jnp.broadcast_to(
-        compact.transpose(2, 0, 1)[:, :, None, :], (27, channels, channels // GW, GW)
-    ).reshape(27, channels, channels)
-    backward = jnp.broadcast_to(
-        compact[:, :, ::-1].transpose(2, 1, 0)[:, None, :, :], (27, channels // GW, GW, channels)
-    ).reshape(27, channels, channels)
-    forward = (forward * mask).reshape(9, 3 * channels, channels)
-    backward = (backward * mask).reshape(9, 3 * channels, channels)
+    mask = (group_of[:, None] == group_of[None, :]).astype(jnp.float32)
+    spread = (jnp.arange(GW)[:, None] == jnp.arange(channels)[None, :] % GW).astype(jnp.float32)
+    compact = group_weight.reshape(channels, GW, 27).astype(jnp.float32)
+    forward = jnp.einsum("ojt,ji->toi", compact, spread)
+    backward = jnp.einsum("ji,ojt->tio", spread, compact[:, :, ::-1])
+    forward = (forward * mask).astype(group_weight.dtype).reshape(9, 3 * channels, channels)
+    backward = (backward * mask).astype(group_weight.dtype).reshape(9, 3 * channels, channels)
     return forward, backward
 
 
@@ -245,14 +242,17 @@
         .reshape(volume.shape)
     )
     grp_count, sub_count = lax.axis_size("grp"), lax.axis_size("sub")
-    kernel_laid = kernel_part.reshape(grp_count, sub_count, -1).transpose(1, 0, 2)
+    digits = grp_count.bit_length() - 1
+    reverse = [int(format(n, f"0{digits}b")[::-1], 2) if digits else 0 for n in range(grp_count)]
+    blocks = kernel_part.reshape(grp_count, sub_count, -1)
+    kernel_laid = jnp.concatenate([blocks[n : n + 1] for n in reverse]).transpose(1, 0, 2)
     first_sum, third_sum, group_sum = tree_sum(
         [
             (first_part, ("sub", "grp"), ("sub", "grp")),
             (third_part, ("sub", "grp"), ("sub", "grp")),
             (kernel_laid, ("sub", "grp"), ("sub",)),
         ],
-        (("sub", True), ("grp", False)),
+        (("sub", True), ("grp", True)),
     )
     first_grad = first_sum.reshape(first_part.shape) * factor
     third_grad = third_sum.reshape(third_part.shape) * factor

time: 128 us -> 107 us (0.84)
  local copies, waits for them, and re-layouts: 29.6 us -> 7.39 us
  matrix products: 2.3 us -> 9.14 us
  waiting for transfers between devices: 31.2 us -> 25 us
  starting transfers between devices: 33.5 us -> 37.2 us
  other arithmetic: 13.1 us -> 10.6 us
    reshape x3 -> x0, local copies, waits for them, and re-layouts: 17.5 us -> none  [the longest x2 17.2 us: conv_weights(): forward = jnp.broadcast_to(compact.transpose(2, 0, 1)[:, :, None, :], (27...]
    dot_general x0 -> x2, matrix products: none -> 6.83 us  [the longest x1 3.96 us: conv_weights(): forward = jnp.einsum('ojt,ji->toi', compact, spread)]
    mul x1 -> x0, other arithmetic: 3.44 us -> none  [conv_weights(): backward = (backward * mask).reshape(9, 3 * channels, channels)]
    ppermute x4, waiting for transfers between devices: 13.9 us -> 10.6 us  [tree_sum(): got = lax.ppermute(jnp.concatenate(sends), axis, pairs)]
    ppermute x4, waiting for transfers between devices: 13.2 us -> 10.3 us  [tree_sum(): lax.ppermute(jnp.concatenate([pieces[n] for n in members]), axis, pairs)]
    broadcast_in_dim x2 -> x0, local copies, waits for them, and re-layouts: 2.85 us -> none  [the longest x1 2.62 us: conv_weights(): jnp.broadcast_to(compact.transpose(2, 0, 1)[:, :, None, :], (27, channels...]
    ppermute x4, starting transfers between devices: 2.95 us -> 5.35 us  [tree_sum(): lax.ppermute(jnp.concatenate([pieces[n] for n in members]), axis, pairs)]
    ppermute x4, starting transfers between devices: 8.43 us -> 9.79 us  [tree_sum(): got = lax.ppermute(jnp.concatenate(sends), axis, pairs)]
  transfers between devices with their start and end apart: 16 -> 16, of which waited for: 10 -> 10; matrix products, arithmetic and copies ran while one was open for 25% -> 13% of each run, Pallas kernels for 4% -> 5%
where the time goes in v7:
time: 107 us; the launch traced here: 106 us
  starting transfers between devices  37.2 us (35%)
  waiting for transfers between devices  25 us (23%)
  Pallas kernels  15.6 us (15%)
  other arithmetic  10.6 us (10%)
  matrix products  9.14 us (9%)
  local copies, waits for them, and re-layouts  7.39 us (7%)
  between operations  1.49 us (1%)
    ppermute x4, starting transfers between devices, halo(): lax.ppermute(lax.slice_in_dim(block, size - 1, size, axis=dim), axis, up)  16.7 us
    ppermute x4, waiting for transfers between devices, tree_sum(): got = lax.ppermute(jnp.concatenate(sends), axis, pairs)  10.6 us
    ppermute x4, waiting for transfers between devices, tree_sum(): lax.ppermute(jnp.concatenate([pieces[n] for n in members]), axis, pairs)  10.3 us
    pallas_call x2, Pallas kernels, conv_call(): pl.pallas_call(conv_body, out_shape=jax.ShapeDtypeStruct((height, channel...  10 us
    ppermute x4, starting transfers between devices, tree_sum(): got = lax.ppermute(jnp.concatenate(sends), axis, pairs)  9.79 us
    pallas_call x1, Pallas kernels, wgrad_call(): pl.pallas_call(wgrad_body, out_shape=jax.ShapeDtypeStruct((blocks, channe...  5.6 us
    ppermute x4, starting transfers between devices, tree_sum(): lax.ppermute(jnp.concatenate([pieces[n] for n in members]), axis, pairs)  5.35 us
    ppermute x4, starting transfers between devices, halo(): high = lax.ppermute(lax.slice_in_dim(block, 0, 1, axis=dim), axis, down)  5.35 us
  transfers between devices with their start and end apart: 16, of which 10 were waited for; matrix products, arithmetic and copies ran while one was open for 13% of the time, Pallas kernels for 5%

profile of v7, /device:TPU:0, one launch (start us, length us, event | category | flops | bytes accessed | tf_op | source)
XLA Modules:
  0.0 106.4 jit_solution(5962907286835465677)
XLA Ops:
  0.7 1.1 %copy.74 = bf16[256,1,2,128]{0,3,2,1:T(8,128)(2,1)S(1)} copy(bf16[256,1,2,128]{3,2,1,0:T(2,128)(2,1)} %param.5) | data formatting | bytes 262144 | tf_op args[0]
  1.7 1.1 %reduce-precision_convert_fusion.2 = (bf16[256,256]{0,1:T(8,128)(2,1)S(1)}, f32[256,256]{0,1:T(8,128)S(1)}) fusion(bf16[256,256]{0,1:T(8,128)(2,1)S(1)} %bitcast.99, bf16[256,256]{1,0:T(8,128)(2,1)} %param.7), kind=kOutput, calls=%fused_computation.39 | convolution fusion | flops 33947648 | bytes 655360 | tf_op jit(solution)/shard_map/dot_general | solution.py:211
  3.0 4.9 %collective-permute-start = (bf16[1,2,256,128]{3,2,1,0:T(8,128)(2,1)S(1)}, bf16[1,2,256,128]{3,2,1,0:T(8,128)(2,1)S(1)}, u32[]{:S(2)}, u32[]{:S(2)}) collective-permute-start(bf16[1,2,256,128]{3,2,1,0:T(8,128)(2,1)S(1)} %bitcast.90), channel_id=1, source_target_pairs={{0,4},{4,8},{8,12},{1,5},{5,9},{9,13},{2,6},{6,10},{10,14},{3,7},{... | collective-permute-start | bytes 393224 | tf_op jit(solution)/shard_map/ppermute | solution.py:168
  7.9 1.3 %collective-permute-start.1 = (bf16[1,2,256,128]{3,2,1,0:T(8,128)(2,1)S(1)}, bf16[1,2,256,128]{3,2,1,0:T(8,128)(2,1)S(1)}, u32[]{:S(2)}, u32[]{:S(2)}) collective-permute-start(bf16[1,2,256,128]{3,2,1,0:T(8,128)(2,1)S(1)} %bitcast.91), channel_id=1, source_target_pairs={{4,0},{8,4},{12,8},{5,1},{9,5},{13,9},{6,2},{10,6},{14,10},{7,3},{... | collective-permute-start | bytes 393224 | tf_op jit(solution)/shard_map/ppermute | solution.py:169
  9.4 4.0 %fusion = bf16[27,256,256]{2,1,0:T(8,128)(2,1)} fusion(f32[256,256]{1,0:T(8,128)S(1)} %compare_convert_fusion.mask_ref, bf16[256,8,27]{0,1,2:T(8,128)(2,1)} %bitcast.109, s32[256]{0:T(256)S(1)} %and_select_fusion.2), kind=kOutput, calls=%fused_computation.1 | convolution fusion | flops 31852544 | bytes 3912704 | tf_op jit(solution)/shard_map/ojt,ji->toi/dot_general | solution.py:185
  13.4 2.9 %multiply_convert_fusion = bf16[256,256,27]{1,0,2:T(8,128)(2,1)} fusion(f32[256,256]{1,0:T(8,128)S(1)} %compare_convert_fusion.mask_ref, bf16[256,8,27]{0,1,2:T(8,128)(2,1)S(1)} %bitcast.110, s32[256]{0:T(256)S(1)} %and_select_fusion.2), kind=kOutput, calls=%fused_computation.2 | convolution fusion | flops 31907840 | bytes 3912704 | tf_op jit(solution)/shard_map/ji,ojt->tio/dot_general | solution.py:186
  16.6 1.5 %collective-permute-start.2 = (bf16[3,1,256,128]{3,2,1,0:T(8,128)(2,1)S(1)}, bf16[3,1,256,128]{3,2,1,0:T(8,128)(2,1)S(1)}, u32[]{:S(2)}, u32[]{:S(2)}) collective-permute-start(bf16[3,1,256,128]{3,2,1,0:T(8,128)(2,1)S(1)} %get-tuple-element.32), channel_id=1, source_target_pairs={{0,1},{1,2},{2,3},{4,5},{5,6},{6,7},{8,9},{9,10},{10,11},{12,13},{... | collective-permute-start | bytes 589832 | tf_op jit(solution)/shard_map/ppermute | solution.py:168
  18.0 1.3 %collective-permute-start.3 = (bf16[3,1,256,128]{3,2,1,0:T(8,128)(2,1)S(1)}, bf16[3,1,256,128]{3,2,1,0:T(8,128)(2,1)S(1)}, u32[]{:S(2)}, u32[]{:S(2)}) collective-permute-start(bf16[3,1,256,128]{3,2,1,0:T(8,128)(2,1)S(1)} %get-tuple-element.33), channel_id=1, source_target_pairs={{1,0},{2,1},{3,2},{5,4},{6,5},{7,6},{9,8},{10,9},{11,10},{13,12},{... | collective-permute-start | bytes 589832 | tf_op jit(solution)/shard_map/ppermute | solution.py:169
  19.3 1.2 %fusion.6.sel_ref = bf16[16,128,128]{2,1,0:T(8,128)(2,1)} fusion(s32[16,128]{1,0:T(8,128)S(1)} %broadcast_add_fusion), kind=kLoop, calls=%fused_computation.13 | loop fusion | flops 524288 | bytes 532480 | tf_op jit(solution)/shard_map/convert_element_type | solution.py:102
  20.5 2.4 %collective-permute-done.3 = bf16[3,1,256,128]{3,2,1,0:T(8,128)(2,1)S(1)} collective-permute-done((bf16[3,1,256,128]{3,2,1,0:T(8,128)(2,1)S(1)}, bf16[3,1,256,128]{3,2,1,0:T(8,128)(2,1)S(1)}, u32[]{:S(2)}, u32[]{:S(2)}) %collective-permute-start.3) | collective-permute-done | bytes 196640 | tf_op jit(solution)/shard_map/ppermute | solution.py:169
  22.9 1.0 pad_maximum_fusion.ext_ref.act_ref
  23.9 5.0 %shard_map.92 = f32[2,256,128]{2,1,0:T(8,128)} custom-call(bf16[3,4,256,128]{3,2,1,0:T(8,128)(2,1)} %pad_maximum_fusion.ext_ref.act_ref, bf16[9,768,256]{2,1,0:T(8,128)(2,1)} %bitcast.88), custom_call_target="tpu_custom_call" | custom-call | flops 905969664 | bytes 4587520 | tf_op jit(solution)/shard_map/pallas_call | solution.py:43
  29.0 1.1 %fusion.16 = bf16[256,2,128]{2,0,1:T(8,128)(2,1)S(1)} fusion(f32[2,256,128]{2,1,0:T(8,128)} %shard_map.92), kind=kLoop, calls=%fused_computation.52 | loop fusion | flops 393216 | bytes 393216 | tf_op jit(solution)/shard_map/transpose | solution.py:208
  30.2 0.3 fusion.14
  30.5 0.2 fusion.5
  30.9 0.8 fusion.10.delta_ref
  31.6 4.5 %collective-permute-start.4 = (bf16[1,2,256,128]{3,2,1,0:T(8,128)(2,1)}, bf16[1,2,256,128]{3,2,1,0:T(8,128)(2,1)S(1)}, u32[]{:S(2)}, u32[]{:S(2)}) collective-permute-start(bf16[1,2,256,128]{3,2,1,0:T(8,128)(2,1)} %bitcast.16), channel_id=1, source_target_pairs={{0,4},{4,8},{8,12},{1,5},{5,9},{9,13},{2,6},{6,10},{10,14},{3,7},{... | collective-permute-start | bytes 393224 | tf_op jit(solution)/shard_map/ppermute | solution.py:168
  36.2 1.3 %collective-permute-start.5 = (bf16[1,2,256,128]{3,2,1,0:T(8,128)(2,1)}, bf16[1,2,256,128]{3,2,1,0:T(8,128)(2,1)S(1)}, u32[]{:S(2)}, u32[]{:S(2)}) collective-permute-start(bf16[1,2,256,128]{3,2,1,0:T(8,128)(2,1)} %bitcast.16), channel_id=1, source_target_pairs={{4,0},{8,4},{12,8},{5,1},{9,5},{13,9},{6,2},{10,6},{14,10},{7,3},{... | collective-permute-start | bytes 393224 | tf_op jit(solution)/shard_map/ppermute | solution.py:169
  37.5 5.6 %shard_map.94 = f32[2,256,128]{2,1,0:T(8,128)} custom-call(bf16[3,4,256,128]{3,2,1,0:T(8,128)(2,1)} %pad_maximum_fusion.ext_ref.act_ref, bf16[2,256,128]{2,1,0:T(8,128)(2,1)} %fusion.10.delta_ref, f32[256,256]{1,0:T(8,128)} %copy-done.1, bf16[16,128,128]{2,1,0:T(8,128)(2,1)} %fusion.6.sel_ref), custom_call_target="tpu_custom_call" | custom-call | flops 1358954496 | bytes 1179648 | tf_op jit(solution)/shard_map/pallas_call | solution.py:103
  43.1 1.1 %copy.85 = f32[256,2,128]{0,2,1:T(8,128)S(1)} copy(f32[256,2,128]{2,0,1:T(8,128)} %bitcast.111) | data formatting | bytes 524288 | tf_op jit(solution)/shard_map/transpose | solution.py:114
  45.4 0.2 fusion.35
  45.6 1.0 pad_maximum_fusion.3
  46.6 5.8 %collective-permute-start.6 = (bf16[3,1,256,128]{3,2,1,0:T(8,128)(2,1)S(1)}, bf16[3,1,256,128]{3,2,1,0:T(8,128)(2,1)S(1)}, u32[]{:S(2)}, u32[]{:S(2)}) collective-permute-start(bf16[3,1,256,128]{3,2,1,0:T(8,128)(2,1)S(1)} %get-tuple-element.30), channel_id=1, source_target_pairs={{0,1},{1,2},{2,3},{4,5},{5,6},{6,7},{8,9},{9,10},{10,11},{12,13},{... | collective-permute-start | bytes 589832 | tf_op jit(solution)/shard_map/ppermute | solution.py:168
  52.4 1.5 %collective-permute-start.7 = (bf16[3,1,256,128]{3,2,1,0:T(8,128)(2,1)S(1)}, bf16[3,1,256,128]{3,2,1,0:T(8,128)(2,1)S(1)}, u32[]{:S(2)}, u32[]{:S(2)}) collective-permute-start(bf16[3,1,256,128]{3,2,1,0:T(8,128)(2,1)S(1)} %get-tuple-element.31), channel_id=1, source_target_pairs={{1,0},{2,1},{3,2},{5,4},{6,5},{7,6},{9,8},{10,9},{11,10},{13,12},{... | collective-permute-start | bytes 589832 | tf_op jit(solution)/shard_map/ppermute | solution.py:169
  54.1 1.6 %collective-permute-done.7 = bf16[3,1,256,128]{3,2,1,0:T(8,128)(2,1)S(1)} collective-permute-done((bf16[3,1,256,128]{3,2,1,0:T(8,128)(2,1)S(1)}, bf16[3,1,256,128]{3,2,1,0:T(8,128)(2,1)S(1)}, u32[]{:S(2)}, u32[]{:S(2)}) %collective-permute-start.7) | collective-permute-done | bytes 196640 | tf_op jit(solution)/shard_map/ppermute | solution.py:169
  55.8 1.9 %pad_maximum_fusion.1.ext_ref = bf16[3,4,256,128]{3,2,1,0:T(8,128)(2,1)} fusion(bf16[3,1,256,128]{3,2,1,0:T(8,128)(2,1)S(1)} %collective-permute-done.7, bf16[1,2,256,128]{3,2,1,0:T(8,128)(2,1)S(1)} %collective-permute-done.5, bf16[1,2,256,128]{3,2,1,0:T(8,128)(2,1)} %bitcast.16, bf16[1,2,256,128]{3,2,1,0:T(8,128)(2,1)S(1)} %collective-permute-done.4, ...), kind=kLoop, calls=%fused_computation.15 | loop fusion | flops 1572864 | bytes 1572864 | tf_op jit(solution)/shard_map/concatenate | solution.py:170
  57.7 5.0 %shard_map.93 = f32[2,256,128]{2,1,0:T(8,128)} custom-call(bf16[3,4,256,128]{3,2,1,0:T(8,128)(2,1)} %pad_maximum_fusion.1.ext_ref, bf16[9,768,256]{2,1,0:T(8,128)(2,1)} %bitcast.87), custom_call_target="tpu_custom_call" | custom-call | flops 905969664 | bytes 4587520 | tf_op jit(solution)/shard_map/pallas_call | solution.py:43
  62.7 1.0 convert_bitcast_fusion
  63.9 0.2 convolution_bitcast_fusion
  64.4 3.8 %collective-permute-start.8 = (f32[93184]{0:T(1024)S(1)}, f32[93184]{0:T(1024)S(1)}, u32[]{:S(2)}, u32[]{:S(2)}) collective-permute-start(f32[93184]{0:T(1024)S(1)} %pad_maximum_fusion.4), channel_id=1, source_target_pairs={{0,1},{1,0},{2,3},{3,2},{4,5},{5,4},{6,7},{7,6},{8,9},{9,8},{10,11... | collective-permute-start | bytes 1118216 | tf_op jit(solution)/shard_map/ppermute | solution.py:138
  68.7 0.9 collective-permute-done.8
  69.8 6.9 %collective-permute-done.9 = f32[46592]{0:T(1024)S(1)} collective-permute-done((f32[46592]{0:T(1024)S(1)}, f32[46592]{0:T(1024)S(1)}, u32[]{:S(2)}, u32[]{:S(2)}) %collective-permute-start.9) | collective-permute-done | bytes 186400 | tf_op jit(solution)/shard_map/ppermute | solution.py:138
  76.9 2.7 %collective-permute-start.10 = (f32[23296]{0:T(1024)S(1)}, f32[23296]{0:T(1024)S(1)}, u32[]{:S(2)}, u32[]{:S(2)}) collective-permute-start(f32[23296]{0:T(1024)S(1)} %pad_maximum_fusion.8), channel_id=1, source_target_pairs={{0,4},{4,0},{8,12},{12,8},{1,5},{5,1},{9,13},{13,9},{2,6},{6,2},{1... | collective-permute-start | bytes 279560 | tf_op jit(solution)/shard_map/ppermute | solution.py:138
  79.6 0.8 copy.99
  80.3 1.8 %collective-permute-done.10 = f32[23296]{0:T(1024)S(1)} collective-permute-done((f32[23296]{0:T(1024)S(1)}, f32[23296]{0:T(1024)S(1)}, u32[]{:S(2)}, u32[]{:S(2)}) %collective-permute-start.10) | collective-permute-done | bytes 93216 | tf_op jit(solution)/shard_map/ppermute | solution.py:138
  82.2 3.1 %collective-permute-start.11 = (f32[11648]{0:T(1024)S(1)}, f32[11648]{0:T(1024)S(1)}, u32[]{:S(2)}, u32[]{:S(2)}) collective-permute-start(f32[11648]{0:T(1024)S(1)} %pad_maximum_fusion.12), channel_id=1, source_target_pairs={{0,8},{4,12},{8,0},{12,4},{1,9},{5,13},{9,1},{13,5},{2,10},{6,14},... | collective-permute-start | bytes 139784 | tf_op jit(solution)/shard_map/ppermute | solution.py:138
  85.5 0.8 copy.100
  86.3 1.1 collective-permute-done.11
  87.4 3.0 %collective-permute-start.12 = (f32[8192]{0:T(1024)S(1)}, f32[8192]{0:T(1024)S(1)}, u32[]{:S(2)}, u32[]{:S(2)}) collective-permute-start(f32[8192]{0:T(1024)S(1)} %pad_maximum_fusion.14), channel_id=1, source_target_pairs={{0,8},{4,12},{8,0},{12,4},{1,9},{5,13},{9,1},{13,5},{2,10},{6,14},... | collective-permute-start | bytes 98312 | tf_op jit(solution)/shard_map/ppermute | solution.py:148
  90.7 1.7 %collective-permute-done.12 = f32[8192]{0:T(1024)S(1)} collective-permute-done((f32[8192]{0:T(1024)S(1)}, f32[8192]{0:T(1024)S(1)}, u32[]{:S(2)}, u32[]{:S(2)}) %collective-permute-start.12) | collective-permute-done | bytes 32800 | tf_op jit(solution)/shard_map/ppermute | solution.py:148
  92.5 1.9 %collective-permute-start.13 = (f32[16384]{0:T(1024)S(1)}, f32[16384]{0:T(1024)S(1)}, u32[]{:S(2)}, u32[]{:S(2)}) collective-permute-start(f32[16384]{0:T(1024)S(1)} %pad_maximum_fusion.10), channel_id=1, source_target_pairs={{0,4},{4,0},{8,12},{12,8},{1,5},{5,1},{9,13},{13,9},{2,6},{6,2},{1... | collective-permute-start | bytes 196616 | tf_op jit(solution)/shard_map/ppermute | solution.py:148
  94.4 2.4 %collective-permute-done.13 = f32[16384]{0:T(1024)S(1)} collective-permute-done((f32[16384]{0:T(1024)S(1)}, f32[16384]{0:T(1024)S(1)}, u32[]{:S(2)}, u32[]{:S(2)}) %collective-permute-start.13) | collective-permute-done | bytes 65568 | tf_op jit(solution)/shard_map/ppermute | solution.py:148
  96.9 0.3 collective-permute-start.14
  97.3 4.8 %collective-permute-done.14 = f32[36224]{0:T(1024)S(1)} collective-permute-done((f32[36224]{0:T(1024)S(1)}, f32[36224]{0:T(1024)S(1)}, u32[]{:S(2)}, u32[]{:S(2)}) %collective-permute-start.14) | collective-permute-done | bytes 144928 | tf_op jit(solution)/shard_map/ppermute | solution.py:148
  102.8 1.4 %collective-permute-done.15 = f32[72448]{0:T(1024)S(1)} collective-permute-done((f32[72448]{0:T(1024)S(1)}, f32[72448]{0:T(1024)S(1)}, u32[]{:S(2)}, u32[]{:S(2)}) %collective-permute-start.15) | collective-permute-done | bytes 289824 | tf_op jit(solution)/shard_map/ppermute | solution.py:148
  104.4 0.3 copy.97
  104.8 0.8 fusion.17
  105.6 0.8 fusion.7
  (121 shorter events, 5.0 us)
Async XLA Ops:
  0.6 29.6 %copy-start = (bf16[256,256]{1,0:T(8,128)(2,1)S(1)}, bf16[256,256]{1,0:T(8,128)(2,1)}, u32[]{:S(2)}) copy-start(bf16[256,256]{1,0:T(8,128)(2,1)} %param.9) | copy-start | bytes 393220
  0.6 12.7 %copy-start.3 = (bf16[256,8,3,3,3]{0,1,4,3,2:T(8,128)(2,1)S(1)}, bf16[256,8,3,3,3]{0,1,4,3,2:T(8,128)(2,1)}, u32[]{:S(2)}) copy-start(bf16[256,8,3,3,3]{0,1,4,3,2:T(8,128)(2,1)} %param.8) | copy-start | bytes 331780
  3.0 13.5 %collective-permute-start = (bf16[1,2,256,128]{3,2,1,0:T(8,128)(2,1)S(1)}, bf16[1,2,256,128]{3,2,1,0:T(8,128)(2,1)S(1)}, u32[]{:S(2)}, u32[]{:S(2)}) collective-permute-start(bf16[1,2,256,128]{3,2,1,0:T(8,128)(2,1)S(1)} %bitcast.90), channel_id=1, source_target_pairs={{0,4},{4,8},{8,12},{1,5},{5,9},{9,13},{2,6},{6,10},{10,14},{3,7},{... | collective-permute-start | bytes 393224 | tf_op jit(solution)/shard_map/ppermute | solution.py:168
  7.9 8.5 %collective-permute-start.1 = (bf16[1,2,256,128]{3,2,1,0:T(8,128)(2,1)S(1)}, bf16[1,2,256,128]{3,2,1,0:T(8,128)(2,1)S(1)}, u32[]{:S(2)}, u32[]{:S(2)}) collective-permute-start(bf16[1,2,256,128]{3,2,1,0:T(8,128)(2,1)S(1)} %bitcast.91), channel_id=1, source_target_pairs={{4,0},{8,4},{12,8},{5,1},{9,5},{13,9},{6,2},{10,6},{14,10},{7,3},{... | collective-permute-start | bytes 393224 | tf_op jit(solution)/shard_map/ppermute | solution.py:169
  9.4 6.9 %copy-start.1 = (f32[256,256]{1,0:T(8,128)}, f32[256,256]{1,0:T(8,128)S(1)}, u32[]{:S(2)}) copy-start(f32[256,256]{1,0:T(8,128)S(1)} %compare_convert_fusion.mask_ref) | copy-start | bytes 786436
  9.4 6.9 %copy-start.4 = (bf16[256,1,2,128]{3,2,1,0:T(2,128)(2,1)S(1)}, bf16[256,1,2,128]{3,2,1,0:T(2,128)(2,1)}, u32[]{:S(2)}) copy-start(bf16[256,1,2,128]{3,2,1,0:T(2,128)(2,1)} %param.6) | copy-start | bytes 393220
  16.6 4.0 %collective-permute-start.2 = (bf16[3,1,256,128]{3,2,1,0:T(8,128)(2,1)S(1)}, bf16[3,1,256,128]{3,2,1,0:T(8,128)(2,1)S(1)}, u32[]{:S(2)}, u32[]{:S(2)}) collective-permute-start(bf16[3,1,256,128]{3,2,1,0:T(8,128)(2,1)S(1)} %get-tuple-element.32), channel_id=1, source_target_pairs={{0,1},{1,2},{2,3},{4,5},{5,6},{6,7},{8,9},{9,10},{10,11},{12,13},{... | collective-permute-start | bytes 589832 | tf_op jit(solution)/shard_map/ppermute | solution.py:168
  18.0 4.9 %collective-permute-start.3 = (bf16[3,1,256,128]{3,2,1,0:T(8,128)(2,1)S(1)}, bf16[3,1,256,128]{3,2,1,0:T(8,128)(2,1)S(1)}, u32[]{:S(2)}, u32[]{:S(2)}) collective-permute-start(bf16[3,1,256,128]{3,2,1,0:T(8,128)(2,1)S(1)} %get-tuple-element.33), channel_id=1, source_target_pairs={{1,0},{2,1},{3,2},{5,4},{6,5},{7,6},{9,8},{10,9},{11,10},{13,12},{... | collective-permute-start | bytes 589832 | tf_op jit(solution)/shard_map/ppermute | solution.py:169
  29.0 1.9 %copy-start.2 = (f32[2,256,128]{2,1,0:T(8,128)S(1)}, f32[2,256,128]{2,1,0:T(8,128)}, u32[]{:S(2)}) copy-start(f32[2,256,128]{2,1,0:T(8,128)} %shard_map.92) | copy-start | bytes 786436
  31.6 14.0 %collective-permute-start.4 = (bf16[1,2,256,128]{3,2,1,0:T(8,128)(2,1)}, bf16[1,2,256,128]{3,2,1,0:T(8,128)(2,1)S(1)}, u32[]{:S(2)}, u32[]{:S(2)}) collective-permute-start(bf16[1,2,256,128]{3,2,1,0:T(8,128)(2,1)} %bitcast.16), channel_id=1, source_target_pairs={{0,4},{4,8},{8,12},{1,5},{5,9},{9,13},{2,6},{6,10},{10,14},{3,7},{... | collective-permute-start | bytes 393224 | tf_op jit(solution)/shard_map/ppermute | solution.py:168
  36.2 9.5 %collective-permute-start.5 = (bf16[1,2,256,128]{3,2,1,0:T(8,128)(2,1)}, bf16[1,2,256,128]{3,2,1,0:T(8,128)(2,1)S(1)}, u32[]{:S(2)}, u32[]{:S(2)}) collective-permute-start(bf16[1,2,256,128]{3,2,1,0:T(8,128)(2,1)} %bitcast.16), channel_id=1, source_target_pairs={{4,0},{8,4},{12,8},{5,1},{9,5},{13,9},{6,2},{10,6},{14,10},{7,3},{... | collective-permute-start | bytes 393224 | tf_op jit(solution)/shard_map/ppermute | solution.py:169
  46.6 7.5 %collective-permute-start.6 = (bf16[3,1,256,128]{3,2,1,0:T(8,128)(2,1)S(1)}, bf16[3,1,256,128]{3,2,1,0:T(8,128)(2,1)S(1)}, u32[]{:S(2)}, u32[]{:S(2)}) collective-permute-start(bf16[3,1,256,128]{3,2,1,0:T(8,128)(2,1)S(1)} %get-tuple-element.30), channel_id=1, source_target_pairs={{0,1},{1,2},{2,3},{4,5},{5,6},{6,7},{8,9},{9,10},{10,11},{12,13},{... | collective-permute-start | bytes 589832 | tf_op jit(solution)/shard_map/ppermute | solution.py:168
  52.4 3.3 %collective-permute-start.7 = (bf16[3,1,256,128]{3,2,1,0:T(8,128)(2,1)S(1)}, bf16[3,1,256,128]{3,2,1,0:T(8,128)(2,1)S(1)}, u32[]{:S(2)}, u32[]{:S(2)}) collective-permute-start(bf16[3,1,256,128]{3,2,1,0:T(8,128)(2,1)S(1)} %get-tuple-element.31), channel_id=1, source_target_pairs={{1,0},{2,1},{3,2},{5,4},{6,5},{7,6},{9,8},{10,9},{11,10},{13,12},{... | collective-permute-start | bytes 589832 | tf_op jit(solution)/shard_map/ppermute | solution.py:169
  64.2 21.1 %copy-start.5 = (bf16[256,256]{1,0:T(8,128)(2,1)S(1)}, bf16[256,256]{1,0:T(8,128)(2,1)}, u32[]{:S(2)}) copy-start(bf16[256,256]{1,0:T(8,128)(2,1)} %param.7) | copy-start | bytes 393220
  64.4 5.2 %collective-permute-start.8 = (f32[93184]{0:T(1024)S(1)}, f32[93184]{0:T(1024)S(1)}, u32[]{:S(2)}, u32[]{:S(2)}) collective-permute-start(f32[93184]{0:T(1024)S(1)} %pad_maximum_fusion.4), channel_id=1, source_target_pairs={{0,1},{1,0},{2,3},{3,2},{4,5},{5,4},{6,7},{7,6},{8,9},{9,8},{10,11... | collective-permute-start | bytes 1118216 | tf_op jit(solution)/shard_map/ppermute | solution.py:138
  69.7 7.1 %collective-permute-start.9 = (f32[46592]{0:T(1024)S(1)}, f32[46592]{0:T(1024)S(1)}, u32[]{:S(2)}, u32[]{:S(2)}) collective-permute-start(f32[46592]{0:T(1024)S(1)} %pad_maximum_fusion.6), channel_id=1, source_target_pairs={{0,2},{1,3},{2,0},{3,1},{4,6},{5,7},{6,4},{7,5},{8,10},{9,11},{10,... | collective-permute-start | bytes 559112 | tf_op jit(solution)/shard_map/ppermute | solution.py:138
  76.9 5.3 %collective-permute-start.10 = (f32[23296]{0:T(1024)S(1)}, f32[23296]{0:T(1024)S(1)}, u32[]{:S(2)}, u32[]{:S(2)}) collective-permute-start(f32[23296]{0:T(1024)S(1)} %pad_maximum_fusion.8), channel_id=1, source_target_pairs={{0,4},{4,0},{8,12},{12,8},{1,5},{5,1},{9,13},{13,9},{2,6},{6,2},{1... | collective-permute-start | bytes 279560 | tf_op jit(solution)/shard_map/ppermute | solution.py:138
  82.2 5.2 %collective-permute-start.11 = (f32[11648]{0:T(1024)S(1)}, f32[11648]{0:T(1024)S(1)}, u32[]{:S(2)}, u32[]{:S(2)}) collective-permute-start(f32[11648]{0:T(1024)S(1)} %pad_maximum_fusion.12), channel_id=1, source_target_pairs={{0,8},{4,12},{8,0},{12,4},{1,9},{5,13},{9,1},{13,5},{2,10},{6,14},... | collective-permute-start | bytes 139784 | tf_op jit(solution)/shard_map/ppermute | solution.py:138
  87.4 5.0 %collective-permute-start.12 = (f32[8192]{0:T(1024)S(1)}, f32[8192]{0:T(1024)S(1)}, u32[]{:S(2)}, u32[]{:S(2)}) collective-permute-start(f32[8192]{0:T(1024)S(1)} %pad_maximum_fusion.14), channel_id=1, source_target_pairs={{0,8},{4,12},{8,0},{12,4},{1,9},{5,13},{9,1},{13,5},{2,10},{6,14},... | collective-permute-start | bytes 98312 | tf_op jit(solution)/shard_map/ppermute | solution.py:148
  92.5 4.3 %collective-permute-start.13 = (f32[16384]{0:T(1024)S(1)}, f32[16384]{0:T(1024)S(1)}, u32[]{:S(2)}, u32[]{:S(2)}) collective-permute-start(f32[16384]{0:T(1024)S(1)} %pad_maximum_fusion.10), channel_id=1, source_target_pairs={{0,4},{4,0},{8,12},{12,8},{1,5},{5,1},{9,13},{13,9},{2,6},{6,2},{1... | collective-permute-start | bytes 196616 | tf_op jit(solution)/shard_map/ppermute | solution.py:148
  96.9 5.2 %collective-permute-start.14 = (f32[36224]{0:T(1024)S(1)}, f32[36224]{0:T(1024)S(1)}, u32[]{:S(2)}, u32[]{:S(2)}) collective-permute-start(f32[36224]{0:T(1024)S(1)} %pad_maximum_fusion.7), channel_id=1, source_target_pairs={{0,2},{1,3},{2,0},{3,1},{4,6},{5,7},{6,4},{7,5},{8,10},{9,11},{10,... | collective-permute-start | bytes 434696 | tf_op jit(solution)/shard_map/ppermute | solution.py:148
  102.6 1.6 %collective-permute-start.15 = (f32[72448]{0:T(1024)S(1)}, f32[72448]{0:T(1024)S(1)}, u32[]{:S(2)}, u32[]{:S(2)}) collective-permute-start(f32[72448]{0:T(1024)S(1)} %pad_maximum_fusion.5), channel_id=1, source_target_pairs={{0,1},{1,0},{2,3},{3,2},{4,5},{5,4},{6,7},{7,6},{8,9},{9,8},{10,11... | collective-permute-start | bytes 869384 | tf_op jit(solution)/shard_map/ppermute | solution.py:148

commit v8 on v7

--- a/solution.py
+++ b/solution.py
@@ -21,19 +21,23 @@
     return jnp.where(lane == edge, jnp.zeros_like(rolled), rolled)
 
 
-def conv_body(ext_ref, w_ref, out_ref):
+def conv_body(ext_ref, w_hbm, out_ref, w_vmem, sems):
     height, channels = out_ref.shape[0], out_ref.shape[1]
+    copies = [pltpu.make_async_copy(w_hbm.at[k], w_vmem.at[k], sems.at[k]) for k in range(9)]
+    for copy in copies:
+        copy.start()
+    parts = None
+    for dz, dy in itertools.product(range(3), repeat=2):
+        rows = jnp.concatenate([ext_ref[dz, dy + y] for y in range(height)], axis=1)
+        copies[dz * 3 + dy].wait()
+        product = jnp.dot(w_vmem[dz * 3 + dy], rows, preferred_element_type=jnp.float32)
+        parts = product if parts is None else parts + product
     for y in range(height):
-        parts = None
-        for dz, dy in itertools.product(range(3), repeat=2):
-            product = jnp.dot(
-                w_ref[dz * 3 + dy], ext_ref[dz, y + dy], preferred_element_type=jnp.float32
-            )
-            parts = product if parts is None else parts + product
+        lanes = slice(y * LANES, (y + 1) * LANES)
         out_ref[y] = (
-            parts[channels : 2 * channels]
-            + shift_lanes(parts[:channels], -1)
-            + shift_lanes(parts[2 * channels :], 1)
+            parts[channels : 2 * channels, lanes]
+            + shift_lanes(parts[:channels, lanes], -1)
+            + shift_lanes(parts[2 * channels :, lanes], 1)
         )
 
 
@@ -43,8 +47,9 @@
     return pl.pallas_call(
         conv_body,
         out_shape=jax.ShapeDtypeStruct((height, channels, width), jnp.float32),
-        in_specs=[pl.BlockSpec(memory_space=pltpu.VMEM)] * 2,
+        in_specs=[pl.BlockSpec(memory_space=pltpu.VMEM), pl.BlockSpec(memory_space=pl.ANY)],
         out_specs=pl.BlockSpec(memory_space=pltpu.VMEM),
+        scratch_shapes=[pltpu.VMEM(weights.shape, weights.dtype), pltpu.SemaphoreType.DMA((9,))],
         cost_estimate=pl.CostEstimate(
             flops=2 * 27 * channels * channels * height * width,
             transcendentals=0,
@@ -63,18 +68,14 @@
                 jnp.bfloat16
             )
         )
+    stacked = jnp.concatenate(stacked, axis=1)
     mask = mask_ref[...]
     totals = [jnp.zeros((channels, LANES), jnp.float32) for _ in range(out_ref.shape[0])]
     for dz, dy in itertools.product(range(3), repeat=2):
-        grads = None
-        for y in range(height):
-            term = lax.dot_general(
-                stacked[y],
-                act_ref[dz, y + dy],
-                (((1,), (1,)), ((), ())),
-                preferred_element_type=jnp.float32,
-            )
-            grads = term if grads is None else grads + term
+        rows = jnp.concatenate([act_ref[dz, dy + y] for y in range(height)], axis=1)
+        grads = lax.dot_general(
+            stacked, rows, (((1,), (1,)), ((), ())), preferred_element_type=jnp.float32
+        )
         for dx in range(3):
             tap = dz * 9 + dy * 3 + dx
             picked = grads[dx * channels : (dx + 1) * channels] * mask

time: 107 us -> 107 us (level)
  transfers between devices with their start and end apart: 16 -> 16, of which waited for: 10 -> 10; matrix products, arithmetic and copies ran while one was open for 13% -> 13% of each run, Pallas kernels for 5% -> 4%
where the time goes in v8:
time: 107 us; the launch traced here: 106 us
  starting transfers between devices  37.2 us (35%)
  waiting for transfers between devices  25 us (23%)
  Pallas kernels  15.2 us (14%)
  other arithmetic  10.6 us (10%)
  matrix products  9.14 us (9%)
  local copies, waits for them, and re-layouts  7.39 us (7%)
  between operations  1.51 us (1%)
    ppermute x4, starting transfers between devices, halo(): lax.ppermute(lax.slice_in_dim(block, size - 1, size, axis=dim), axis, up)  16.7 us
    pallas_call x2, Pallas kernels, conv_call(): pl.pallas_call(conv_body, out_shape=jax.ShapeDtypeStruct((height, channel...  10.6 us
    ppermute x4, waiting for transfers between devices, tree_sum(): got = lax.ppermute(jnp.concatenate(sends), axis, pairs)  10.6 us
    ppermute x4, waiting for transfers between devices, tree_sum(): lax.ppermute(jnp.concatenate([pieces[n] for n in members]), axis, pairs)  10.3 us
    ppermute x4, starting transfers between devices, tree_sum(): got = lax.ppermute(jnp.concatenate(sends), axis, pairs)  9.8 us
    ppermute x4, starting transfers between devices, tree_sum(): lax.ppermute(jnp.concatenate([pieces[n] for n in members]), axis, pairs)  5.35 us
    ppermute x4, starting transfers between devices, halo(): high = lax.ppermute(lax.slice_in_dim(block, 0, 1, axis=dim), axis, down)  5.35 us
    pallas_call x1, Pallas kernels, wgrad_call(): pl.pallas_call(wgrad_body, out_shape=jax.ShapeDtypeStruct((blocks, channe...  4.56 us
  transfers between devices with their start and end apart: 16, of which 10 were waited for; matrix products, arithmetic and copies ran while one was open for 13% of the time, Pallas kernels for 4%

profile of v8, /device:TPU:0, one launch (start us, length us, event | category | flops | bytes accessed | tf_op | source)
XLA Modules:
  0.0 106.0 jit_solution(13623491586711207191)
XLA Ops:
  0.7 1.1 %copy.74 = bf16[256,1,2,128]{0,3,2,1:T(8,128)(2,1)S(1)} copy(bf16[256,1,2,128]{3,2,1,0:T(2,128)(2,1)} %param.5) | data formatting | bytes 262144 | tf_op args[0]
  1.7 1.1 %reduce-precision_convert_fusion.2 = (bf16[256,256]{0,1:T(8,128)(2,1)S(1)}, f32[256,256]{0,1:T(8,128)S(1)}) fusion(bf16[256,256]{0,1:T(8,128)(2,1)S(1)} %bitcast.99, bf16[256,256]{1,0:T(8,128)(2,1)} %param.7), kind=kOutput, calls=%fused_computation.39 | convolution fusion | flops 33947648 | bytes 655360 | tf_op jit(solution)/shard_map/dot_general | solution.py:212
  3.0 4.9 %collective-permute-start = (bf16[1,2,256,128]{3,2,1,0:T(8,128)(2,1)S(1)}, bf16[1,2,256,128]{3,2,1,0:T(8,128)(2,1)S(1)}, u32[]{:S(2)}, u32[]{:S(2)}) collective-permute-start(bf16[1,2,256,128]{3,2,1,0:T(8,128)(2,1)S(1)} %bitcast.90), channel_id=1, source_target_pairs={{0,4},{4,8},{8,12},{1,5},{5,9},{9,13},{2,6},{6,10},{10,14},{3,7},{... | collective-permute-start | bytes 393224 | tf_op jit(solution)/shard_map/ppermute | solution.py:169
  7.9 1.3 %collective-permute-start.1 = (bf16[1,2,256,128]{3,2,1,0:T(8,128)(2,1)S(1)}, bf16[1,2,256,128]{3,2,1,0:T(8,128)(2,1)S(1)}, u32[]{:S(2)}, u32[]{:S(2)}) collective-permute-start(bf16[1,2,256,128]{3,2,1,0:T(8,128)(2,1)S(1)} %bitcast.91), channel_id=1, source_target_pairs={{4,0},{8,4},{12,8},{5,1},{9,5},{13,9},{6,2},{10,6},{14,10},{7,3},{... | collective-permute-start | bytes 393224 | tf_op jit(solution)/shard_map/ppermute | solution.py:170
  9.4 4.0 %fusion = bf16[27,256,256]{2,1,0:T(8,128)(2,1)} fusion(f32[256,256]{1,0:T(8,128)S(1)} %compare_convert_fusion.mask_ref, bf16[256,8,27]{0,1,2:T(8,128)(2,1)} %bitcast.109, s32[256]{0:T(256)S(1)} %and_select_fusion.2), kind=kOutput, calls=%fused_computation.1 | convolution fusion | flops 31852544 | bytes 3912704 | tf_op jit(solution)/shard_map/ojt,ji->toi/dot_general | solution.py:186
  13.4 2.9 %multiply_convert_fusion = bf16[256,256,27]{1,0,2:T(8,128)(2,1)} fusion(f32[256,256]{1,0:T(8,128)S(1)} %compare_convert_fusion.mask_ref, bf16[256,8,27]{0,1,2:T(8,128)(2,1)S(1)} %bitcast.110, s32[256]{0:T(256)S(1)} %and_select_fusion.2), kind=kOutput, calls=%fused_computation.2 | convolution fusion | flops 31907840 | bytes 3912704 | tf_op jit(solution)/shard_map/ji,ojt->tio/dot_general | solution.py:187
  16.6 1.5 %collective-permute-start.2 = (bf16[3,1,256,128]{3,2,1,0:T(8,128)(2,1)S(1)}, bf16[3,1,256,128]{3,2,1,0:T(8,128)(2,1)S(1)}, u32[]{:S(2)}, u32[]{:S(2)}) collective-permute-start(bf16[3,1,256,128]{3,2,1,0:T(8,128)(2,1)S(1)} %get-tuple-element.32), channel_id=1, source_target_pairs={{0,1},{1,2},{2,3},{4,5},{5,6},{6,7},{8,9},{9,10},{10,11},{12,13},{... | collective-permute-start | bytes 589832 | tf_op jit(solution)/shard_map/ppermute | solution.py:169
  18.0 1.3 %collective-permute-start.3 = (bf16[3,1,256,128]{3,2,1,0:T(8,128)(2,1)S(1)}, bf16[3,1,256,128]{3,2,1,0:T(8,128)(2,1)S(1)}, u32[]{:S(2)}, u32[]{:S(2)}) collective-permute-start(bf16[3,1,256,128]{3,2,1,0:T(8,128)(2,1)S(1)} %get-tuple-element.33), channel_id=1, source_target_pairs={{1,0},{2,1},{3,2},{5,4},{6,5},{7,6},{9,8},{10,9},{11,10},{13,12},{... | collective-permute-start | bytes 589832 | tf_op jit(solution)/shard_map/ppermute | solution.py:170
  19.3 1.2 %fusion.6.sel_ref = bf16[16,128,128]{2,1,0:T(8,128)(2,1)} fusion(s32[16,128]{1,0:T(8,128)S(1)} %broadcast_add_fusion), kind=kLoop, calls=%fused_computation.13 | loop fusion | flops 524288 | bytes 532480 | tf_op jit(solution)/shard_map/convert_element_type | solution.py:103
  20.5 2.4 %collective-permute-done.3 = bf16[3,1,256,128]{3,2,1,0:T(8,128)(2,1)S(1)} collective-permute-done((bf16[3,1,256,128]{3,2,1,0:T(8,128)(2,1)S(1)}, bf16[3,1,256,128]{3,2,1,0:T(8,128)(2,1)S(1)}, u32[]{:S(2)}, u32[]{:S(2)}) %collective-permute-start.3) | collective-permute-done | bytes 196640 | tf_op jit(solution)/shard_map/ppermute | solution.py:170
  22.9 1.0 pad_maximum_fusion.ext_ref.act_ref
  23.9 5.3 %shard_map.92 = f32[2,256,128]{2,1,0:T(8,128)} custom-call(bf16[3,4,256,128]{3,2,1,0:T(8,128)(2,1)} %pad_maximum_fusion.ext_ref.act_ref, bf16[9,768,256]{2,1,0:T(8,128)(2,1)} %bitcast.88), custom_call_target="tpu_custom_call" | custom-call | flops 905969664 | bytes 4587520 | tf_op jit(solution)/shard_map/pallas_call | solution.py:47
  29.3 1.1 %fusion.16 = bf16[256,2,128]{2,0,1:T(8,128)(2,1)S(1)} fusion(f32[2,256,128]{2,1,0:T(8,128)} %shard_map.92), kind=kLoop, calls=%fused_computation.52 | loop fusion | flops 393216 | bytes 393216 | tf_op jit(solution)/shard_map/transpose | solution.py:209
  30.5 0.3 fusion.14
  30.8 0.2 fusion.5
  31.2 0.8 fusion.10.delta_ref
  31.9 4.5 %collective-permute-start.4 = (bf16[1,2,256,128]{3,2,1,0:T(8,128)(2,1)}, bf16[1,2,256,128]{3,2,1,0:T(8,128)(2,1)S(1)}, u32[]{:S(2)}, u32[]{:S(2)}) collective-permute-start(bf16[1,2,256,128]{3,2,1,0:T(8,128)(2,1)} %bitcast.16), channel_id=1, source_target_pairs={{0,4},{4,8},{8,12},{1,5},{5,9},{9,13},{2,6},{6,10},{10,14},{3,7},{... | collective-permute-start | bytes 393224 | tf_op jit(solution)/shard_map/ppermute | solution.py:169
  36.5 1.3 %collective-permute-start.5 = (bf16[1,2,256,128]{3,2,1,0:T(8,128)(2,1)}, bf16[1,2,256,128]{3,2,1,0:T(8,128)(2,1)S(1)}, u32[]{:S(2)}, u32[]{:S(2)}) collective-permute-start(bf16[1,2,256,128]{3,2,1,0:T(8,128)(2,1)} %bitcast.16), channel_id=1, source_target_pairs={{4,0},{8,4},{12,8},{5,1},{9,5},{13,9},{6,2},{10,6},{14,10},{7,3},{... | collective-permute-start | bytes 393224 | tf_op jit(solution)/shard_map/ppermute | solution.py:170
  37.8 4.6 %shard_map.94 = f32[2,256,128]{2,1,0:T(8,128)} custom-call(bf16[3,4,256,128]{3,2,1,0:T(8,128)(2,1)} %pad_maximum_fusion.ext_ref.act_ref, bf16[2,256,128]{2,1,0:T(8,128)(2,1)} %fusion.10.delta_ref, f32[256,256]{1,0:T(8,128)} %copy-done.1, bf16[16,128,128]{2,1,0:T(8,128)(2,1)} %fusion.6.sel_ref), custom_call_target="tpu_custom_call" | custom-call | flops 1358954496 | bytes 1179648 | tf_op jit(solution)/shard_map/pallas_call | solution.py:104
  42.3 1.1 %copy.85 = f32[256,2,128]{0,2,1:T(8,128)S(1)} copy(f32[256,2,128]{2,0,1:T(8,128)} %bitcast.111) | data formatting | bytes 524288 | tf_op jit(solution)/shard_map/transpose | solution.py:115
  44.7 0.2 fusion.35
  44.9 1.0 pad_maximum_fusion.3
  45.9 5.8 %collective-permute-start.6 = (bf16[3,1,256,128]{3,2,1,0:T(8,128)(2,1)S(1)}, bf16[3,1,256,128]{3,2,1,0:T(8,128)(2,1)S(1)}, u32[]{:S(2)}, u32[]{:S(2)}) collective-permute-start(bf16[3,1,256,128]{3,2,1,0:T(8,128)(2,1)S(1)} %get-tuple-element.30), channel_id=1, source_target_pairs={{0,1},{1,2},{2,3},{4,5},{5,6},{6,7},{8,9},{9,10},{10,11},{12,13},{... | collective-permute-start | bytes 589832 | tf_op jit(solution)/shard_map/ppermute | solution.py:169
  51.7 1.5 %collective-permute-start.7 = (bf16[3,1,256,128]{3,2,1,0:T(8,128)(2,1)S(1)}, bf16[3,1,256,128]{3,2,1,0:T(8,128)(2,1)S(1)}, u32[]{:S(2)}, u32[]{:S(2)}) collective-permute-start(bf16[3,1,256,128]{3,2,1,0:T(8,128)(2,1)S(1)} %get-tuple-element.31), channel_id=1, source_target_pairs={{1,0},{2,1},{3,2},{5,4},{6,5},{7,6},{9,8},{10,9},{11,10},{13,12},{... | collective-permute-start | bytes 589832 | tf_op jit(solution)/shard_map/ppermute | solution.py:170
  53.4 1.6 %collective-permute-done.7 = bf16[3,1,256,128]{3,2,1,0:T(8,128)(2,1)S(1)} collective-permute-done((bf16[3,1,256,128]{3,2,1,0:T(8,128)(2,1)S(1)}, bf16[3,1,256,128]{3,2,1,0:T(8,128)(2,1)S(1)}, u32[]{:S(2)}, u32[]{:S(2)}) %collective-permute-start.7) | collective-permute-done | bytes 196640 | tf_op jit(solution)/shard_map/ppermute | solution.py:170
  55.0 1.9 %pad_maximum_fusion.1.ext_ref = bf16[3,4,256,128]{3,2,1,0:T(8,128)(2,1)} fusion(bf16[3,1,256,128]{3,2,1,0:T(8,128)(2,1)S(1)} %collective-permute-done.7, bf16[1,2,256,128]{3,2,1,0:T(8,128)(2,1)S(1)} %collective-permute-done.5, bf16[1,2,256,128]{3,2,1,0:T(8,128)(2,1)} %bitcast.16, bf16[1,2,256,128]{3,2,1,0:T(8,128)(2,1)S(1)} %collective-permute-done.4, ...), kind=kLoop, calls=%fused_computation.15 | loop fusion | flops 1572864 | bytes 1572864 | tf_op jit(solution)/shard_map/concatenate | solution.py:171
  56.9 5.3 %shard_map.93 = f32[2,256,128]{2,1,0:T(8,128)} custom-call(bf16[3,4,256,128]{3,2,1,0:T(8,128)(2,1)} %pad_maximum_fusion.1.ext_ref, bf16[9,768,256]{2,1,0:T(8,128)(2,1)} %bitcast.87), custom_call_target="tpu_custom_call" | custom-call | flops 905969664 | bytes 4587520 | tf_op jit(solution)/shard_map/pallas_call | solution.py:47
  62.3 1.0 convert_bitcast_fusion
  64.0 3.8 %collective-permute-start.8 = (f32[93184]{0:T(1024)S(1)}, f32[93184]{0:T(1024)S(1)}, u32[]{:S(2)}, u32[]{:S(2)}) collective-permute-start(f32[93184]{0:T(1024)S(1)} %pad_maximum_fusion.4), channel_id=1, source_target_pairs={{0,1},{1,0},{2,3},{3,2},{4,5},{5,4},{6,7},{7,6},{8,9},{9,8},{10,11... | collective-permute-start | bytes 1118216 | tf_op jit(solution)/shard_map/ppermute | solution.py:139
  68.3 0.9 collective-permute-done.8
  69.4 6.9 %collective-permute-done.9 = f32[46592]{0:T(1024)S(1)} collective-permute-done((f32[46592]{0:T(1024)S(1)}, f32[46592]{0:T(1024)S(1)}, u32[]{:S(2)}, u32[]{:S(2)}) %collective-permute-start.9) | collective-permute-done | bytes 186400 | tf_op jit(solution)/shard_map/ppermute | solution.py:139
  76.4 2.7 %collective-permute-start.10 = (f32[23296]{0:T(1024)S(1)}, f32[23296]{0:T(1024)S(1)}, u32[]{:S(2)}, u32[]{:S(2)}) collective-permute-start(f32[23296]{0:T(1024)S(1)} %pad_maximum_fusion.8), channel_id=1, source_target_pairs={{0,4},{4,0},{8,12},{12,8},{1,5},{5,1},{9,13},{13,9},{2,6},{6,2},{1... | collective-permute-start | bytes 279560 | tf_op jit(solution)/shard_map/ppermute | solution.py:139
  79.1 0.8 copy.99
  79.9 1.8 %collective-permute-done.10 = f32[23296]{0:T(1024)S(1)} collective-permute-done((f32[23296]{0:T(1024)S(1)}, f32[23296]{0:T(1024)S(1)}, u32[]{:S(2)}, u32[]{:S(2)}) %collective-permute-start.10) | collective-permute-done | bytes 93216 | tf_op jit(solution)/shard_map/ppermute | solution.py:139
  81.8 3.1 %collective-permute-start.11 = (f32[11648]{0:T(1024)S(1)}, f32[11648]{0:T(1024)S(1)}, u32[]{:S(2)}, u32[]{:S(2)}) collective-permute-start(f32[11648]{0:T(1024)S(1)} %pad_maximum_fusion.12), channel_id=1, source_target_pairs={{0,8},{4,12},{8,0},{12,4},{1,9},{5,13},{9,1},{13,5},{2,10},{6,14},... | collective-permute-start | bytes 139784 | tf_op jit(solution)/shard_map/ppermute | solution.py:139
  84.9 0.2 fusion.3
  85.1 0.8 copy.100
  85.9 1.1 collective-permute-done.11
  87.0 3.0 %collective-permute-start.12 = (f32[8192]{0:T(1024)S(1)}, f32[8192]{0:T(1024)S(1)}, u32[]{:S(2)}, u32[]{:S(2)}) collective-permute-start(f32[8192]{0:T(1024)S(1)} %pad_maximum_fusion.14), channel_id=1, source_target_pairs={{0,8},{4,12},{8,0},{12,4},{1,9},{5,13},{9,1},{13,5},{2,10},{6,14},... | collective-permute-start | bytes 98312 | tf_op jit(solution)/shard_map/ppermute | solution.py:149
  90.3 1.7 %collective-permute-done.12 = f32[8192]{0:T(1024)S(1)} collective-permute-done((f32[8192]{0:T(1024)S(1)}, f32[8192]{0:T(1024)S(1)}, u32[]{:S(2)}, u32[]{:S(2)}) %collective-permute-start.12) | collective-permute-done | bytes 32800 | tf_op jit(solution)/shard_map/ppermute | solution.py:149
  92.1 1.9 %collective-permute-start.13 = (f32[16384]{0:T(1024)S(1)}, f32[16384]{0:T(1024)S(1)}, u32[]{:S(2)}, u32[]{:S(2)}) collective-permute-start(f32[16384]{0:T(1024)S(1)} %pad_maximum_fusion.10), channel_id=1, source_target_pairs={{0,4},{4,0},{8,12},{12,8},{1,5},{5,1},{9,13},{13,9},{2,6},{6,2},{1... | collective-permute-start | bytes 196616 | tf_op jit(solution)/shard_map/ppermute | solution.py:149
  94.0 2.4 %collective-permute-done.13 = f32[16384]{0:T(1024)S(1)} collective-permute-done((f32[16384]{0:T(1024)S(1)}, f32[16384]{0:T(1024)S(1)}, u32[]{:S(2)}, u32[]{:S(2)}) %collective-permute-start.13) | collective-permute-done | bytes 65568 | tf_op jit(solution)/shard_map/ppermute | solution.py:149
  96.5 0.3 collective-permute-start.14
  96.9 4.8 %collective-permute-done.14 = f32[36224]{0:T(1024)S(1)} collective-permute-done((f32[36224]{0:T(1024)S(1)}, f32[36224]{0:T(1024)S(1)}, u32[]{:S(2)}, u32[]{:S(2)}) %collective-permute-start.14) | collective-permute-done | bytes 144928 | tf_op jit(solution)/shard_map/ppermute | solution.py:149
  102.4 1.4 %collective-permute-done.15 = f32[72448]{0:T(1024)S(1)} collective-permute-done((f32[72448]{0:T(1024)S(1)}, f32[72448]{0:T(1024)S(1)}, u32[]{:S(2)}, u32[]{:S(2)}) %collective-permute-start.15) | collective-permute-done | bytes 289824 | tf_op jit(solution)/shard_map/ppermute | solution.py:149
  104.0 0.3 copy.97
  104.4 0.8 fusion.17
  105.2 0.8 fusion.7
  (121 shorter events, 5.0 us)
Async XLA Ops:
  0.6 29.9 %copy-start = (bf16[256,256]{1,0:T(8,128)(2,1)S(1)}, bf16[256,256]{1,0:T(8,128)(2,1)}, u32[]{:S(2)}) copy-start(bf16[256,256]{1,0:T(8,128)(2,1)} %param.9) | copy-start | bytes 393220
  0.6 12.7 %copy-start.3 = (bf16[256,8,3,3,3]{0,1,4,3,2:T(8,128)(2,1)S(1)}, bf16[256,8,3,3,3]{0,1,4,3,2:T(8,128)(2,1)}, u32[]{:S(2)}) copy-start(bf16[256,8,3,3,3]{0,1,4,3,2:T(8,128)(2,1)} %param.8) | copy-start | bytes 331780
  3.0 13.5 %collective-permute-start = (bf16[1,2,256,128]{3,2,1,0:T(8,128)(2,1)S(1)}, bf16[1,2,256,128]{3,2,1,0:T(8,128)(2,1)S(1)}, u32[]{:S(2)}, u32[]{:S(2)}) collective-permute-start(bf16[1,2,256,128]{3,2,1,0:T(8,128)(2,1)S(1)} %bitcast.90), channel_id=1, source_target_pairs={{0,4},{4,8},{8,12},{1,5},{5,9},{9,13},{2,6},{6,10},{10,14},{3,7},{... | collective-permute-start | bytes 393224 | tf_op jit(solution)/shard_map/ppermute | solution.py:169
  7.9 8.5 %collective-permute-start.1 = (bf16[1,2,256,128]{3,2,1,0:T(8,128)(2,1)S(1)}, bf16[1,2,256,128]{3,2,1,0:T(8,128)(2,1)S(1)}, u32[]{:S(2)}, u32[]{:S(2)}) collective-permute-start(bf16[1,2,256,128]{3,2,1,0:T(8,128)(2,1)S(1)} %bitcast.91), channel_id=1, source_target_pairs={{4,0},{8,4},{12,8},{5,1},{9,5},{13,9},{6,2},{10,6},{14,10},{7,3},{... | collective-permute-start | bytes 393224 | tf_op jit(solution)/shard_map/ppermute | solution.py:170
  9.4 6.9 %copy-start.1 = (f32[256,256]{1,0:T(8,128)}, f32[256,256]{1,0:T(8,128)S(1)}, u32[]{:S(2)}) copy-start(f32[256,256]{1,0:T(8,128)S(1)} %compare_convert_fusion.mask_ref) | copy-start | bytes 786436
  9.4 6.9 %copy-start.4 = (bf16[256,1,2,128]{3,2,1,0:T(2,128)(2,1)S(1)}, bf16[256,1,2,128]{3,2,1,0:T(2,128)(2,1)}, u32[]{:S(2)}) copy-start(bf16[256,1,2,128]{3,2,1,0:T(2,128)(2,1)} %param.6) | copy-start | bytes 393220
  16.6 4.0 %collective-permute-start.2 = (bf16[3,1,256,128]{3,2,1,0:T(8,128)(2,1)S(1)}, bf16[3,1,256,128]{3,2,1,0:T(8,128)(2,1)S(1)}, u32[]{:S(2)}, u32[]{:S(2)}) collective-permute-start(bf16[3,1,256,128]{3,2,1,0:T(8,128)(2,1)S(1)} %get-tuple-element.32), channel_id=1, source_target_pairs={{0,1},{1,2},{2,3},{4,5},{5,6},{6,7},{8,9},{9,10},{10,11},{12,13},{... | collective-permute-start | bytes 589832 | tf_op jit(solution)/shard_map/ppermute | solution.py:169
  18.0 4.9 %collective-permute-start.3 = (bf16[3,1,256,128]{3,2,1,0:T(8,128)(2,1)S(1)}, bf16[3,1,256,128]{3,2,1,0:T(8,128)(2,1)S(1)}, u32[]{:S(2)}, u32[]{:S(2)}) collective-permute-start(bf16[3,1,256,128]{3,2,1,0:T(8,128)(2,1)S(1)} %get-tuple-element.33), channel_id=1, source_target_pairs={{1,0},{2,1},{3,2},{5,4},{6,5},{7,6},{9,8},{10,9},{11,10},{13,12},{... | collective-permute-start | bytes 589832 | tf_op jit(solution)/shard_map/ppermute | solution.py:170
  29.3 1.9 %copy-start.2 = (f32[2,256,128]{2,1,0:T(8,128)S(1)}, f32[2,256,128]{2,1,0:T(8,128)}, u32[]{:S(2)}) copy-start(f32[2,256,128]{2,1,0:T(8,128)} %shard_map.92) | copy-start | bytes 786436
  31.9 13.0 %collective-permute-start.4 = (bf16[1,2,256,128]{3,2,1,0:T(8,128)(2,1)}, bf16[1,2,256,128]{3,2,1,0:T(8,128)(2,1)S(1)}, u32[]{:S(2)}, u32[]{:S(2)}) collective-permute-start(bf16[1,2,256,128]{3,2,1,0:T(8,128)(2,1)} %bitcast.16), channel_id=1, source_target_pairs={{0,4},{4,8},{8,12},{1,5},{5,9},{9,13},{2,6},{6,10},{10,14},{3,7},{... | collective-permute-start | bytes 393224 | tf_op jit(solution)/shard_map/ppermute | solution.py:169
  36.5 8.4 %collective-permute-start.5 = (bf16[1,2,256,128]{3,2,1,0:T(8,128)(2,1)}, bf16[1,2,256,128]{3,2,1,0:T(8,128)(2,1)S(1)}, u32[]{:S(2)}, u32[]{:S(2)}) collective-permute-start(bf16[1,2,256,128]{3,2,1,0:T(8,128)(2,1)} %bitcast.16), channel_id=1, source_target_pairs={{4,0},{8,4},{12,8},{5,1},{9,5},{13,9},{6,2},{10,6},{14,10},{7,3},{... | collective-permute-start | bytes 393224 | tf_op jit(solution)/shard_map/ppermute | solution.py:170
  45.9 7.5 %collective-permute-start.6 = (bf16[3,1,256,128]{3,2,1,0:T(8,128)(2,1)S(1)}, bf16[3,1,256,128]{3,2,1,0:T(8,128)(2,1)S(1)}, u32[]{:S(2)}, u32[]{:S(2)}) collective-permute-start(bf16[3,1,256,128]{3,2,1,0:T(8,128)(2,1)S(1)} %get-tuple-element.30), channel_id=1, source_target_pairs={{0,1},{1,2},{2,3},{4,5},{5,6},{6,7},{8,9},{9,10},{10,11},{12,13},{... | collective-permute-start | bytes 589832 | tf_op jit(solution)/shard_map/ppermute | solution.py:169
  51.7 3.3 %collective-permute-start.7 = (bf16[3,1,256,128]{3,2,1,0:T(8,128)(2,1)S(1)}, bf16[3,1,256,128]{3,2,1,0:T(8,128)(2,1)S(1)}, u32[]{:S(2)}, u32[]{:S(2)}) collective-permute-start(bf16[3,1,256,128]{3,2,1,0:T(8,128)(2,1)S(1)} %get-tuple-element.31), channel_id=1, source_target_pairs={{1,0},{2,1},{3,2},{5,4},{6,5},{7,6},{9,8},{10,9},{11,10},{13,12},{... | collective-permute-start | bytes 589832 | tf_op jit(solution)/shard_map/ppermute | solution.py:170
  63.7 21.1 %copy-start.5 = (bf16[256,256]{1,0:T(8,128)(2,1)S(1)}, bf16[256,256]{1,0:T(8,128)(2,1)}, u32[]{:S(2)}) copy-start(bf16[256,256]{1,0:T(8,128)(2,1)} %param.7) | copy-start | bytes 393220
  64.0 5.2 %collective-permute-start.8 = (f32[93184]{0:T(1024)S(1)}, f32[93184]{0:T(1024)S(1)}, u32[]{:S(2)}, u32[]{:S(2)}) collective-permute-start(f32[93184]{0:T(1024)S(1)} %pad_maximum_fusion.4), channel_id=1, source_target_pairs={{0,1},{1,0},{2,3},{3,2},{4,5},{5,4},{6,7},{7,6},{8,9},{9,8},{10,11... | collective-permute-start | bytes 1118216 | tf_op jit(solution)/shard_map/ppermute | solution.py:139
  69.3 7.1 %collective-permute-start.9 = (f32[46592]{0:T(1024)S(1)}, f32[46592]{0:T(1024)S(1)}, u32[]{:S(2)}, u32[]{:S(2)}) collective-permute-start(f32[46592]{0:T(1024)S(1)} %pad_maximum_fusion.6), channel_id=1, source_target_pairs={{0,2},{1,3},{2,0},{3,1},{4,6},{5,7},{6,4},{7,5},{8,10},{9,11},{10,... | collective-permute-start | bytes 559112 | tf_op jit(solution)/shard_map/ppermute | solution.py:139
  76.4 5.3 %collective-permute-start.10 = (f32[23296]{0:T(1024)S(1)}, f32[23296]{0:T(1024)S(1)}, u32[]{:S(2)}, u32[]{:S(2)}) collective-permute-start(f32[23296]{0:T(1024)S(1)} %pad_maximum_fusion.8), channel_id=1, source_target_pairs={{0,4},{4,0},{8,12},{12,8},{1,5},{5,1},{9,13},{13,9},{2,6},{6,2},{1... | collective-permute-start | bytes 279560 | tf_op jit(solution)/shard_map/ppermute | solution.py:139
  81.8 5.2 %collective-permute-start.11 = (f32[11648]{0:T(1024)S(1)}, f32[11648]{0:T(1024)S(1)}, u32[]{:S(2)}, u32[]{:S(2)}) collective-permute-start(f32[11648]{0:T(1024)S(1)} %pad_maximum_fusion.12), channel_id=1, source_target_pairs={{0,8},{4,12},{8,0},{12,4},{1,9},{5,13},{9,1},{13,5},{2,10},{6,14},... | collective-permute-start | bytes 139784 | tf_op jit(solution)/shard_map/ppermute | solution.py:139
  87.0 5.0 %collective-permute-start.12 = (f32[8192]{0:T(1024)S(1)}, f32[8192]{0:T(1024)S(1)}, u32[]{:S(2)}, u32[]{:S(2)}) collective-permute-start(f32[8192]{0:T(1024)S(1)} %pad_maximum_fusion.14), channel_id=1, source_target_pairs={{0,8},{4,12},{8,0},{12,4},{1,9},{5,13},{9,1},{13,5},{2,10},{6,14},... | collective-permute-start | bytes 98312 | tf_op jit(solution)/shard_map/ppermute | solution.py:149
  92.1 4.3 %collective-permute-start.13 = (f32[16384]{0:T(1024)S(1)}, f32[16384]{0:T(1024)S(1)}, u32[]{:S(2)}, u32[]{:S(2)}) collective-permute-start(f32[16384]{0:T(1024)S(1)} %pad_maximum_fusion.10), channel_id=1, source_target_pairs={{0,4},{4,0},{8,12},{12,8},{1,5},{5,1},{9,13},{13,9},{2,6},{6,2},{1... | collective-permute-start | bytes 196616 | tf_op jit(solution)/shard_map/ppermute | solution.py:149
  96.5 5.2 %collective-permute-start.14 = (f32[36224]{0:T(1024)S(1)}, f32[36224]{0:T(1024)S(1)}, u32[]{:S(2)}, u32[]{:S(2)}) collective-permute-start(f32[36224]{0:T(1024)S(1)} %pad_maximum_fusion.7), channel_id=1, source_target_pairs={{0,2},{1,3},{2,0},{3,1},{4,6},{5,7},{6,4},{7,5},{8,10},{9,11},{10,... | collective-permute-start | bytes 434696 | tf_op jit(solution)/shard_map/ppermute | solution.py:149
  102.2 1.6 %collective-permute-start.15 = (f32[72448]{0:T(1024)S(1)}, f32[72448]{0:T(1024)S(1)}, u32[]{:S(2)}, u32[]{:S(2)}) collective-permute-start(f32[72448]{0:T(1024)S(1)} %pad_maximum_fusion.5), channel_id=1, source_target_pairs={{0,1},{1,0},{2,3},{3,2},{4,5},{5,4},{6,7},{7,6},{8,9},{9,8},{10,11... | collective-permute-start | bytes 869384 | tf_op jit(solution)/shard_map/ppermute | solution.py:149

commit v9 on v8

--- a/solution.py
+++ b/solution.py
@@ -21,17 +21,16 @@
     return jnp.where(lane == edge, jnp.zeros_like(rolled), rolled)
 
 
-def conv_body(ext_ref, w_hbm, out_ref, w_vmem, sems):
+def conv_body(ext_ref, w_ref, out_ref):
     height, channels = out_ref.shape[0], out_ref.shape[1]
-    copies = [pltpu.make_async_copy(w_hbm.at[k], w_vmem.at[k], sems.at[k]) for k in range(9)]
-    for copy in copies:
-        copy.start()
-    parts = None
-    for dz, dy in itertools.product(range(3), repeat=2):
-        rows = jnp.concatenate([ext_ref[dz, dy + y] for y in range(height)], axis=1)
-        copies[dz * 3 + dy].wait()
-        product = jnp.dot(w_vmem[dz * 3 + dy], rows, preferred_element_type=jnp.float32)
-        parts = product if parts is None else parts + product
+    rows = jnp.concatenate(
+        [
+            jnp.concatenate([ext_ref[dz, dy + y] for y in range(height)], axis=1)
+            for dz, dy in itertools.product(range(3), repeat=2)
+        ],
+        axis=0,
+    )
+    parts = jnp.dot(w_ref[...], rows, preferred_element_type=jnp.float32)
     for y in range(height):
         lanes = slice(y * LANES, (y + 1) * LANES)
         out_ref[y] = (
@@ -47,9 +46,8 @@
     return pl.pallas_call(
         conv_body,
         out_shape=jax.ShapeDtypeStruct((height, channels, width), jnp.float32),
-        in_specs=[pl.BlockSpec(memory_space=pltpu.VMEM), pl.BlockSpec(memory_space=pl.ANY)],
+        in_specs=[pl.BlockSpec(memory_space=pltpu.VMEM)] * 2,
         out_specs=pl.BlockSpec(memory_space=pltpu.VMEM),
-        scratch_shapes=[pltpu.VMEM(weights.shape, weights.dtype), pltpu.SemaphoreType.DMA((9,))],
         cost_estimate=pl.CostEstimate(
             flops=2 * 27 * channels * channels * height * width,
             transcendentals=0,
@@ -182,11 +180,13 @@
     group_of = jnp.arange(channels) // GW
     mask = (group_of[:, None] == group_of[None, :]).astype(jnp.float32)
     spread = (jnp.arange(GW)[:, None] == jnp.arange(channels)[None, :] % GW).astype(jnp.float32)
-    compact = group_weight.reshape(channels, GW, 27).astype(jnp.float32)
-    forward = jnp.einsum("ojt,ji->toi", compact, spread)
-    backward = jnp.einsum("ji,ojt->tio", spread, compact[:, :, ::-1])
-    forward = (forward * mask).astype(group_weight.dtype).reshape(9, 3 * channels, channels)
-    backward = (backward * mask).astype(group_weight.dtype).reshape(9, 3 * channels, channels)
+    compact = group_weight.reshape(channels, GW, 9, 3).astype(jnp.float32)
+    flipped = group_weight.reshape(channels, GW, 27)[:, :, ::-1].reshape(channels, GW, 9, 3)
+    forward = jnp.einsum("ojkd,ji->doki", compact, spread)
+    backward = jnp.einsum("ji,ojkd->diko", spread, flipped.astype(jnp.float32))
+    mask4 = mask[None, :, None, :]
+    forward = (forward * mask4).astype(group_weight.dtype).reshape(3 * channels, 9 * channels)
+    backward = (backward * mask4).astype(group_weight.dtype).reshape(3 * channels, 9 * channels)
     return forward, backward
 
 

time: 107 us -> 125 us (1.17)
  local copies, waits for them, and re-layouts: 7.39 us -> 29.1 us
  Pallas kernels: 15.2 us -> 12.8 us
  matrix products: 9.14 us -> 7.31 us
    unnamed x19, local copies, waits for them, and re-layouts: 2.94 us -> 14.1 us
    reshape x0 -> x2, local copies, waits for them, and re-layouts: none -> 10.4 us  [the longest x1 8.01 us: conv_weights(): (forward * mask4).astype(group_weight.dtype)]
    pallas_call x2, Pallas kernels: 10.6 us -> 8.23 us  [conv_call(): pl.pallas_call(conv_body, out_shape=jax.ShapeDtypeStruct((height, channel...]
    dot_general x2, matrix products: 6.83 us -> 5.01 us  [the longest x1 3.87 us: conv_weights(): forward = jnp.einsum('ojkd,ji->doki', compact, spread)]
  transfers between devices with their start and end apart: 16 -> 16, of which waited for: 10 -> 10; matrix products, arithmetic and copies ran while one was open for 13% -> 27% of each run, Pallas kernels for 4% -> 4%
where the time goes in v9:
time: 125 us; the launch traced here: 124 us
  starting transfers between devices  37.2 us (30%)
  local copies, waits for them, and re-layouts  29.1 us (23%)
  waiting for transfers between devices  25 us (20%)
  Pallas kernels  12.8 us (10%)
  other arithmetic  11.3 us (9%)
  matrix products  7.31 us (6%)
  between operations  1.5 us (1%)
    ppermute x4, starting transfers between devices, halo(): lax.ppermute(lax.slice_in_dim(block, size - 1, size, axis=dim), axis, up)  16.7 us
    unnamed x19, local copies, waits for them, and re-layouts  14.1 us
    ppermute x4, waiting for transfers between devices, tree_sum(): got = lax.ppermute(jnp.concatenate(sends), axis, pairs)  10.6 us
    ppermute x4, waiting for transfers between devices, tree_sum(): lax.ppermute(jnp.concatenate([pieces[n] for n in members]), axis, pairs)  10.3 us
    ppermute x4, starting transfers between devices, tree_sum(): got = lax.ppermute(jnp.concatenate(sends), axis, pairs)  9.78 us
    pallas_call x2, Pallas kernels, conv_call(): pl.pallas_call(conv_body, out_shape=jax.ShapeDtypeStruct((height, channel...  8.23 us
    reshape x1, local copies, waits for them, and re-layouts, conv_weights(): (forward * mask4).astype(group_weight.dtype)  8.01 us
    ppermute x4, starting transfers between devices, tree_sum(): lax.ppermute(jnp.concatenate([pieces[n] for n in members]), axis, pairs)  5.35 us
  transfers between devices with their start and end apart: 16, of which 10 were waited for; matrix products, arithmetic and copies ran while one was open for 27% of the time, Pallas kernels for 4%

profile of v9, /device:TPU:0, one launch (start us, length us, event | category | flops | bytes accessed | tf_op | source)
XLA Modules:
  0.0 124.2 jit_solution(1815937011174446134)
XLA Ops:
  0.6 1.0 copy.92
  1.7 1.1 reduce-precision_convert_fusion.2
  3.0 4.9 %collective-permute-start = (bf16[1,2,256,128]{3,2,1,0:T(8,128)(2,1)S(1)}, bf16[1,2,256,128]{3,2,1,0:T(8,128)(2,1)S(1)}, u32[]{:S(2)}, u32[]{:S(2)}) collective-permute-start(bf16[1,2,256,128]{3,2,1,0:T(8,128)(2,1)S(1)} %bitcast.101), channel_id=1, source_target_pairs={{0,4},{4,8},{8,12},{1,5},{5,9},{9,13},{2,6},{6,10},{10,14},{3,7},{... | collective-permute-start | bytes 393224 | tf_op jit(solution)/shard_map/ppermute | solution.py:167
  7.9 1.3 %collective-permute-start.1 = (bf16[1,2,256,128]{3,2,1,0:T(8,128)(2,1)S(1)}, bf16[1,2,256,128]{3,2,1,0:T(8,128)(2,1)S(1)}, u32[]{:S(2)}, u32[]{:S(2)}) collective-permute-start(bf16[1,2,256,128]{3,2,1,0:T(8,128)(2,1)S(1)} %bitcast.102), channel_id=1, source_target_pairs={{4,0},{8,4},{12,8},{5,1},{9,5},{13,9},{6,2},{10,6},{14,10},{7,3},{... | collective-permute-start | bytes 393224 | tf_op jit(solution)/shard_map/ppermute | solution.py:168
  9.5 3.9 %fusion = bf16[3,256,9,256]{1,3,0,2:T(8,128)(2,1)} fusion(f32[256,256]{0,1:T(8,128)S(1)} %copy.94, bf16[256,8,9,3]{0,1,3,2:T(8,128)(2,1)} %bitcast.120, s32[256]{0:T(256)S(1)} %and_select_fusion.2), kind=kOutput, calls=%fused_computation.1 | convolution fusion | flops 31852544 | bytes 3912704 | tf_op jit(solution)/shard_map/ojkd,ji->doki/dot_general | solution.py:185
  13.4 8.0 %copy.126 = bf16[3,256,9,256]{3,2,1,0:T(8,128)(2,1)} copy(bf16[3,256,9,256]{1,3,0,2:T(8,128)(2,1)} %fusion) | data formatting | bytes 7077888 | tf_op jit(solution)/shard_map/reshape | solution.py:188
  21.4 7.0 %copy.130 = bf16[96,8,9,256]{3,1,2,0:T(8,128)(2,1)} copy(bf16[96,8,9,256]{3,2,1,0:T(8,128)(2,1)} %bitcast.96) | data formatting | bytes 7077888
  28.6 1.1 fusion.1
  29.7 2.4 %copy.127 = bf16[3,256,9,256]{3,2,1,0:T(8,128)(2,1)S(1)} copy(bf16[3,256,9,256]{3,1,0,2:T(8,128)(2,1)S(1)} %fusion.1) | data formatting | bytes 7077888 | tf_op jit(solution)/shard_map/reshape | solution.py:189
  32.1 4.2 %copy.131 = bf16[96,8,9,256]{3,1,2,0:T(8,128)(2,1)} copy(bf16[96,8,9,256]{3,2,1,0:T(8,128)(2,1)S(1)} %bitcast.97) | data formatting | bytes 7077888
  36.4 1.5 %collective-permute-start.2 = (bf16[3,1,256,128]{3,2,1,0:T(8,128)(2,1)S(1)}, bf16[3,1,256,128]{3,2,1,0:T(8,128)(2,1)S(1)}, u32[]{:S(2)}, u32[]{:S(2)}) collective-permute-start(bf16[3,1,256,128]{3,2,1,0:T(8,128)(2,1)S(1)} %get-tuple-element.32), channel_id=1, source_target_pairs={{0,1},{1,2},{2,3},{4,5},{5,6},{6,7},{8,9},{9,10},{10,11},{12,13},{... | collective-permute-start | bytes 589832 | tf_op jit(solution)/shard_map/ppermute | solution.py:167
  37.9 1.5 %collective-permute-start.3 = (bf16[3,1,256,128]{3,2,1,0:T(8,128)(2,1)S(1)}, bf16[3,1,256,128]{3,2,1,0:T(8,128)(2,1)S(1)}, u32[]{:S(2)}, u32[]{:S(2)}) collective-permute-start(bf16[3,1,256,128]{3,2,1,0:T(8,128)(2,1)S(1)} %get-tuple-element.33), channel_id=1, source_target_pairs={{1,0},{2,1},{3,2},{5,4},{6,5},{7,6},{9,8},{10,9},{11,10},{13,12},{... | collective-permute-start | bytes 589832 | tf_op jit(solution)/shard_map/ppermute | solution.py:168
  39.4 1.1 fusion.7.sel_ref
  40.5 2.3 %collective-permute-done.3 = bf16[3,1,256,128]{3,2,1,0:T(8,128)(2,1)S(1)} collective-permute-done((bf16[3,1,256,128]{3,2,1,0:T(8,128)(2,1)S(1)}, bf16[3,1,256,128]{3,2,1,0:T(8,128)(2,1)S(1)}, u32[]{:S(2)}, u32[]{:S(2)}) %collective-permute-start.3) | collective-permute-done | bytes 196640 | tf_op jit(solution)/shard_map/ppermute | solution.py:168
  42.8 1.0 pad_maximum_fusion.ext_ref.act_ref
  43.8 4.1 %shard_map.92 = f32[2,256,128]{2,1,0:T(8,128)} custom-call(bf16[3,4,256,128]{3,2,1,0:T(8,128)(2,1)} %pad_maximum_fusion.ext_ref.act_ref, bf16[768,2304]{1,0:T(8,128)(2,1)} %bitcast.99), custom_call_target="tpu_custom_call" | custom-call | flops 905969664 | bytes 4587520 | tf_op jit(solution)/shard_map/pallas_call | solution.py:46
  47.9 1.0 fusion.16
  49.0 0.3 fusion.15
  49.7 1.7 %fusion.11.delta_ref = bf16[2,256,128]{2,1,0:T(8,128)(2,1)} fusion(f32[256,1,2,128]{3,0,2,1:T(8,128)S(1)} %copy.99, f32[2,256,128]{2,1,0:T(8,128)} %shard_map.92), kind=kLoop, calls=%fused_computation.27 | loop fusion | flops 655360 | bytes 655360 | tf_op jit(solution)/shard_map/convert_element_type | solution.py:194
  51.4 4.5 %collective-permute-start.4 = (bf16[1,2,256,128]{3,2,1,0:T(8,128)(2,1)}, bf16[1,2,256,128]{3,2,1,0:T(8,128)(2,1)S(1)}, u32[]{:S(2)}, u32[]{:S(2)}) collective-permute-start(bf16[1,2,256,128]{3,2,1,0:T(8,128)(2,1)} %bitcast.16), channel_id=1, source_target_pairs={{0,4},{4,8},{8,12},{1,5},{5,9},{9,13},{2,6},{6,10},{10,14},{3,7},{... | collective-permute-start | bytes 393224 | tf_op jit(solution)/shard_map/ppermute | solution.py:167
  56.0 1.3 %collective-permute-start.5 = (bf16[1,2,256,128]{3,2,1,0:T(8,128)(2,1)}, bf16[1,2,256,128]{3,2,1,0:T(8,128)(2,1)S(1)}, u32[]{:S(2)}, u32[]{:S(2)}) collective-permute-start(bf16[1,2,256,128]{3,2,1,0:T(8,128)(2,1)} %bitcast.16), channel_id=1, source_target_pairs={{4,0},{8,4},{12,8},{5,1},{9,5},{13,9},{6,2},{10,6},{14,10},{7,3},{... | collective-permute-start | bytes 393224 | tf_op jit(solution)/shard_map/ppermute | solution.py:168
  57.3 4.6 %shard_map.94 = f32[2,256,128]{2,1,0:T(8,128)} custom-call(bf16[3,4,256,128]{3,2,1,0:T(8,128)(2,1)} %pad_maximum_fusion.ext_ref.act_ref, bf16[2,256,128]{2,1,0:T(8,128)(2,1)} %fusion.11.delta_ref, f32[256,256]{1,0:T(8,128)} %copy-done.1, bf16[16,128,128]{2,1,0:T(8,128)(2,1)} %fusion.7.sel_ref), custom_call_target="tpu_custom_call" | custom-call | flops 1358954496 | bytes 1179648 | tf_op jit(solution)/shard_map/pallas_call | solution.py:102
  61.8 1.1 copy.108
  64.4 1.0 pad_maximum_fusion.3
  65.4 5.8 %collective-permute-start.6 = (bf16[3,1,256,128]{3,2,1,0:T(8,128)(2,1)S(1)}, bf16[3,1,256,128]{3,2,1,0:T(8,128)(2,1)S(1)}, u32[]{:S(2)}, u32[]{:S(2)}) collective-permute-start(bf16[3,1,256,128]{3,2,1,0:T(8,128)(2,1)S(1)} %get-tuple-element.30), channel_id=1, source_target_pairs={{0,1},{1,2},{2,3},{4,5},{5,6},{6,7},{8,9},{9,10},{10,11},{12,13},{... | collective-permute-start | bytes 589832 | tf_op jit(solution)/shard_map/ppermute | solution.py:167
  71.2 1.3 %collective-permute-start.7 = (bf16[3,1,256,128]{3,2,1,0:T(8,128)(2,1)S(1)}, bf16[3,1,256,128]{3,2,1,0:T(8,128)(2,1)S(1)}, u32[]{:S(2)}, u32[]{:S(2)}) collective-permute-start(bf16[3,1,256,128]{3,2,1,0:T(8,128)(2,1)S(1)} %get-tuple-element.31), channel_id=1, source_target_pairs={{1,0},{2,1},{3,2},{5,4},{6,5},{7,6},{9,8},{10,9},{11,10},{13,12},{... | collective-permute-start | bytes 589832 | tf_op jit(solution)/shard_map/ppermute | solution.py:168
  72.7 1.8 %collective-permute-done.7 = bf16[3,1,256,128]{3,2,1,0:T(8,128)(2,1)S(1)} collective-permute-done((bf16[3,1,256,128]{3,2,1,0:T(8,128)(2,1)S(1)}, bf16[3,1,256,128]{3,2,1,0:T(8,128)(2,1)S(1)}, u32[]{:S(2)}, u32[]{:S(2)}) %collective-permute-start.7) | collective-permute-done | bytes 196640 | tf_op jit(solution)/shard_map/ppermute | solution.py:168
  74.5 1.9 %pad_maximum_fusion.1.ext_ref = bf16[3,4,256,128]{3,2,1,0:T(8,128)(2,1)} fusion(bf16[3,1,256,128]{3,2,1,0:T(8,128)(2,1)S(1)} %collective-permute-done.7, bf16[1,2,256,128]{3,2,1,0:T(8,128)(2,1)S(1)} %collective-permute-done.5, bf16[1,2,256,128]{3,2,1,0:T(8,128)(2,1)} %bitcast.16, bf16[1,2,256,128]{3,2,1,0:T(8,128)(2,1)S(1)} %collective-permute-done.4, ...), kind=kLoop, calls=%fused_computation.16 | loop fusion | flops 1572864 | bytes 1572864 | tf_op jit(solution)/shard_map/concatenate | solution.py:169
  76.4 4.1 %shard_map.93 = f32[2,256,128]{2,1,0:T(8,128)} custom-call(bf16[3,4,256,128]{3,2,1,0:T(8,128)(2,1)} %pad_maximum_fusion.1.ext_ref, bf16[768,2304]{1,0:T(8,128)(2,1)} %bitcast.98), custom_call_target="tpu_custom_call" | custom-call | flops 905969664 | bytes 4587520 | tf_op jit(solution)/shard_map/pallas_call | solution.py:46
  80.5 1.0 convert_bitcast_fusion
  82.2 3.8 %collective-permute-start.8 = (f32[93184]{0:T(1024)S(1)}, f32[93184]{0:T(1024)S(1)}, u32[]{:S(2)}, u32[]{:S(2)}) collective-permute-start(f32[93184]{0:T(1024)S(1)} %pad_maximum_fusion.4), channel_id=1, source_target_pairs={{0,1},{1,0},{2,3},{3,2},{4,5},{5,4},{6,7},{7,6},{8,9},{9,8},{10,11... | collective-permute-start | bytes 1118216 | tf_op jit(solution)/shard_map/ppermute | solution.py:137
  86.5 0.9 collective-permute-done.8
  87.7 6.9 %collective-permute-done.9 = f32[46592]{0:T(1024)S(1)} collective-permute-done((f32[46592]{0:T(1024)S(1)}, f32[46592]{0:T(1024)S(1)}, u32[]{:S(2)}, u32[]{:S(2)}) %collective-permute-start.9) | collective-permute-done | bytes 186400 | tf_op jit(solution)/shard_map/ppermute | solution.py:137
  94.7 2.7 %collective-permute-start.10 = (f32[23296]{0:T(1024)S(1)}, f32[23296]{0:T(1024)S(1)}, u32[]{:S(2)}, u32[]{:S(2)}) collective-permute-start(f32[23296]{0:T(1024)S(1)} %pad_maximum_fusion.8), channel_id=1, source_target_pairs={{0,4},{4,0},{8,12},{12,8},{1,5},{5,1},{9,13},{13,9},{2,6},{6,2},{1... | collective-permute-start | bytes 279560 | tf_op jit(solution)/shard_map/ppermute | solution.py:137
  97.4 0.8 copy.122
  98.2 1.8 %collective-permute-done.10 = f32[23296]{0:T(1024)S(1)} collective-permute-done((f32[23296]{0:T(1024)S(1)}, f32[23296]{0:T(1024)S(1)}, u32[]{:S(2)}, u32[]{:S(2)}) %collective-permute-start.10) | collective-permute-done | bytes 93216 | tf_op jit(solution)/shard_map/ppermute | solution.py:137
  100.0 3.1 %collective-permute-start.11 = (f32[11648]{0:T(1024)S(1)}, f32[11648]{0:T(1024)S(1)}, u32[]{:S(2)}, u32[]{:S(2)}) collective-permute-start(f32[11648]{0:T(1024)S(1)} %pad_maximum_fusion.12), channel_id=1, source_target_pairs={{0,8},{4,12},{8,0},{12,4},{1,9},{5,13},{9,1},{13,5},{2,10},{6,14},... | collective-permute-start | bytes 139784 | tf_op jit(solution)/shard_map/ppermute | solution.py:137
  103.4 0.8 copy.123
  104.1 1.1 collective-permute-done.11
  105.2 3.0 %collective-permute-start.12 = (f32[8192]{0:T(1024)S(1)}, f32[8192]{0:T(1024)S(1)}, u32[]{:S(2)}, u32[]{:S(2)}) collective-permute-start(f32[8192]{0:T(1024)S(1)} %pad_maximum_fusion.14), channel_id=1, source_target_pairs={{0,8},{4,12},{8,0},{12,4},{1,9},{5,13},{9,1},{13,5},{2,10},{6,14},... | collective-permute-start | bytes 98312 | tf_op jit(solution)/shard_map/ppermute | solution.py:147
  108.6 1.7 %collective-permute-done.12 = f32[8192]{0:T(1024)S(1)} collective-permute-done((f32[8192]{0:T(1024)S(1)}, f32[8192]{0:T(1024)S(1)}, u32[]{:S(2)}, u32[]{:S(2)}) %collective-permute-start.12) | collective-permute-done | bytes 32800 | tf_op jit(solution)/shard_map/ppermute | solution.py:147
  110.3 1.9 %collective-permute-start.13 = (f32[16384]{0:T(1024)S(1)}, f32[16384]{0:T(1024)S(1)}, u32[]{:S(2)}, u32[]{:S(2)}) collective-permute-start(f32[16384]{0:T(1024)S(1)} %pad_maximum_fusion.10), channel_id=1, source_target_pairs={{0,4},{4,0},{8,12},{12,8},{1,5},{5,1},{9,13},{13,9},{2,6},{6,2},{1... | collective-permute-start | bytes 196616 | tf_op jit(solution)/shard_map/ppermute | solution.py:147
  112.2 2.4 %collective-permute-done.13 = f32[16384]{0:T(1024)S(1)} collective-permute-done((f32[16384]{0:T(1024)S(1)}, f32[16384]{0:T(1024)S(1)}, u32[]{:S(2)}, u32[]{:S(2)}) %collective-permute-start.13) | collective-permute-done | bytes 65568 | tf_op jit(solution)/shard_map/ppermute | solution.py:147
  114.7 0.4 collective-permute-start.14
  115.1 4.8 %collective-permute-done.14 = f32[36224]{0:T(1024)S(1)} collective-permute-done((f32[36224]{0:T(1024)S(1)}, f32[36224]{0:T(1024)S(1)}, u32[]{:S(2)}, u32[]{:S(2)}) %collective-permute-start.14) | collective-permute-done | bytes 144928 | tf_op jit(solution)/shard_map/ppermute | solution.py:147
  120.7 1.4 %collective-permute-done.15 = f32[72448]{0:T(1024)S(1)} collective-permute-done((f32[72448]{0:T(1024)S(1)}, f32[72448]{0:T(1024)S(1)}, u32[]{:S(2)}, u32[]{:S(2)}) %collective-permute-start.15) | collective-permute-done | bytes 289824 | tf_op jit(solution)/shard_map/ppermute | solution.py:147
  122.6 0.8 fusion.17
  123.4 0.8 fusion.8
  (125 shorter events, 6.0 us)
Async XLA Ops:
  0.6 48.4 %copy-start = (bf16[256,256]{1,0:T(8,128)(2,1)S(1)}, bf16[256,256]{1,0:T(8,128)(2,1)}, u32[]{:S(2)}) copy-start(bf16[256,256]{1,0:T(8,128)(2,1)} %param.9) | copy-start | bytes 393220
  3.0 33.4 %collective-permute-start = (bf16[1,2,256,128]{3,2,1,0:T(8,128)(2,1)S(1)}, bf16[1,2,256,128]{3,2,1,0:T(8,128)(2,1)S(1)}, u32[]{:S(2)}, u32[]{:S(2)}) collective-permute-start(bf16[1,2,256,128]{3,2,1,0:T(8,128)(2,1)S(1)} %bitcast.101), channel_id=1, source_target_pairs={{0,4},{4,8},{8,12},{1,5},{5,9},{9,13},{2,6},{6,10},{10,14},{3,7},{... | collective-permute-start | bytes 393224 | tf_op jit(solution)/shard_map/ppermute | solution.py:167
  7.9 28.4 %collective-permute-start.1 = (bf16[1,2,256,128]{3,2,1,0:T(8,128)(2,1)S(1)}, bf16[1,2,256,128]{3,2,1,0:T(8,128)(2,1)S(1)}, u32[]{:S(2)}, u32[]{:S(2)}) collective-permute-start(bf16[1,2,256,128]{3,2,1,0:T(8,128)(2,1)S(1)} %bitcast.102), channel_id=1, source_target_pairs={{4,0},{8,4},{12,8},{5,1},{9,5},{13,9},{6,2},{10,6},{14,10},{7,3},{... | collective-permute-start | bytes 393224 | tf_op jit(solution)/shard_map/ppermute | solution.py:168
  9.4 19.2 %copy-start.1 = (f32[256,256]{1,0:T(8,128)}, f32[256,256]{1,0:T(8,128)S(1)}, u32[]{:S(2)}) copy-start(f32[256,256]{1,0:T(8,128)S(1)} %compare_convert_fusion.mask_ref) | copy-start | bytes 786436
  21.4 7.0 %copy-start.3 = (bf16[256,1,2,128]{3,2,1,0:T(2,128)(2,1)S(1)}, bf16[256,1,2,128]{3,2,1,0:T(2,128)(2,1)}, u32[]{:S(2)}) copy-start(bf16[256,1,2,128]{3,2,1,0:T(2,128)(2,1)} %param.6) | copy-start | bytes 393220
  21.4 7.1 %copy-start.2 = (bf16[256,8,3,3,3]{0,1,4,3,2:T(8,128)(2,1)S(1)}, bf16[256,8,3,3,3]{0,1,4,3,2:T(8,128)(2,1)}, u32[]{:S(2)}) copy-start(bf16[256,8,3,3,3]{0,1,4,3,2:T(8,128)(2,1)} %param.8) | copy-start | bytes 331780
  36.4 4.1 %collective-permute-start.2 = (bf16[3,1,256,128]{3,2,1,0:T(8,128)(2,1)S(1)}, bf16[3,1,256,128]{3,2,1,0:T(8,128)(2,1)S(1)}, u32[]{:S(2)}, u32[]{:S(2)}) collective-permute-start(bf16[3,1,256,128]{3,2,1,0:T(8,128)(2,1)S(1)} %get-tuple-element.32), channel_id=1, source_target_pairs={{0,1},{1,2},{2,3},{4,5},{5,6},{6,7},{8,9},{9,10},{10,11},{12,13},{... | collective-permute-start | bytes 589832 | tf_op jit(solution)/shard_map/ppermute | solution.py:167
  37.9 4.9 %collective-permute-start.3 = (bf16[3,1,256,128]{3,2,1,0:T(8,128)(2,1)S(1)}, bf16[3,1,256,128]{3,2,1,0:T(8,128)(2,1)S(1)}, u32[]{:S(2)}, u32[]{:S(2)}) collective-permute-start(bf16[3,1,256,128]{3,2,1,0:T(8,128)(2,1)S(1)} %get-tuple-element.33), channel_id=1, source_target_pairs={{1,0},{2,1},{3,2},{5,4},{6,5},{7,6},{9,8},{10,9},{11,10},{13,12},{... | collective-permute-start | bytes 589832 | tf_op jit(solution)/shard_map/ppermute | solution.py:168
  51.4 13.0 %collective-permute-start.4 = (bf16[1,2,256,128]{3,2,1,0:T(8,128)(2,1)}, bf16[1,2,256,128]{3,2,1,0:T(8,128)(2,1)S(1)}, u32[]{:S(2)}, u32[]{:S(2)}) collective-permute-start(bf16[1,2,256,128]{3,2,1,0:T(8,128)(2,1)} %bitcast.16), channel_id=1, source_target_pairs={{0,4},{4,8},{8,12},{1,5},{5,9},{9,13},{2,6},{6,10},{10,14},{3,7},{... | collective-permute-start | bytes 393224 | tf_op jit(solution)/shard_map/ppermute | solution.py:167
  56.0 8.4 %collective-permute-start.5 = (bf16[1,2,256,128]{3,2,1,0:T(8,128)(2,1)}, bf16[1,2,256,128]{3,2,1,0:T(8,128)(2,1)S(1)}, u32[]{:S(2)}, u32[]{:S(2)}) collective-permute-start(bf16[1,2,256,128]{3,2,1,0:T(8,128)(2,1)} %bitcast.16), channel_id=1, source_target_pairs={{4,0},{8,4},{12,8},{5,1},{9,5},{13,9},{6,2},{10,6},{14,10},{7,3},{... | collective-permute-start | bytes 393224 | tf_op jit(solution)/shard_map/ppermute | solution.py:168
  65.4 7.3 %collective-permute-start.6 = (bf16[3,1,256,128]{3,2,1,0:T(8,128)(2,1)S(1)}, bf16[3,1,256,128]{3,2,1,0:T(8,128)(2,1)S(1)}, u32[]{:S(2)}, u32[]{:S(2)}) collective-permute-start(bf16[3,1,256,128]{3,2,1,0:T(8,128)(2,1)S(1)} %get-tuple-element.30), channel_id=1, source_target_pairs={{0,1},{1,2},{2,3},{4,5},{5,6},{6,7},{8,9},{9,10},{10,11},{12,13},{... | collective-permute-start | bytes 589832 | tf_op jit(solution)/shard_map/ppermute | solution.py:167
  71.2 3.3 %collective-permute-start.7 = (bf16[3,1,256,128]{3,2,1,0:T(8,128)(2,1)S(1)}, bf16[3,1,256,128]{3,2,1,0:T(8,128)(2,1)S(1)}, u32[]{:S(2)}, u32[]{:S(2)}) collective-permute-start(bf16[3,1,256,128]{3,2,1,0:T(8,128)(2,1)S(1)} %get-tuple-element.31), channel_id=1, source_target_pairs={{1,0},{2,1},{3,2},{5,4},{6,5},{7,6},{9,8},{10,9},{11,10},{13,12},{... | collective-permute-start | bytes 589832 | tf_op jit(solution)/shard_map/ppermute | solution.py:168
  76.4 26.7 %copy-start.4 = (bf16[256,256]{1,0:T(8,128)(2,1)S(1)}, bf16[256,256]{1,0:T(8,128)(2,1)}, u32[]{:S(2)}) copy-start(bf16[256,256]{1,0:T(8,128)(2,1)} %param.7) | copy-start | bytes 393220
  82.2 5.1 %collective-permute-start.8 = (f32[93184]{0:T(1024)S(1)}, f32[93184]{0:T(1024)S(1)}, u32[]{:S(2)}, u32[]{:S(2)}) collective-permute-start(f32[93184]{0:T(1024)S(1)} %pad_maximum_fusion.4), channel_id=1, source_target_pairs={{0,1},{1,0},{2,3},{3,2},{4,5},{5,4},{6,7},{7,6},{8,9},{9,8},{10,11... | collective-permute-start | bytes 1118216 | tf_op jit(solution)/shard_map/ppermute | solution.py:137
  87.5 7.1 %collective-permute-start.9 = (f32[46592]{0:T(1024)S(1)}, f32[46592]{0:T(1024)S(1)}, u32[]{:S(2)}, u32[]{:S(2)}) collective-permute-start(f32[46592]{0:T(1024)S(1)} %pad_maximum_fusion.6), channel_id=1, source_target_pairs={{0,2},{1,3},{2,0},{3,1},{4,6},{5,7},{6,4},{7,5},{8,10},{9,11},{10,... | collective-permute-start | bytes 559112 | tf_op jit(solution)/shard_map/ppermute | solution.py:137
  94.7 5.3 %collective-permute-start.10 = (f32[23296]{0:T(1024)S(1)}, f32[23296]{0:T(1024)S(1)}, u32[]{:S(2)}, u32[]{:S(2)}) collective-permute-start(f32[23296]{0:T(1024)S(1)} %pad_maximum_fusion.8), channel_id=1, source_target_pairs={{0,4},{4,0},{8,12},{12,8},{1,5},{5,1},{9,13},{13,9},{2,6},{6,2},{1... | collective-permute-start | bytes 279560 | tf_op jit(solution)/shard_map/ppermute | solution.py:137
  100.0 5.2 %collective-permute-start.11 = (f32[11648]{0:T(1024)S(1)}, f32[11648]{0:T(1024)S(1)}, u32[]{:S(2)}, u32[]{:S(2)}) collective-permute-start(f32[11648]{0:T(1024)S(1)} %pad_maximum_fusion.12), channel_id=1, source_target_pairs={{0,8},{4,12},{8,0},{12,4},{1,9},{5,13},{9,1},{13,5},{2,10},{6,14},... | collective-permute-start | bytes 139784 | tf_op jit(solution)/shard_map/ppermute | solution.py:137
  105.2 5.0 %collective-permute-start.12 = (f32[8192]{0:T(1024)S(1)}, f32[8192]{0:T(1024)S(1)}, u32[]{:S(2)}, u32[]{:S(2)}) collective-permute-start(f32[8192]{0:T(1024)S(1)} %pad_maximum_fusion.14), channel_id=1, source_target_pairs={{0,8},{4,12},{8,0},{12,4},{1,9},{5,13},{9,1},{13,5},{2,10},{6,14},... | collective-permute-start | bytes 98312 | tf_op jit(solution)/shard_map/ppermute | solution.py:147
  110.3 4.3 %collective-permute-start.13 = (f32[16384]{0:T(1024)S(1)}, f32[16384]{0:T(1024)S(1)}, u32[]{:S(2)}, u32[]{:S(2)}) collective-permute-start(f32[16384]{0:T(1024)S(1)} %pad_maximum_fusion.10), channel_id=1, source_target_pairs={{0,4},{4,0},{8,12},{12,8},{1,5},{5,1},{9,13},{13,9},{2,6},{6,2},{1... | collective-permute-start | bytes 196616 | tf_op jit(solution)/shard_map/ppermute | solution.py:147
  114.7 5.2 %collective-permute-start.14 = (f32[36224]{0:T(1024)S(1)}, f32[36224]{0:T(1024)S(1)}, u32[]{:S(2)}, u32[]{:S(2)}) collective-permute-start(f32[36224]{0:T(1024)S(1)} %pad_maximum_fusion.7), channel_id=1, source_target_pairs={{0,2},{1,3},{2,0},{3,1},{4,6},{5,7},{6,4},{7,5},{8,10},{9,11},{10,... | collective-permute-start | bytes 434696 | tf_op jit(solution)/shard_map/ppermute | solution.py:147
  120.4 1.6 %collective-permute-start.15 = (f32[72448]{0:T(1024)S(1)}, f32[72448]{0:T(1024)S(1)}, u32[]{:S(2)}, u32[]{:S(2)}) collective-permute-start(f32[72448]{0:T(1024)S(1)} %pad_maximum_fusion.5), channel_id=1, source_target_pairs={{0,1},{1,0},{2,3},{3,2},{4,5},{5,4},{6,7},{7,6},{8,9},{9,8},{10,11... | collective-permute-start | bytes 869384 | tf_op jit(solution)/shard_map/ppermute | solution.py:147

commit v10 on v8

--- a/solution.py
+++ b/solution.py
@@ -247,14 +247,11 @@
     reverse = [int(format(n, f"0{digits}b")[::-1], 2) if digits else 0 for n in range(grp_count)]
     blocks = kernel_part.reshape(grp_count, sub_count, -1)
     kernel_laid = jnp.concatenate([blocks[n : n + 1] for n in reverse]).transpose(1, 0, 2)
-    first_sum, third_sum, group_sum = tree_sum(
-        [
-            (first_part, ("sub", "grp"), ("sub", "grp")),
-            (third_part, ("sub", "grp"), ("sub", "grp")),
-            (kernel_laid, ("sub", "grp"), ("sub",)),
-        ],
-        (("sub", True), ("grp", True)),
-    )
+    order = (("sub", True), ("grp", True))
+    third_sum, group_sum = tree_sum(
+        [(third_part, ("sub", "grp"), ("sub", "grp")), (kernel_laid, ("sub", "grp"), ("sub",))], order
+    )
+    (first_sum,) = tree_sum([(first_part, ("sub", "grp"), ("sub", "grp"))], order)
     first_grad = first_sum.reshape(first_part.shape) * factor
     third_grad = third_sum.reshape(third_part.shape) * factor
     own_rows = channels // grp_count

time: 107 us -> 113 us (1.056)
  starting transfers between devices: 37.2 us -> 51.6 us
  waiting for transfers between devices: 25 us -> 16 us
    ppermute x4 -> x8, starting transfers between devices: 9.8 us -> 23.3 us  [tree_sum(): got = lax.ppermute(jnp.concatenate(sends), axis, pairs)]
    ppermute x4 -> x8, waiting for transfers between devices: 10.6 us -> 4.96 us  [tree_sum(): got = lax.ppermute(jnp.concatenate(sends), axis, pairs)]
    ppermute x4 -> x8, starting transfers between devices: 5.35 us -> 10 us  [tree_sum(): lax.ppermute(jnp.concatenate([pieces[n] for n in members]), axis, pairs)]
    ppermute x4, starting transfers between devices: 16.7 us -> 12.9 us  [halo(): lax.ppermute(lax.slice_in_dim(block, size - 1, size, axis=dim), axis, up)]
    ppermute x4 -> x8, waiting for transfers between devices: 10.3 us -> 8.64 us  [tree_sum(): lax.ppermute(jnp.concatenate([pieces[n] for n in members]), axis, pairs)]
    ppermute x4, waiting for transfers between devices: 4.05 us -> 2.41 us  [halo(): high = lax.ppermute(lax.slice_in_dim(block, 0, 1, axis=dim), axis, down)]
  transfers between devices with their start and end apart: 16 -> 24, of which waited for: 10 -> 8; matrix products, arithmetic and copies ran while one was open for 13% -> 18% of each run, Pallas kernels for 4% -> 9%
where the time goes in v10:
time: 113 us; the launch traced here: 112 us
  starting transfers between devices  51.6 us (46%)
  waiting for transfers between devices  16 us (14%)
  Pallas kernels  15.2 us (13%)
  other arithmetic  11.1 us (10%)
  matrix products  9.15 us (8%)
  local copies, waits for them, and re-layouts  7.36 us (7%)
  between operations  1.5 us (1%)
    ppermute x8, starting transfers between devices, tree_sum(): got = lax.ppermute(jnp.concatenate(sends), axis, pairs)  23.3 us
    ppermute x4, starting transfers between devices, halo(): lax.ppermute(lax.slice_in_dim(block, size - 1, size, axis=dim), axis, up)  12.9 us
    pallas_call x2, Pallas kernels, conv_call(): pl.pallas_call(conv_body, out_shape=jax.ShapeDtypeStruct((height, channel...  10.7 us
    ppermute x8, starting transfers between devices, tree_sum(): lax.ppermute(jnp.concatenate([pieces[n] for n in members]), axis, pairs)  10 us
    ppermute x8, waiting for transfers between devices, tree_sum(): lax.ppermute(jnp.concatenate([pieces[n] for n in members]), axis, pairs)  8.64 us
    ppermute x4, starting transfers between devices, halo(): high = lax.ppermute(lax.slice_in_dim(block, 0, 1, axis=dim), axis, down)  5.35 us
    ppermute x8, waiting for transfers between devices, tree_sum(): got = lax.ppermute(jnp.concatenate(sends), axis, pairs)  4.96 us
    pallas_call x1, Pallas kernels, wgrad_call(): pl.pallas_call(wgrad_body, out_shape=jax.ShapeDtypeStruct((blocks, channe...  4.56 us
  transfers between devices with their start and end apart: 24, of which 8 were waited for; matrix products, arithmetic and copies ran while one was open for 18% of the time, Pallas kernels for 9%

profile of v10, /device:TPU:0, one launch (start us, length us, event | category | flops | bytes accessed | tf_op | source)
XLA Modules:
  0.0 112.0 jit_solution(4158505657104910211)
XLA Ops:
  0.7 1.1 copy.74
  1.7 1.1 %reduce-precision_convert_fusion.2 = (bf16[256,256]{0,1:T(8,128)(2,1)S(1)}, f32[256,256]{0,1:T(8,128)S(1)}) fusion(bf16[256,256]{0,1:T(8,128)(2,1)S(1)} %bitcast.101, bf16[256,256]{1,0:T(8,128)(2,1)} %param.7), kind=kOutput, calls=%fused_computation.37 | convolution fusion | flops 33947648 | bytes 655360 | tf_op jit(solution)/shard_map/dot_general | solution.py:212
  3.0 4.9 %collective-permute-start = (bf16[1,2,256,128]{3,2,1,0:T(8,128)(2,1)S(1)}, bf16[1,2,256,128]{3,2,1,0:T(8,128)(2,1)S(1)}, u32[]{:S(2)}, u32[]{:S(2)}) collective-permute-start(bf16[1,2,256,128]{3,2,1,0:T(8,128)(2,1)S(1)} %bitcast.90), channel_id=1, source_target_pairs={{0,4},{4,8},{8,12},{1,5},{5,9},{9,13},{2,6},{6,10},{10,14},{3,7},{... | collective-permute-start | bytes 393224 | tf_op jit(solution)/shard_map/ppermute | solution.py:169
  7.9 1.3 %collective-permute-start.1 = (bf16[1,2,256,128]{3,2,1,0:T(8,128)(2,1)S(1)}, bf16[1,2,256,128]{3,2,1,0:T(8,128)(2,1)S(1)}, u32[]{:S(2)}, u32[]{:S(2)}) collective-permute-start(bf16[1,2,256,128]{3,2,1,0:T(8,128)(2,1)S(1)} %bitcast.91), channel_id=1, source_target_pairs={{4,0},{8,4},{12,8},{5,1},{9,5},{13,9},{6,2},{10,6},{14,10},{7,3},{... | collective-permute-start | bytes 393224 | tf_op jit(solution)/shard_map/ppermute | solution.py:170
  9.4 4.0 %fusion = bf16[27,256,256]{2,1,0:T(8,128)(2,1)} fusion(f32[256,256]{1,0:T(8,128)S(1)} %compare_convert_fusion.mask_ref, bf16[256,8,27]{0,1,2:T(8,128)(2,1)} %bitcast.108, s32[256]{0:T(256)S(1)} %and_select_fusion.2), kind=kOutput, calls=%fused_computation.1 | convolution fusion | flops 31852544 | bytes 3912704 | tf_op jit(solution)/shard_map/ojt,ji->toi/dot_general | solution.py:186
  13.4 2.9 %multiply_convert_fusion = bf16[256,256,27]{1,0,2:T(8,128)(2,1)} fusion(f32[256,256]{1,0:T(8,128)S(1)} %compare_convert_fusion.mask_ref, bf16[256,8,27]{0,1,2:T(8,128)(2,1)S(1)} %bitcast.109, s32[256]{0:T(256)S(1)} %and_select_fusion.2), kind=kOutput, calls=%fused_computation.2 | convolution fusion | flops 31907840 | bytes 3912704 | tf_op jit(solution)/shard_map/ji,ojt->tio/dot_general | solution.py:187
  16.6 1.5 %collective-permute-start.2 = (bf16[3,1,256,128]{3,2,1,0:T(8,128)(2,1)S(1)}, bf16[3,1,256,128]{3,2,1,0:T(8,128)(2,1)S(1)}, u32[]{:S(2)}, u32[]{:S(2)}) collective-permute-start(bf16[3,1,256,128]{3,2,1,0:T(8,128)(2,1)S(1)} %get-tuple-element.32), channel_id=1, source_target_pairs={{0,1},{1,2},{2,3},{4,5},{5,6},{6,7},{8,9},{9,10},{10,11},{12,13},{... | collective-permute-start | bytes 589832 | tf_op jit(solution)/shard_map/ppermute | solution.py:169
  18.1 1.3 %collective-permute-start.3 = (bf16[3,1,256,128]{3,2,1,0:T(8,128)(2,1)S(1)}, bf16[3,1,256,128]{3,2,1,0:T(8,128)(2,1)S(1)}, u32[]{:S(2)}, u32[]{:S(2)}) collective-permute-start(bf16[3,1,256,128]{3,2,1,0:T(8,128)(2,1)S(1)} %get-tuple-element.33), channel_id=1, source_target_pairs={{1,0},{2,1},{3,2},{5,4},{6,5},{7,6},{9,8},{10,9},{11,10},{13,12},{... | collective-permute-start | bytes 589832 | tf_op jit(solution)/shard_map/ppermute | solution.py:170
  19.4 1.2 %fusion.6.sel_ref = bf16[16,128,128]{2,1,0:T(8,128)(2,1)} fusion(s32[16,128]{1,0:T(8,128)S(1)} %broadcast_add_fusion), kind=kLoop, calls=%fused_computation.13 | loop fusion | flops 524288 | bytes 532480 | tf_op jit(solution)/shard_map/convert_element_type | solution.py:103
  20.5 2.4 %collective-permute-done.3 = bf16[3,1,256,128]{3,2,1,0:T(8,128)(2,1)S(1)} collective-permute-done((bf16[3,1,256,128]{3,2,1,0:T(8,128)(2,1)S(1)}, bf16[3,1,256,128]{3,2,1,0:T(8,128)(2,1)S(1)}, u32[]{:S(2)}, u32[]{:S(2)}) %collective-permute-start.3) | collective-permute-done | bytes 196640 | tf_op jit(solution)/shard_map/ppermute | solution.py:170
  22.9 1.0 pad_maximum_fusion.ext_ref.act_ref
  24.0 5.3 %shard_map.92 = f32[2,256,128]{2,1,0:T(8,128)} custom-call(bf16[3,4,256,128]{3,2,1,0:T(8,128)(2,1)} %pad_maximum_fusion.ext_ref.act_ref, bf16[9,768,256]{2,1,0:T(8,128)(2,1)} %bitcast.88), custom_call_target="tpu_custom_call" | custom-call | flops 905969664 | bytes 4587520 | tf_op jit(solution)/shard_map/pallas_call | solution.py:47
  29.3 1.1 fusion.16
  31.4 0.8 fusion.10.delta_ref
  32.2 4.5 %collective-permute-start.4 = (bf16[1,2,256,128]{3,2,1,0:T(8,128)(2,1)}, bf16[1,2,256,128]{3,2,1,0:T(8,128)(2,1)S(1)}, u32[]{:S(2)}, u32[]{:S(2)}) collective-permute-start(bf16[1,2,256,128]{3,2,1,0:T(8,128)(2,1)} %bitcast.16), channel_id=1, source_target_pairs={{0,4},{4,8},{8,12},{1,5},{5,9},{9,13},{2,6},{6,10},{10,14},{3,7},{... | collective-permute-start | bytes 393224 | tf_op jit(solution)/shard_map/ppermute | solution.py:169
  36.7 1.3 %collective-permute-start.5 = (bf16[1,2,256,128]{3,2,1,0:T(8,128)(2,1)}, bf16[1,2,256,128]{3,2,1,0:T(8,128)(2,1)S(1)}, u32[]{:S(2)}, u32[]{:S(2)}) collective-permute-start(bf16[1,2,256,128]{3,2,1,0:T(8,128)(2,1)} %bitcast.16), channel_id=1, source_target_pairs={{4,0},{8,4},{12,8},{5,1},{9,5},{13,9},{6,2},{10,6},{14,10},{7,3},{... | collective-permute-start | bytes 393224 | tf_op jit(solution)/shard_map/ppermute | solution.py:170
  38.0 4.6 %shard_map.94 = f32[2,256,128]{2,1,0:T(8,128)} custom-call(bf16[3,4,256,128]{3,2,1,0:T(8,128)(2,1)} %pad_maximum_fusion.ext_ref.act_ref, bf16[2,256,128]{2,1,0:T(8,128)(2,1)} %fusion.10.delta_ref, f32[256,256]{1,0:T(8,128)} %copy-done.1, bf16[16,128,128]{2,1,0:T(8,128)(2,1)} %fusion.6.sel_ref), custom_call_target="tpu_custom_call" | custom-call | flops 1358954496 | bytes 1179648 | tf_op jit(solution)/shard_map/pallas_call | solution.py:104
  42.6 1.1 copy.86
  45.2 3.9 %collective-permute-start.16 = (f32[60416]{0:T(1024)S(1)}, f32[60416]{0:T(1024)S(1)}, u32[]{:S(2)}, u32[]{:S(2)}) collective-permute-start(f32[60416]{0:T(1024)S(1)} %pad_maximum_fusion.4), channel_id=1, source_target_pairs={{0,1},{1,0},{2,3},{3,2},{4,5},{5,4},{6,7},{7,6},{8,9},{9,8},{10,11... | collective-permute-start | bytes 725000 | tf_op jit(solution)/shard_map/ppermute | solution.py:139
  49.4 0.8 copy.99
  50.2 1.0 pad_maximum_fusion.3
  51.2 1.9 %collective-permute-start.6 = (bf16[3,1,256,128]{3,2,1,0:T(8,128)(2,1)S(1)}, bf16[3,1,256,128]{3,2,1,0:T(8,128)(2,1)S(1)}, u32[]{:S(2)}, u32[]{:S(2)}) collective-permute-start(bf16[3,1,256,128]{3,2,1,0:T(8,128)(2,1)S(1)} %get-tuple-element.30), channel_id=1, source_target_pairs={{0,1},{1,2},{2,3},{4,5},{5,6},{6,7},{8,9},{9,10},{10,11},{12,13},{... | collective-permute-start | bytes 589832 | tf_op jit(solution)/shard_map/ppermute | solution.py:169
  53.1 1.5 %collective-permute-start.7 = (bf16[3,1,256,128]{3,2,1,0:T(8,128)(2,1)S(1)}, bf16[3,1,256,128]{3,2,1,0:T(8,128)(2,1)S(1)}, u32[]{:S(2)}, u32[]{:S(2)}) collective-permute-start(bf16[3,1,256,128]{3,2,1,0:T(8,128)(2,1)S(1)} %get-tuple-element.31), channel_id=1, source_target_pairs={{1,0},{2,1},{3,2},{5,4},{6,5},{7,6},{9,8},{10,9},{11,10},{13,12},{... | collective-permute-start | bytes 589832 | tf_op jit(solution)/shard_map/ppermute | solution.py:170
  54.7 2.4 %collective-permute-start.17 = (f32[30208]{0:T(1024)S(1)}, f32[30208]{0:T(1024)S(1)}, u32[]{:S(2)}, u32[]{:S(2)}) collective-permute-start(f32[30208]{0:T(1024)S(1)} %pad_maximum_fusion.6), channel_id=1, source_target_pairs={{0,2},{1,3},{2,0},{3,1},{4,6},{5,7},{6,4},{7,5},{8,10},{9,11},{10,... | collective-permute-start | bytes 362504 | tf_op jit(solution)/shard_map/ppermute | solution.py:139
  57.1 1.9 %pad_maximum_fusion.1.ext_ref = bf16[3,4,256,128]{3,2,1,0:T(8,128)(2,1)} fusion(bf16[3,1,256,128]{3,2,1,0:T(8,128)(2,1)S(1)} %collective-permute-done.7, bf16[1,2,256,128]{3,2,1,0:T(8,128)(2,1)S(1)} %collective-permute-done.5, bf16[1,2,256,128]{3,2,1,0:T(8,128)(2,1)} %bitcast.16, bf16[1,2,256,128]{3,2,1,0:T(8,128)(2,1)S(1)} %collective-permute-done.4, ...), kind=kLoop, calls=%fused_computation.15 | loop fusion | flops 1572864 | bytes 1572864 | tf_op jit(solution)/shard_map/concatenate | solution.py:171
  59.0 5.4 %shard_map.93 = f32[2,256,128]{2,1,0:T(8,128)} custom-call(bf16[3,4,256,128]{3,2,1,0:T(8,128)(2,1)} %pad_maximum_fusion.1.ext_ref, bf16[9,768,256]{2,1,0:T(8,128)(2,1)} %bitcast.87), custom_call_target="tpu_custom_call" | custom-call | flops 905969664 | bytes 4587520 | tf_op jit(solution)/shard_map/pallas_call | solution.py:47
  64.4 1.0 convert_bitcast_fusion
  65.9 2.7 %collective-permute-start.18 = (f32[15104]{0:T(1024)S(1)}, f32[15104]{0:T(1024)S(1)}, u32[]{:S(2)}, u32[]{:S(2)}) collective-permute-start(f32[15104]{0:T(1024)S(1)} %pad_maximum_fusion.8), channel_id=1, source_target_pairs={{0,4},{4,0},{8,12},{12,8},{1,5},{5,1},{9,13},{13,9},{2,6},{6,2},{1... | collective-permute-start | bytes 181256 | tf_op jit(solution)/shard_map/ppermute | solution.py:139
  68.9 2.0 %collective-permute-done.18 = f32[15104]{0:T(1024)S(1)} collective-permute-done((f32[15104]{0:T(1024)S(1)}, f32[15104]{0:T(1024)S(1)}, u32[]{:S(2)}, u32[]{:S(2)}) %collective-permute-start.18) | collective-permute-done | bytes 60448 | tf_op jit(solution)/shard_map/ppermute | solution.py:139
  70.9 3.1 %collective-permute-start.19 = (f32[7552]{0:T(1024)S(1)}, f32[7552]{0:T(1024)S(1)}, u32[]{:S(2)}, u32[]{:S(2)}) collective-permute-start(f32[7552]{0:T(1024)S(1)} %pad_maximum_fusion.9), channel_id=1, source_target_pairs={{0,8},{4,12},{8,0},{12,4},{1,9},{5,13},{9,1},{13,5},{2,10},{6,14},... | collective-permute-start | bytes 90632 | tf_op jit(solution)/shard_map/ppermute | solution.py:139
  74.2 3.0 %collective-permute-start.8 = (f32[32768]{0:T(1024)S(1)}, f32[32768]{0:T(1024)S(1)}, u32[]{:S(2)}, u32[]{:S(2)}) collective-permute-start(f32[32768]{0:T(1024)S(1)} %bitcast.112), channel_id=1, source_target_pairs={{0,1},{1,0},{2,3},{3,2},{4,5},{5,4},{6,7},{7,6},{8,9},{9,8},{10,11... | collective-permute-start | bytes 393224 | tf_op jit(solution)/shard_map/ppermute | solution.py:139
  77.3 0.8 copy.100
  79.2 4.1 %collective-permute-start.9 = (f32[16384]{0:T(1024)S(1)}, f32[16384]{0:T(1024)S(1)}, u32[]{:S(2)}, u32[]{:S(2)}) collective-permute-start(f32[16384]{0:T(1024)S(1)} %slice_select_fusion.5), channel_id=1, source_target_pairs={{0,2},{1,3},{2,0},{3,1},{4,6},{5,7},{6,4},{7,5},{8,10},{9,11},{10,... | collective-permute-start | bytes 196616 | tf_op jit(solution)/shard_map/ppermute | solution.py:139
  83.3 1.9 %collective-permute-start.21 = (f32[8192]{0:T(1024)S(1)}, f32[8192]{0:T(1024)S(1)}, u32[]{:S(2)}, u32[]{:S(2)}) collective-permute-start(f32[8192]{0:T(1024)S(1)} %maximum_select_fusion.14), channel_id=1, source_target_pairs={{0,4},{4,0},{8,12},{12,8},{1,5},{5,1},{9,13},{13,9},{2,6},{6,2},{1... | collective-permute-start | bytes 98312 | tf_op jit(solution)/shard_map/ppermute | solution.py:149
  85.2 2.2 %collective-permute-done.21 = f32[8192]{0:T(1024)S(1)} collective-permute-done((f32[8192]{0:T(1024)S(1)}, f32[8192]{0:T(1024)S(1)}, u32[]{:S(2)}, u32[]{:S(2)}) %collective-permute-start.21) | collective-permute-done | bytes 32800 | tf_op jit(solution)/shard_map/ppermute | solution.py:149
  87.4 1.9 %collective-permute-start.10 = (f32[8192]{0:T(1024)S(1)}, f32[8192]{0:T(1024)S(1)}, u32[]{:S(2)}, u32[]{:S(2)}) collective-permute-start(f32[8192]{0:T(1024)S(1)} %slice_select_fusion.8), channel_id=1, source_target_pairs={{0,4},{4,0},{8,12},{12,8},{1,5},{5,1},{9,13},{13,9},{2,6},{6,2},{1... | collective-permute-start | bytes 98312 | tf_op jit(solution)/shard_map/ppermute | solution.py:139
  89.3 1.6 %collective-permute-start.22 = (f32[19840]{0:T(1024)S(1)}, f32[19840]{0:T(1024)S(1)}, u32[]{:S(2)}, u32[]{:S(2)}) collective-permute-start(f32[19840]{0:T(1024)S(1)} %pad_maximum_fusion.7), channel_id=1, source_target_pairs={{0,2},{1,3},{2,0},{3,1},{4,6},{5,7},{6,4},{7,5},{8,10},{9,11},{10,... | collective-permute-start | bytes 238088 | tf_op jit(solution)/shard_map/ppermute | solution.py:149
  91.4 2.1 %collective-permute-start.11 = (f32[4096]{0:T(1024)S(1)}, f32[4096]{0:T(1024)S(1)}, u32[]{:S(2)}, u32[]{:S(2)}) collective-permute-start(f32[4096]{0:T(1024)S(1)} %slice_select_fusion.12), channel_id=1, source_target_pairs={{0,8},{4,12},{8,0},{12,4},{1,9},{5,13},{9,1},{13,5},{2,10},{6,14},... | collective-permute-start | bytes 49160 | tf_op jit(solution)/shard_map/ppermute | solution.py:139
  93.5 2.6 %collective-permute-done.11 = f32[4096]{0:T(1024)S(1)} collective-permute-done((f32[4096]{0:T(1024)S(1)}, f32[4096]{0:T(1024)S(1)}, u32[]{:S(2)}, u32[]{:S(2)}) %collective-permute-start.11) | collective-permute-done | bytes 16416 | tf_op jit(solution)/shard_map/ppermute | solution.py:139
  96.1 2.2 %collective-permute-start.12 = (f32[4096]{0:T(1024)S(1)}, f32[4096]{0:T(1024)S(1)}, u32[]{:S(2)}, u32[]{:S(2)}) collective-permute-start(f32[4096]{0:T(1024)S(1)} %select_add_fusion.2), channel_id=1, source_target_pairs={{0,8},{4,12},{8,0},{12,4},{1,9},{5,13},{9,1},{13,5},{2,10},{6,14},... | collective-permute-start | bytes 49160 | tf_op jit(solution)/shard_map/ppermute | solution.py:149
  98.9 1.8 %collective-permute-done.12 = f32[4096]{0:T(1024)S(1)} collective-permute-done((f32[4096]{0:T(1024)S(1)}, f32[4096]{0:T(1024)S(1)}, u32[]{:S(2)}, u32[]{:S(2)}) %collective-permute-start.12) | collective-permute-done | bytes 16416 | tf_op jit(solution)/shard_map/ppermute | solution.py:149
  100.7 1.8 %collective-permute-start.13 = (f32[8192]{0:T(1024)S(1)}, f32[8192]{0:T(1024)S(1)}, u32[]{:S(2)}, u32[]{:S(2)}) collective-permute-start(f32[8192]{0:T(1024)S(1)} %maximum_select_fusion.12), channel_id=1, source_target_pairs={{0,4},{4,0},{8,12},{12,8},{1,5},{5,1},{9,13},{13,9},{2,6},{6,2},{1... | collective-permute-start | bytes 98312 | tf_op jit(solution)/shard_map/ppermute | solution.py:149
  102.6 2.1 %collective-permute-done.13 = f32[8192]{0:T(1024)S(1)} collective-permute-done((f32[8192]{0:T(1024)S(1)}, f32[8192]{0:T(1024)S(1)}, u32[]{:S(2)}, u32[]{:S(2)}) %collective-permute-start.13) | collective-permute-done | bytes 32800 | tf_op jit(solution)/shard_map/ppermute | solution.py:149
  104.7 1.7 %collective-permute-start.14 = (f32[16384]{0:T(1024)S(1)}, f32[16384]{0:T(1024)S(1)}, u32[]{:S(2)}, u32[]{:S(2)}) collective-permute-start(f32[16384]{0:T(1024)S(1)} %maximum_select_fusion.8), channel_id=1, source_target_pairs={{0,2},{1,3},{2,0},{3,1},{4,6},{5,7},{6,4},{7,5},{8,10},{9,11},{10,... | collective-permute-start | bytes 196616 | tf_op jit(solution)/shard_map/ppermute | solution.py:149
  106.4 2.6 %collective-permute-done.14 = f32[16384]{0:T(1024)S(1)} collective-permute-done((f32[16384]{0:T(1024)S(1)}, f32[16384]{0:T(1024)S(1)}, u32[]{:S(2)}, u32[]{:S(2)}) %collective-permute-start.14) | collective-permute-done | bytes 65568 | tf_op jit(solution)/shard_map/ppermute | solution.py:149
  109.6 0.8 fusion.17
  110.5 0.7 fusion.8
  111.2 0.7 fusion.7
  (138 shorter events, 7.2 us)
Async XLA Ops:
  0.6 29.9 %copy-start = (bf16[256,256]{1,0:T(8,128)(2,1)S(1)}, bf16[256,256]{1,0:T(8,128)(2,1)}, u32[]{:S(2)}) copy-start(bf16[256,256]{1,0:T(8,128)(2,1)} %param.9) | copy-start | bytes 393220
  0.6 12.7 %copy-start.3 = (bf16[256,8,3,3,3]{0,1,4,3,2:T(8,128)(2,1)S(1)}, bf16[256,8,3,3,3]{0,1,4,3,2:T(8,128)(2,1)}, u32[]{:S(2)}) copy-start(bf16[256,8,3,3,3]{0,1,4,3,2:T(8,128)(2,1)} %param.8) | copy-start | bytes 331780
  3.0 13.5 %collective-permute-start = (bf16[1,2,256,128]{3,2,1,0:T(8,128)(2,1)S(1)}, bf16[1,2,256,128]{3,2,1,0:T(8,128)(2,1)S(1)}, u32[]{:S(2)}, u32[]{:S(2)}) collective-permute-start(bf16[1,2,256,128]{3,2,1,0:T(8,128)(2,1)S(1)} %bitcast.90), channel_id=1, source_target_pairs={{0,4},{4,8},{8,12},{1,5},{5,9},{9,13},{2,6},{6,10},{10,14},{3,7},{... | collective-permute-start | bytes 393224 | tf_op jit(solution)/shard_map/ppermute | solution.py:169
  7.9 8.5 %collective-permute-start.1 = (bf16[1,2,256,128]{3,2,1,0:T(8,128)(2,1)S(1)}, bf16[1,2,256,128]{3,2,1,0:T(8,128)(2,1)S(1)}, u32[]{:S(2)}, u32[]{:S(2)}) collective-permute-start(bf16[1,2,256,128]{3,2,1,0:T(8,128)(2,1)S(1)} %bitcast.91), channel_id=1, source_target_pairs={{4,0},{8,4},{12,8},{5,1},{9,5},{13,9},{6,2},{10,6},{14,10},{7,3},{... | collective-permute-start | bytes 393224 | tf_op jit(solution)/shard_map/ppermute | solution.py:170
  9.4 6.9 %copy-start.1 = (f32[256,256]{1,0:T(8,128)}, f32[256,256]{1,0:T(8,128)S(1)}, u32[]{:S(2)}) copy-start(f32[256,256]{1,0:T(8,128)S(1)} %compare_convert_fusion.mask_ref) | copy-start | bytes 786436
  9.4 6.9 %copy-start.4 = (bf16[256,1,2,128]{3,2,1,0:T(2,128)(2,1)S(1)}, bf16[256,1,2,128]{3,2,1,0:T(2,128)(2,1)}, u32[]{:S(2)}) copy-start(bf16[256,1,2,128]{3,2,1,0:T(2,128)(2,1)} %param.6) | copy-start | bytes 393220
  16.6 4.0 %collective-permute-start.2 = (bf16[3,1,256,128]{3,2,1,0:T(8,128)(2,1)S(1)}, bf16[3,1,256,128]{3,2,1,0:T(8,128)(2,1)S(1)}, u32[]{:S(2)}, u32[]{:S(2)}) collective-permute-start(bf16[3,1,256,128]{3,2,1,0:T(8,128)(2,1)S(1)} %get-tuple-element.32), channel_id=1, source_target_pairs={{0,1},{1,2},{2,3},{4,5},{5,6},{6,7},{8,9},{9,10},{10,11},{12,13},{... | collective-permute-start | bytes 589832 | tf_op jit(solution)/shard_map/ppermute | solution.py:169
  18.1 4.9 %collective-permute-start.3 = (bf16[3,1,256,128]{3,2,1,0:T(8,128)(2,1)S(1)}, bf16[3,1,256,128]{3,2,1,0:T(8,128)(2,1)S(1)}, u32[]{:S(2)}, u32[]{:S(2)}) collective-permute-start(bf16[3,1,256,128]{3,2,1,0:T(8,128)(2,1)S(1)} %get-tuple-element.33), channel_id=1, source_target_pairs={{1,0},{2,1},{3,2},{5,4},{6,5},{7,6},{9,8},{10,9},{11,10},{13,12},{... | collective-permute-start | bytes 589832 | tf_op jit(solution)/shard_map/ppermute | solution.py:170
  29.3 2.1 %copy-start.2 = (f32[2,256,128]{2,1,0:T(8,128)S(1)}, f32[2,256,128]{2,1,0:T(8,128)}, u32[]{:S(2)}) copy-start(f32[2,256,128]{2,1,0:T(8,128)} %shard_map.92) | copy-start | bytes 786436
  32.2 18.0 %collective-permute-start.4 = (bf16[1,2,256,128]{3,2,1,0:T(8,128)(2,1)}, bf16[1,2,256,128]{3,2,1,0:T(8,128)(2,1)S(1)}, u32[]{:S(2)}, u32[]{:S(2)}) collective-permute-start(bf16[1,2,256,128]{3,2,1,0:T(8,128)(2,1)} %bitcast.16), channel_id=1, source_target_pairs={{0,4},{4,8},{8,12},{1,5},{5,9},{9,13},{2,6},{6,10},{10,14},{3,7},{... | collective-permute-start | bytes 393224 | tf_op jit(solution)/shard_map/ppermute | solution.py:169
  36.7 13.4 %collective-permute-start.5 = (bf16[1,2,256,128]{3,2,1,0:T(8,128)(2,1)}, bf16[1,2,256,128]{3,2,1,0:T(8,128)(2,1)S(1)}, u32[]{:S(2)}, u32[]{:S(2)}) collective-permute-start(bf16[1,2,256,128]{3,2,1,0:T(8,128)(2,1)} %bitcast.16), channel_id=1, source_target_pairs={{4,0},{8,4},{12,8},{5,1},{9,5},{13,9},{6,2},{10,6},{14,10},{7,3},{... | collective-permute-start | bytes 393224 | tf_op jit(solution)/shard_map/ppermute | solution.py:170
  45.2 9.4 %collective-permute-start.16 = (f32[60416]{0:T(1024)S(1)}, f32[60416]{0:T(1024)S(1)}, u32[]{:S(2)}, u32[]{:S(2)}) collective-permute-start(f32[60416]{0:T(1024)S(1)} %pad_maximum_fusion.4), channel_id=1, source_target_pairs={{0,1},{1,0},{2,3},{3,2},{4,5},{5,4},{6,7},{7,6},{8,9},{9,8},{10,11... | collective-permute-start | bytes 725000 | tf_op jit(solution)/shard_map/ppermute | solution.py:139
  51.2 6.0 %collective-permute-start.6 = (bf16[3,1,256,128]{3,2,1,0:T(8,128)(2,1)S(1)}, bf16[3,1,256,128]{3,2,1,0:T(8,128)(2,1)S(1)}, u32[]{:S(2)}, u32[]{:S(2)}) collective-permute-start(bf16[3,1,256,128]{3,2,1,0:T(8,128)(2,1)S(1)} %get-tuple-element.30), channel_id=1, source_target_pairs={{0,1},{1,2},{2,3},{4,5},{5,6},{6,7},{8,9},{9,10},{10,11},{12,13},{... | collective-permute-start | bytes 589832 | tf_op jit(solution)/shard_map/ppermute | solution.py:169
  53.1 4.0 %collective-permute-start.7 = (bf16[3,1,256,128]{3,2,1,0:T(8,128)(2,1)S(1)}, bf16[3,1,256,128]{3,2,1,0:T(8,128)(2,1)S(1)}, u32[]{:S(2)}, u32[]{:S(2)}) collective-permute-start(bf16[3,1,256,128]{3,2,1,0:T(8,128)(2,1)S(1)} %get-tuple-element.31), channel_id=1, source_target_pairs={{1,0},{2,1},{3,2},{5,4},{6,5},{7,6},{9,8},{10,9},{11,10},{13,12},{... | collective-permute-start | bytes 589832 | tf_op jit(solution)/shard_map/ppermute | solution.py:170
  54.7 11.1 %collective-permute-start.17 = (f32[30208]{0:T(1024)S(1)}, f32[30208]{0:T(1024)S(1)}, u32[]{:S(2)}, u32[]{:S(2)}) collective-permute-start(f32[30208]{0:T(1024)S(1)} %pad_maximum_fusion.6), channel_id=1, source_target_pairs={{0,2},{1,3},{2,0},{3,1},{4,6},{5,7},{6,4},{7,5},{8,10},{9,11},{10,... | collective-permute-start | bytes 362504 | tf_op jit(solution)/shard_map/ppermute | solution.py:139
  59.0 6.6 %copy-start.5 = (bf16[256,256]{1,0:T(8,128)(2,1)S(1)}, bf16[256,256]{1,0:T(8,128)(2,1)}, u32[]{:S(2)}) copy-start(bf16[256,256]{1,0:T(8,128)(2,1)} %param.7) | copy-start | bytes 393220
  65.9 4.9 %collective-permute-start.18 = (f32[15104]{0:T(1024)S(1)}, f32[15104]{0:T(1024)S(1)}, u32[]{:S(2)}, u32[]{:S(2)}) collective-permute-start(f32[15104]{0:T(1024)S(1)} %pad_maximum_fusion.8), channel_id=1, source_target_pairs={{0,4},{4,0},{8,12},{12,8},{1,5},{5,1},{9,13},{13,9},{2,6},{6,2},{1... | collective-permute-start | bytes 181256 | tf_op jit(solution)/shard_map/ppermute | solution.py:139
  70.9 7.2 %collective-permute-start.19 = (f32[7552]{0:T(1024)S(1)}, f32[7552]{0:T(1024)S(1)}, u32[]{:S(2)}, u32[]{:S(2)}) collective-permute-start(f32[7552]{0:T(1024)S(1)} %pad_maximum_fusion.9), channel_id=1, source_target_pairs={{0,8},{4,12},{8,0},{12,4},{1,9},{5,13},{9,1},{13,5},{2,10},{6,14},... | collective-permute-start | bytes 90632 | tf_op jit(solution)/shard_map/ppermute | solution.py:139
  74.2 5.0 %collective-permute-start.8 = (f32[32768]{0:T(1024)S(1)}, f32[32768]{0:T(1024)S(1)}, u32[]{:S(2)}, u32[]{:S(2)}) collective-permute-start(f32[32768]{0:T(1024)S(1)} %bitcast.112), channel_id=1, source_target_pairs={{0,1},{1,0},{2,3},{3,2},{4,5},{5,4},{6,7},{7,6},{8,9},{9,8},{10,11... | collective-permute-start | bytes 393224 | tf_op jit(solution)/shard_map/ppermute | solution.py:139
  78.1 5.2 %collective-permute-start.20 = (f32[4096]{0:T(1024)S(1)}, f32[4096]{0:T(1024)S(1)}, u32[]{:S(2)}, u32[]{:S(2)}) collective-permute-start(f32[4096]{0:T(1024)S(1)} %slice_add_fusion.7), channel_id=1, source_target_pairs={{0,8},{4,12},{8,0},{12,4},{1,9},{5,13},{9,1},{13,5},{2,10},{6,14},... | collective-permute-start | bytes 49160 | tf_op jit(solution)/shard_map/ppermute | solution.py:149
  79.2 8.2 %collective-permute-start.9 = (f32[16384]{0:T(1024)S(1)}, f32[16384]{0:T(1024)S(1)}, u32[]{:S(2)}, u32[]{:S(2)}) collective-permute-start(f32[16384]{0:T(1024)S(1)} %slice_select_fusion.5), channel_id=1, source_target_pairs={{0,2},{1,3},{2,0},{3,1},{4,6},{5,7},{6,4},{7,5},{8,10},{9,11},{10,... | collective-permute-start | bytes 196616 | tf_op jit(solution)/shard_map/ppermute | solution.py:139
  83.3 4.0 %collective-permute-start.21 = (f32[8192]{0:T(1024)S(1)}, f32[8192]{0:T(1024)S(1)}, u32[]{:S(2)}, u32[]{:S(2)}) collective-permute-start(f32[8192]{0:T(1024)S(1)} %maximum_select_fusion.14), channel_id=1, source_target_pairs={{0,4},{4,0},{8,12},{12,8},{1,5},{5,1},{9,13},{13,9},{2,6},{6,2},{1... | collective-permute-start | bytes 98312 | tf_op jit(solution)/shard_map/ppermute | solution.py:149
  87.4 4.0 %collective-permute-start.10 = (f32[8192]{0:T(1024)S(1)}, f32[8192]{0:T(1024)S(1)}, u32[]{:S(2)}, u32[]{:S(2)}) collective-permute-start(f32[8192]{0:T(1024)S(1)} %slice_select_fusion.8), channel_id=1, source_target_pairs={{0,4},{4,0},{8,12},{12,8},{1,5},{5,1},{9,13},{13,9},{2,6},{6,2},{1... | collective-permute-start | bytes 98312 | tf_op jit(solution)/shard_map/ppermute | solution.py:139
  89.3 9.0 %collective-permute-start.22 = (f32[19840]{0:T(1024)S(1)}, f32[19840]{0:T(1024)S(1)}, u32[]{:S(2)}, u32[]{:S(2)}) collective-permute-start(f32[19840]{0:T(1024)S(1)} %pad_maximum_fusion.7), channel_id=1, source_target_pairs={{0,2},{1,3},{2,0},{3,1},{4,6},{5,7},{6,4},{7,5},{8,10},{9,11},{10,... | collective-permute-start | bytes 238088 | tf_op jit(solution)/shard_map/ppermute | solution.py:149
  91.4 4.7 %collective-permute-start.11 = (f32[4096]{0:T(1024)S(1)}, f32[4096]{0:T(1024)S(1)}, u32[]{:S(2)}, u32[]{:S(2)}) collective-permute-start(f32[4096]{0:T(1024)S(1)} %slice_select_fusion.12), channel_id=1, source_target_pairs={{0,8},{4,12},{8,0},{12,4},{1,9},{5,13},{9,1},{13,5},{2,10},{6,14},... | collective-permute-start | bytes 49160 | tf_op jit(solution)/shard_map/ppermute | solution.py:139
  96.1 4.6 %collective-permute-start.12 = (f32[4096]{0:T(1024)S(1)}, f32[4096]{0:T(1024)S(1)}, u32[]{:S(2)}, u32[]{:S(2)}) collective-permute-start(f32[4096]{0:T(1024)S(1)} %select_add_fusion.2), channel_id=1, source_target_pairs={{0,8},{4,12},{8,0},{12,4},{1,9},{5,13},{9,1},{13,5},{2,10},{6,14},... | collective-permute-start | bytes 49160 | tf_op jit(solution)/shard_map/ppermute | solution.py:149
  98.5 10.6 %collective-permute-start.23 = (f32[39680]{0:T(1024)S(1)}, f32[39680]{0:T(1024)S(1)}, u32[]{:S(2)}, u32[]{:S(2)}) collective-permute-start(f32[39680]{0:T(1024)S(1)} %pad_maximum_fusion.5), channel_id=1, source_target_pairs={{0,1},{1,0},{2,3},{3,2},{4,5},{5,4},{6,7},{7,6},{8,9},{9,8},{10,11... | collective-permute-start | bytes 476168 | tf_op jit(solution)/shard_map/ppermute | solution.py:149
  100.7 3.9 %collective-permute-start.13 = (f32[8192]{0:T(1024)S(1)}, f32[8192]{0:T(1024)S(1)}, u32[]{:S(2)}, u32[]{:S(2)}) collective-permute-start(f32[8192]{0:T(1024)S(1)} %maximum_select_fusion.12), channel_id=1, source_target_pairs={{0,4},{4,0},{8,12},{12,8},{1,5},{5,1},{9,13},{13,9},{2,6},{6,2},{1... | collective-permute-start | bytes 98312 | tf_op jit(solution)/shard_map/ppermute | solution.py:149
  104.7 4.3 %collective-permute-start.14 = (f32[16384]{0:T(1024)S(1)}, f32[16384]{0:T(1024)S(1)}, u32[]{:S(2)}, u32[]{:S(2)}) collective-permute-start(f32[16384]{0:T(1024)S(1)} %maximum_select_fusion.8), channel_id=1, source_target_pairs={{0,2},{1,3},{2,0},{3,1},{4,6},{5,7},{6,4},{7,5},{8,10},{9,11},{10,... | collective-permute-start | bytes 196616 | tf_op jit(solution)/shard_map/ppermute | solution.py:149
  109.0 2.2 %collective-permute-start.15 = (f32[32768]{0:T(1024)S(1)}, f32[32768]{0:T(1024)S(1)}, u32[]{:S(2)}, u32[]{:S(2)}) collective-permute-start(f32[32768]{0:T(1024)S(1)} %maximum_select_fusion.2), channel_id=1, source_target_pairs={{0,1},{1,0},{2,3},{3,2},{4,5},{5,4},{6,7},{7,6},{8,9},{9,8},{10,11... | collective-permute-start | bytes 393224 | tf_op jit(solution)/shard_map/ppermute | solution.py:149

commit v11 on v8

--- a/solution.py
+++ b/solution.py
@@ -21,14 +21,15 @@
     return jnp.where(lane == edge, jnp.zeros_like(rolled), rolled)
 
 
-def conv_body(ext_ref, w_hbm, out_ref, w_vmem, sems):
+def conv_body(block_ref, below_ref, above_ref, before_ref, after_ref, w_hbm, out_ref, w_vmem, sems):
+    pieces = (block_ref, below_ref, above_ref, before_ref, after_ref)
     height, channels = out_ref.shape[0], out_ref.shape[1]
     copies = [pltpu.make_async_copy(w_hbm.at[k], w_vmem.at[k], sems.at[k]) for k in range(9)]
     for copy in copies:
         copy.start()
     parts = None
     for dz, dy in itertools.product(range(3), repeat=2):
-        rows = jnp.concatenate([ext_ref[dz, dy + y] for y in range(height)], axis=1)
+        rows = jnp.concatenate([source_row(pieces, dz, dy + y) for y in range(height)], axis=1)
         copies[dz * 3 + dy].wait()
         product = jnp.dot(w_vmem[dz * 3 + dy], rows, preferred_element_type=jnp.float32)
         parts = product if parts is None else parts + product
@@ -41,24 +42,24 @@
         )
 
 
-def conv_call(ext, weights):
-    _, rows, channels, width = ext.shape
-    height = rows - 2
+def conv_call(pieces, weights):
+    _, height, channels, width = pieces[0].shape
     return pl.pallas_call(
         conv_body,
         out_shape=jax.ShapeDtypeStruct((height, channels, width), jnp.float32),
-        in_specs=[pl.BlockSpec(memory_space=pltpu.VMEM), pl.BlockSpec(memory_space=pl.ANY)],
+        in_specs=[pl.BlockSpec(memory_space=pltpu.VMEM)] * 5 + [pl.BlockSpec(memory_space=pl.ANY)],
         out_specs=pl.BlockSpec(memory_space=pltpu.VMEM),
         scratch_shapes=[pltpu.VMEM(weights.shape, weights.dtype), pltpu.SemaphoreType.DMA((9,))],
         cost_estimate=pl.CostEstimate(
             flops=2 * 27 * channels * channels * height * width,
             transcendentals=0,
-            bytes_accessed=ext.size * 2 + weights.size * 2 + height * channels * width * 4,
+            bytes_accessed=sum(p.size for p in pieces) * 2 + weights.size * 2 + height * channels * width * 4,
         ),
-    )(ext, weights)
-
-
-def wgrad_body(act_ref, delta_ref, mask_ref, sel_ref, out_ref):
+    )(*pieces, weights)
+
+
+def wgrad_body(block_ref, below_ref, above_ref, before_ref, after_ref, delta_ref, out_ref):
+    pieces = (block_ref, below_ref, above_ref, before_ref, after_ref)
     height, channels = delta_ref.shape[0], delta_ref.shape[1]
     stacked = []
     for y in range(height):
@@ -69,10 +70,14 @@
             )
         )
     stacked = jnp.concatenate(stacked, axis=1)
-    mask = mask_ref[...]
+    rows_of = lax.broadcasted_iota(jnp.int32, (channels, channels), 0) >> 3
+    cols_of = lax.broadcasted_iota(jnp.int32, (channels, channels), 1) >> 3
+    mask = jnp.where(rows_of == cols_of, 1.0, 0.0).astype(jnp.float32)
+    entry = lax.broadcasted_iota(jnp.int32, (LANES, LANES), 0) & (GW - 1)
+    column = lax.broadcasted_iota(jnp.int32, (LANES, LANES), 1)
     totals = [jnp.zeros((channels, LANES), jnp.float32) for _ in range(out_ref.shape[0])]
     for dz, dy in itertools.product(range(3), repeat=2):
-        rows = jnp.concatenate([act_ref[dz, dy + y] for y in range(height)], axis=1)
+        rows = jnp.concatenate([source_row(pieces, dz, dy + y) for y in range(height)], axis=1)
         grads = lax.dot_general(
             stacked, rows, (((1,), (1,)), ((), ())), preferred_element_type=jnp.float32
         )
@@ -84,7 +89,8 @@
                 folded = folded + picked[:, start : start + LANES]
             high = folded.astype(jnp.bfloat16)
             low = (folded - high.astype(jnp.float32)).astype(jnp.bfloat16)
-            sel = sel_ref[tap % TAPS_PER_BLOCK]
+            slot = (tap % TAPS_PER_BLOCK) * GW
+            sel = jnp.where(column == entry + slot, 1.0, 0.0).astype(jnp.bfloat16)
             totals[tap // TAPS_PER_BLOCK] += jnp.dot(
                 high, sel, preferred_element_type=jnp.float32
             ) + jnp.dot(low, sel, preferred_element_type=jnp.float32)
@@ -92,26 +98,20 @@
         out_ref[n] = total
 
 
-def wgrad_call(act_ext, delta):
+def wgrad_call(pieces, delta):
     height, channels, width = delta.shape
     blocks = -(-27 // TAPS_PER_BLOCK)
-    group_of = jnp.arange(channels) // GW
-    mask = (group_of[:, None] == group_of[None, :]).astype(jnp.float32)
-    lane = jnp.arange(LANES)
-    sel = (
-        lane[None, None, :] == jnp.arange(TAPS_PER_BLOCK)[:, None, None] * GW + (lane % GW)[None, :, None]
-    ).astype(jnp.bfloat16)
     out = pl.pallas_call(
         wgrad_body,
         out_shape=jax.ShapeDtypeStruct((blocks, channels, LANES), jnp.float32),
-        in_specs=[pl.BlockSpec(memory_space=pltpu.VMEM)] * 4,
+        in_specs=[pl.BlockSpec(memory_space=pltpu.VMEM)] * 6,
         out_specs=pl.BlockSpec(memory_space=pltpu.VMEM),
         cost_estimate=pl.CostEstimate(
             flops=2 * 27 * channels * channels * height * width + 4 * 27 * channels * LANES * LANES,
             transcendentals=0,
-            bytes_accessed=act_ext.size * 2 + delta.size * 2 + blocks * channels * LANES * 4,
+            bytes_accessed=sum(p.size for p in pieces) * 2 + delta.size * 2 + blocks * channels * LANES * 4,
         ),
-    )(act_ext, delta, mask, sel)
+    )(*pieces, delta)
     return out.transpose(1, 0, 2).reshape(channels, blocks * LANES)[:, : 27 * GW]
 
 
@@ -161,15 +161,30 @@
 
 
 def halo(block):
-    for axis, dim in (("grp", 0), ("sub", 1)):
-        count = lax.axis_size(axis)
-        up = [(i, i + 1) for i in range(count - 1)]
-        down = [(i + 1, i) for i in range(count - 1)]
-        size = block.shape[dim]
-        low = lax.ppermute(lax.slice_in_dim(block, size - 1, size, axis=dim), axis, up)
-        high = lax.ppermute(lax.slice_in_dim(block, 0, 1, axis=dim), axis, down)
-        block = jnp.concatenate([low, block, high], axis=dim)
-    return block
+    count = lax.axis_size("grp")
+    up = [(i, i + 1) for i in range(count - 1)]
+    down = [(i + 1, i) for i in range(count - 1)]
+    depth, height = block.shape[0], block.shape[1]
+    below = lax.ppermute(block[depth - 1 :], "grp", up)
+    above = lax.ppermute(block[:1], "grp", down)
+    count = lax.axis_size("sub")
+    up = [(i, i + 1) for i in range(count - 1)]
+    down = [(i + 1, i) for i in range(count - 1)]
+    last = jnp.concatenate([below[:, height - 1 :], block[:, height - 1 :], above[:, height - 1 :]])
+    first = jnp.concatenate([below[:, :1], block[:, :1], above[:, :1]])
+    before = lax.ppermute(last, "sub", up)
+    after = lax.ppermute(first, "sub", down)
+    return block, below, above, before, after
+
+
+def source_row(pieces, dz, yy):
+    block, below, above, before, after = pieces
+    height = block.shape[1]
+    if yy == 0:
+        return before[dz, 0]
+    if yy == height + 1:
+        return after[dz, 0]
+    return (below, block, above)[dz][0, yy - 1]
 
 
 def silu_slope(values):
@@ -213,8 +228,9 @@
         first_weight, flattened, contract_lead, preferred_element_type=jnp.float32
     )
     first_act = rounded(jax.nn.silu(first_pre))
-    act_ext = halo(to_rows(first_act))
-    group_pre = conv_call(act_ext, forward_kernel)
+    assert depth == 1
+    act_pieces = halo(to_rows(first_act))
+    group_pre = conv_call(act_pieces, forward_kernel)
     group_act = rounded(jax.nn.silu(group_pre))
     act_flat = from_rows(group_act)
     summed = flattened.astype(jnp.float32) + lax.dot_general(
@@ -227,9 +243,9 @@
     )
     hidden_grad = rounded(jnp.dot(third_weight, third_delta, preferred_element_type=jnp.float32))
     group_delta = rounded(to_rows(hidden_grad)[0].astype(jnp.float32) * silu_slope(group_pre))
-    delta_ext = halo(group_delta[None])
-    inner_grad = from_rows(rounded(conv_call(delta_ext, backward_kernel)))
-    kernel_part = wgrad_call(act_ext, group_delta)
+    delta_pieces = halo(group_delta[None])
+    inner_grad = from_rows(rounded(conv_call(delta_pieces, backward_kernel)))
+    kernel_part = wgrad_call(act_pieces, group_delta)
     first_delta = rounded(inner_grad.astype(jnp.float32) * silu_slope(first_pre))
     first_part = lax.dot_general(
         flattened, first_delta, contract_tail, preferred_element_type=jnp.float32

time: 107 us -> 101 us (0.944)
  waiting for transfers between devices: 25 us -> 18.7 us
  other arithmetic: 10.6 us -> 5.49 us
  local copies, waits for them, and re-layouts: 7.39 us -> 10.6 us
  starting transfers between devices: 37.2 us -> 40.2 us
    concatenate x4, other arithmetic: 3.92 us -> 0.1 us  [the longest x2 0.05 us: halo(): first = jnp.concatenate([below[:, :1], block[:, :1], above[:, :1]])]
    ppermute x8, waiting for transfers between devices: 4.06 us -> 1.14 us  [the longest x2 0.63 us: halo(): before = lax.ppermute(last, 'sub', up)]
    ppermute x4, starting transfers between devices: 9.8 us -> 12.6 us  [tree_sum(): got = lax.ppermute(jnp.concatenate(sends), axis, pairs)]
    ppermute x4, waiting for transfers between devices: 10.6 us -> 8.74 us  [tree_sum(): got = lax.ppermute(jnp.concatenate(sends), axis, pairs)]
    ppermute x4, starting transfers between devices: 5.35 us -> 6.86 us  [tree_sum(): lax.ppermute(jnp.concatenate([pieces[n] for n in members]), axis, pairs)]
    ppermute x4, waiting for transfers between devices: 10.3 us -> 8.79 us  [tree_sum(): lax.ppermute(jnp.concatenate([pieces[n] for n in members]), axis, pairs)]
    unnamed x19 -> x33, local copies, waits for them, and re-layouts: 2.94 us -> 4.32 us
    ppermute x8, starting transfers between devices: 22.1 us -> 20.8 us  [the longest x2 9.01 us: halo(): below = lax.ppermute(block[depth - 1:], 'grp', up)]
  transfers between devices with their start and end apart: 16 -> 16, of which waited for: 10 -> 10; matrix products, arithmetic and copies ran while one was open for 13% -> 14% of each run, Pallas kernels for 4% -> 4%
where the time goes in v11:
time: 101 us
  starting transfers between devices  40.2 us (40%)
  waiting for transfers between devices  18.7 us (19%)
  Pallas kernels  15.2 us (15%)
  local copies, waits for them, and re-layouts  10.6 us (10%)
  matrix products  9.01 us (9%)
  other arithmetic  5.49 us (5%)
  between operations  1.6 us (2%)
    ppermute x4, starting transfers between devices, tree_sum(): got = lax.ppermute(jnp.concatenate(sends), axis, pairs)  12.6 us
    pallas_call x2, Pallas kernels, conv_call(): pl.pallas_call(conv_body, out_shape=jax.ShapeDtypeStruct((height, channel...  10.8 us
    ppermute x2, starting transfers between devices, halo(): below = lax.ppermute(block[depth - 1:], 'grp', up)  9.01 us
    ppermute x4, waiting for transfers between devices, tree_sum(): lax.ppermute(jnp.concatenate([pieces[n] for n in members]), axis, pairs)  8.79 us
    ppermute x4, waiting for transfers between devices, tree_sum(): got = lax.ppermute(jnp.concatenate(sends), axis, pairs)  8.74 us
    ppermute x4, starting transfers between devices, tree_sum(): lax.ppermute(jnp.concatenate([pieces[n] for n in members]), axis, pairs)  6.86 us
    ppermute x2, starting transfers between devices, halo(): before = lax.ppermute(last, 'sub', up)  6.59 us
    pallas_call x1, Pallas kernels, wgrad_call(): pl.pallas_call(wgrad_body, out_shape=jax.ShapeDtypeStruct((blocks, channe...  4.39 us
  transfers between devices with their start and end apart: 16, of which 10 were waited for; matrix products, arithmetic and copies ran while one was open for 14% of the time, Pallas kernels for 4%

profile of v11, /device:TPU:0, one launch (start us, length us, event | category | flops | bytes accessed | tf_op | source)
XLA Modules:
  0.0 100.8 jit_solution(15513547447367996864)
XLA Ops:
  0.6 1.0 %copy.74 = bf16[256,1,2,128]{0,3,2,1:T(8,128)(2,1)S(1)} copy(bf16[256,1,2,128]{3,2,1,0:T(2,128)(2,1)} %param.5) | data formatting | bytes 262144 | tf_op args[0]
  1.7 1.1 %reduce-precision_convert_fusion.2 = (bf16[256,256]{0,1:T(8,128)(2,1)S(1)}, f32[256,256]{0,1:T(8,128)S(1)}) fusion(bf16[256,256]{0,1:T(8,128)(2,1)S(1)} %bitcast.100, bf16[256,256]{1,0:T(8,128)(2,1)} %param.7), kind=kOutput, calls=%fused_computation.33 | convolution fusion | flops 33947648 | bytes 655360 | tf_op jit(solution)/shard_map/dot_general | solution.py:227
  3.0 4.9 %collective-permute-start = (bf16[1,2,256,128]{3,2,1,0:T(8,128)(2,1)S(1)}, bf16[1,2,256,128]{3,2,1,0:T(8,128)(2,1)S(1)}, u32[]{:S(2)}, u32[]{:S(2)}) collective-permute-start(bf16[1,2,256,128]{3,2,1,0:T(8,128)(2,1)S(1)} %bitcast.90), channel_id=1, source_target_pairs={{0,4},{4,8},{8,12},{1,5},{5,9},{9,13},{2,6},{6,10},{10,14},{3,7},{... | collective-permute-start | bytes 393224 | tf_op jit(solution)/shard_map/ppermute | solution.py:168
  7.9 1.3 %collective-permute-start.1 = (bf16[1,2,256,128]{3,2,1,0:T(8,128)(2,1)S(1)}, bf16[1,2,256,128]{3,2,1,0:T(8,128)(2,1)S(1)}, u32[]{:S(2)}, u32[]{:S(2)}) collective-permute-start(bf16[1,2,256,128]{3,2,1,0:T(8,128)(2,1)S(1)} %bitcast.91), channel_id=1, source_target_pairs={{4,0},{8,4},{12,8},{5,1},{9,5},{13,9},{6,2},{10,6},{14,10},{7,3},{... | collective-permute-start | bytes 393224 | tf_op jit(solution)/shard_map/ppermute | solution.py:169
  9.4 1.0 %copy.77 = f32[256,1,2,128]{0,3,2,1:T(8,128)S(1)} copy(bf16[256,1,2,128]{3,2,1,0:T(2,128)(2,1)} %param.6) | data formatting | bytes 393216 | tf_op jit(solution)/shard_map/convert_element_type | solution.py:240
  10.4 3.8 %fusion = bf16[27,256,256]{2,1,0:T(8,128)(2,1)} fusion(f32[256,256]{1,0:T(8,128)S(1)} %compare_convert_fusion, bf16[256,8,27]{0,1,2:T(8,128)(2,1)} %bitcast.110, s32[256]{0:T(256)S(1)} %and_select_fusion.1), kind=kOutput, calls=%fused_computation.1 | convolution fusion | flops 31852544 | bytes 3912704 | tf_op jit(solution)/shard_map/ojt,ji->toi/dot_general | solution.py:201
  14.3 0.5 collective-permute-done.1.above_ref
  14.8 1.3 %collective-permute-start.3 = (bf16[3,1,256,128]{3,2,1,0:T(8,128)(2,1)S(1)}, bf16[3,1,256,128]{3,2,1,0:T(8,128)(2,1)S(1)}, u32[]{:S(2)}, u32[]{:S(2)}) collective-permute-start(bf16[3,1,256,128]{3,2,1,0:T(8,128)(2,1)S(1)} %pad_maximum_fusion.3), channel_id=1, source_target_pairs={{1,0},{2,1},{3,2},{5,4},{6,5},{7,6},{9,8},{10,9},{11,10},{13,12},{... | collective-permute-start | bytes 589832 | tf_op jit(solution)/shard_map/ppermute | solution.py:176
  16.2 3.0 %collective-permute-start.2 = (bf16[3,1,256,128]{3,2,1,0:T(8,128)(2,1)S(1)}, bf16[3,1,256,128]{3,2,1,0:T(8,128)(2,1)S(1)}, u32[]{:S(2)}, u32[]{:S(2)}) collective-permute-start(bf16[3,1,256,128]{3,2,1,0:T(8,128)(2,1)S(1)} %pad_maximum_fusion.2), channel_id=1, source_target_pairs={{0,1},{1,2},{2,3},{4,5},{5,6},{6,7},{8,9},{9,10},{10,11},{12,13},{... | collective-permute-start | bytes 589832 | tf_op jit(solution)/shard_map/ppermute | solution.py:175
  19.2 2.9 %multiply_convert_fusion = bf16[256,256,27]{1,0,2:T(8,128)(2,1)} fusion(f32[256,256]{1,0:T(8,128)S(1)} %compare_convert_fusion, bf16[256,8,27]{0,1,2:T(8,128)(2,1)S(1)} %bitcast.111, s32[256]{0:T(256)S(1)} %and_select_fusion.1), kind=kOutput, calls=%fused_computation.2 | convolution fusion | flops 31907840 | bytes 3912704 | tf_op jit(solution)/shard_map/ji,ojt->tio/dot_general | solution.py:202
  22.2 0.6 copy-done.8
  22.9 5.4 %shard_map.92 = f32[2,256,128]{2,1,0:T(8,128)} custom-call(bf16[1,2,256,128]{3,2,1,0:T(8,128)(2,1)} %bitcast.93, bf16[1,2,256,128]{3,2,1,0:T(8,128)(2,1)} %copy-done.5, bf16[1,2,256,128]{3,2,1,0:T(8,128)(2,1)} %copy-done.6, bf16[3,1,256,128]{3,2,1,0:T(8,128)(2,1)} %copy-done.9, bf16[3,1,256,128]{3,2,1,0:T(8,128)(2,1)} %copy-done.8, bf16[9,768,256]{2,1,0:T(8,128)(2,1)} %bitcast.88), custom_call_target="tpu_custom_call" | custom-call | flops 905969664 | bytes 4587520 | tf_op jit(solution)/shard_map/pallas_call | solution.py:47
  28.3 1.1 %fusion.15 = bf16[256,2,128]{2,0,1:T(8,128)(2,1)S(1)} fusion(f32[2,256,128]{2,1,0:T(8,128)} %shard_map.92), kind=kLoop, calls=%fused_computation.50 | loop fusion | flops 393216 | bytes 393216 | tf_op jit(solution)/shard_map/transpose | solution.py:224
  29.5 0.3 fusion.13
  30.2 0.8 fusion.9.delta_ref
  30.9 4.1 %collective-permute-start.4 = (bf16[1,2,256,128]{3,2,1,0:T(8,128)(2,1)}, bf16[1,2,256,128]{3,2,1,0:T(8,128)(2,1)S(1)}, u32[]{:S(2)}, u32[]{:S(2)}) collective-permute-start(bf16[1,2,256,128]{3,2,1,0:T(8,128)(2,1)} %bitcast.16.block_ref), channel_id=1, source_target_pairs={{0,4},{4,8},{8,12},{1,5},{5,9},{9,13},{2,6},{6,10},{10,14},{3,7},{... | collective-permute-start | bytes 393224 | tf_op jit(solution)/shard_map/ppermute | solution.py:168
  35.0 1.3 %collective-permute-start.5 = (bf16[1,2,256,128]{3,2,1,0:T(8,128)(2,1)}, bf16[1,2,256,128]{3,2,1,0:T(8,128)(2,1)S(1)}, u32[]{:S(2)}, u32[]{:S(2)}) collective-permute-start(bf16[1,2,256,128]{3,2,1,0:T(8,128)(2,1)} %bitcast.16.block_ref), channel_id=1, source_target_pairs={{4,0},{8,4},{12,8},{5,1},{9,5},{13,9},{6,2},{10,6},{14,10},{7,3},{... | collective-permute-start | bytes 393224 | tf_op jit(solution)/shard_map/ppermute | solution.py:169
  36.3 0.2 fusion.38
  36.6 4.4 %shard_map.94 = f32[2,256,128]{2,1,0:T(8,128)} custom-call(bf16[1,2,256,128]{3,2,1,0:T(8,128)(2,1)} %bitcast.94, bf16[1,2,256,128]{3,2,1,0:T(8,128)(2,1)} %copy-done.5, bf16[1,2,256,128]{3,2,1,0:T(8,128)(2,1)} %copy-done.6, bf16[3,1,256,128]{3,2,1,0:T(8,128)(2,1)} %copy-done.9, bf16[3,1,256,128]{3,2,1,0:T(8,128)(2,1)} %copy-done.8, ...), custom_call_target="tpu_custom_call" | custom-call | flops 1358954496 | bytes 1179648 | tf_op jit(solution)/shard_map/pallas_call | solution.py:104
  40.9 1.1 %copy.85 = f32[256,2,128]{0,2,1:T(8,128)S(1)} copy(f32[256,2,128]{2,0,1:T(8,128)} %bitcast.112) | data formatting | bytes 524288 | tf_op jit(solution)/shard_map/transpose | solution.py:115
  43.3 0.9 fusion.31
  44.3 1.3 %collective-permute-start.7 = (bf16[3,1,256,128]{3,2,1,0:T(8,128)(2,1)S(1)}, bf16[3,1,256,128]{3,2,1,0:T(8,128)(2,1)S(1)}, u32[]{:S(2)}, u32[]{:S(2)}) collective-permute-start(bf16[3,1,256,128]{3,2,1,0:T(8,128)(2,1)S(1)} %pad_maximum_fusion.5), channel_id=1, source_target_pairs={{1,0},{2,1},{3,2},{5,4},{6,5},{7,6},{9,8},{10,9},{11,10},{13,12},{... | collective-permute-start | bytes 589832 | tf_op jit(solution)/shard_map/ppermute | solution.py:176
  45.6 3.5 %collective-permute-start.6 = (bf16[3,1,256,128]{3,2,1,0:T(8,128)(2,1)S(1)}, bf16[3,1,256,128]{3,2,1,0:T(8,128)(2,1)S(1)}, u32[]{:S(2)}, u32[]{:S(2)}) collective-permute-start(bf16[3,1,256,128]{3,2,1,0:T(8,128)(2,1)S(1)} %pad_maximum_fusion.4), channel_id=1, source_target_pairs={{0,1},{1,2},{2,3},{4,5},{5,6},{6,7},{8,9},{9,10},{10,11},{12,13},{... | collective-permute-start | bytes 589832 | tf_op jit(solution)/shard_map/ppermute | solution.py:175
  49.4 0.6 collective-permute-done.6.before_ref
  50.1 0.6 copy-done.11
  50.7 5.4 %shard_map.93 = f32[2,256,128]{2,1,0:T(8,128)} custom-call(bf16[1,2,256,128]{3,2,1,0:T(8,128)(2,1)} %bitcast.16.block_ref, bf16[1,2,256,128]{3,2,1,0:T(8,128)(2,1)} %copy-done.3, bf16[1,2,256,128]{3,2,1,0:T(8,128)(2,1)} %copy-done.4, bf16[3,1,256,128]{3,2,1,0:T(8,128)(2,1)} %copy-done.11, bf16[3,1,256,128]{3,2,1,0:T(8,128)(2,1)} %copy-done.10, ...), custom_call_target="tpu_custom_call" | custom-call | flops 905969664 | bytes 4587520 | tf_op jit(solution)/shard_map/pallas_call | solution.py:47
  56.1 1.0 convert_bitcast_fusion
  57.3 0.2 convolution_bitcast_fusion
  57.8 4.0 %collective-permute-start.8 = (f32[93184]{0:T(1024)S(1)}, f32[93184]{0:T(1024)S(1)}, u32[]{:S(2)}, u32[]{:S(2)}) collective-permute-start(f32[93184]{0:T(1024)S(1)} %pad_maximum_fusion), channel_id=1, source_target_pairs={{0,1},{1,0},{2,3},{3,2},{4,5},{5,4},{6,7},{7,6},{8,9},{9,8},{10,11... | collective-permute-start | bytes 1118216 | tf_op jit(solution)/shard_map/ppermute | solution.py:139
  62.3 0.9 collective-permute-done.8
  63.3 2.8 %collective-permute-start.9 = (f32[46592]{0:T(1024)S(1)}, f32[46592]{0:T(1024)S(1)}, u32[]{:S(2)}, u32[]{:S(2)}) collective-permute-start(f32[46592]{0:T(1024)S(1)} %pad_maximum_fusion.6), channel_id=1, source_target_pairs={{0,2},{1,3},{2,0},{3,1},{4,6},{5,7},{6,4},{7,5},{8,10},{9,11},{10,... | collective-permute-start | bytes 559112 | tf_op jit(solution)/shard_map/ppermute | solution.py:139
  66.1 5.0 %collective-permute-done.9 = f32[46592]{0:T(1024)S(1)} collective-permute-done((f32[46592]{0:T(1024)S(1)}, f32[46592]{0:T(1024)S(1)}, u32[]{:S(2)}, u32[]{:S(2)}) %collective-permute-start.9) | collective-permute-done | bytes 186400 | tf_op jit(solution)/shard_map/ppermute | solution.py:139
  71.2 2.7 %collective-permute-start.10 = (f32[23296]{0:T(1024)S(1)}, f32[23296]{0:T(1024)S(1)}, u32[]{:S(2)}, u32[]{:S(2)}) collective-permute-start(f32[23296]{0:T(1024)S(1)} %pad_maximum_fusion.8), channel_id=1, source_target_pairs={{0,4},{4,0},{8,12},{12,8},{1,5},{5,1},{9,13},{13,9},{2,6},{6,2},{1... | collective-permute-start | bytes 279560 | tf_op jit(solution)/shard_map/ppermute | solution.py:139
  73.9 0.8 copy.99
  74.7 1.8 %collective-permute-done.10 = f32[23296]{0:T(1024)S(1)} collective-permute-done((f32[23296]{0:T(1024)S(1)}, f32[23296]{0:T(1024)S(1)}, u32[]{:S(2)}, u32[]{:S(2)}) %collective-permute-start.10) | collective-permute-done | bytes 93216 | tf_op jit(solution)/shard_map/ppermute | solution.py:139
  76.6 3.1 %collective-permute-start.11 = (f32[11648]{0:T(1024)S(1)}, f32[11648]{0:T(1024)S(1)}, u32[]{:S(2)}, u32[]{:S(2)}) collective-permute-start(f32[11648]{0:T(1024)S(1)} %pad_maximum_fusion.12), channel_id=1, source_target_pairs={{0,8},{4,12},{8,0},{12,4},{1,9},{5,13},{9,1},{13,5},{2,10},{6,14},... | collective-permute-start | bytes 139784 | tf_op jit(solution)/shard_map/ppermute | solution.py:139
  79.9 0.8 copy.100
  80.7 1.1 %collective-permute-done.11 = f32[11648]{0:T(1024)S(1)} collective-permute-done((f32[11648]{0:T(1024)S(1)}, f32[11648]{0:T(1024)S(1)}, u32[]{:S(2)}, u32[]{:S(2)}) %collective-permute-start.11) | collective-permute-done | bytes 46624 | tf_op jit(solution)/shard_map/ppermute | solution.py:139
  81.7 3.0 %collective-permute-start.12 = (f32[8192]{0:T(1024)S(1)}, f32[8192]{0:T(1024)S(1)}, u32[]{:S(2)}, u32[]{:S(2)}) collective-permute-start(f32[8192]{0:T(1024)S(1)} %pad_maximum_fusion.14), channel_id=1, source_target_pairs={{0,8},{4,12},{8,0},{12,4},{1,9},{5,13},{9,1},{13,5},{2,10},{6,14},... | collective-permute-start | bytes 98312 | tf_op jit(solution)/shard_map/ppermute | solution.py:149
  85.1 1.7 %collective-permute-done.12 = f32[8192]{0:T(1024)S(1)} collective-permute-done((f32[8192]{0:T(1024)S(1)}, f32[8192]{0:T(1024)S(1)}, u32[]{:S(2)}, u32[]{:S(2)}) %collective-permute-start.12) | collective-permute-done | bytes 32800 | tf_op jit(solution)/shard_map/ppermute | solution.py:149
  86.8 1.9 %collective-permute-start.13 = (f32[16384]{0:T(1024)S(1)}, f32[16384]{0:T(1024)S(1)}, u32[]{:S(2)}, u32[]{:S(2)}) collective-permute-start(f32[16384]{0:T(1024)S(1)} %pad_maximum_fusion.10), channel_id=1, source_target_pairs={{0,4},{4,0},{8,12},{12,8},{1,5},{5,1},{9,13},{13,9},{2,6},{6,2},{1... | collective-permute-start | bytes 196616 | tf_op jit(solution)/shard_map/ppermute | solution.py:149
  88.8 2.4 %collective-permute-done.13 = f32[16384]{0:T(1024)S(1)} collective-permute-done((f32[16384]{0:T(1024)S(1)}, f32[16384]{0:T(1024)S(1)}, u32[]{:S(2)}, u32[]{:S(2)}) %collective-permute-start.13) | collective-permute-done | bytes 65568 | tf_op jit(solution)/shard_map/ppermute | solution.py:149
  91.2 1.9 %collective-permute-start.14 = (f32[36224]{0:T(1024)S(1)}, f32[36224]{0:T(1024)S(1)}, u32[]{:S(2)}, u32[]{:S(2)}) collective-permute-start(f32[36224]{0:T(1024)S(1)} %pad_maximum_fusion.7), channel_id=1, source_target_pairs={{0,2},{1,3},{2,0},{3,1},{4,6},{5,7},{6,4},{7,5},{8,10},{9,11},{10,... | collective-permute-start | bytes 434696 | tf_op jit(solution)/shard_map/ppermute | solution.py:149
  93.1 3.3 %collective-permute-done.14 = f32[36224]{0:T(1024)S(1)} collective-permute-done((f32[36224]{0:T(1024)S(1)}, f32[36224]{0:T(1024)S(1)}, u32[]{:S(2)}, u32[]{:S(2)}) %collective-permute-start.14) | collective-permute-done | bytes 144928 | tf_op jit(solution)/shard_map/ppermute | solution.py:149
  97.2 1.4 %collective-permute-done.15 = f32[72448]{0:T(1024)S(1)} collective-permute-done((f32[72448]{0:T(1024)S(1)}, f32[72448]{0:T(1024)S(1)}, u32[]{:S(2)}, u32[]{:S(2)}) %collective-permute-start.15) | collective-permute-done | bytes 289824 | tf_op jit(solution)/shard_map/ppermute | solution.py:149
  98.8 0.3 copy.97
  99.2 0.8 fusion.16
  99.9 0.8 fusion.6
  (135 shorter events, 5.0 us)
Async XLA Ops:
  0.6 28.9 %copy-start = (bf16[256,256]{1,0:T(8,128)(2,1)S(1)}, bf16[256,256]{1,0:T(8,128)(2,1)}, u32[]{:S(2)}) copy-start(bf16[256,256]{1,0:T(8,128)(2,1)} %param.9) | copy-start | bytes 393220
  2.8 16.4 %copy-start.7 = (bf16[256,8,3,3,3]{0,1,4,3,2:T(8,128)(2,1)S(1)}, bf16[256,8,3,3,3]{0,1,4,3,2:T(8,128)(2,1)}, u32[]{:S(2)}) copy-start(bf16[256,8,3,3,3]{0,1,4,3,2:T(8,128)(2,1)} %param.8) | copy-start | bytes 331780
  3.0 19.2 %copy-start.2 = (bf16[256,1,2,128]{3,0,2,1:T(8,128)(2,1)}, bf16[256,1,2,128]{3,0,2,1:T(8,128)(2,1)S(1)}, u32[]{:S(2)}) copy-start(bf16[256,1,2,128]{3,0,2,1:T(8,128)(2,1)S(1)} %copy.75) | copy-start | bytes 393220
  3.0 11.3 %collective-permute-start = (bf16[1,2,256,128]{3,2,1,0:T(8,128)(2,1)S(1)}, bf16[1,2,256,128]{3,2,1,0:T(8,128)(2,1)S(1)}, u32[]{:S(2)}, u32[]{:S(2)}) collective-permute-start(bf16[1,2,256,128]{3,2,1,0:T(8,128)(2,1)S(1)} %bitcast.90), channel_id=1, source_target_pairs={{0,4},{4,8},{8,12},{1,5},{5,9},{9,13},{2,6},{6,10},{10,14},{3,7},{... | collective-permute-start | bytes 393224 | tf_op jit(solution)/shard_map/ppermute | solution.py:168
  7.9 6.9 %collective-permute-start.1 = (bf16[1,2,256,128]{3,2,1,0:T(8,128)(2,1)S(1)}, bf16[1,2,256,128]{3,2,1,0:T(8,128)(2,1)S(1)}, u32[]{:S(2)}, u32[]{:S(2)}) collective-permute-start(bf16[1,2,256,128]{3,2,1,0:T(8,128)(2,1)S(1)} %bitcast.91), channel_id=1, source_target_pairs={{4,0},{8,4},{12,8},{5,1},{9,5},{13,9},{6,2},{10,6},{14,10},{7,3},{... | collective-permute-start | bytes 393224 | tf_op jit(solution)/shard_map/ppermute | solution.py:169
  14.3 7.9 %copy-start.5 = (bf16[1,2,256,128]{3,2,1,0:T(8,128)(2,1)}, bf16[1,2,256,128]{3,2,1,0:T(8,128)(2,1)S(1)}, u32[]{:S(2)}) copy-start(bf16[1,2,256,128]{3,2,1,0:T(8,128)(2,1)S(1)} %collective-permute-done.below_ref) | copy-start | bytes 393220
  14.8 7.4 %copy-start.6 = (bf16[1,2,256,128]{3,2,1,0:T(8,128)(2,1)}, bf16[1,2,256,128]{3,2,1,0:T(8,128)(2,1)S(1)}, u32[]{:S(2)}) copy-start(bf16[1,2,256,128]{3,2,1,0:T(8,128)(2,1)S(1)} %collective-permute-done.1.above_ref) | copy-start | bytes 393220
  14.8 7.3 %collective-permute-start.3 = (bf16[3,1,256,128]{3,2,1,0:T(8,128)(2,1)S(1)}, bf16[3,1,256,128]{3,2,1,0:T(8,128)(2,1)S(1)}, u32[]{:S(2)}, u32[]{:S(2)}) collective-permute-start(bf16[3,1,256,128]{3,2,1,0:T(8,128)(2,1)S(1)} %pad_maximum_fusion.3), channel_id=1, source_target_pairs={{1,0},{2,1},{3,2},{5,4},{6,5},{7,6},{9,8},{10,9},{11,10},{13,12},{... | collective-permute-start | bytes 589832 | tf_op jit(solution)/shard_map/ppermute | solution.py:176
  16.2 6.0 %collective-permute-start.2 = (bf16[3,1,256,128]{3,2,1,0:T(8,128)(2,1)S(1)}, bf16[3,1,256,128]{3,2,1,0:T(8,128)(2,1)S(1)}, u32[]{:S(2)}, u32[]{:S(2)}) collective-permute-start(bf16[3,1,256,128]{3,2,1,0:T(8,128)(2,1)S(1)} %pad_maximum_fusion.2), channel_id=1, source_target_pairs={{0,1},{1,2},{2,3},{4,5},{5,6},{6,7},{8,9},{9,10},{10,11},{12,13},{... | collective-permute-start | bytes 589832 | tf_op jit(solution)/shard_map/ppermute | solution.py:175
  22.1 0.7 copy-start.8
  22.1 0.7 copy-start.9
  28.3 1.9 %copy-start.1 = (f32[2,256,128]{2,1,0:T(8,128)S(1)}, f32[2,256,128]{2,1,0:T(8,128)}, u32[]{:S(2)}) copy-start(f32[2,256,128]{2,1,0:T(8,128)} %shard_map.92) | copy-start | bytes 786436
  30.9 13.2 %collective-permute-start.4 = (bf16[1,2,256,128]{3,2,1,0:T(8,128)(2,1)}, bf16[1,2,256,128]{3,2,1,0:T(8,128)(2,1)S(1)}, u32[]{:S(2)}, u32[]{:S(2)}) collective-permute-start(bf16[1,2,256,128]{3,2,1,0:T(8,128)(2,1)} %bitcast.16.block_ref), channel_id=1, source_target_pairs={{0,4},{4,8},{8,12},{1,5},{5,9},{9,13},{2,6},{6,10},{10,14},{3,7},{... | collective-permute-start | bytes 393224 | tf_op jit(solution)/shard_map/ppermute | solution.py:168
  35.0 9.2 %collective-permute-start.5 = (bf16[1,2,256,128]{3,2,1,0:T(8,128)(2,1)}, bf16[1,2,256,128]{3,2,1,0:T(8,128)(2,1)S(1)}, u32[]{:S(2)}, u32[]{:S(2)}) collective-permute-start(bf16[1,2,256,128]{3,2,1,0:T(8,128)(2,1)} %bitcast.16.block_ref), channel_id=1, source_target_pairs={{4,0},{8,4},{12,8},{5,1},{9,5},{13,9},{6,2},{10,6},{14,10},{7,3},{... | collective-permute-start | bytes 393224 | tf_op jit(solution)/shard_map/ppermute | solution.py:169
  44.2 5.9 %copy-start.3 = (bf16[1,2,256,128]{3,2,1,0:T(8,128)(2,1)}, bf16[1,2,256,128]{3,2,1,0:T(8,128)(2,1)S(1)}, u32[]{:S(2)}) copy-start(bf16[1,2,256,128]{3,2,1,0:T(8,128)(2,1)S(1)} %collective-permute-done.4.below_ref) | copy-start | bytes 393220
  44.2 5.8 %copy-start.4 = (bf16[1,2,256,128]{3,2,1,0:T(8,128)(2,1)}, bf16[1,2,256,128]{3,2,1,0:T(8,128)(2,1)S(1)}, u32[]{:S(2)}) copy-start(bf16[1,2,256,128]{3,2,1,0:T(8,128)(2,1)S(1)} %collective-permute-done.5.above_ref) | copy-start | bytes 393220
  44.3 5.1 %collective-permute-start.7 = (bf16[3,1,256,128]{3,2,1,0:T(8,128)(2,1)S(1)}, bf16[3,1,256,128]{3,2,1,0:T(8,128)(2,1)S(1)}, u32[]{:S(2)}, u32[]{:S(2)}) collective-permute-start(bf16[3,1,256,128]{3,2,1,0:T(8,128)(2,1)S(1)} %pad_maximum_fusion.5), channel_id=1, source_target_pairs={{1,0},{2,1},{3,2},{5,4},{6,5},{7,6},{9,8},{10,9},{11,10},{13,12},{... | collective-permute-start | bytes 589832 | tf_op jit(solution)/shard_map/ppermute | solution.py:176
  45.6 4.4 %collective-permute-start.6 = (bf16[3,1,256,128]{3,2,1,0:T(8,128)(2,1)S(1)}, bf16[3,1,256,128]{3,2,1,0:T(8,128)(2,1)S(1)}, u32[]{:S(2)}, u32[]{:S(2)}) collective-permute-start(bf16[3,1,256,128]{3,2,1,0:T(8,128)(2,1)S(1)} %pad_maximum_fusion.4), channel_id=1, source_target_pairs={{0,1},{1,2},{2,3},{4,5},{5,6},{6,7},{8,9},{9,10},{10,11},{12,13},{... | collective-permute-start | bytes 589832 | tf_op jit(solution)/shard_map/ppermute | solution.py:175
  49.4 0.7 copy-start.10
  50.0 0.7 copy-start.11
  57.6 22.1 %copy-start.12 = (bf16[256,256]{1,0:T(8,128)(2,1)S(1)}, bf16[256,256]{1,0:T(8,128)(2,1)}, u32[]{:S(2)}) copy-start(bf16[256,256]{1,0:T(8,128)(2,1)} %param.7) | copy-start | bytes 393220
  57.8 5.3 %collective-permute-start.8 = (f32[93184]{0:T(1024)S(1)}, f32[93184]{0:T(1024)S(1)}, u32[]{:S(2)}, u32[]{:S(2)}) collective-permute-start(f32[93184]{0:T(1024)S(1)} %pad_maximum_fusion), channel_id=1, source_target_pairs={{0,1},{1,0},{2,3},{3,2},{4,5},{5,4},{6,7},{7,6},{8,9},{9,8},{10,11... | collective-permute-start | bytes 1118216 | tf_op jit(solution)/shard_map/ppermute | solution.py:139
  63.3 7.8 %collective-permute-start.9 = (f32[46592]{0:T(1024)S(1)}, f32[46592]{0:T(1024)S(1)}, u32[]{:S(2)}, u32[]{:S(2)}) collective-permute-start(f32[46592]{0:T(1024)S(1)} %pad_maximum_fusion.6), channel_id=1, source_target_pairs={{0,2},{1,3},{2,0},{3,1},{4,6},{5,7},{6,4},{7,5},{8,10},{9,11},{10,... | collective-permute-start | bytes 559112 | tf_op jit(solution)/shard_map/ppermute | solution.py:139
  71.2 5.3 %collective-permute-start.10 = (f32[23296]{0:T(1024)S(1)}, f32[23296]{0:T(1024)S(1)}, u32[]{:S(2)}, u32[]{:S(2)}) collective-permute-start(f32[23296]{0:T(1024)S(1)} %pad_maximum_fusion.8), channel_id=1, source_target_pairs={{0,4},{4,0},{8,12},{12,8},{1,5},{5,1},{9,13},{13,9},{2,6},{6,2},{1... | collective-permute-start | bytes 279560 | tf_op jit(solution)/shard_map/ppermute | solution.py:139
  76.6 5.2 %collective-permute-start.11 = (f32[11648]{0:T(1024)S(1)}, f32[11648]{0:T(1024)S(1)}, u32[]{:S(2)}, u32[]{:S(2)}) collective-permute-start(f32[11648]{0:T(1024)S(1)} %pad_maximum_fusion.12), channel_id=1, source_target_pairs={{0,8},{4,12},{8,0},{12,4},{1,9},{5,13},{9,1},{13,5},{2,10},{6,14},... | collective-permute-start | bytes 139784 | tf_op jit(solution)/shard_map/ppermute | solution.py:139
  81.7 5.0 %collective-permute-start.12 = (f32[8192]{0:T(1024)S(1)}, f32[8192]{0:T(1024)S(1)}, u32[]{:S(2)}, u32[]{:S(2)}) collective-permute-start(f32[8192]{0:T(1024)S(1)} %pad_maximum_fusion.14), channel_id=1, source_target_pairs={{0,8},{4,12},{8,0},{12,4},{1,9},{5,13},{9,1},{13,5},{2,10},{6,14},... | collective-permute-start | bytes 98312 | tf_op jit(solution)/shard_map/ppermute | solution.py:149
  86.8 4.3 %collective-permute-start.13 = (f32[16384]{0:T(1024)S(1)}, f32[16384]{0:T(1024)S(1)}, u32[]{:S(2)}, u32[]{:S(2)}) collective-permute-start(f32[16384]{0:T(1024)S(1)} %pad_maximum_fusion.10), channel_id=1, source_target_pairs={{0,4},{4,0},{8,12},{12,8},{1,5},{5,1},{9,13},{13,9},{2,6},{6,2},{1... | collective-permute-start | bytes 196616 | tf_op jit(solution)/shard_map/ppermute | solution.py:149
  91.2 5.2 %collective-permute-start.14 = (f32[36224]{0:T(1024)S(1)}, f32[36224]{0:T(1024)S(1)}, u32[]{:S(2)}, u32[]{:S(2)}) collective-permute-start(f32[36224]{0:T(1024)S(1)} %pad_maximum_fusion.7), channel_id=1, source_target_pairs={{0,2},{1,3},{2,0},{3,1},{4,6},{5,7},{6,4},{7,5},{8,10},{9,11},{10,... | collective-permute-start | bytes 434696 | tf_op jit(solution)/shard_map/ppermute | solution.py:149
  96.9 1.6 %collective-permute-start.15 = (f32[72448]{0:T(1024)S(1)}, f32[72448]{0:T(1024)S(1)}, u32[]{:S(2)}, u32[]{:S(2)}) collective-permute-start(f32[72448]{0:T(1024)S(1)} %pad_maximum_fusion.1), channel_id=1, source_target_pairs={{0,1},{1,0},{2,3},{3,2},{4,5},{5,4},{6,7},{7,6},{8,9},{9,8},{10,11... | collective-permute-start | bytes 869384 | tf_op jit(solution)/shard_map/ppermute | solution.py:149

commit v12 on v11

--- a/solution.py
+++ b/solution.py
@@ -27,12 +27,22 @@
     copies = [pltpu.make_async_copy(w_hbm.at[k], w_vmem.at[k], sems.at[k]) for k in range(9)]
     for copy in copies:
         copy.start()
-    parts = None
-    for dz, dy in itertools.product(range(3), repeat=2):
-        rows = jnp.concatenate([source_row(pieces, dz, dy + y) for y in range(height)], axis=1)
-        copies[dz * 3 + dy].wait()
-        product = jnp.dot(w_vmem[dz * 3 + dy], rows, preferred_element_type=jnp.float32)
-        parts = product if parts is None else parts + product
+    sources = [
+        jnp.concatenate([source_row(pieces, dz, dy + y) for y in range(height)], axis=1)
+        for dz, dy in itertools.product(range(3), repeat=2)
+    ]
+    chunks = []
+    for start in range(0, 3 * channels, LANES):
+        total = None
+        for k, source in enumerate(sources):
+            if start == 0:
+                copies[k].wait()
+            product = jnp.dot(
+                w_vmem[k, start : start + LANES], source, preferred_element_type=jnp.float32
+            )
+            total = product if total is None else total + product
+        chunks.append(total)
+    parts = jnp.concatenate(chunks, axis=0)
     for y in range(height):
         lanes = slice(y * LANES, (y + 1) * LANES)
         out_ref[y] = (

time: 101 us -> 101 us (level)
  no operation moved by 1% of the time
where the time goes in v12:
time: 101 us; the launch traced here: 100 us
  starting transfers between devices  40.2 us (40%)
  waiting for transfers between devices  18.7 us (19%)
  Pallas kernels  14.6 us (14%)
  local copies, waits for them, and re-layouts  10.6 us (10%)
  matrix products  9.02 us (9%)
  other arithmetic  5.49 us (5%)
  between operations  1.6 us (2%)
    ppermute x4, starting transfers between devices, tree_sum(): got = lax.ppermute(jnp.concatenate(sends), axis, pairs)  12.6 us
    pallas_call x2, Pallas kernels, conv_call(): pl.pallas_call(conv_body, out_shape=jax.ShapeDtypeStruct((height, channel...  10.2 us
    ppermute x2, starting transfers between devices, halo(): below = lax.ppermute(block[depth - 1:], 'grp', up)  9 us
    ppermute x4, waiting for transfers between devices, tree_sum(): lax.ppermute(jnp.concatenate([pieces[n] for n in members]), axis, pairs)  8.79 us
    ppermute x4, waiting for transfers between devices, tree_sum(): got = lax.ppermute(jnp.concatenate(sends), axis, pairs)  8.73 us
    ppermute x4, starting transfers between devices, tree_sum(): lax.ppermute(jnp.concatenate([pieces[n] for n in members]), axis, pairs)  6.86 us
    ppermute x2, starting transfers between devices, halo(): before = lax.ppermute(last, 'sub', up)  6.59 us
    pallas_call x1, Pallas kernels, wgrad_call(): pl.pallas_call(wgrad_body, out_shape=jax.ShapeDtypeStruct((blocks, channe...  4.39 us
  transfers between devices with their start and end apart: 16, of which 10 were waited for; matrix products, arithmetic and copies ran while one was open for 14% of the time, Pallas kernels for 4%

profile of v12, /device:TPU:0, one launch (start us, length us, event | category | flops | bytes accessed | tf_op | source)
XLA Modules:
  0.0 100.2 jit_solution(18420890580603321549)
XLA Ops:
  0.6 1.0 %copy.74 = bf16[256,1,2,128]{0,3,2,1:T(8,128)(2,1)S(1)} copy(bf16[256,1,2,128]{3,2,1,0:T(2,128)(2,1)} %param.5) | data formatting | bytes 262144 | tf_op args[0]
  1.7 1.1 %reduce-precision_convert_fusion.2 = (bf16[256,256]{0,1:T(8,128)(2,1)S(1)}, f32[256,256]{0,1:T(8,128)S(1)}) fusion(bf16[256,256]{0,1:T(8,128)(2,1)S(1)} %bitcast.100, bf16[256,256]{1,0:T(8,128)(2,1)} %param.7), kind=kOutput, calls=%fused_computation.33 | convolution fusion | flops 33947648 | bytes 655360 | tf_op jit(solution)/shard_map/dot_general | solution.py:237
  3.0 4.9 %collective-permute-start = (bf16[1,2,256,128]{3,2,1,0:T(8,128)(2,1)S(1)}, bf16[1,2,256,128]{3,2,1,0:T(8,128)(2,1)S(1)}, u32[]{:S(2)}, u32[]{:S(2)}) collective-permute-start(bf16[1,2,256,128]{3,2,1,0:T(8,128)(2,1)S(1)} %bitcast.90), channel_id=1, source_target_pairs={{0,4},{4,8},{8,12},{1,5},{5,9},{9,13},{2,6},{6,10},{10,14},{3,7},{... | collective-permute-start | bytes 393224 | tf_op jit(solution)/shard_map/ppermute | solution.py:178
  7.9 1.3 %collective-permute-start.1 = (bf16[1,2,256,128]{3,2,1,0:T(8,128)(2,1)S(1)}, bf16[1,2,256,128]{3,2,1,0:T(8,128)(2,1)S(1)}, u32[]{:S(2)}, u32[]{:S(2)}) collective-permute-start(bf16[1,2,256,128]{3,2,1,0:T(8,128)(2,1)S(1)} %bitcast.91), channel_id=1, source_target_pairs={{4,0},{8,4},{12,8},{5,1},{9,5},{13,9},{6,2},{10,6},{14,10},{7,3},{... | collective-permute-start | bytes 393224 | tf_op jit(solution)/shard_map/ppermute | solution.py:179
  9.4 1.0 %copy.77 = f32[256,1,2,128]{0,3,2,1:T(8,128)S(1)} copy(bf16[256,1,2,128]{3,2,1,0:T(2,128)(2,1)} %param.6) | data formatting | bytes 393216 | tf_op jit(solution)/shard_map/convert_element_type | solution.py:250
  10.4 3.8 %fusion = bf16[27,256,256]{2,1,0:T(8,128)(2,1)} fusion(f32[256,256]{1,0:T(8,128)S(1)} %compare_convert_fusion, bf16[256,8,27]{0,1,2:T(8,128)(2,1)} %bitcast.110, s32[256]{0:T(256)S(1)} %and_select_fusion.1), kind=kOutput, calls=%fused_computation.1 | convolution fusion | flops 31852544 | bytes 3912704 | tf_op jit(solution)/shard_map/ojt,ji->toi/dot_general | solution.py:211
  14.3 0.5 collective-permute-done.1.above_ref
  14.8 1.3 %collective-permute-start.3 = (bf16[3,1,256,128]{3,2,1,0:T(8,128)(2,1)S(1)}, bf16[3,1,256,128]{3,2,1,0:T(8,128)(2,1)S(1)}, u32[]{:S(2)}, u32[]{:S(2)}) collective-permute-start(bf16[3,1,256,128]{3,2,1,0:T(8,128)(2,1)S(1)} %pad_maximum_fusion.3), channel_id=1, source_target_pairs={{1,0},{2,1},{3,2},{5,4},{6,5},{7,6},{9,8},{10,9},{11,10},{13,12},{... | collective-permute-start | bytes 589832 | tf_op jit(solution)/shard_map/ppermute | solution.py:186
  16.2 3.0 %collective-permute-start.2 = (bf16[3,1,256,128]{3,2,1,0:T(8,128)(2,1)S(1)}, bf16[3,1,256,128]{3,2,1,0:T(8,128)(2,1)S(1)}, u32[]{:S(2)}, u32[]{:S(2)}) collective-permute-start(bf16[3,1,256,128]{3,2,1,0:T(8,128)(2,1)S(1)} %pad_maximum_fusion.2), channel_id=1, source_target_pairs={{0,1},{1,2},{2,3},{4,5},{5,6},{6,7},{8,9},{9,10},{10,11},{12,13},{... | collective-permute-start | bytes 589832 | tf_op jit(solution)/shard_map/ppermute | solution.py:185
  19.2 2.9 %multiply_convert_fusion = bf16[256,256,27]{1,0,2:T(8,128)(2,1)} fusion(f32[256,256]{1,0:T(8,128)S(1)} %compare_convert_fusion, bf16[256,8,27]{0,1,2:T(8,128)(2,1)S(1)} %bitcast.111, s32[256]{0:T(256)S(1)} %and_select_fusion.1), kind=kOutput, calls=%fused_computation.2 | convolution fusion | flops 31907840 | bytes 3912704 | tf_op jit(solution)/shard_map/ji,ojt->tio/dot_general | solution.py:212
  22.2 0.6 copy-done.8
  22.9 5.1 %shard_map.92 = f32[2,256,128]{2,1,0:T(8,128)} custom-call(bf16[1,2,256,128]{3,2,1,0:T(8,128)(2,1)} %bitcast.93, bf16[1,2,256,128]{3,2,1,0:T(8,128)(2,1)} %copy-done.5, bf16[1,2,256,128]{3,2,1,0:T(8,128)(2,1)} %copy-done.6, bf16[3,1,256,128]{3,2,1,0:T(8,128)(2,1)} %copy-done.9, bf16[3,1,256,128]{3,2,1,0:T(8,128)(2,1)} %copy-done.8, bf16[9,768,256]{2,1,0:T(8,128)(2,1)} %bitcast.88), custom_call_target="tpu_custom_call" | custom-call | flops 905969664 | bytes 4587520 | tf_op jit(solution)/shard_map/pallas_call | solution.py:57
  28.0 1.1 %fusion.15 = bf16[256,2,128]{2,0,1:T(8,128)(2,1)S(1)} fusion(f32[2,256,128]{2,1,0:T(8,128)} %shard_map.92), kind=kLoop, calls=%fused_computation.50 | loop fusion | flops 393216 | bytes 393216 | tf_op jit(solution)/shard_map/transpose | solution.py:234
  29.2 0.3 fusion.13
  29.9 0.8 fusion.9.delta_ref
  30.6 4.1 %collective-permute-start.4 = (bf16[1,2,256,128]{3,2,1,0:T(8,128)(2,1)}, bf16[1,2,256,128]{3,2,1,0:T(8,128)(2,1)S(1)}, u32[]{:S(2)}, u32[]{:S(2)}) collective-permute-start(bf16[1,2,256,128]{3,2,1,0:T(8,128)(2,1)} %bitcast.16.block_ref), channel_id=1, source_target_pairs={{0,4},{4,8},{8,12},{1,5},{5,9},{9,13},{2,6},{6,10},{10,14},{3,7},{... | collective-permute-start | bytes 393224 | tf_op jit(solution)/shard_map/ppermute | solution.py:178
  34.7 1.3 %collective-permute-start.5 = (bf16[1,2,256,128]{3,2,1,0:T(8,128)(2,1)}, bf16[1,2,256,128]{3,2,1,0:T(8,128)(2,1)S(1)}, u32[]{:S(2)}, u32[]{:S(2)}) collective-permute-start(bf16[1,2,256,128]{3,2,1,0:T(8,128)(2,1)} %bitcast.16.block_ref), channel_id=1, source_target_pairs={{4,0},{8,4},{12,8},{5,1},{9,5},{13,9},{6,2},{10,6},{14,10},{7,3},{... | collective-permute-start | bytes 393224 | tf_op jit(solution)/shard_map/ppermute | solution.py:179
  36.0 0.2 fusion.38
  36.3 4.4 %shard_map.94 = f32[2,256,128]{2,1,0:T(8,128)} custom-call(bf16[1,2,256,128]{3,2,1,0:T(8,128)(2,1)} %bitcast.94, bf16[1,2,256,128]{3,2,1,0:T(8,128)(2,1)} %copy-done.5, bf16[1,2,256,128]{3,2,1,0:T(8,128)(2,1)} %copy-done.6, bf16[3,1,256,128]{3,2,1,0:T(8,128)(2,1)} %copy-done.9, bf16[3,1,256,128]{3,2,1,0:T(8,128)(2,1)} %copy-done.8, ...), custom_call_target="tpu_custom_call" | custom-call | flops 1358954496 | bytes 1179648 | tf_op jit(solution)/shard_map/pallas_call | solution.py:114
  40.6 1.1 %copy.85 = f32[256,2,128]{0,2,1:T(8,128)S(1)} copy(f32[256,2,128]{2,0,1:T(8,128)} %bitcast.112) | data formatting | bytes 524288 | tf_op jit(solution)/shard_map/transpose | solution.py:125
  43.0 0.9 fusion.31
  44.0 1.3 %collective-permute-start.7 = (bf16[3,1,256,128]{3,2,1,0:T(8,128)(2,1)S(1)}, bf16[3,1,256,128]{3,2,1,0:T(8,128)(2,1)S(1)}, u32[]{:S(2)}, u32[]{:S(2)}) collective-permute-start(bf16[3,1,256,128]{3,2,1,0:T(8,128)(2,1)S(1)} %pad_maximum_fusion.5), channel_id=1, source_target_pairs={{1,0},{2,1},{3,2},{5,4},{6,5},{7,6},{9,8},{10,9},{11,10},{13,12},{... | collective-permute-start | bytes 589832 | tf_op jit(solution)/shard_map/ppermute | solution.py:186
  45.3 3.5 %collective-permute-start.6 = (bf16[3,1,256,128]{3,2,1,0:T(8,128)(2,1)S(1)}, bf16[3,1,256,128]{3,2,1,0:T(8,128)(2,1)S(1)}, u32[]{:S(2)}, u32[]{:S(2)}) collective-permute-start(bf16[3,1,256,128]{3,2,1,0:T(8,128)(2,1)S(1)} %pad_maximum_fusion.4), channel_id=1, source_target_pairs={{0,1},{1,2},{2,3},{4,5},{5,6},{6,7},{8,9},{9,10},{10,11},{12,13},{... | collective-permute-start | bytes 589832 | tf_op jit(solution)/shard_map/ppermute | solution.py:185
  49.1 0.6 collective-permute-done.6.before_ref
  49.8 0.6 copy-done.11
  50.4 5.1 %shard_map.93 = f32[2,256,128]{2,1,0:T(8,128)} custom-call(bf16[1,2,256,128]{3,2,1,0:T(8,128)(2,1)} %bitcast.16.block_ref, bf16[1,2,256,128]{3,2,1,0:T(8,128)(2,1)} %copy-done.3, bf16[1,2,256,128]{3,2,1,0:T(8,128)(2,1)} %copy-done.4, bf16[3,1,256,128]{3,2,1,0:T(8,128)(2,1)} %copy-done.11, bf16[3,1,256,128]{3,2,1,0:T(8,128)(2,1)} %copy-done.10, ...), custom_call_target="tpu_custom_call" | custom-call | flops 905969664 | bytes 4587520 | tf_op jit(solution)/shard_map/pallas_call | solution.py:57
  55.5 1.0 convert_bitcast_fusion
  57.2 4.0 %collective-permute-start.8 = (f32[93184]{0:T(1024)S(1)}, f32[93184]{0:T(1024)S(1)}, u32[]{:S(2)}, u32[]{:S(2)}) collective-permute-start(f32[93184]{0:T(1024)S(1)} %pad_maximum_fusion), channel_id=1, source_target_pairs={{0,1},{1,0},{2,3},{3,2},{4,5},{5,4},{6,7},{7,6},{8,9},{9,8},{10,11... | collective-permute-start | bytes 1118216 | tf_op jit(solution)/shard_map/ppermute | solution.py:149
  61.6 0.9 collective-permute-done.8
  62.6 2.8 %collective-permute-start.9 = (f32[46592]{0:T(1024)S(1)}, f32[46592]{0:T(1024)S(1)}, u32[]{:S(2)}, u32[]{:S(2)}) collective-permute-start(f32[46592]{0:T(1024)S(1)} %pad_maximum_fusion.6), channel_id=1, source_target_pairs={{0,2},{1,3},{2,0},{3,1},{4,6},{5,7},{6,4},{7,5},{8,10},{9,11},{10,... | collective-permute-start | bytes 559112 | tf_op jit(solution)/shard_map/ppermute | solution.py:149
  65.5 5.0 %collective-permute-done.9 = f32[46592]{0:T(1024)S(1)} collective-permute-done((f32[46592]{0:T(1024)S(1)}, f32[46592]{0:T(1024)S(1)}, u32[]{:S(2)}, u32[]{:S(2)}) %collective-permute-start.9) | collective-permute-done | bytes 186400 | tf_op jit(solution)/shard_map/ppermute | solution.py:149
  70.6 2.7 %collective-permute-start.10 = (f32[23296]{0:T(1024)S(1)}, f32[23296]{0:T(1024)S(1)}, u32[]{:S(2)}, u32[]{:S(2)}) collective-permute-start(f32[23296]{0:T(1024)S(1)} %pad_maximum_fusion.8), channel_id=1, source_target_pairs={{0,4},{4,0},{8,12},{12,8},{1,5},{5,1},{9,13},{13,9},{2,6},{6,2},{1... | collective-permute-start | bytes 279560 | tf_op jit(solution)/shard_map/ppermute | solution.py:149
  73.3 0.8 copy.99
  74.1 1.8 %collective-permute-done.10 = f32[23296]{0:T(1024)S(1)} collective-permute-done((f32[23296]{0:T(1024)S(1)}, f32[23296]{0:T(1024)S(1)}, u32[]{:S(2)}, u32[]{:S(2)}) %collective-permute-start.10) | collective-permute-done | bytes 93216 | tf_op jit(solution)/shard_map/ppermute | solution.py:149
  75.9 3.1 %collective-permute-start.11 = (f32[11648]{0:T(1024)S(1)}, f32[11648]{0:T(1024)S(1)}, u32[]{:S(2)}, u32[]{:S(2)}) collective-permute-start(f32[11648]{0:T(1024)S(1)} %pad_maximum_fusion.12), channel_id=1, source_target_pairs={{0,8},{4,12},{8,0},{12,4},{1,9},{5,13},{9,1},{13,5},{2,10},{6,14},... | collective-permute-start | bytes 139784 | tf_op jit(solution)/shard_map/ppermute | solution.py:149
  79.0 0.2 fusion.3
  79.3 0.8 copy.100
  80.0 1.1 %collective-permute-done.11 = f32[11648]{0:T(1024)S(1)} collective-permute-done((f32[11648]{0:T(1024)S(1)}, f32[11648]{0:T(1024)S(1)}, u32[]{:S(2)}, u32[]{:S(2)}) %collective-permute-start.11) | collective-permute-done | bytes 46624 | tf_op jit(solution)/shard_map/ppermute | solution.py:149
  81.1 3.0 %collective-permute-start.12 = (f32[8192]{0:T(1024)S(1)}, f32[8192]{0:T(1024)S(1)}, u32[]{:S(2)}, u32[]{:S(2)}) collective-permute-start(f32[8192]{0:T(1024)S(1)} %pad_maximum_fusion.14), channel_id=1, source_target_pairs={{0,8},{4,12},{8,0},{12,4},{1,9},{5,13},{9,1},{13,5},{2,10},{6,14},... | collective-permute-start | bytes 98312 | tf_op jit(solution)/shard_map/ppermute | solution.py:159
  84.5 1.7 %collective-permute-done.12 = f32[8192]{0:T(1024)S(1)} collective-permute-done((f32[8192]{0:T(1024)S(1)}, f32[8192]{0:T(1024)S(1)}, u32[]{:S(2)}, u32[]{:S(2)}) %collective-permute-start.12) | collective-permute-done | bytes 32800 | tf_op jit(solution)/shard_map/ppermute | solution.py:159
  86.2 1.9 %collective-permute-start.13 = (f32[16384]{0:T(1024)S(1)}, f32[16384]{0:T(1024)S(1)}, u32[]{:S(2)}, u32[]{:S(2)}) collective-permute-start(f32[16384]{0:T(1024)S(1)} %pad_maximum_fusion.10), channel_id=1, source_target_pairs={{0,4},{4,0},{8,12},{12,8},{1,5},{5,1},{9,13},{13,9},{2,6},{6,2},{1... | collective-permute-start | bytes 196616 | tf_op jit(solution)/shard_map/ppermute | solution.py:159
  88.2 2.4 %collective-permute-done.13 = f32[16384]{0:T(1024)S(1)} collective-permute-done((f32[16384]{0:T(1024)S(1)}, f32[16384]{0:T(1024)S(1)}, u32[]{:S(2)}, u32[]{:S(2)}) %collective-permute-start.13) | collective-permute-done | bytes 65568 | tf_op jit(solution)/shard_map/ppermute | solution.py:159
  90.6 1.9 %collective-permute-start.14 = (f32[36224]{0:T(1024)S(1)}, f32[36224]{0:T(1024)S(1)}, u32[]{:S(2)}, u32[]{:S(2)}) collective-permute-start(f32[36224]{0:T(1024)S(1)} %pad_maximum_fusion.7), channel_id=1, source_target_pairs={{0,2},{1,3},{2,0},{3,1},{4,6},{5,7},{6,4},{7,5},{8,10},{9,11},{10,... | collective-permute-start | bytes 434696 | tf_op jit(solution)/shard_map/ppermute | solution.py:159
  92.5 3.3 %collective-permute-done.14 = f32[36224]{0:T(1024)S(1)} collective-permute-done((f32[36224]{0:T(1024)S(1)}, f32[36224]{0:T(1024)S(1)}, u32[]{:S(2)}, u32[]{:S(2)}) %collective-permute-start.14) | collective-permute-done | bytes 144928 | tf_op jit(solution)/shard_map/ppermute | solution.py:159
  96.6 1.4 %collective-permute-done.15 = f32[72448]{0:T(1024)S(1)} collective-permute-done((f32[72448]{0:T(1024)S(1)}, f32[72448]{0:T(1024)S(1)}, u32[]{:S(2)}, u32[]{:S(2)}) %collective-permute-start.15) | collective-permute-done | bytes 289824 | tf_op jit(solution)/shard_map/ppermute | solution.py:159
  98.1 0.3 copy.97
  98.5 0.8 fusion.16
  99.3 0.8 fusion.6
  (135 shorter events, 5.0 us)
Async XLA Ops:
  0.6 28.6 %copy-start = (bf16[256,256]{1,0:T(8,128)(2,1)S(1)}, bf16[256,256]{1,0:T(8,128)(2,1)}, u32[]{:S(2)}) copy-start(bf16[256,256]{1,0:T(8,128)(2,1)} %param.9) | copy-start | bytes 393220
  2.8 16.4 %copy-start.7 = (bf16[256,8,3,3,3]{0,1,4,3,2:T(8,128)(2,1)S(1)}, bf16[256,8,3,3,3]{0,1,4,3,2:T(8,128)(2,1)}, u32[]{:S(2)}) copy-start(bf16[256,8,3,3,3]{0,1,4,3,2:T(8,128)(2,1)} %param.8) | copy-start | bytes 331780
  3.0 19.2 %copy-start.2 = (bf16[256,1,2,128]{3,0,2,1:T(8,128)(2,1)}, bf16[256,1,2,128]{3,0,2,1:T(8,128)(2,1)S(1)}, u32[]{:S(2)}) copy-start(bf16[256,1,2,128]{3,0,2,1:T(8,128)(2,1)S(1)} %copy.75) | copy-start | bytes 393220
  3.0 11.3 %collective-permute-start = (bf16[1,2,256,128]{3,2,1,0:T(8,128)(2,1)S(1)}, bf16[1,2,256,128]{3,2,1,0:T(8,128)(2,1)S(1)}, u32[]{:S(2)}, u32[]{:S(2)}) collective-permute-start(bf16[1,2,256,128]{3,2,1,0:T(8,128)(2,1)S(1)} %bitcast.90), channel_id=1, source_target_pairs={{0,4},{4,8},{8,12},{1,5},{5,9},{9,13},{2,6},{6,10},{10,14},{3,7},{... | collective-permute-start | bytes 393224 | tf_op jit(solution)/shard_map/ppermute | solution.py:178
  7.9 6.9 %collective-permute-start.1 = (bf16[1,2,256,128]{3,2,1,0:T(8,128)(2,1)S(1)}, bf16[1,2,256,128]{3,2,1,0:T(8,128)(2,1)S(1)}, u32[]{:S(2)}, u32[]{:S(2)}) collective-permute-start(bf16[1,2,256,128]{3,2,1,0:T(8,128)(2,1)S(1)} %bitcast.91), channel_id=1, source_target_pairs={{4,0},{8,4},{12,8},{5,1},{9,5},{13,9},{6,2},{10,6},{14,10},{7,3},{... | collective-permute-start | bytes 393224 | tf_op jit(solution)/shard_map/ppermute | solution.py:179
  14.3 7.9 %copy-start.5 = (bf16[1,2,256,128]{3,2,1,0:T(8,128)(2,1)}, bf16[1,2,256,128]{3,2,1,0:T(8,128)(2,1)S(1)}, u32[]{:S(2)}) copy-start(bf16[1,2,256,128]{3,2,1,0:T(8,128)(2,1)S(1)} %collective-permute-done.below_ref) | copy-start | bytes 393220
  14.8 7.4 %copy-start.6 = (bf16[1,2,256,128]{3,2,1,0:T(8,128)(2,1)}, bf16[1,2,256,128]{3,2,1,0:T(8,128)(2,1)S(1)}, u32[]{:S(2)}) copy-start(bf16[1,2,256,128]{3,2,1,0:T(8,128)(2,1)S(1)} %collective-permute-done.1.above_ref) | copy-start | bytes 393220
  14.8 7.3 %collective-permute-start.3 = (bf16[3,1,256,128]{3,2,1,0:T(8,128)(2,1)S(1)}, bf16[3,1,256,128]{3,2,1,0:T(8,128)(2,1)S(1)}, u32[]{:S(2)}, u32[]{:S(2)}) collective-permute-start(bf16[3,1,256,128]{3,2,1,0:T(8,128)(2,1)S(1)} %pad_maximum_fusion.3), channel_id=1, source_target_pairs={{1,0},{2,1},{3,2},{5,4},{6,5},{7,6},{9,8},{10,9},{11,10},{13,12},{... | collective-permute-start | bytes 589832 | tf_op jit(solution)/shard_map/ppermute | solution.py:186
  16.2 6.0 %collective-permute-start.2 = (bf16[3,1,256,128]{3,2,1,0:T(8,128)(2,1)S(1)}, bf16[3,1,256,128]{3,2,1,0:T(8,128)(2,1)S(1)}, u32[]{:S(2)}, u32[]{:S(2)}) collective-permute-start(bf16[3,1,256,128]{3,2,1,0:T(8,128)(2,1)S(1)} %pad_maximum_fusion.2), channel_id=1, source_target_pairs={{0,1},{1,2},{2,3},{4,5},{5,6},{6,7},{8,9},{9,10},{10,11},{12,13},{... | collective-permute-start | bytes 589832 | tf_op jit(solution)/shard_map/ppermute | solution.py:185
  22.1 0.7 copy-start.8
  22.1 0.7 copy-start.9
  28.0 1.9 %copy-start.1 = (f32[2,256,128]{2,1,0:T(8,128)S(1)}, f32[2,256,128]{2,1,0:T(8,128)}, u32[]{:S(2)}) copy-start(f32[2,256,128]{2,1,0:T(8,128)} %shard_map.92) | copy-start | bytes 786436
  30.6 13.2 %collective-permute-start.4 = (bf16[1,2,256,128]{3,2,1,0:T(8,128)(2,1)}, bf16[1,2,256,128]{3,2,1,0:T(8,128)(2,1)S(1)}, u32[]{:S(2)}, u32[]{:S(2)}) collective-permute-start(bf16[1,2,256,128]{3,2,1,0:T(8,128)(2,1)} %bitcast.16.block_ref), channel_id=1, source_target_pairs={{0,4},{4,8},{8,12},{1,5},{5,9},{9,13},{2,6},{6,10},{10,14},{3,7},{... | collective-permute-start | bytes 393224 | tf_op jit(solution)/shard_map/ppermute | solution.py:178
  34.7 9.2 %collective-permute-start.5 = (bf16[1,2,256,128]{3,2,1,0:T(8,128)(2,1)}, bf16[1,2,256,128]{3,2,1,0:T(8,128)(2,1)S(1)}, u32[]{:S(2)}, u32[]{:S(2)}) collective-permute-start(bf16[1,2,256,128]{3,2,1,0:T(8,128)(2,1)} %bitcast.16.block_ref), channel_id=1, source_target_pairs={{4,0},{8,4},{12,8},{5,1},{9,5},{13,9},{6,2},{10,6},{14,10},{7,3},{... | collective-permute-start | bytes 393224 | tf_op jit(solution)/shard_map/ppermute | solution.py:179
  43.9 5.9 %copy-start.3 = (bf16[1,2,256,128]{3,2,1,0:T(8,128)(2,1)}, bf16[1,2,256,128]{3,2,1,0:T(8,128)(2,1)S(1)}, u32[]{:S(2)}) copy-start(bf16[1,2,256,128]{3,2,1,0:T(8,128)(2,1)S(1)} %collective-permute-done.4.below_ref) | copy-start | bytes 393220
  43.9 5.8 %copy-start.4 = (bf16[1,2,256,128]{3,2,1,0:T(8,128)(2,1)}, bf16[1,2,256,128]{3,2,1,0:T(8,128)(2,1)S(1)}, u32[]{:S(2)}) copy-start(bf16[1,2,256,128]{3,2,1,0:T(8,128)(2,1)S(1)} %collective-permute-done.5.above_ref) | copy-start | bytes 393220
  44.0 5.1 %collective-permute-start.7 = (bf16[3,1,256,128]{3,2,1,0:T(8,128)(2,1)S(1)}, bf16[3,1,256,128]{3,2,1,0:T(8,128)(2,1)S(1)}, u32[]{:S(2)}, u32[]{:S(2)}) collective-permute-start(bf16[3,1,256,128]{3,2,1,0:T(8,128)(2,1)S(1)} %pad_maximum_fusion.5), channel_id=1, source_target_pairs={{1,0},{2,1},{3,2},{5,4},{6,5},{7,6},{9,8},{10,9},{11,10},{13,12},{... | collective-permute-start | bytes 589832 | tf_op jit(solution)/shard_map/ppermute | solution.py:186
  45.3 4.4 %collective-permute-start.6 = (bf16[3,1,256,128]{3,2,1,0:T(8,128)(2,1)S(1)}, bf16[3,1,256,128]{3,2,1,0:T(8,128)(2,1)S(1)}, u32[]{:S(2)}, u32[]{:S(2)}) collective-permute-start(bf16[3,1,256,128]{3,2,1,0:T(8,128)(2,1)S(1)} %pad_maximum_fusion.4), channel_id=1, source_target_pairs={{0,1},{1,2},{2,3},{4,5},{5,6},{6,7},{8,9},{9,10},{10,11},{12,13},{... | collective-permute-start | bytes 589832 | tf_op jit(solution)/shard_map/ppermute | solution.py:185
  49.1 0.7 copy-start.10
  49.7 0.7 copy-start.11
  57.0 22.0 %copy-start.12 = (bf16[256,256]{1,0:T(8,128)(2,1)S(1)}, bf16[256,256]{1,0:T(8,128)(2,1)}, u32[]{:S(2)}) copy-start(bf16[256,256]{1,0:T(8,128)(2,1)} %param.7) | copy-start | bytes 393220
  57.2 5.3 %collective-permute-start.8 = (f32[93184]{0:T(1024)S(1)}, f32[93184]{0:T(1024)S(1)}, u32[]{:S(2)}, u32[]{:S(2)}) collective-permute-start(f32[93184]{0:T(1024)S(1)} %pad_maximum_fusion), channel_id=1, source_target_pairs={{0,1},{1,0},{2,3},{3,2},{4,5},{5,4},{6,7},{7,6},{8,9},{9,8},{10,11... | collective-permute-start | bytes 1118216 | tf_op jit(solution)/shard_map/ppermute | solution.py:149
  62.6 7.8 %collective-permute-start.9 = (f32[46592]{0:T(1024)S(1)}, f32[46592]{0:T(1024)S(1)}, u32[]{:S(2)}, u32[]{:S(2)}) collective-permute-start(f32[46592]{0:T(1024)S(1)} %pad_maximum_fusion.6), channel_id=1, source_target_pairs={{0,2},{1,3},{2,0},{3,1},{4,6},{5,7},{6,4},{7,5},{8,10},{9,11},{10,... | collective-permute-start | bytes 559112 | tf_op jit(solution)/shard_map/ppermute | solution.py:149
  70.6 5.2 %collective-permute-start.10 = (f32[23296]{0:T(1024)S(1)}, f32[23296]{0:T(1024)S(1)}, u32[]{:S(2)}, u32[]{:S(2)}) collective-permute-start(f32[23296]{0:T(1024)S(1)} %pad_maximum_fusion.8), channel_id=1, source_target_pairs={{0,4},{4,0},{8,12},{12,8},{1,5},{5,1},{9,13},{13,9},{2,6},{6,2},{1... | collective-permute-start | bytes 279560 | tf_op jit(solution)/shard_map/ppermute | solution.py:149
  75.9 5.2 %collective-permute-start.11 = (f32[11648]{0:T(1024)S(1)}, f32[11648]{0:T(1024)S(1)}, u32[]{:S(2)}, u32[]{:S(2)}) collective-permute-start(f32[11648]{0:T(1024)S(1)} %pad_maximum_fusion.12), channel_id=1, source_target_pairs={{0,8},{4,12},{8,0},{12,4},{1,9},{5,13},{9,1},{13,5},{2,10},{6,14},... | collective-permute-start | bytes 139784 | tf_op jit(solution)/shard_map/ppermute | solution.py:149
  81.1 5.0 %collective-permute-start.12 = (f32[8192]{0:T(1024)S(1)}, f32[8192]{0:T(1024)S(1)}, u32[]{:S(2)}, u32[]{:S(2)}) collective-permute-start(f32[8192]{0:T(1024)S(1)} %pad_maximum_fusion.14), channel_id=1, source_target_pairs={{0,8},{4,12},{8,0},{12,4},{1,9},{5,13},{9,1},{13,5},{2,10},{6,14},... | collective-permute-start | bytes 98312 | tf_op jit(solution)/shard_map/ppermute | solution.py:159
  86.2 4.3 %collective-permute-start.13 = (f32[16384]{0:T(1024)S(1)}, f32[16384]{0:T(1024)S(1)}, u32[]{:S(2)}, u32[]{:S(2)}) collective-permute-start(f32[16384]{0:T(1024)S(1)} %pad_maximum_fusion.10), channel_id=1, source_target_pairs={{0,4},{4,0},{8,12},{12,8},{1,5},{5,1},{9,13},{13,9},{2,6},{6,2},{1... | collective-permute-start | bytes 196616 | tf_op jit(solution)/shard_map/ppermute | solution.py:159
  90.6 5.2 %collective-permute-start.14 = (f32[36224]{0:T(1024)S(1)}, f32[36224]{0:T(1024)S(1)}, u32[]{:S(2)}, u32[]{:S(2)}) collective-permute-start(f32[36224]{0:T(1024)S(1)} %pad_maximum_fusion.7), channel_id=1, source_target_pairs={{0,2},{1,3},{2,0},{3,1},{4,6},{5,7},{6,4},{7,5},{8,10},{9,11},{10,... | collective-permute-start | bytes 434696 | tf_op jit(solution)/shard_map/ppermute | solution.py:159
  96.3 1.6 %collective-permute-start.15 = (f32[72448]{0:T(1024)S(1)}, f32[72448]{0:T(1024)S(1)}, u32[]{:S(2)}, u32[]{:S(2)}) collective-permute-start(f32[72448]{0:T(1024)S(1)} %pad_maximum_fusion.1), channel_id=1, source_target_pairs={{0,1},{1,0},{2,3},{3,2},{4,5},{5,4},{6,7},{7,6},{8,9},{9,8},{10,11... | collective-permute-start | bytes 869384 | tf_op jit(solution)/shard_map/ppermute | solution.py:159

commit v13 on v12

--- a/solution.py
+++ b/solution.py
@@ -31,15 +31,18 @@
         jnp.concatenate([source_row(pieces, dz, dy + y) for y in range(height)], axis=1)
         for dz, dy in itertools.product(range(3), repeat=2)
     ]
+    out_group = lax.broadcasted_iota(jnp.int32, (LANES, channels), 0) >> 3
+    in_group = lax.broadcasted_iota(jnp.int32, (LANES, channels), 1) >> 3
     chunks = []
     for start in range(0, 3 * channels, LANES):
+        same = out_group + (start % channels) // GW == in_group
         total = None
         for k, source in enumerate(sources):
             if start == 0:
                 copies[k].wait()
-            product = jnp.dot(
-                w_vmem[k, start : start + LANES], source, preferred_element_type=jnp.float32
-            )
+            weight = w_vmem[k, start : start + LANES]
+            weight = jnp.where(same, weight, jnp.zeros_like(weight))
+            product = jnp.dot(weight, source, preferred_element_type=jnp.float32)
             total = product if total is None else total + product
         chunks.append(total)
     parts = jnp.concatenate(chunks, axis=0)
@@ -204,14 +207,12 @@
 
 def conv_weights(group_weight):
     channels = group_weight.shape[0]
-    group_of = jnp.arange(channels) // GW
-    mask = (group_of[:, None] == group_of[None, :]).astype(jnp.float32)
     spread = (jnp.arange(GW)[:, None] == jnp.arange(channels)[None, :] % GW).astype(jnp.float32)
     compact = group_weight.reshape(channels, GW, 27).astype(jnp.float32)
     forward = jnp.einsum("ojt,ji->toi", compact, spread)
     backward = jnp.einsum("ji,ojt->tio", spread, compact[:, :, ::-1])
-    forward = (forward * mask).astype(group_weight.dtype).reshape(9, 3 * channels, channels)
-    backward = (backward * mask).astype(group_weight.dtype).reshape(9, 3 * channels, channels)
+    forward = forward.astype(group_weight.dtype).reshape(9, 3 * channels, channels)
+    backward = backward.astype(group_weight.dtype).reshape(9, 3 * channels, channels)
     return forward, backward
 
 

time: 101 us -> 101 us (level)
  no operation moved by 1% of the time
where the time goes in v13:
time: 101 us; the launch traced here: 100 us
  starting transfers between devices  40.1 us (40%)
  waiting for transfers between devices  18.8 us (19%)
  Pallas kernels  14.6 us (14%)
  local copies, waits for them, and re-layouts  10.6 us (10%)
  matrix products  9.05 us (9%)
  other arithmetic  5.38 us (5%)
  between operations  1.59 us (2%)
    ppermute x4, starting transfers between devices, tree_sum(): got = lax.ppermute(jnp.concatenate(sends), axis, pairs)  12.6 us
    pallas_call x2, Pallas kernels, conv_call(): pl.pallas_call(conv_body, out_shape=jax.ShapeDtypeStruct((height, channel...  10.2 us
    ppermute x2, starting transfers between devices, halo(): below = lax.ppermute(block[depth - 1:], 'grp', up)  8.88 us
    ppermute x4, waiting for transfers between devices, tree_sum(): lax.ppermute(jnp.concatenate([pieces[n] for n in members]), axis, pairs)  8.77 us
    ppermute x4, waiting for transfers between devices, tree_sum(): got = lax.ppermute(jnp.concatenate(sends), axis, pairs)  8.73 us
    ppermute x4, starting transfers between devices, tree_sum(): lax.ppermute(jnp.concatenate([pieces[n] for n in members]), axis, pairs)  6.86 us
    ppermute x2, starting transfers between devices, halo(): before = lax.ppermute(last, 'sub', up)  6.59 us
    pallas_call x1, Pallas kernels, wgrad_call(): pl.pallas_call(wgrad_body, out_shape=jax.ShapeDtypeStruct((blocks, channe...  4.38 us
  transfers between devices with their start and end apart: 16, of which 10 were waited for; matrix products, arithmetic and copies ran while one was open for 14% of the time, Pallas kernels for 4%

profile of v13, /device:TPU:0, one launch (start us, length us, event | category | flops | bytes accessed | tf_op | source)
XLA Modules:
  0.0 100.0 jit_solution(13700715849966871471)
XLA Ops:
  0.6 1.0 %copy.74 = bf16[256,1,2,128]{0,3,2,1:T(8,128)(2,1)S(1)} copy(bf16[256,1,2,128]{3,2,1,0:T(2,128)(2,1)} %param.5) | data formatting | bytes 262144 | tf_op args[0]
  1.7 1.2 %reduce-precision_convert_fusion.2 = (bf16[256,256]{0,1:T(8,128)(2,1)S(1)}, f32[256,256]{0,1:T(8,128)S(1)}) fusion(bf16[256,256]{0,1:T(8,128)(2,1)S(1)} %bitcast.98, bf16[256,256]{1,0:T(8,128)(2,1)} %param.7), kind=kOutput, calls=%fused_computation.32 | convolution fusion | flops 33947648 | bytes 655360 | tf_op jit(solution)/shard_map/dot_general | solution.py:238
  3.0 4.9 %collective-permute-start = (bf16[1,2,256,128]{3,2,1,0:T(8,128)(2,1)S(1)}, bf16[1,2,256,128]{3,2,1,0:T(8,128)(2,1)S(1)}, u32[]{:S(2)}, u32[]{:S(2)}) collective-permute-start(bf16[1,2,256,128]{3,2,1,0:T(8,128)(2,1)S(1)} %bitcast.88), channel_id=1, source_target_pairs={{0,4},{4,8},{8,12},{1,5},{5,9},{9,13},{2,6},{6,10},{10,14},{3,7},{... | collective-permute-start | bytes 393224 | tf_op jit(solution)/shard_map/ppermute | solution.py:181
  8.0 1.3 %collective-permute-start.1 = (bf16[1,2,256,128]{3,2,1,0:T(8,128)(2,1)S(1)}, bf16[1,2,256,128]{3,2,1,0:T(8,128)(2,1)S(1)}, u32[]{:S(2)}, u32[]{:S(2)}) collective-permute-start(bf16[1,2,256,128]{3,2,1,0:T(8,128)(2,1)S(1)} %bitcast.89), channel_id=1, source_target_pairs={{4,0},{8,4},{12,8},{5,1},{9,5},{13,9},{6,2},{10,6},{14,10},{7,3},{... | collective-permute-start | bytes 393224 | tf_op jit(solution)/shard_map/ppermute | solution.py:182
  9.3 1.0 %copy.77 = f32[256,1,2,128]{0,3,2,1:T(8,128)S(1)} copy(bf16[256,1,2,128]{3,2,1,0:T(2,128)(2,1)} %param.6) | data formatting | bytes 393216 | tf_op jit(solution)/shard_map/convert_element_type | solution.py:251
  10.3 3.8 %convolution_convert_fusion.1 = bf16[256,256,27]{0,1,2:T(8,128)(2,1)} fusion(bf16[256,8,27]{0,1,2:T(8,128)(2,1)} %bitcast.108, s32[256]{0:T(256)S(1)} %and_select_fusion), kind=kOutput, calls=%fused_computation.1 | convolution fusion | flops 30083072 | bytes 3650560 | tf_op jit(solution)/shard_map/ojt,ji->toi/dot_general | solution.py:212
  14.2 0.6 collective-permute-done.1.above_ref
  14.9 1.3 %collective-permute-start.3 = (bf16[3,1,256,128]{3,2,1,0:T(8,128)(2,1)S(1)}, bf16[3,1,256,128]{3,2,1,0:T(8,128)(2,1)S(1)}, u32[]{:S(2)}, u32[]{:S(2)}) collective-permute-start(bf16[3,1,256,128]{3,2,1,0:T(8,128)(2,1)S(1)} %pad_maximum_fusion.3), channel_id=1, source_target_pairs={{1,0},{2,1},{3,2},{5,4},{6,5},{7,6},{9,8},{10,9},{11,10},{13,12},{... | collective-permute-start | bytes 589832 | tf_op jit(solution)/shard_map/ppermute | solution.py:189
  16.2 3.0 %collective-permute-start.2 = (bf16[3,1,256,128]{3,2,1,0:T(8,128)(2,1)S(1)}, bf16[3,1,256,128]{3,2,1,0:T(8,128)(2,1)S(1)}, u32[]{:S(2)}, u32[]{:S(2)}) collective-permute-start(bf16[3,1,256,128]{3,2,1,0:T(8,128)(2,1)S(1)} %pad_maximum_fusion.2), channel_id=1, source_target_pairs={{0,1},{1,2},{2,3},{4,5},{5,6},{6,7},{8,9},{9,10},{10,11},{12,13},{... | collective-permute-start | bytes 589832 | tf_op jit(solution)/shard_map/ppermute | solution.py:188
  19.3 2.9 %convolution_convert_fusion = bf16[256,256,27]{1,0,2:T(8,128)(2,1)} fusion(bf16[256,8,27]{0,1,2:T(8,128)(2,1)S(1)} %bitcast.109, s32[256]{0:T(256)S(1)} %and_select_fusion), kind=kOutput, calls=%fused_computation | convolution fusion | flops 30138368 | bytes 3650560 | tf_op jit(solution)/shard_map/ji,ojt->tio/dot_general | solution.py:213
  22.2 0.6 copy-done.8
  22.9 5.1 %shard_map.92 = f32[2,256,128]{2,1,0:T(8,128)} custom-call(bf16[1,2,256,128]{3,2,1,0:T(8,128)(2,1)} %bitcast.91, bf16[1,2,256,128]{3,2,1,0:T(8,128)(2,1)} %copy-done.5, bf16[1,2,256,128]{3,2,1,0:T(8,128)(2,1)} %copy-done.6, bf16[3,1,256,128]{3,2,1,0:T(8,128)(2,1)} %copy-done.9, bf16[3,1,256,128]{3,2,1,0:T(8,128)(2,1)} %copy-done.8, bf16[9,768,256]{2,1,0:T(8,128)(2,1)} %bitcast.86), custom_call_target="tpu_custom_call" | custom-call | flops 905969664 | bytes 4587520 | tf_op jit(solution)/shard_map/pallas_call | solution.py:60
  28.0 1.1 %fusion.14 = bf16[256,2,128]{2,0,1:T(8,128)(2,1)S(1)} fusion(f32[2,256,128]{2,1,0:T(8,128)} %shard_map.92), kind=kLoop, calls=%fused_computation.48 | loop fusion | flops 393216 | bytes 393216 | tf_op jit(solution)/shard_map/transpose | solution.py:235
  29.3 0.3 fusion.12
  29.9 0.8 fusion.8.delta_ref
  30.7 3.9 %collective-permute-start.4 = (bf16[1,2,256,128]{3,2,1,0:T(8,128)(2,1)}, bf16[1,2,256,128]{3,2,1,0:T(8,128)(2,1)S(1)}, u32[]{:S(2)}, u32[]{:S(2)}) collective-permute-start(bf16[1,2,256,128]{3,2,1,0:T(8,128)(2,1)} %bitcast.16.block_ref), channel_id=1, source_target_pairs={{0,4},{4,8},{8,12},{1,5},{5,9},{9,13},{2,6},{6,10},{10,14},{3,7},{... | collective-permute-start | bytes 393224 | tf_op jit(solution)/shard_map/ppermute | solution.py:181
  34.6 1.3 %collective-permute-start.5 = (bf16[1,2,256,128]{3,2,1,0:T(8,128)(2,1)}, bf16[1,2,256,128]{3,2,1,0:T(8,128)(2,1)S(1)}, u32[]{:S(2)}, u32[]{:S(2)}) collective-permute-start(bf16[1,2,256,128]{3,2,1,0:T(8,128)(2,1)} %bitcast.16.block_ref), channel_id=1, source_target_pairs={{4,0},{8,4},{12,8},{5,1},{9,5},{13,9},{6,2},{10,6},{14,10},{7,3},{... | collective-permute-start | bytes 393224 | tf_op jit(solution)/shard_map/ppermute | solution.py:182
  35.9 0.2 fusion.36
  36.2 4.4 %shard_map.94 = f32[2,256,128]{2,1,0:T(8,128)} custom-call(bf16[1,2,256,128]{3,2,1,0:T(8,128)(2,1)} %bitcast.92, bf16[1,2,256,128]{3,2,1,0:T(8,128)(2,1)} %copy-done.5, bf16[1,2,256,128]{3,2,1,0:T(8,128)(2,1)} %copy-done.6, bf16[3,1,256,128]{3,2,1,0:T(8,128)(2,1)} %copy-done.9, bf16[3,1,256,128]{3,2,1,0:T(8,128)(2,1)} %copy-done.8, ...), custom_call_target="tpu_custom_call" | custom-call | flops 1358954496 | bytes 1179648 | tf_op jit(solution)/shard_map/pallas_call | solution.py:117
  40.5 1.1 %copy.85 = f32[256,2,128]{0,2,1:T(8,128)S(1)} copy(f32[256,2,128]{2,0,1:T(8,128)} %bitcast.110) | data formatting | bytes 524288 | tf_op jit(solution)/shard_map/transpose | solution.py:128
  42.9 0.9 fusion.29
  43.9 1.3 %collective-permute-start.7 = (bf16[3,1,256,128]{3,2,1,0:T(8,128)(2,1)S(1)}, bf16[3,1,256,128]{3,2,1,0:T(8,128)(2,1)S(1)}, u32[]{:S(2)}, u32[]{:S(2)}) collective-permute-start(bf16[3,1,256,128]{3,2,1,0:T(8,128)(2,1)S(1)} %pad_maximum_fusion.5), channel_id=1, source_target_pairs={{1,0},{2,1},{3,2},{5,4},{6,5},{7,6},{9,8},{10,9},{11,10},{13,12},{... | collective-permute-start | bytes 589832 | tf_op jit(solution)/shard_map/ppermute | solution.py:189
  45.2 3.5 %collective-permute-start.6 = (bf16[3,1,256,128]{3,2,1,0:T(8,128)(2,1)S(1)}, bf16[3,1,256,128]{3,2,1,0:T(8,128)(2,1)S(1)}, u32[]{:S(2)}, u32[]{:S(2)}) collective-permute-start(bf16[3,1,256,128]{3,2,1,0:T(8,128)(2,1)S(1)} %pad_maximum_fusion.4), channel_id=1, source_target_pairs={{0,1},{1,2},{2,3},{4,5},{5,6},{6,7},{8,9},{9,10},{10,11},{12,13},{... | collective-permute-start | bytes 589832 | tf_op jit(solution)/shard_map/ppermute | solution.py:188
  49.0 0.6 collective-permute-done.6.before_ref
  49.7 0.6 copy-done.11
  50.3 5.1 %shard_map.93 = f32[2,256,128]{2,1,0:T(8,128)} custom-call(bf16[1,2,256,128]{3,2,1,0:T(8,128)(2,1)} %bitcast.16.block_ref, bf16[1,2,256,128]{3,2,1,0:T(8,128)(2,1)} %copy-done.3, bf16[1,2,256,128]{3,2,1,0:T(8,128)(2,1)} %copy-done.4, bf16[3,1,256,128]{3,2,1,0:T(8,128)(2,1)} %copy-done.11, bf16[3,1,256,128]{3,2,1,0:T(8,128)(2,1)} %copy-done.10, ...), custom_call_target="tpu_custom_call" | custom-call | flops 905969664 | bytes 4587520 | tf_op jit(solution)/shard_map/pallas_call | solution.py:60
  55.4 1.0 convert_bitcast_fusion
  57.1 4.0 %collective-permute-start.8 = (f32[93184]{0:T(1024)S(1)}, f32[93184]{0:T(1024)S(1)}, u32[]{:S(2)}, u32[]{:S(2)}) collective-permute-start(f32[93184]{0:T(1024)S(1)} %pad_maximum_fusion), channel_id=1, source_target_pairs={{0,1},{1,0},{2,3},{3,2},{4,5},{5,4},{6,7},{7,6},{8,9},{9,8},{10,11... | collective-permute-start | bytes 1118216 | tf_op jit(solution)/shard_map/ppermute | solution.py:152
  61.6 0.9 collective-permute-done.8
  62.6 2.8 %collective-permute-start.9 = (f32[46592]{0:T(1024)S(1)}, f32[46592]{0:T(1024)S(1)}, u32[]{:S(2)}, u32[]{:S(2)}) collective-permute-start(f32[46592]{0:T(1024)S(1)} %pad_maximum_fusion.6), channel_id=1, source_target_pairs={{0,2},{1,3},{2,0},{3,1},{4,6},{5,7},{6,4},{7,5},{8,10},{9,11},{10,... | collective-permute-start | bytes 559112 | tf_op jit(solution)/shard_map/ppermute | solution.py:152
  65.4 5.0 %collective-permute-done.9 = f32[46592]{0:T(1024)S(1)} collective-permute-done((f32[46592]{0:T(1024)S(1)}, f32[46592]{0:T(1024)S(1)}, u32[]{:S(2)}, u32[]{:S(2)}) %collective-permute-start.9) | collective-permute-done | bytes 186400 | tf_op jit(solution)/shard_map/ppermute | solution.py:152
  70.5 2.7 %collective-permute-start.10 = (f32[23296]{0:T(1024)S(1)}, f32[23296]{0:T(1024)S(1)}, u32[]{:S(2)}, u32[]{:S(2)}) collective-permute-start(f32[23296]{0:T(1024)S(1)} %pad_maximum_fusion.8), channel_id=1, source_target_pairs={{0,4},{4,0},{8,12},{12,8},{1,5},{5,1},{9,13},{13,9},{2,6},{6,2},{1... | collective-permute-start | bytes 279560 | tf_op jit(solution)/shard_map/ppermute | solution.py:152
  73.2 0.8 copy.99
  74.0 1.8 %collective-permute-done.10 = f32[23296]{0:T(1024)S(1)} collective-permute-done((f32[23296]{0:T(1024)S(1)}, f32[23296]{0:T(1024)S(1)}, u32[]{:S(2)}, u32[]{:S(2)}) %collective-permute-start.10) | collective-permute-done | bytes 93216 | tf_op jit(solution)/shard_map/ppermute | solution.py:152
  75.8 3.1 %collective-permute-start.11 = (f32[11648]{0:T(1024)S(1)}, f32[11648]{0:T(1024)S(1)}, u32[]{:S(2)}, u32[]{:S(2)}) collective-permute-start(f32[11648]{0:T(1024)S(1)} %pad_maximum_fusion.12), channel_id=1, source_target_pairs={{0,8},{4,12},{8,0},{12,4},{1,9},{5,13},{9,1},{13,5},{2,10},{6,14},... | collective-permute-start | bytes 139784 | tf_op jit(solution)/shard_map/ppermute | solution.py:152
  78.9 0.2 fusion.2
  79.2 0.8 copy.100
  79.9 1.1 %collective-permute-done.11 = f32[11648]{0:T(1024)S(1)} collective-permute-done((f32[11648]{0:T(1024)S(1)}, f32[11648]{0:T(1024)S(1)}, u32[]{:S(2)}, u32[]{:S(2)}) %collective-permute-start.11) | collective-permute-done | bytes 46624 | tf_op jit(solution)/shard_map/ppermute | solution.py:152
  81.0 3.0 %collective-permute-start.12 = (f32[8192]{0:T(1024)S(1)}, f32[8192]{0:T(1024)S(1)}, u32[]{:S(2)}, u32[]{:S(2)}) collective-permute-start(f32[8192]{0:T(1024)S(1)} %pad_maximum_fusion.14), channel_id=1, source_target_pairs={{0,8},{4,12},{8,0},{12,4},{1,9},{5,13},{9,1},{13,5},{2,10},{6,14},... | collective-permute-start | bytes 98312 | tf_op jit(solution)/shard_map/ppermute | solution.py:162
  84.4 1.7 %collective-permute-done.12 = f32[8192]{0:T(1024)S(1)} collective-permute-done((f32[8192]{0:T(1024)S(1)}, f32[8192]{0:T(1024)S(1)}, u32[]{:S(2)}, u32[]{:S(2)}) %collective-permute-start.12) | collective-permute-done | bytes 32800 | tf_op jit(solution)/shard_map/ppermute | solution.py:162
  86.1 1.9 %collective-permute-start.13 = (f32[16384]{0:T(1024)S(1)}, f32[16384]{0:T(1024)S(1)}, u32[]{:S(2)}, u32[]{:S(2)}) collective-permute-start(f32[16384]{0:T(1024)S(1)} %pad_maximum_fusion.10), channel_id=1, source_target_pairs={{0,4},{4,0},{8,12},{12,8},{1,5},{5,1},{9,13},{13,9},{2,6},{6,2},{1... | collective-permute-start | bytes 196616 | tf_op jit(solution)/shard_map/ppermute | solution.py:162
  88.1 2.4 %collective-permute-done.13 = f32[16384]{0:T(1024)S(1)} collective-permute-done((f32[16384]{0:T(1024)S(1)}, f32[16384]{0:T(1024)S(1)}, u32[]{:S(2)}, u32[]{:S(2)}) %collective-permute-start.13) | collective-permute-done | bytes 65568 | tf_op jit(solution)/shard_map/ppermute | solution.py:162
  90.5 1.9 %collective-permute-start.14 = (f32[36224]{0:T(1024)S(1)}, f32[36224]{0:T(1024)S(1)}, u32[]{:S(2)}, u32[]{:S(2)}) collective-permute-start(f32[36224]{0:T(1024)S(1)} %pad_maximum_fusion.7), channel_id=1, source_target_pairs={{0,2},{1,3},{2,0},{3,1},{4,6},{5,7},{6,4},{7,5},{8,10},{9,11},{10,... | collective-permute-start | bytes 434696 | tf_op jit(solution)/shard_map/ppermute | solution.py:162
  92.4 3.3 %collective-permute-done.14 = f32[36224]{0:T(1024)S(1)} collective-permute-done((f32[36224]{0:T(1024)S(1)}, f32[36224]{0:T(1024)S(1)}, u32[]{:S(2)}, u32[]{:S(2)}) %collective-permute-start.14) | collective-permute-done | bytes 144928 | tf_op jit(solution)/shard_map/ppermute | solution.py:162
  96.5 1.4 %collective-permute-done.15 = f32[72448]{0:T(1024)S(1)} collective-permute-done((f32[72448]{0:T(1024)S(1)}, f32[72448]{0:T(1024)S(1)}, u32[]{:S(2)}, u32[]{:S(2)}) %collective-permute-start.15) | collective-permute-done | bytes 289824 | tf_op jit(solution)/shard_map/ppermute | solution.py:162
  98.0 0.3 copy.97
  98.4 0.8 fusion.15
  99.2 0.8 fusion.5
  (133 shorter events, 4.9 us)
Async XLA Ops:
  0.6 28.6 %copy-start = (bf16[256,256]{1,0:T(8,128)(2,1)S(1)}, bf16[256,256]{1,0:T(8,128)(2,1)}, u32[]{:S(2)}) copy-start(bf16[256,256]{1,0:T(8,128)(2,1)} %param.9) | copy-start | bytes 393220
  1.7 17.6 %copy-start.7 = (bf16[256,8,3,3,3]{0,1,4,3,2:T(8,128)(2,1)S(1)}, bf16[256,8,3,3,3]{0,1,4,3,2:T(8,128)(2,1)}, u32[]{:S(2)}) copy-start(bf16[256,8,3,3,3]{0,1,4,3,2:T(8,128)(2,1)} %param.8) | copy-start | bytes 331780
  3.0 19.2 %copy-start.2 = (bf16[256,1,2,128]{3,0,2,1:T(8,128)(2,1)}, bf16[256,1,2,128]{3,0,2,1:T(8,128)(2,1)S(1)}, u32[]{:S(2)}) copy-start(bf16[256,1,2,128]{3,0,2,1:T(8,128)(2,1)S(1)} %copy.75) | copy-start | bytes 393220
  3.0 11.1 %collective-permute-start = (bf16[1,2,256,128]{3,2,1,0:T(8,128)(2,1)S(1)}, bf16[1,2,256,128]{3,2,1,0:T(8,128)(2,1)S(1)}, u32[]{:S(2)}, u32[]{:S(2)}) collective-permute-start(bf16[1,2,256,128]{3,2,1,0:T(8,128)(2,1)S(1)} %bitcast.88), channel_id=1, source_target_pairs={{0,4},{4,8},{8,12},{1,5},{5,9},{9,13},{2,6},{6,10},{10,14},{3,7},{... | collective-permute-start | bytes 393224 | tf_op jit(solution)/shard_map/ppermute | solution.py:181
  8.0 6.9 %collective-permute-start.1 = (bf16[1,2,256,128]{3,2,1,0:T(8,128)(2,1)S(1)}, bf16[1,2,256,128]{3,2,1,0:T(8,128)(2,1)S(1)}, u32[]{:S(2)}, u32[]{:S(2)}) collective-permute-start(bf16[1,2,256,128]{3,2,1,0:T(8,128)(2,1)S(1)} %bitcast.89), channel_id=1, source_target_pairs={{4,0},{8,4},{12,8},{5,1},{9,5},{13,9},{6,2},{10,6},{14,10},{7,3},{... | collective-permute-start | bytes 393224 | tf_op jit(solution)/shard_map/ppermute | solution.py:182
  14.2 8.0 %copy-start.5 = (bf16[1,2,256,128]{3,2,1,0:T(8,128)(2,1)}, bf16[1,2,256,128]{3,2,1,0:T(8,128)(2,1)S(1)}, u32[]{:S(2)}) copy-start(bf16[1,2,256,128]{3,2,1,0:T(8,128)(2,1)S(1)} %collective-permute-done.below_ref) | copy-start | bytes 393220
  14.8 7.4 %copy-start.6 = (bf16[1,2,256,128]{3,2,1,0:T(8,128)(2,1)}, bf16[1,2,256,128]{3,2,1,0:T(8,128)(2,1)S(1)}, u32[]{:S(2)}) copy-start(bf16[1,2,256,128]{3,2,1,0:T(8,128)(2,1)S(1)} %collective-permute-done.1.above_ref) | copy-start | bytes 393220
  14.9 7.3 %collective-permute-start.3 = (bf16[3,1,256,128]{3,2,1,0:T(8,128)(2,1)S(1)}, bf16[3,1,256,128]{3,2,1,0:T(8,128)(2,1)S(1)}, u32[]{:S(2)}, u32[]{:S(2)}) collective-permute-start(bf16[3,1,256,128]{3,2,1,0:T(8,128)(2,1)S(1)} %pad_maximum_fusion.3), channel_id=1, source_target_pairs={{1,0},{2,1},{3,2},{5,4},{6,5},{7,6},{9,8},{10,9},{11,10},{13,12},{... | collective-permute-start | bytes 589832 | tf_op jit(solution)/shard_map/ppermute | solution.py:189
  16.2 6.0 %collective-permute-start.2 = (bf16[3,1,256,128]{3,2,1,0:T(8,128)(2,1)S(1)}, bf16[3,1,256,128]{3,2,1,0:T(8,128)(2,1)S(1)}, u32[]{:S(2)}, u32[]{:S(2)}) collective-permute-start(bf16[3,1,256,128]{3,2,1,0:T(8,128)(2,1)S(1)} %pad_maximum_fusion.2), channel_id=1, source_target_pairs={{0,1},{1,2},{2,3},{4,5},{5,6},{6,7},{8,9},{9,10},{10,11},{12,13},{... | collective-permute-start | bytes 589832 | tf_op jit(solution)/shard_map/ppermute | solution.py:188
  22.2 0.7 copy-start.8
  22.2 0.7 copy-start.9
  28.0 1.9 %copy-start.1 = (f32[2,256,128]{2,1,0:T(8,128)S(1)}, f32[2,256,128]{2,1,0:T(8,128)}, u32[]{:S(2)}) copy-start(f32[2,256,128]{2,1,0:T(8,128)} %shard_map.92) | copy-start | bytes 786436
  30.7 13.1 %collective-permute-start.4 = (bf16[1,2,256,128]{3,2,1,0:T(8,128)(2,1)}, bf16[1,2,256,128]{3,2,1,0:T(8,128)(2,1)S(1)}, u32[]{:S(2)}, u32[]{:S(2)}) collective-permute-start(bf16[1,2,256,128]{3,2,1,0:T(8,128)(2,1)} %bitcast.16.block_ref), channel_id=1, source_target_pairs={{0,4},{4,8},{8,12},{1,5},{5,9},{9,13},{2,6},{6,10},{10,14},{3,7},{... | collective-permute-start | bytes 393224 | tf_op jit(solution)/shard_map/ppermute | solution.py:181
  34.6 9.2 %collective-permute-start.5 = (bf16[1,2,256,128]{3,2,1,0:T(8,128)(2,1)}, bf16[1,2,256,128]{3,2,1,0:T(8,128)(2,1)S(1)}, u32[]{:S(2)}, u32[]{:S(2)}) collective-permute-start(bf16[1,2,256,128]{3,2,1,0:T(8,128)(2,1)} %bitcast.16.block_ref), channel_id=1, source_target_pairs={{4,0},{8,4},{12,8},{5,1},{9,5},{13,9},{6,2},{10,6},{14,10},{7,3},{... | collective-permute-start | bytes 393224 | tf_op jit(solution)/shard_map/ppermute | solution.py:182
  43.8 5.9 %copy-start.3 = (bf16[1,2,256,128]{3,2,1,0:T(8,128)(2,1)}, bf16[1,2,256,128]{3,2,1,0:T(8,128)(2,1)S(1)}, u32[]{:S(2)}) copy-start(bf16[1,2,256,128]{3,2,1,0:T(8,128)(2,1)S(1)} %collective-permute-done.4.below_ref) | copy-start | bytes 393220
  43.8 5.8 %copy-start.4 = (bf16[1,2,256,128]{3,2,1,0:T(8,128)(2,1)}, bf16[1,2,256,128]{3,2,1,0:T(8,128)(2,1)S(1)}, u32[]{:S(2)}) copy-start(bf16[1,2,256,128]{3,2,1,0:T(8,128)(2,1)S(1)} %collective-permute-done.5.above_ref) | copy-start | bytes 393220
  43.9 5.1 %collective-permute-start.7 = (bf16[3,1,256,128]{3,2,1,0:T(8,128)(2,1)S(1)}, bf16[3,1,256,128]{3,2,1,0:T(8,128)(2,1)S(1)}, u32[]{:S(2)}, u32[]{:S(2)}) collective-permute-start(bf16[3,1,256,128]{3,2,1,0:T(8,128)(2,1)S(1)} %pad_maximum_fusion.5), channel_id=1, source_target_pairs={{1,0},{2,1},{3,2},{5,4},{6,5},{7,6},{9,8},{10,9},{11,10},{13,12},{... | collective-permute-start | bytes 589832 | tf_op jit(solution)/shard_map/ppermute | solution.py:189
  45.2 4.4 %collective-permute-start.6 = (bf16[3,1,256,128]{3,2,1,0:T(8,128)(2,1)S(1)}, bf16[3,1,256,128]{3,2,1,0:T(8,128)(2,1)S(1)}, u32[]{:S(2)}, u32[]{:S(2)}) collective-permute-start(bf16[3,1,256,128]{3,2,1,0:T(8,128)(2,1)S(1)} %pad_maximum_fusion.4), channel_id=1, source_target_pairs={{0,1},{1,2},{2,3},{4,5},{5,6},{6,7},{8,9},{9,10},{10,11},{12,13},{... | collective-permute-start | bytes 589832 | tf_op jit(solution)/shard_map/ppermute | solution.py:188
  49.0 0.7 copy-start.10
  49.6 0.7 copy-start.11
  56.9 22.1 %copy-start.12 = (bf16[256,256]{1,0:T(8,128)(2,1)S(1)}, bf16[256,256]{1,0:T(8,128)(2,1)}, u32[]{:S(2)}) copy-start(bf16[256,256]{1,0:T(8,128)(2,1)} %param.7) | copy-start | bytes 393220
  57.1 5.3 %collective-permute-start.8 = (f32[93184]{0:T(1024)S(1)}, f32[93184]{0:T(1024)S(1)}, u32[]{:S(2)}, u32[]{:S(2)}) collective-permute-start(f32[93184]{0:T(1024)S(1)} %pad_maximum_fusion), channel_id=1, source_target_pairs={{0,1},{1,0},{2,3},{3,2},{4,5},{5,4},{6,7},{7,6},{8,9},{9,8},{10,11... | collective-permute-start | bytes 1118216 | tf_op jit(solution)/shard_map/ppermute | solution.py:152
  62.6 7.8 %collective-permute-start.9 = (f32[46592]{0:T(1024)S(1)}, f32[46592]{0:T(1024)S(1)}, u32[]{:S(2)}, u32[]{:S(2)}) collective-permute-start(f32[46592]{0:T(1024)S(1)} %pad_maximum_fusion.6), channel_id=1, source_target_pairs={{0,2},{1,3},{2,0},{3,1},{4,6},{5,7},{6,4},{7,5},{8,10},{9,11},{10,... | collective-permute-start | bytes 559112 | tf_op jit(solution)/shard_map/ppermute | solution.py:152
  70.5 5.3 %collective-permute-start.10 = (f32[23296]{0:T(1024)S(1)}, f32[23296]{0:T(1024)S(1)}, u32[]{:S(2)}, u32[]{:S(2)}) collective-permute-start(f32[23296]{0:T(1024)S(1)} %pad_maximum_fusion.8), channel_id=1, source_target_pairs={{0,4},{4,0},{8,12},{12,8},{1,5},{5,1},{9,13},{13,9},{2,6},{6,2},{1... | collective-permute-start | bytes 279560 | tf_op jit(solution)/shard_map/ppermute | solution.py:152
  75.8 5.2 %collective-permute-start.11 = (f32[11648]{0:T(1024)S(1)}, f32[11648]{0:T(1024)S(1)}, u32[]{:S(2)}, u32[]{:S(2)}) collective-permute-start(f32[11648]{0:T(1024)S(1)} %pad_maximum_fusion.12), channel_id=1, source_target_pairs={{0,8},{4,12},{8,0},{12,4},{1,9},{5,13},{9,1},{13,5},{2,10},{6,14},... | collective-permute-start | bytes 139784 | tf_op jit(solution)/shard_map/ppermute | solution.py:152
  81.0 5.0 %collective-permute-start.12 = (f32[8192]{0:T(1024)S(1)}, f32[8192]{0:T(1024)S(1)}, u32[]{:S(2)}, u32[]{:S(2)}) collective-permute-start(f32[8192]{0:T(1024)S(1)} %pad_maximum_fusion.14), channel_id=1, source_target_pairs={{0,8},{4,12},{8,0},{12,4},{1,9},{5,13},{9,1},{13,5},{2,10},{6,14},... | collective-permute-start | bytes 98312 | tf_op jit(solution)/shard_map/ppermute | solution.py:162
  86.1 4.3 %collective-permute-start.13 = (f32[16384]{0:T(1024)S(1)}, f32[16384]{0:T(1024)S(1)}, u32[]{:S(2)}, u32[]{:S(2)}) collective-permute-start(f32[16384]{0:T(1024)S(1)} %pad_maximum_fusion.10), channel_id=1, source_target_pairs={{0,4},{4,0},{8,12},{12,8},{1,5},{5,1},{9,13},{13,9},{2,6},{6,2},{1... | collective-permute-start | bytes 196616 | tf_op jit(solution)/shard_map/ppermute | solution.py:162
  90.5 5.2 %collective-permute-start.14 = (f32[36224]{0:T(1024)S(1)}, f32[36224]{0:T(1024)S(1)}, u32[]{:S(2)}, u32[]{:S(2)}) collective-permute-start(f32[36224]{0:T(1024)S(1)} %pad_maximum_fusion.7), channel_id=1, source_target_pairs={{0,2},{1,3},{2,0},{3,1},{4,6},{5,7},{6,4},{7,5},{8,10},{9,11},{10,... | collective-permute-start | bytes 434696 | tf_op jit(solution)/shard_map/ppermute | solution.py:162
  96.2 1.6 %collective-permute-start.15 = (f32[72448]{0:T(1024)S(1)}, f32[72448]{0:T(1024)S(1)}, u32[]{:S(2)}, u32[]{:S(2)}) collective-permute-start(f32[72448]{0:T(1024)S(1)} %pad_maximum_fusion.1), channel_id=1, source_target_pairs={{0,1},{1,0},{2,3},{3,2},{4,5},{5,4},{6,7},{7,6},{8,9},{9,8},{10,11... | collective-permute-start | bytes 869384 | tf_op jit(solution)/shard_map/ppermute | solution.py:162

commit v14 on v13

--- a/solution.py
+++ b/solution.py
@@ -234,7 +234,7 @@
     def from_rows(block):
         return block.transpose(1, 0, 2).reshape(channels, -1)
 
-    forward_kernel, backward_kernel = conv_weights(group_weight)
+    forward_kernel, _ = conv_weights(group_weight)
     first_pre = lax.dot_general(
         first_weight, flattened, contract_lead, preferred_element_type=jnp.float32
     )
@@ -242,6 +242,8 @@
     assert depth == 1
     act_pieces = halo(to_rows(first_act))
     group_pre = conv_call(act_pieces, forward_kernel)
+    late_weight, group_pre = lax.optimization_barrier((group_weight, group_pre))
+    _, backward_kernel = conv_weights(late_weight)
     group_act = rounded(jax.nn.silu(group_pre))
     act_flat = from_rows(group_act)
     summed = flattened.astype(jnp.float32) + lax.dot_general(

time: 101 us -> 100 us (0.990)
  waiting for transfers between devices: 18.8 us -> 21.9 us
  starting transfers between devices: 40.1 us -> 37.7 us
    ppermute x2, waiting for transfers between devices: 0.62 us -> 4.12 us  [halo(): above = lax.ppermute(block[:1], 'grp', down)]
    ppermute x4, starting transfers between devices: 12.6 us -> 10.5 us  [tree_sum(): got = lax.ppermute(jnp.concatenate(sends), axis, pairs)]
  transfers between devices with their start and end apart: 16 -> 16, of which waited for: 10 -> 10; matrix products, arithmetic and copies ran while one was open for 14% -> 13% of each run, Pallas kernels for 4% -> 4%
where the time goes in v14:
time: 100 us; the launch traced here: 99.8 us
  starting transfers between devices  37.7 us (38%)
  waiting for transfers between devices  21.9 us (22%)
  Pallas kernels  14.6 us (15%)
  local copies, waits for them, and re-layouts  10.6 us (11%)
  matrix products  8.06 us (8%)
  other arithmetic  5.39 us (5%)
  between operations  1.61 us (2%)
    ppermute x4, starting transfers between devices, tree_sum(): got = lax.ppermute(jnp.concatenate(sends), axis, pairs)  10.5 us
    pallas_call x2, Pallas kernels, conv_call(): pl.pallas_call(conv_body, out_shape=jax.ShapeDtypeStruct((height, channel...  10.2 us
    ppermute x4, waiting for transfers between devices, tree_sum(): got = lax.ppermute(jnp.concatenate(sends), axis, pairs)  8.74 us
    ppermute x4, waiting for transfers between devices, tree_sum(): lax.ppermute(jnp.concatenate([pieces[n] for n in members]), axis, pairs)  8.66 us
    ppermute x2, starting transfers between devices, halo(): below = lax.ppermute(block[depth - 1:], 'grp', up)  8.42 us
    ppermute x4, starting transfers between devices, tree_sum(): lax.ppermute(jnp.concatenate([pieces[n] for n in members]), axis, pairs)  6.97 us
    ppermute x2, starting transfers between devices, halo(): before = lax.ppermute(last, 'sub', up)  6.59 us
    pallas_call x1, Pallas kernels, wgrad_call(): pl.pallas_call(wgrad_body, out_shape=jax.ShapeDtypeStruct((blocks, channe...  4.39 us
  transfers between devices with their start and end apart: 16, of which 10 were waited for; matrix products, arithmetic and copies ran while one was open for 13% of the time, Pallas kernels for 4%

profile of v14, /device:TPU:0, one launch (start us, length us, event | category | flops | bytes accessed | tf_op | source)
XLA Modules:
  0.0 99.8 jit_solution(398703863183269127)
XLA Ops:
  0.7 1.1 %copy.74 = bf16[256,1,2,128]{0,3,2,1:T(8,128)(2,1)S(1)} copy(bf16[256,1,2,128]{3,2,1,0:T(2,128)(2,1)} %param.5) | data formatting | bytes 262144 | tf_op args[0]
  1.7 1.1 %reduce-precision_convert_fusion.2 = (bf16[256,256]{0,1:T(8,128)(2,1)S(1)}, f32[256,256]{0,1:T(8,128)S(1)}) fusion(bf16[256,256]{0,1:T(8,128)(2,1)S(1)} %bitcast.103, bf16[256,256]{1,0:T(8,128)(2,1)} %param.7), kind=kOutput, calls=%fused_computation.32 | convolution fusion | flops 33947648 | bytes 655360 | tf_op jit(solution)/shard_map/dot_general | solution.py:238
  3.0 4.9 %collective-permute-start = (bf16[1,2,256,128]{3,2,1,0:T(8,128)(2,1)S(1)}, bf16[1,2,256,128]{3,2,1,0:T(8,128)(2,1)S(1)}, u32[]{:S(2)}, u32[]{:S(2)}) collective-permute-start(bf16[1,2,256,128]{3,2,1,0:T(8,128)(2,1)S(1)} %bitcast.93), channel_id=1, source_target_pairs={{0,4},{4,8},{8,12},{1,5},{5,9},{9,13},{2,6},{6,10},{10,14},{3,7},{... | collective-permute-start | bytes 393224 | tf_op jit(solution)/shard_map/ppermute | solution.py:181
  8.0 1.3 %collective-permute-start.1 = (bf16[1,2,256,128]{3,2,1,0:T(8,128)(2,1)S(1)}, bf16[1,2,256,128]{3,2,1,0:T(8,128)(2,1)S(1)}, u32[]{:S(2)}, u32[]{:S(2)}) collective-permute-start(bf16[1,2,256,128]{3,2,1,0:T(8,128)(2,1)S(1)} %bitcast.94), channel_id=1, source_target_pairs={{4,0},{8,4},{12,8},{5,1},{9,5},{13,9},{6,2},{10,6},{14,10},{7,3},{... | collective-permute-start | bytes 393224 | tf_op jit(solution)/shard_map/ppermute | solution.py:182
  9.3 1.0 %copy.77 = f32[256,1,2,128]{0,3,2,1:T(8,128)S(1)} copy(bf16[256,1,2,128]{3,2,1,0:T(2,128)(2,1)} %param.6) | data formatting | bytes 393216 | tf_op jit(solution)/shard_map/convert_element_type | solution.py:253
  10.4 0.3 collective-permute-done.below_ref
  10.7 4.1 %collective-permute-done.1.above_ref = bf16[1,2,256,128]{3,2,1,0:T(8,128)(2,1)S(1)} collective-permute-done((bf16[1,2,256,128]{3,2,1,0:T(8,128)(2,1)S(1)}, bf16[1,2,256,128]{3,2,1,0:T(8,128)(2,1)S(1)}, u32[]{:S(2)}, u32[]{:S(2)}) %collective-permute-start.1) | collective-permute-done | bytes 131104 | tf_op jit(solution)/shard_map/ppermute | solution.py:182
  14.9 1.3 %collective-permute-start.3 = (bf16[3,1,256,128]{3,2,1,0:T(8,128)(2,1)S(1)}, bf16[3,1,256,128]{3,2,1,0:T(8,128)(2,1)S(1)}, u32[]{:S(2)}, u32[]{:S(2)}) collective-permute-start(bf16[3,1,256,128]{3,2,1,0:T(8,128)(2,1)S(1)} %pad_maximum_fusion.3), channel_id=1, source_target_pairs={{1,0},{2,1},{3,2},{5,4},{6,5},{7,6},{9,8},{10,9},{11,10},{13,12},{... | collective-permute-start | bytes 589832 | tf_op jit(solution)/shard_map/ppermute | solution.py:189
  16.2 3.0 %collective-permute-start.2 = (bf16[3,1,256,128]{3,2,1,0:T(8,128)(2,1)S(1)}, bf16[3,1,256,128]{3,2,1,0:T(8,128)(2,1)S(1)}, u32[]{:S(2)}, u32[]{:S(2)}) collective-permute-start(bf16[3,1,256,128]{3,2,1,0:T(8,128)(2,1)S(1)} %pad_maximum_fusion.2), channel_id=1, source_target_pairs={{0,1},{1,2},{2,3},{4,5},{5,6},{6,7},{8,9},{9,10},{10,11},{12,13},{... | collective-permute-start | bytes 589832 | tf_op jit(solution)/shard_map/ppermute | solution.py:188
  19.3 2.9 %convolution_convert_fusion.1 = bf16[256,256,27]{0,1,2:T(8,128)(2,1)} fusion(bf16[256,8,27]{0,1,2:T(8,128)(2,1)S(1)} %bitcast.113, s32[256]{0:T(256)S(1)} %and_select_fusion), kind=kOutput, calls=%fused_computation.1 | convolution fusion | flops 30083072 | bytes 3650560 | tf_op jit(solution)/shard_map/ojt,ji->toi/dot_general | solution.py:212
  22.2 0.6 copy-done.8
  22.9 5.1 %shard_map.92 = f32[2,256,128]{2,1,0:T(8,128)} custom-call(bf16[1,2,256,128]{3,2,1,0:T(8,128)(2,1)} %bitcast.96, bf16[1,2,256,128]{3,2,1,0:T(8,128)(2,1)} %copy-done.5, bf16[1,2,256,128]{3,2,1,0:T(8,128)(2,1)} %copy-done.6, bf16[3,1,256,128]{3,2,1,0:T(8,128)(2,1)} %copy-done.9, bf16[3,1,256,128]{3,2,1,0:T(8,128)(2,1)} %copy-done.8, bf16[9,768,256]{2,1,0:T(8,128)(2,1)} %bitcast.91), custom_call_target="tpu_custom_call" | custom-call | flops 905969664 | bytes 4587520 | tf_op jit(solution)/shard_map/pallas_call | solution.py:60
  28.0 1.1 %fusion.13 = bf16[256,2,128]{2,0,1:T(8,128)(2,1)S(1)} fusion(f32[2,256,128]{2,1,0:T(8,128)} %shard_map.92), kind=kLoop, calls=%fused_computation.47 | loop fusion | flops 393216 | bytes 393216 | tf_op jit(solution)/shard_map/transpose | solution.py:235
  29.2 0.3 fusion.12
  29.5 0.2 fusion.4
  29.9 0.8 fusion.8.delta_ref
  30.7 3.5 %collective-permute-start.4 = (bf16[1,2,256,128]{3,2,1,0:T(8,128)(2,1)}, bf16[1,2,256,128]{3,2,1,0:T(8,128)(2,1)S(1)}, u32[]{:S(2)}, u32[]{:S(2)}) collective-permute-start(bf16[1,2,256,128]{3,2,1,0:T(8,128)(2,1)} %bitcast.16.block_ref), channel_id=1, source_target_pairs={{0,4},{4,8},{8,12},{1,5},{5,9},{9,13},{2,6},{6,10},{10,14},{3,7},{... | collective-permute-start | bytes 393224 | tf_op jit(solution)/shard_map/ppermute | solution.py:181
  34.1 1.3 %collective-permute-start.5 = (bf16[1,2,256,128]{3,2,1,0:T(8,128)(2,1)}, bf16[1,2,256,128]{3,2,1,0:T(8,128)(2,1)S(1)}, u32[]{:S(2)}, u32[]{:S(2)}) collective-permute-start(bf16[1,2,256,128]{3,2,1,0:T(8,128)(2,1)} %bitcast.16.block_ref), channel_id=1, source_target_pairs={{4,0},{8,4},{12,8},{5,1},{9,5},{13,9},{6,2},{10,6},{14,10},{7,3},{... | collective-permute-start | bytes 393224 | tf_op jit(solution)/shard_map/ppermute | solution.py:182
  35.4 0.2 fusion.35
  35.7 4.4 %shard_map.94 = f32[2,256,128]{2,1,0:T(8,128)} custom-call(bf16[1,2,256,128]{3,2,1,0:T(8,128)(2,1)} %bitcast.97, bf16[1,2,256,128]{3,2,1,0:T(8,128)(2,1)} %copy-done.5, bf16[1,2,256,128]{3,2,1,0:T(8,128)(2,1)} %copy-done.6, bf16[3,1,256,128]{3,2,1,0:T(8,128)(2,1)} %copy-done.9, bf16[3,1,256,128]{3,2,1,0:T(8,128)(2,1)} %copy-done.8, ...), custom_call_target="tpu_custom_call" | custom-call | flops 1358954496 | bytes 1179648 | tf_op jit(solution)/shard_map/pallas_call | solution.py:117
  40.1 1.1 %copy.85 = f32[256,2,128]{0,2,1:T(8,128)S(1)} copy(f32[256,2,128]{2,0,1:T(8,128)} %bitcast.115) | data formatting | bytes 524288 | tf_op jit(solution)/shard_map/transpose | solution.py:128
  42.6 0.9 fusion.28
  43.6 1.3 %collective-permute-start.7 = (bf16[3,1,256,128]{3,2,1,0:T(8,128)(2,1)S(1)}, bf16[3,1,256,128]{3,2,1,0:T(8,128)(2,1)S(1)}, u32[]{:S(2)}, u32[]{:S(2)}) collective-permute-start(bf16[3,1,256,128]{3,2,1,0:T(8,128)(2,1)S(1)} %pad_maximum_fusion.5), channel_id=1, source_target_pairs={{1,0},{2,1},{3,2},{5,4},{6,5},{7,6},{9,8},{10,9},{11,10},{13,12},{... | collective-permute-start | bytes 589832 | tf_op jit(solution)/shard_map/ppermute | solution.py:189
  45.0 3.5 %collective-permute-start.6 = (bf16[3,1,256,128]{3,2,1,0:T(8,128)(2,1)S(1)}, bf16[3,1,256,128]{3,2,1,0:T(8,128)(2,1)S(1)}, u32[]{:S(2)}, u32[]{:S(2)}) collective-permute-start(bf16[3,1,256,128]{3,2,1,0:T(8,128)(2,1)S(1)} %pad_maximum_fusion.4), channel_id=1, source_target_pairs={{0,1},{1,2},{2,3},{4,5},{5,6},{6,7},{8,9},{9,10},{10,11},{12,13},{... | collective-permute-start | bytes 589832 | tf_op jit(solution)/shard_map/ppermute | solution.py:188
  48.5 2.9 %convolution_convert_fusion = bf16[256,27,256]{0,2,1:T(8,128)(2,1)} fusion(bf16[256,8,27]{0,1,2:T(8,128)(2,1)S(1)} %rev.3, s32[256]{0:T(256)S(1)} %and_select_fusion), kind=kOutput, calls=%fused_computation | convolution fusion | flops 28313600 | bytes 3650560 | tf_op jit(solution)/shard_map/ji,ojt->tio/dot_general | solution.py:213
  51.4 0.6 copy-done.10
  52.1 5.1 %shard_map.93 = f32[2,256,128]{2,1,0:T(8,128)} custom-call(bf16[1,2,256,128]{3,2,1,0:T(8,128)(2,1)} %bitcast.16.block_ref, bf16[1,2,256,128]{3,2,1,0:T(8,128)(2,1)} %copy-done.3, bf16[1,2,256,128]{3,2,1,0:T(8,128)(2,1)} %copy-done.4, bf16[3,1,256,128]{3,2,1,0:T(8,128)(2,1)} %copy-done.11, bf16[3,1,256,128]{3,2,1,0:T(8,128)(2,1)} %copy-done.10, ...), custom_call_target="tpu_custom_call" | custom-call | flops 905969664 | bytes 4587520 | tf_op jit(solution)/shard_map/pallas_call | solution.py:60
  57.2 1.0 convert_bitcast_fusion
  58.9 2.5 %collective-permute-start.8 = (f32[93184]{0:T(1024)S(1)}, f32[93184]{0:T(1024)S(1)}, u32[]{:S(2)}, u32[]{:S(2)}) collective-permute-start(f32[93184]{0:T(1024)S(1)} %pad_maximum_fusion), channel_id=1, source_target_pairs={{0,1},{1,0},{2,3},{3,2},{4,5},{5,4},{6,7},{7,6},{8,9},{9,8},{10,11... | collective-permute-start | bytes 1118216 | tf_op jit(solution)/shard_map/ppermute | solution.py:152
  61.8 0.9 collective-permute-done.8
  62.9 2.3 %collective-permute-start.9 = (f32[46592]{0:T(1024)S(1)}, f32[46592]{0:T(1024)S(1)}, u32[]{:S(2)}, u32[]{:S(2)}) collective-permute-start(f32[46592]{0:T(1024)S(1)} %pad_maximum_fusion.6), channel_id=1, source_target_pairs={{0,2},{1,3},{2,0},{3,1},{4,6},{5,7},{6,4},{7,5},{8,10},{9,11},{10,... | collective-permute-start | bytes 559112 | tf_op jit(solution)/shard_map/ppermute | solution.py:152
  65.1 5.0 %collective-permute-done.9 = f32[46592]{0:T(1024)S(1)} collective-permute-done((f32[46592]{0:T(1024)S(1)}, f32[46592]{0:T(1024)S(1)}, u32[]{:S(2)}, u32[]{:S(2)}) %collective-permute-start.9) | collective-permute-done | bytes 186400 | tf_op jit(solution)/shard_map/ppermute | solution.py:152
  70.2 2.7 %collective-permute-start.10 = (f32[23296]{0:T(1024)S(1)}, f32[23296]{0:T(1024)S(1)}, u32[]{:S(2)}, u32[]{:S(2)}) collective-permute-start(f32[23296]{0:T(1024)S(1)} %pad_maximum_fusion.8), channel_id=1, source_target_pairs={{0,4},{4,0},{8,12},{12,8},{1,5},{5,1},{9,13},{13,9},{2,6},{6,2},{1... | collective-permute-start | bytes 279560 | tf_op jit(solution)/shard_map/ppermute | solution.py:152
  72.9 0.8 copy.99
  73.7 1.8 %collective-permute-done.10 = f32[23296]{0:T(1024)S(1)} collective-permute-done((f32[23296]{0:T(1024)S(1)}, f32[23296]{0:T(1024)S(1)}, u32[]{:S(2)}, u32[]{:S(2)}) %collective-permute-start.10) | collective-permute-done | bytes 93216 | tf_op jit(solution)/shard_map/ppermute | solution.py:152
  75.6 3.1 %collective-permute-start.11 = (f32[11648]{0:T(1024)S(1)}, f32[11648]{0:T(1024)S(1)}, u32[]{:S(2)}, u32[]{:S(2)}) collective-permute-start(f32[11648]{0:T(1024)S(1)} %pad_maximum_fusion.12), channel_id=1, source_target_pairs={{0,8},{4,12},{8,0},{12,4},{1,9},{5,13},{9,1},{13,5},{2,10},{6,14},... | collective-permute-start | bytes 139784 | tf_op jit(solution)/shard_map/ppermute | solution.py:152
  78.9 0.8 copy.100
  79.7 1.1 %collective-permute-done.11 = f32[11648]{0:T(1024)S(1)} collective-permute-done((f32[11648]{0:T(1024)S(1)}, f32[11648]{0:T(1024)S(1)}, u32[]{:S(2)}, u32[]{:S(2)}) %collective-permute-start.11) | collective-permute-done | bytes 46624 | tf_op jit(solution)/shard_map/ppermute | solution.py:152
  80.8 3.0 %collective-permute-start.12 = (f32[8192]{0:T(1024)S(1)}, f32[8192]{0:T(1024)S(1)}, u32[]{:S(2)}, u32[]{:S(2)}) collective-permute-start(f32[8192]{0:T(1024)S(1)} %pad_maximum_fusion.14), channel_id=1, source_target_pairs={{0,8},{4,12},{8,0},{12,4},{1,9},{5,13},{9,1},{13,5},{2,10},{6,14},... | collective-permute-start | bytes 98312 | tf_op jit(solution)/shard_map/ppermute | solution.py:162
  84.1 1.7 %collective-permute-done.12 = f32[8192]{0:T(1024)S(1)} collective-permute-done((f32[8192]{0:T(1024)S(1)}, f32[8192]{0:T(1024)S(1)}, u32[]{:S(2)}, u32[]{:S(2)}) %collective-permute-start.12) | collective-permute-done | bytes 32800 | tf_op jit(solution)/shard_map/ppermute | solution.py:162
  85.9 1.9 %collective-permute-start.13 = (f32[16384]{0:T(1024)S(1)}, f32[16384]{0:T(1024)S(1)}, u32[]{:S(2)}, u32[]{:S(2)}) collective-permute-start(f32[16384]{0:T(1024)S(1)} %pad_maximum_fusion.10), channel_id=1, source_target_pairs={{0,4},{4,0},{8,12},{12,8},{1,5},{5,1},{9,13},{13,9},{2,6},{6,2},{1... | collective-permute-start | bytes 196616 | tf_op jit(solution)/shard_map/ppermute | solution.py:162
  87.8 2.4 %collective-permute-done.13 = f32[16384]{0:T(1024)S(1)} collective-permute-done((f32[16384]{0:T(1024)S(1)}, f32[16384]{0:T(1024)S(1)}, u32[]{:S(2)}, u32[]{:S(2)}) %collective-permute-start.13) | collective-permute-done | bytes 65568 | tf_op jit(solution)/shard_map/ppermute | solution.py:162
  90.3 2.0 %collective-permute-start.14 = (f32[36224]{0:T(1024)S(1)}, f32[36224]{0:T(1024)S(1)}, u32[]{:S(2)}, u32[]{:S(2)}) collective-permute-start(f32[36224]{0:T(1024)S(1)} %pad_maximum_fusion.7), channel_id=1, source_target_pairs={{0,2},{1,3},{2,0},{3,1},{4,6},{5,7},{6,4},{7,5},{8,10},{9,11},{10,... | collective-permute-start | bytes 434696 | tf_op jit(solution)/shard_map/ppermute | solution.py:162
  92.3 3.2 %collective-permute-done.14 = f32[36224]{0:T(1024)S(1)} collective-permute-done((f32[36224]{0:T(1024)S(1)}, f32[36224]{0:T(1024)S(1)}, u32[]{:S(2)}, u32[]{:S(2)}) %collective-permute-start.14) | collective-permute-done | bytes 144928 | tf_op jit(solution)/shard_map/ppermute | solution.py:162
  96.2 1.4 %collective-permute-done.15 = f32[72448]{0:T(1024)S(1)} collective-permute-done((f32[72448]{0:T(1024)S(1)}, f32[72448]{0:T(1024)S(1)}, u32[]{:S(2)}, u32[]{:S(2)}) %collective-permute-start.15) | collective-permute-done | bytes 289824 | tf_op jit(solution)/shard_map/ppermute | solution.py:162
  97.8 0.3 copy.97
  98.2 0.8 fusion.14
  98.9 0.8 fusion.5
  (134 shorter events, 4.9 us)
Async XLA Ops:
  0.6 28.6 %copy-start = (bf16[256,256]{1,0:T(8,128)(2,1)S(1)}, bf16[256,256]{1,0:T(8,128)(2,1)}, u32[]{:S(2)}) copy-start(bf16[256,256]{1,0:T(8,128)(2,1)} %param.9) | copy-start | bytes 393220
  0.6 18.6 %copy-start.7 = (bf16[256,8,3,3,3]{0,1,4,3,2:T(8,128)(2,1)S(1)}, bf16[256,8,3,3,3]{0,1,4,3,2:T(8,128)(2,1)}, u32[]{:S(2)}) copy-start(bf16[256,8,3,3,3]{0,1,4,3,2:T(8,128)(2,1)} %param.8) | copy-start | bytes 331780
  3.0 19.2 %copy-start.2 = (bf16[256,1,2,128]{3,0,2,1:T(8,128)(2,1)}, bf16[256,1,2,128]{3,0,2,1:T(8,128)(2,1)S(1)}, u32[]{:S(2)}) copy-start(bf16[256,1,2,128]{3,0,2,1:T(8,128)(2,1)S(1)} %copy.75) | copy-start | bytes 393220
  3.0 7.7 %collective-permute-start = (bf16[1,2,256,128]{3,2,1,0:T(8,128)(2,1)S(1)}, bf16[1,2,256,128]{3,2,1,0:T(8,128)(2,1)S(1)}, u32[]{:S(2)}, u32[]{:S(2)}) collective-permute-start(bf16[1,2,256,128]{3,2,1,0:T(8,128)(2,1)S(1)} %bitcast.93), channel_id=1, source_target_pairs={{0,4},{4,8},{8,12},{1,5},{5,9},{9,13},{2,6},{6,10},{10,14},{3,7},{... | collective-permute-start | bytes 393224 | tf_op jit(solution)/shard_map/ppermute | solution.py:181
  8.0 6.9 %collective-permute-start.1 = (bf16[1,2,256,128]{3,2,1,0:T(8,128)(2,1)S(1)}, bf16[1,2,256,128]{3,2,1,0:T(8,128)(2,1)S(1)}, u32[]{:S(2)}, u32[]{:S(2)}) collective-permute-start(bf16[1,2,256,128]{3,2,1,0:T(8,128)(2,1)S(1)} %bitcast.94), channel_id=1, source_target_pairs={{4,0},{8,4},{12,8},{5,1},{9,5},{13,9},{6,2},{10,6},{14,10},{7,3},{... | collective-permute-start | bytes 393224 | tf_op jit(solution)/shard_map/ppermute | solution.py:182
  10.7 11.5 %copy-start.5 = (bf16[1,2,256,128]{3,2,1,0:T(8,128)(2,1)}, bf16[1,2,256,128]{3,2,1,0:T(8,128)(2,1)S(1)}, u32[]{:S(2)}) copy-start(bf16[1,2,256,128]{3,2,1,0:T(8,128)(2,1)S(1)} %collective-permute-done.below_ref) | copy-start | bytes 393220
  14.8 7.4 %copy-start.6 = (bf16[1,2,256,128]{3,2,1,0:T(8,128)(2,1)}, bf16[1,2,256,128]{3,2,1,0:T(8,128)(2,1)S(1)}, u32[]{:S(2)}) copy-start(bf16[1,2,256,128]{3,2,1,0:T(8,128)(2,1)S(1)} %collective-permute-done.1.above_ref) | copy-start | bytes 393220
  14.9 7.3 %collective-permute-start.3 = (bf16[3,1,256,128]{3,2,1,0:T(8,128)(2,1)S(1)}, bf16[3,1,256,128]{3,2,1,0:T(8,128)(2,1)S(1)}, u32[]{:S(2)}, u32[]{:S(2)}) collective-permute-start(bf16[3,1,256,128]{3,2,1,0:T(8,128)(2,1)S(1)} %pad_maximum_fusion.3), channel_id=1, source_target_pairs={{1,0},{2,1},{3,2},{5,4},{6,5},{7,6},{9,8},{10,9},{11,10},{13,12},{... | collective-permute-start | bytes 589832 | tf_op jit(solution)/shard_map/ppermute | solution.py:189
  16.2 5.9 %collective-permute-start.2 = (bf16[3,1,256,128]{3,2,1,0:T(8,128)(2,1)S(1)}, bf16[3,1,256,128]{3,2,1,0:T(8,128)(2,1)S(1)}, u32[]{:S(2)}, u32[]{:S(2)}) collective-permute-start(bf16[3,1,256,128]{3,2,1,0:T(8,128)(2,1)S(1)} %pad_maximum_fusion.2), channel_id=1, source_target_pairs={{0,1},{1,2},{2,3},{4,5},{5,6},{6,7},{8,9},{9,10},{10,11},{12,13},{... | collective-permute-start | bytes 589832 | tf_op jit(solution)/shard_map/ppermute | solution.py:188
  22.1 0.7 copy-start.8
  22.2 0.7 copy-start.9
  28.0 1.9 %copy-start.1 = (f32[2,256,128]{2,1,0:T(8,128)S(1)}, f32[2,256,128]{2,1,0:T(8,128)}, u32[]{:S(2)}) copy-start(f32[2,256,128]{2,1,0:T(8,128)} %shard_map.92) | copy-start | bytes 786436
  30.7 12.9 %collective-permute-start.4 = (bf16[1,2,256,128]{3,2,1,0:T(8,128)(2,1)}, bf16[1,2,256,128]{3,2,1,0:T(8,128)(2,1)S(1)}, u32[]{:S(2)}, u32[]{:S(2)}) collective-permute-start(bf16[1,2,256,128]{3,2,1,0:T(8,128)(2,1)} %bitcast.16.block_ref), channel_id=1, source_target_pairs={{0,4},{4,8},{8,12},{1,5},{5,9},{9,13},{2,6},{6,10},{10,14},{3,7},{... | collective-permute-start | bytes 393224 | tf_op jit(solution)/shard_map/ppermute | solution.py:181
  34.1 9.4 %collective-permute-start.5 = (bf16[1,2,256,128]{3,2,1,0:T(8,128)(2,1)}, bf16[1,2,256,128]{3,2,1,0:T(8,128)(2,1)S(1)}, u32[]{:S(2)}, u32[]{:S(2)}) collective-permute-start(bf16[1,2,256,128]{3,2,1,0:T(8,128)(2,1)} %bitcast.16.block_ref), channel_id=1, source_target_pairs={{4,0},{8,4},{12,8},{5,1},{9,5},{13,9},{6,2},{10,6},{14,10},{7,3},{... | collective-permute-start | bytes 393224 | tf_op jit(solution)/shard_map/ppermute | solution.py:182
  43.5 7.9 %copy-start.3 = (bf16[1,2,256,128]{3,2,1,0:T(8,128)(2,1)}, bf16[1,2,256,128]{3,2,1,0:T(8,128)(2,1)S(1)}, u32[]{:S(2)}) copy-start(bf16[1,2,256,128]{3,2,1,0:T(8,128)(2,1)S(1)} %collective-permute-done.4.below_ref) | copy-start | bytes 393220
  43.6 7.9 %copy-start.4 = (bf16[1,2,256,128]{3,2,1,0:T(8,128)(2,1)}, bf16[1,2,256,128]{3,2,1,0:T(8,128)(2,1)S(1)}, u32[]{:S(2)}) copy-start(bf16[1,2,256,128]{3,2,1,0:T(8,128)(2,1)S(1)} %collective-permute-done.5.above_ref) | copy-start | bytes 393220
  43.6 7.8 %collective-permute-start.7 = (bf16[3,1,256,128]{3,2,1,0:T(8,128)(2,1)S(1)}, bf16[3,1,256,128]{3,2,1,0:T(8,128)(2,1)S(1)}, u32[]{:S(2)}, u32[]{:S(2)}) collective-permute-start(bf16[3,1,256,128]{3,2,1,0:T(8,128)(2,1)S(1)} %pad_maximum_fusion.5), channel_id=1, source_target_pairs={{1,0},{2,1},{3,2},{5,4},{6,5},{7,6},{9,8},{10,9},{11,10},{13,12},{... | collective-permute-start | bytes 589832 | tf_op jit(solution)/shard_map/ppermute | solution.py:189
  45.0 6.5 %collective-permute-start.6 = (bf16[3,1,256,128]{3,2,1,0:T(8,128)(2,1)S(1)}, bf16[3,1,256,128]{3,2,1,0:T(8,128)(2,1)S(1)}, u32[]{:S(2)}, u32[]{:S(2)}) collective-permute-start(bf16[3,1,256,128]{3,2,1,0:T(8,128)(2,1)S(1)} %pad_maximum_fusion.4), channel_id=1, source_target_pairs={{0,1},{1,2},{2,3},{4,5},{5,6},{6,7},{8,9},{9,10},{10,11},{12,13},{... | collective-permute-start | bytes 589832 | tf_op jit(solution)/shard_map/ppermute | solution.py:188
  51.4 0.7 copy-start.10
  51.4 0.7 copy-start.11
  58.7 20.0 %copy-start.12 = (bf16[256,256]{1,0:T(8,128)(2,1)S(1)}, bf16[256,256]{1,0:T(8,128)(2,1)}, u32[]{:S(2)}) copy-start(bf16[256,256]{1,0:T(8,128)(2,1)} %param.7) | copy-start | bytes 393220
  58.9 3.8 %collective-permute-start.8 = (f32[93184]{0:T(1024)S(1)}, f32[93184]{0:T(1024)S(1)}, u32[]{:S(2)}, u32[]{:S(2)}) collective-permute-start(f32[93184]{0:T(1024)S(1)} %pad_maximum_fusion), channel_id=1, source_target_pairs={{0,1},{1,0},{2,3},{3,2},{4,5},{5,4},{6,7},{7,6},{8,9},{9,8},{10,11... | collective-permute-start | bytes 1118216 | tf_op jit(solution)/shard_map/ppermute | solution.py:152
  62.9 7.3 %collective-permute-start.9 = (f32[46592]{0:T(1024)S(1)}, f32[46592]{0:T(1024)S(1)}, u32[]{:S(2)}, u32[]{:S(2)}) collective-permute-start(f32[46592]{0:T(1024)S(1)} %pad_maximum_fusion.6), channel_id=1, source_target_pairs={{0,2},{1,3},{2,0},{3,1},{4,6},{5,7},{6,4},{7,5},{8,10},{9,11},{10,... | collective-permute-start | bytes 559112 | tf_op jit(solution)/shard_map/ppermute | solution.py:152
  70.2 5.3 %collective-permute-start.10 = (f32[23296]{0:T(1024)S(1)}, f32[23296]{0:T(1024)S(1)}, u32[]{:S(2)}, u32[]{:S(2)}) collective-permute-start(f32[23296]{0:T(1024)S(1)} %pad_maximum_fusion.8), channel_id=1, source_target_pairs={{0,4},{4,0},{8,12},{12,8},{1,5},{5,1},{9,13},{13,9},{2,6},{6,2},{1... | collective-permute-start | bytes 279560 | tf_op jit(solution)/shard_map/ppermute | solution.py:152
  75.6 5.2 %collective-permute-start.11 = (f32[11648]{0:T(1024)S(1)}, f32[11648]{0:T(1024)S(1)}, u32[]{:S(2)}, u32[]{:S(2)}) collective-permute-start(f32[11648]{0:T(1024)S(1)} %pad_maximum_fusion.12), channel_id=1, source_target_pairs={{0,8},{4,12},{8,0},{12,4},{1,9},{5,13},{9,1},{13,5},{2,10},{6,14},... | collective-permute-start | bytes 139784 | tf_op jit(solution)/shard_map/ppermute | solution.py:152
  80.8 5.0 %collective-permute-start.12 = (f32[8192]{0:T(1024)S(1)}, f32[8192]{0:T(1024)S(1)}, u32[]{:S(2)}, u32[]{:S(2)}) collective-permute-start(f32[8192]{0:T(1024)S(1)} %pad_maximum_fusion.14), channel_id=1, source_target_pairs={{0,8},{4,12},{8,0},{12,4},{1,9},{5,13},{9,1},{13,5},{2,10},{6,14},... | collective-permute-start | bytes 98312 | tf_op jit(solution)/shard_map/ppermute | solution.py:162
  85.9 4.3 %collective-permute-start.13 = (f32[16384]{0:T(1024)S(1)}, f32[16384]{0:T(1024)S(1)}, u32[]{:S(2)}, u32[]{:S(2)}) collective-permute-start(f32[16384]{0:T(1024)S(1)} %pad_maximum_fusion.10), channel_id=1, source_target_pairs={{0,4},{4,0},{8,12},{12,8},{1,5},{5,1},{9,13},{13,9},{2,6},{6,2},{1... | collective-permute-start | bytes 196616 | tf_op jit(solution)/shard_map/ppermute | solution.py:162
  90.3 5.2 %collective-permute-start.14 = (f32[36224]{0:T(1024)S(1)}, f32[36224]{0:T(1024)S(1)}, u32[]{:S(2)}, u32[]{:S(2)}) collective-permute-start(f32[36224]{0:T(1024)S(1)} %pad_maximum_fusion.7), channel_id=1, source_target_pairs={{0,2},{1,3},{2,0},{3,1},{4,6},{5,7},{6,4},{7,5},{8,10},{9,11},{10,... | collective-permute-start | bytes 434696 | tf_op jit(solution)/shard_map/ppermute | solution.py:162
  95.9 1.6 %collective-permute-start.15 = (f32[72448]{0:T(1024)S(1)}, f32[72448]{0:T(1024)S(1)}, u32[]{:S(2)}, u32[]{:S(2)}) collective-permute-start(f32[72448]{0:T(1024)S(1)} %pad_maximum_fusion.1), channel_id=1, source_target_pairs={{0,1},{1,0},{2,3},{3,2},{4,5},{5,4},{6,7},{7,6},{8,9},{9,8},{10,11... | collective-permute-start | bytes 869384 | tf_op jit(solution)/shard_map/ppermute | solution.py:162

commit v15 on v13

--- a/solution.py
+++ b/solution.py
@@ -173,13 +173,16 @@
     return pieces
 
 
-def halo(block):
+def halo(block, planes=None):
     count = lax.axis_size("grp")
     up = [(i, i + 1) for i in range(count - 1)]
     down = [(i + 1, i) for i in range(count - 1)]
     depth, height = block.shape[0], block.shape[1]
-    below = lax.ppermute(block[depth - 1 :], "grp", up)
-    above = lax.ppermute(block[:1], "grp", down)
+    if planes is None:
+        below = lax.ppermute(block[depth - 1 :], "grp", up)
+        above = lax.ppermute(block[:1], "grp", down)
+    else:
+        below, above = planes
     count = lax.axis_size("sub")
     up = [(i, i + 1) for i in range(count - 1)]
     down = [(i + 1, i) for i in range(count - 1)]
@@ -240,7 +243,26 @@
     )
     first_act = rounded(jax.nn.silu(first_pre))
     assert depth == 1
-    act_pieces = halo(to_rows(first_act))
+    count = lax.axis_size("grp")
+    up = [(i, i + 1) for i in range(count - 1)]
+    down = [(i + 1, i) for i in range(count - 1)]
+    near = [lax.ppermute(volume, "grp", up), lax.ppermute(volume, "grp", down)]
+    near = [
+        to_rows(
+            rounded(
+                jax.nn.silu(
+                    lax.dot_general(
+                        first_weight,
+                        plane.reshape(channels, -1),
+                        contract_lead,
+                        preferred_element_type=jnp.float32,
+                    )
+                )
+            )
+        )
+        for plane in near
+    ]
+    act_pieces = halo(to_rows(first_act), near)
     group_pre = conv_call(act_pieces, forward_kernel)
     group_act = rounded(jax.nn.silu(group_pre))
     act_flat = from_rows(group_act)

time: 101 us -> 100 us (0.990)
    ppermute x0 -> x2, starting transfers between devices: none -> 6.36 us  [per_device(): near = [lax.ppermute(volume, 'grp', up), lax.ppermute(volume, 'grp', down)]]
    ppermute x2 -> x1, starting transfers between devices: 8.88 us -> 4.55 us  [halo(): below = lax.ppermute(block[depth - 1:], 'grp', up)]
    ppermute x2 -> x1, starting transfers between devices: 2.58 us -> 1.29 us  [halo(): above = lax.ppermute(block[:1], 'grp', down)]
    unnamed x33 -> x35, local copies, waits for them, and re-layouts: 4.32 us -> 4.28 us
  transfers between devices with their start and end apart: 16 -> 16, of which waited for: 10 -> 9; matrix products, arithmetic and copies ran while one was open for 14% -> 15% of each run, Pallas kernels for 4% -> 4%
where the time goes in v15:
time: 100 us; the launch traced here: 99.7 us
  starting transfers between devices  41 us (41%)
  waiting for transfers between devices  18 us (18%)
  Pallas kernels  14.6 us (15%)
  local copies, waits for them, and re-layouts  9.86 us (10%)
  matrix products  8.62 us (9%)
  other arithmetic  6 us (6%)
  between operations  1.65 us (2%)
    ppermute x4, starting transfers between devices, tree_sum(): got = lax.ppermute(jnp.concatenate(sends), axis, pairs)  12.6 us
    pallas_call x2, Pallas kernels, conv_call(): pl.pallas_call(conv_body, out_shape=jax.ShapeDtypeStruct((height, channel...  10.2 us
    ppermute x4, waiting for transfers between devices, tree_sum(): got = lax.ppermute(jnp.concatenate(sends), axis, pairs)  8.74 us
    ppermute x4, waiting for transfers between devices, tree_sum(): lax.ppermute(jnp.concatenate([pieces[n] for n in members]), axis, pairs)  8.63 us
    ppermute x4, starting transfers between devices, tree_sum(): lax.ppermute(jnp.concatenate([pieces[n] for n in members]), axis, pairs)  6.85 us
    ppermute x2, starting transfers between devices, halo(): before = lax.ppermute(last, 'sub', up)  6.72 us
    ppermute x2, starting transfers between devices, per_device(): near = [lax.ppermute(volume, 'grp', up), lax.ppermute(volume, 'grp', down)]  6.36 us
    ppermute x1, starting transfers between devices, halo(): below = lax.ppermute(block[depth - 1:], 'grp', up)  4.55 us
  transfers between devices with their start and end apart: 16, of which 9 were waited for; matrix products, arithmetic and copies ran while one was open for 15% of the time, Pallas kernels for 4%

profile of v15, /device:TPU:0, one launch (start us, length us, event | category | flops | bytes accessed | tf_op | source)
XLA Modules:
  0.0 99.7 jit_solution(986282355667934199)
XLA Ops:
  0.7 5.1 %collective-permute-start = (bf16[256,1,2,128]{3,2,1,0:T(2,128)(2,1)}, bf16[256,1,2,128]{3,2,1,0:T(2,128)(2,1)S(1)}, u32[]{:S(2)}, u32[]{:S(2)}) collective-permute-start(bf16[256,1,2,128]{3,2,1,0:T(2,128)(2,1)} %param.5), channel_id=1, source_target_pairs={{0,4},{4,8},{8,12},{1,5},{5,9},{9,13},{2,6},{6,10},{10,14},{3,7},{... | collective-permute-start | bytes 393224 | tf_op jit(solution)/shard_map/ppermute | solution.py:249
  5.7 1.3 %collective-permute-start.1 = (bf16[256,1,2,128]{3,2,1,0:T(2,128)(2,1)}, bf16[256,1,2,128]{3,2,1,0:T(2,128)(2,1)S(1)}, u32[]{:S(2)}, u32[]{:S(2)}) collective-permute-start(bf16[256,1,2,128]{3,2,1,0:T(2,128)(2,1)} %param.5), channel_id=1, source_target_pairs={{4,0},{8,4},{12,8},{5,1},{9,5},{13,9},{6,2},{10,6},{14,10},{7,3},{... | collective-permute-start | bytes 393224 | tf_op jit(solution)/shard_map/ppermute | solution.py:249
  7.0 1.0 %copy.80 = bf16[256,1,2,128]{0,3,2,1:T(8,128)(2,1)S(1)} copy(bf16[256,1,2,128]{3,2,1,0:T(2,128)(2,1)} %param.5) | data formatting | bytes 262144 | tf_op args[0]
  8.1 3.8 %convolution_convert_fusion.1 = bf16[256,256,27]{0,1,2:T(8,128)(2,1)} fusion(bf16[256,8,27]{0,1,2:T(8,128)(2,1)} %bitcast.132, s32[256]{0:T(256)S(1)} %and_select_fusion), kind=kOutput, calls=%fused_computation.1 | convolution fusion | flops 30083072 | bytes 3650560 | tf_op jit(solution)/shard_map/ojt,ji->toi/dot_general | solution.py:215
  11.9 0.2 reduce-precision_convert_fusion.4
  12.4 0.3 reduce-precision_convert_fusion.3
  12.8 0.3 reduce-precision_convert_fusion.2
  13.3 1.3 %collective-permute-start.3 = (bf16[3,1,256,128]{3,2,1,0:T(8,128)(2,1)S(1)}, bf16[3,1,256,128]{3,2,1,0:T(8,128)(2,1)S(1)}, u32[]{:S(2)}, u32[]{:S(2)}) collective-permute-start(bf16[3,1,256,128]{3,2,1,0:T(8,128)(2,1)S(1)} %pad_maximum_fusion.3), channel_id=1, source_target_pairs={{1,0},{2,1},{3,2},{5,4},{6,5},{7,6},{9,8},{10,9},{11,10},{13,12},{... | collective-permute-start | bytes 589832 | tf_op jit(solution)/shard_map/ppermute | solution.py:192
  14.7 3.2 %collective-permute-start.2 = (bf16[3,1,256,128]{3,2,1,0:T(8,128)(2,1)S(1)}, bf16[3,1,256,128]{3,2,1,0:T(8,128)(2,1)S(1)}, u32[]{:S(2)}, u32[]{:S(2)}) collective-permute-start(bf16[3,1,256,128]{3,2,1,0:T(8,128)(2,1)S(1)} %pad_maximum_fusion.2), channel_id=1, source_target_pairs={{0,1},{1,2},{2,3},{4,5},{5,6},{6,7},{8,9},{9,10},{10,11},{12,13},{... | collective-permute-start | bytes 589832 | tf_op jit(solution)/shard_map/ppermute | solution.py:191
  17.9 2.9 %convolution_convert_fusion = bf16[256,256,27]{1,0,2:T(8,128)(2,1)} fusion(bf16[256,8,27]{0,1,2:T(8,128)(2,1)S(1)} %bitcast.133, s32[256]{0:T(256)S(1)} %and_select_fusion), kind=kOutput, calls=%fused_computation | convolution fusion | flops 30138368 | bytes 3650560 | tf_op jit(solution)/shard_map/ji,ojt->tio/dot_general | solution.py:216
  20.8 0.6 copy-done.8
  21.5 5.1 %shard_map.92 = f32[2,256,128]{2,1,0:T(8,128)} custom-call(bf16[1,2,256,128]{3,2,1,0:T(8,128)(2,1)} %bitcast.112, bf16[1,2,256,128]{3,2,1,0:T(8,128)(2,1)} %bitcast.115, bf16[1,2,256,128]{3,2,1,0:T(8,128)(2,1)} %bitcast.109, bf16[3,1,256,128]{3,2,1,0:T(8,128)(2,1)} %copy-done.9, bf16[3,1,256,128]{3,2,1,0:T(8,128)(2,1)} %copy-done.8, ...), custom_call_target="tpu_custom_call" | custom-call | flops 905969664 | bytes 4587520 | tf_op jit(solution)/shard_map/pallas_call | solution.py:60
  26.6 1.1 %fusion.24 = bf16[256,2,128]{2,0,1:T(8,128)(2,1)S(1)} fusion(f32[2,256,128]{2,1,0:T(8,128)} %shard_map.92), kind=kLoop, calls=%fused_computation.56 | loop fusion | flops 393216 | bytes 393216 | tf_op jit(solution)/shard_map/transpose | solution.py:238
  27.8 0.3 fusion.12
  28.5 0.8 fusion.8.delta_ref
  29.2 4.6 %collective-permute-start.4 = (bf16[1,2,256,128]{3,2,1,0:T(8,128)(2,1)}, bf16[1,2,256,128]{3,2,1,0:T(8,128)(2,1)S(1)}, u32[]{:S(2)}, u32[]{:S(2)}) collective-permute-start(bf16[1,2,256,128]{3,2,1,0:T(8,128)(2,1)} %bitcast.20.block_ref), channel_id=1, source_target_pairs={{0,4},{4,8},{8,12},{1,5},{5,9},{9,13},{2,6},{6,10},{10,14},{3,7},{... | collective-permute-start | bytes 393224 | tf_op jit(solution)/shard_map/ppermute | solution.py:182
  33.8 1.3 %collective-permute-start.5 = (bf16[1,2,256,128]{3,2,1,0:T(8,128)(2,1)}, bf16[1,2,256,128]{3,2,1,0:T(8,128)(2,1)S(1)}, u32[]{:S(2)}, u32[]{:S(2)}) collective-permute-start(bf16[1,2,256,128]{3,2,1,0:T(8,128)(2,1)} %bitcast.20.block_ref), channel_id=1, source_target_pairs={{4,0},{8,4},{12,8},{5,1},{9,5},{13,9},{6,2},{10,6},{14,10},{7,3},{... | collective-permute-start | bytes 393224 | tf_op jit(solution)/shard_map/ppermute | solution.py:183
  35.1 0.2 fusion.46
  35.3 4.4 %shard_map.94 = f32[2,256,128]{2,1,0:T(8,128)} custom-call(bf16[1,2,256,128]{3,2,1,0:T(8,128)(2,1)} %bitcast.113, bf16[1,2,256,128]{3,2,1,0:T(8,128)(2,1)} %bitcast.116, bf16[1,2,256,128]{3,2,1,0:T(8,128)(2,1)} %bitcast.110, bf16[3,1,256,128]{3,2,1,0:T(8,128)(2,1)} %copy-done.9, bf16[3,1,256,128]{3,2,1,0:T(8,128)(2,1)} %copy-done.8, ...), custom_call_target="tpu_custom_call" | custom-call | flops 1358954496 | bytes 1179648 | tf_op jit(solution)/shard_map/pallas_call | solution.py:117
  39.7 1.1 %copy.93 = f32[256,2,128]{0,2,1:T(8,128)S(1)} copy(f32[256,2,128]{2,0,1:T(8,128)} %bitcast.134) | data formatting | bytes 524288 | tf_op jit(solution)/shard_map/transpose | solution.py:128
  42.1 0.9 fusion.39
  43.1 1.3 %collective-permute-start.7 = (bf16[3,1,256,128]{3,2,1,0:T(8,128)(2,1)S(1)}, bf16[3,1,256,128]{3,2,1,0:T(8,128)(2,1)S(1)}, u32[]{:S(2)}, u32[]{:S(2)}) collective-permute-start(bf16[3,1,256,128]{3,2,1,0:T(8,128)(2,1)S(1)} %pad_maximum_fusion.5), channel_id=1, source_target_pairs={{1,0},{2,1},{3,2},{5,4},{6,5},{7,6},{9,8},{10,9},{11,10},{13,12},{... | collective-permute-start | bytes 589832 | tf_op jit(solution)/shard_map/ppermute | solution.py:192
  44.4 3.5 %collective-permute-start.6 = (bf16[3,1,256,128]{3,2,1,0:T(8,128)(2,1)S(1)}, bf16[3,1,256,128]{3,2,1,0:T(8,128)(2,1)S(1)}, u32[]{:S(2)}, u32[]{:S(2)}) collective-permute-start(bf16[3,1,256,128]{3,2,1,0:T(8,128)(2,1)S(1)} %pad_maximum_fusion.4), channel_id=1, source_target_pairs={{0,1},{1,2},{2,3},{4,5},{5,6},{6,7},{8,9},{9,10},{10,11},{12,13},{... | collective-permute-start | bytes 589832 | tf_op jit(solution)/shard_map/ppermute | solution.py:191
  48.2 0.6 collective-permute-done.6.before_ref
  48.8 0.6 copy-done.11
  49.5 5.1 %shard_map.93 = f32[2,256,128]{2,1,0:T(8,128)} custom-call(bf16[1,2,256,128]{3,2,1,0:T(8,128)(2,1)} %bitcast.20.block_ref, bf16[1,2,256,128]{3,2,1,0:T(8,128)(2,1)} %copy-done.5, bf16[1,2,256,128]{3,2,1,0:T(8,128)(2,1)} %copy-done.6, bf16[3,1,256,128]{3,2,1,0:T(8,128)(2,1)} %copy-done.11, bf16[3,1,256,128]{3,2,1,0:T(8,128)(2,1)} %copy-done.10, ...), custom_call_target="tpu_custom_call" | custom-call | flops 905969664 | bytes 4587520 | tf_op jit(solution)/shard_map/pallas_call | solution.py:60
  54.6 1.0 convert_bitcast_fusion
  56.3 4.0 %collective-permute-start.8 = (f32[93184]{0:T(1024)S(1)}, f32[93184]{0:T(1024)S(1)}, u32[]{:S(2)}, u32[]{:S(2)}) collective-permute-start(f32[93184]{0:T(1024)S(1)} %pad_maximum_fusion), channel_id=1, source_target_pairs={{0,1},{1,0},{2,3},{3,2},{4,5},{5,4},{6,7},{7,6},{8,9},{9,8},{10,11... | collective-permute-start | bytes 1118216 | tf_op jit(solution)/shard_map/ppermute | solution.py:152
  60.7 0.9 collective-permute-done.8
  61.7 2.8 %collective-permute-start.9 = (f32[46592]{0:T(1024)S(1)}, f32[46592]{0:T(1024)S(1)}, u32[]{:S(2)}, u32[]{:S(2)}) collective-permute-start(f32[46592]{0:T(1024)S(1)} %pad_maximum_fusion.6), channel_id=1, source_target_pairs={{0,2},{1,3},{2,0},{3,1},{4,6},{5,7},{6,4},{7,5},{8,10},{9,11},{10,... | collective-permute-start | bytes 559112 | tf_op jit(solution)/shard_map/ppermute | solution.py:152
  64.5 5.0 %collective-permute-done.9 = f32[46592]{0:T(1024)S(1)} collective-permute-done((f32[46592]{0:T(1024)S(1)}, f32[46592]{0:T(1024)S(1)}, u32[]{:S(2)}, u32[]{:S(2)}) %collective-permute-start.9) | collective-permute-done | bytes 186400 | tf_op jit(solution)/shard_map/ppermute | solution.py:152
  69.7 2.7 %collective-permute-start.10 = (f32[23296]{0:T(1024)S(1)}, f32[23296]{0:T(1024)S(1)}, u32[]{:S(2)}, u32[]{:S(2)}) collective-permute-start(f32[23296]{0:T(1024)S(1)} %pad_maximum_fusion.8), channel_id=1, source_target_pairs={{0,4},{4,0},{8,12},{12,8},{1,5},{5,1},{9,13},{13,9},{2,6},{6,2},{1... | collective-permute-start | bytes 279560 | tf_op jit(solution)/shard_map/ppermute | solution.py:152
  72.4 0.8 copy.107
  73.2 1.8 %collective-permute-done.10 = f32[23296]{0:T(1024)S(1)} collective-permute-done((f32[23296]{0:T(1024)S(1)}, f32[23296]{0:T(1024)S(1)}, u32[]{:S(2)}, u32[]{:S(2)}) %collective-permute-start.10) | collective-permute-done | bytes 93216 | tf_op jit(solution)/shard_map/ppermute | solution.py:152
  75.0 3.1 %collective-permute-start.11 = (f32[11648]{0:T(1024)S(1)}, f32[11648]{0:T(1024)S(1)}, u32[]{:S(2)}, u32[]{:S(2)}) collective-permute-start(f32[11648]{0:T(1024)S(1)} %pad_maximum_fusion.12), channel_id=1, source_target_pairs={{0,8},{4,12},{8,0},{12,4},{1,9},{5,13},{9,1},{13,5},{2,10},{6,14},... | collective-permute-start | bytes 139784 | tf_op jit(solution)/shard_map/ppermute | solution.py:152
  78.3 0.8 copy.108
  79.1 1.1 %collective-permute-done.11 = f32[11648]{0:T(1024)S(1)} collective-permute-done((f32[11648]{0:T(1024)S(1)}, f32[11648]{0:T(1024)S(1)}, u32[]{:S(2)}, u32[]{:S(2)}) %collective-permute-start.11) | collective-permute-done | bytes 46624 | tf_op jit(solution)/shard_map/ppermute | solution.py:152
  80.2 3.0 %collective-permute-start.12 = (f32[8192]{0:T(1024)S(1)}, f32[8192]{0:T(1024)S(1)}, u32[]{:S(2)}, u32[]{:S(2)}) collective-permute-start(f32[8192]{0:T(1024)S(1)} %pad_maximum_fusion.14), channel_id=1, source_target_pairs={{0,8},{4,12},{8,0},{12,4},{1,9},{5,13},{9,1},{13,5},{2,10},{6,14},... | collective-permute-start | bytes 98312 | tf_op jit(solution)/shard_map/ppermute | solution.py:162
  83.6 1.7 %collective-permute-done.12 = f32[8192]{0:T(1024)S(1)} collective-permute-done((f32[8192]{0:T(1024)S(1)}, f32[8192]{0:T(1024)S(1)}, u32[]{:S(2)}, u32[]{:S(2)}) %collective-permute-start.12) | collective-permute-done | bytes 32800 | tf_op jit(solution)/shard_map/ppermute | solution.py:162
  85.3 1.9 %collective-permute-start.13 = (f32[16384]{0:T(1024)S(1)}, f32[16384]{0:T(1024)S(1)}, u32[]{:S(2)}, u32[]{:S(2)}) collective-permute-start(f32[16384]{0:T(1024)S(1)} %pad_maximum_fusion.10), channel_id=1, source_target_pairs={{0,4},{4,0},{8,12},{12,8},{1,5},{5,1},{9,13},{13,9},{2,6},{6,2},{1... | collective-permute-start | bytes 196616 | tf_op jit(solution)/shard_map/ppermute | solution.py:162
  87.2 2.4 %collective-permute-done.13 = f32[16384]{0:T(1024)S(1)} collective-permute-done((f32[16384]{0:T(1024)S(1)}, f32[16384]{0:T(1024)S(1)}, u32[]{:S(2)}, u32[]{:S(2)}) %collective-permute-start.13) | collective-permute-done | bytes 65568 | tf_op jit(solution)/shard_map/ppermute | solution.py:162
  89.7 1.8 %collective-permute-start.14 = (f32[36224]{0:T(1024)S(1)}, f32[36224]{0:T(1024)S(1)}, u32[]{:S(2)}, u32[]{:S(2)}) collective-permute-start(f32[36224]{0:T(1024)S(1)} %pad_maximum_fusion.7), channel_id=1, source_target_pairs={{0,2},{1,3},{2,0},{3,1},{4,6},{5,7},{6,4},{7,5},{8,10},{9,11},{10,... | collective-permute-start | bytes 434696 | tf_op jit(solution)/shard_map/ppermute | solution.py:162
  91.6 3.3 %collective-permute-done.14 = f32[36224]{0:T(1024)S(1)} collective-permute-done((f32[36224]{0:T(1024)S(1)}, f32[36224]{0:T(1024)S(1)}, u32[]{:S(2)}, u32[]{:S(2)}) %collective-permute-start.14) | collective-permute-done | bytes 144928 | tf_op jit(solution)/shard_map/ppermute | solution.py:162
  95.7 1.2 %collective-permute-done.15 = f32[72448]{0:T(1024)S(1)} collective-permute-done((f32[72448]{0:T(1024)S(1)}, f32[72448]{0:T(1024)S(1)}, u32[]{:S(2)}, u32[]{:S(2)}) %collective-permute-start.15) | collective-permute-done | bytes 289824 | tf_op jit(solution)/shard_map/ppermute | solution.py:162
  97.1 0.3 copy.105
  97.5 0.7 fusion.6
  98.2 0.8 fusion.25
  99.0 0.7 fusion.5
  (139 shorter events, 5.5 us)
Async XLA Ops:
  0.6 11.2 %copy-start = (bf16[256,256]{1,0:T(8,128)(2,1)S(1)}, bf16[256,256]{1,0:T(8,128)(2,1)}, u32[]{:S(2)}) copy-start(bf16[256,256]{1,0:T(8,128)(2,1)} %param.7) | copy-start | bytes 393220
  0.6 11.6 %copy-start.12 = (bf16[256,1,2,128]{3,2,1,0:T(2,128)(2,1)S(1)}, bf16[256,1,2,128]{3,2,1,0:T(2,128)(2,1)}, u32[]{:S(2)}) copy-start(bf16[256,1,2,128]{3,2,1,0:T(2,128)(2,1)} %param.6) | copy-start | bytes 393220
  0.7 11.7 %collective-permute-start = (bf16[256,1,2,128]{3,2,1,0:T(2,128)(2,1)}, bf16[256,1,2,128]{3,2,1,0:T(2,128)(2,1)S(1)}, u32[]{:S(2)}, u32[]{:S(2)}) collective-permute-start(bf16[256,1,2,128]{3,2,1,0:T(2,128)(2,1)} %param.5), channel_id=1, source_target_pairs={{0,4},{4,8},{8,12},{1,5},{5,9},{9,13},{2,6},{6,10},{10,14},{3,7},{... | collective-permute-start | bytes 393224 | tf_op jit(solution)/shard_map/ppermute | solution.py:249
  5.7 7.1 %collective-permute-start.1 = (bf16[256,1,2,128]{3,2,1,0:T(2,128)(2,1)}, bf16[256,1,2,128]{3,2,1,0:T(2,128)(2,1)S(1)}, u32[]{:S(2)}, u32[]{:S(2)}) collective-permute-start(bf16[256,1,2,128]{3,2,1,0:T(2,128)(2,1)} %param.5), channel_id=1, source_target_pairs={{4,0},{8,4},{12,8},{5,1},{9,5},{13,9},{6,2},{10,6},{14,10},{7,3},{... | collective-permute-start | bytes 393224 | tf_op jit(solution)/shard_map/ppermute | solution.py:249
  11.9 6.0 %copy-start.7 = (bf16[256,8,3,3,3]{0,1,4,3,2:T(8,128)(2,1)S(1)}, bf16[256,8,3,3,3]{0,1,4,3,2:T(8,128)(2,1)}, u32[]{:S(2)}) copy-start(bf16[256,8,3,3,3]{0,1,4,3,2:T(8,128)(2,1)} %param.8) | copy-start | bytes 331780
  12.2 8.5 %copy-start.3 = (bf16[256,1,2,128]{3,0,2,1:T(8,128)(2,1)}, bf16[256,1,2,128]{3,0,2,1:T(8,128)(2,1)S(1)}, u32[]{:S(2)}) copy-start(bf16[256,1,2,128]{3,0,2,1:T(8,128)(2,1)S(1)} %copy.81) | copy-start | bytes 393220
  12.8 8.0 %copy-start.4 = (bf16[256,1,2,128]{3,0,2,1:T(8,128)(2,1)}, bf16[256,1,2,128]{3,0,2,1:T(8,128)(2,1)S(1)}, u32[]{:S(2)}) copy-start(bf16[256,1,2,128]{3,0,2,1:T(8,128)(2,1)S(1)} %copy.82) | copy-start | bytes 393220
  13.2 7.5 %copy-start.2 = (bf16[256,1,2,128]{3,0,2,1:T(8,128)(2,1)}, bf16[256,1,2,128]{3,0,2,1:T(8,128)(2,1)S(1)}, u32[]{:S(2)}) copy-start(bf16[256,1,2,128]{3,0,2,1:T(8,128)(2,1)S(1)} %copy.83) | copy-start | bytes 393220
  13.3 7.4 %collective-permute-start.3 = (bf16[3,1,256,128]{3,2,1,0:T(8,128)(2,1)S(1)}, bf16[3,1,256,128]{3,2,1,0:T(8,128)(2,1)S(1)}, u32[]{:S(2)}, u32[]{:S(2)}) collective-permute-start(bf16[3,1,256,128]{3,2,1,0:T(8,128)(2,1)S(1)} %pad_maximum_fusion.3), channel_id=1, source_target_pairs={{1,0},{2,1},{3,2},{5,4},{6,5},{7,6},{9,8},{10,9},{11,10},{13,12},{... | collective-permute-start | bytes 589832 | tf_op jit(solution)/shard_map/ppermute | solution.py:192
  14.6 13.2 %copy-start.13 = (bf16[256,256]{1,0:T(8,128)(2,1)S(1)}, bf16[256,256]{1,0:T(8,128)(2,1)}, u32[]{:S(2)}) copy-start(bf16[256,256]{1,0:T(8,128)(2,1)} %param.9) | copy-start | bytes 393220
  14.7 6.1 %collective-permute-start.2 = (bf16[3,1,256,128]{3,2,1,0:T(8,128)(2,1)S(1)}, bf16[3,1,256,128]{3,2,1,0:T(8,128)(2,1)S(1)}, u32[]{:S(2)}, u32[]{:S(2)}) collective-permute-start(bf16[3,1,256,128]{3,2,1,0:T(8,128)(2,1)S(1)} %pad_maximum_fusion.2), channel_id=1, source_target_pairs={{0,1},{1,2},{2,3},{4,5},{5,6},{6,7},{8,9},{9,10},{10,11},{12,13},{... | collective-permute-start | bytes 589832 | tf_op jit(solution)/shard_map/ppermute | solution.py:191
  20.7 0.7 copy-start.8
  20.7 0.7 copy-start.9
  26.6 1.9 %copy-start.1 = (f32[2,256,128]{2,1,0:T(8,128)S(1)}, f32[2,256,128]{2,1,0:T(8,128)}, u32[]{:S(2)}) copy-start(f32[2,256,128]{2,1,0:T(8,128)} %shard_map.92) | copy-start | bytes 786436
  29.2 13.7 %collective-permute-start.4 = (bf16[1,2,256,128]{3,2,1,0:T(8,128)(2,1)}, bf16[1,2,256,128]{3,2,1,0:T(8,128)(2,1)S(1)}, u32[]{:S(2)}, u32[]{:S(2)}) collective-permute-start(bf16[1,2,256,128]{3,2,1,0:T(8,128)(2,1)} %bitcast.20.block_ref), channel_id=1, source_target_pairs={{0,4},{4,8},{8,12},{1,5},{5,9},{9,13},{2,6},{6,10},{10,14},{3,7},{... | collective-permute-start | bytes 393224 | tf_op jit(solution)/shard_map/ppermute | solution.py:182
  33.8 9.2 %collective-permute-start.5 = (bf16[1,2,256,128]{3,2,1,0:T(8,128)(2,1)}, bf16[1,2,256,128]{3,2,1,0:T(8,128)(2,1)S(1)}, u32[]{:S(2)}, u32[]{:S(2)}) collective-permute-start(bf16[1,2,256,128]{3,2,1,0:T(8,128)(2,1)} %bitcast.20.block_ref), channel_id=1, source_target_pairs={{4,0},{8,4},{12,8},{5,1},{9,5},{13,9},{6,2},{10,6},{14,10},{7,3},{... | collective-permute-start | bytes 393224 | tf_op jit(solution)/shard_map/ppermute | solution.py:183
  43.0 5.9 %copy-start.5 = (bf16[1,2,256,128]{3,2,1,0:T(8,128)(2,1)}, bf16[1,2,256,128]{3,2,1,0:T(8,128)(2,1)S(1)}, u32[]{:S(2)}) copy-start(bf16[1,2,256,128]{3,2,1,0:T(8,128)(2,1)S(1)} %collective-permute-done.4.below_ref) | copy-start | bytes 393220
  43.0 5.8 %copy-start.6 = (bf16[1,2,256,128]{3,2,1,0:T(8,128)(2,1)}, bf16[1,2,256,128]{3,2,1,0:T(8,128)(2,1)S(1)}, u32[]{:S(2)}) copy-start(bf16[1,2,256,128]{3,2,1,0:T(8,128)(2,1)S(1)} %collective-permute-done.5.above_ref) | copy-start | bytes 393220
  43.1 5.1 %collective-permute-start.7 = (bf16[3,1,256,128]{3,2,1,0:T(8,128)(2,1)S(1)}, bf16[3,1,256,128]{3,2,1,0:T(8,128)(2,1)S(1)}, u32[]{:S(2)}, u32[]{:S(2)}) collective-permute-start(bf16[3,1,256,128]{3,2,1,0:T(8,128)(2,1)S(1)} %pad_maximum_fusion.5), channel_id=1, source_target_pairs={{1,0},{2,1},{3,2},{5,4},{6,5},{7,6},{9,8},{10,9},{11,10},{13,12},{... | collective-permute-start | bytes 589832 | tf_op jit(solution)/shard_map/ppermute | solution.py:192
  44.4 4.4 %collective-permute-start.6 = (bf16[3,1,256,128]{3,2,1,0:T(8,128)(2,1)S(1)}, bf16[3,1,256,128]{3,2,1,0:T(8,128)(2,1)S(1)}, u32[]{:S(2)}, u32[]{:S(2)}) collective-permute-start(bf16[3,1,256,128]{3,2,1,0:T(8,128)(2,1)S(1)} %pad_maximum_fusion.4), channel_id=1, source_target_pairs={{0,1},{1,2},{2,3},{4,5},{5,6},{6,7},{8,9},{9,10},{10,11},{12,13},{... | collective-permute-start | bytes 589832 | tf_op jit(solution)/shard_map/ppermute | solution.py:191
  48.2 0.7 copy-start.10
  48.8 0.7 copy-start.11
  56.3 5.3 %collective-permute-start.8 = (f32[93184]{0:T(1024)S(1)}, f32[93184]{0:T(1024)S(1)}, u32[]{:S(2)}, u32[]{:S(2)}) collective-permute-start(f32[93184]{0:T(1024)S(1)} %pad_maximum_fusion), channel_id=1, source_target_pairs={{0,1},{1,0},{2,3},{3,2},{4,5},{5,4},{6,7},{7,6},{8,9},{9,8},{10,11... | collective-permute-start | bytes 1118216 | tf_op jit(solution)/shard_map/ppermute | solution.py:152
  61.7 7.8 %collective-permute-start.9 = (f32[46592]{0:T(1024)S(1)}, f32[46592]{0:T(1024)S(1)}, u32[]{:S(2)}, u32[]{:S(2)}) collective-permute-start(f32[46592]{0:T(1024)S(1)} %pad_maximum_fusion.6), channel_id=1, source_target_pairs={{0,2},{1,3},{2,0},{3,1},{4,6},{5,7},{6,4},{7,5},{8,10},{9,11},{10,... | collective-permute-start | bytes 559112 | tf_op jit(solution)/shard_map/ppermute | solution.py:152
  69.7 5.3 %collective-permute-start.10 = (f32[23296]{0:T(1024)S(1)}, f32[23296]{0:T(1024)S(1)}, u32[]{:S(2)}, u32[]{:S(2)}) collective-permute-start(f32[23296]{0:T(1024)S(1)} %pad_maximum_fusion.8), channel_id=1, source_target_pairs={{0,4},{4,0},{8,12},{12,8},{1,5},{5,1},{9,13},{13,9},{2,6},{6,2},{1... | collective-permute-start | bytes 279560 | tf_op jit(solution)/shard_map/ppermute | solution.py:152
  75.0 5.2 %collective-permute-start.11 = (f32[11648]{0:T(1024)S(1)}, f32[11648]{0:T(1024)S(1)}, u32[]{:S(2)}, u32[]{:S(2)}) collective-permute-start(f32[11648]{0:T(1024)S(1)} %pad_maximum_fusion.12), channel_id=1, source_target_pairs={{0,8},{4,12},{8,0},{12,4},{1,9},{5,13},{9,1},{13,5},{2,10},{6,14},... | collective-permute-start | bytes 139784 | tf_op jit(solution)/shard_map/ppermute | solution.py:152
  80.2 5.0 %collective-permute-start.12 = (f32[8192]{0:T(1024)S(1)}, f32[8192]{0:T(1024)S(1)}, u32[]{:S(2)}, u32[]{:S(2)}) collective-permute-start(f32[8192]{0:T(1024)S(1)} %pad_maximum_fusion.14), channel_id=1, source_target_pairs={{0,8},{4,12},{8,0},{12,4},{1,9},{5,13},{9,1},{13,5},{2,10},{6,14},... | collective-permute-start | bytes 98312 | tf_op jit(solution)/shard_map/ppermute | solution.py:162
  85.3 4.3 %collective-permute-start.13 = (f32[16384]{0:T(1024)S(1)}, f32[16384]{0:T(1024)S(1)}, u32[]{:S(2)}, u32[]{:S(2)}) collective-permute-start(f32[16384]{0:T(1024)S(1)} %pad_maximum_fusion.10), channel_id=1, source_target_pairs={{0,4},{4,0},{8,12},{12,8},{1,5},{5,1},{9,13},{13,9},{2,6},{6,2},{1... | collective-permute-start | bytes 196616 | tf_op jit(solution)/shard_map/ppermute | solution.py:162
  89.7 5.2 %collective-permute-start.14 = (f32[36224]{0:T(1024)S(1)}, f32[36224]{0:T(1024)S(1)}, u32[]{:S(2)}, u32[]{:S(2)}) collective-permute-start(f32[36224]{0:T(1024)S(1)} %pad_maximum_fusion.7), channel_id=1, source_target_pairs={{0,2},{1,3},{2,0},{3,1},{4,6},{5,7},{6,4},{7,5},{8,10},{9,11},{10,... | collective-permute-start | bytes 434696 | tf_op jit(solution)/shard_map/ppermute | solution.py:162
  95.2 1.6 %collective-permute-start.15 = (f32[72448]{0:T(1024)S(1)}, f32[72448]{0:T(1024)S(1)}, u32[]{:S(2)}, u32[]{:S(2)}) collective-permute-start(f32[72448]{0:T(1024)S(1)} %pad_maximum_fusion.1), channel_id=1, source_target_pairs={{0,1},{1,0},{2,3},{3,2},{4,5},{5,4},{6,7},{7,6},{8,9},{9,8},{10,11... | collective-permute-start | bytes 869384 | tf_op jit(solution)/shard_map/ppermute | solution.py:162

commit v16 on v15

--- a/solution.py
+++ b/solution.py
@@ -128,7 +128,7 @@
     return out.transpose(1, 0, 2).reshape(channels, blocks * LANES)[:, : 27 * GW]
 
 
-def tree_sum(blocks, order):
+def tree_sum(blocks, order, scale):
     steps = []
     for axis, rising in order:
         bits = []
@@ -155,6 +155,7 @@
             pieces[n] = keep + got[offset : offset + keep.shape[0]]
             offset += keep.shape[0]
         done.append((axis, pairs, upper))
+    pieces = [piece * scale for piece in pieces]
     for axis, pairs, upper in reversed(done):
         members = [n for n, (_, _, axes) in enumerate(blocks) if axis in axes]
         if not members:
@@ -303,12 +304,13 @@
             (kernel_laid, ("sub", "grp"), ("sub",)),
         ],
         (("sub", True), ("grp", True)),
-    )
-    first_grad = first_sum.reshape(first_part.shape) * factor
-    third_grad = third_sum.reshape(third_part.shape) * factor
+        factor,
+    )
+    first_grad = first_sum.reshape(first_part.shape)
+    third_grad = third_sum.reshape(third_part.shape)
     own_rows = channels // grp_count
     group_grad = (
-        group_sum.reshape(own_rows, 27, GW).transpose(0, 2, 1).reshape(own_rows, GW, 3, 3, 3) * factor
+        group_sum.reshape(own_rows, 27, GW).transpose(0, 2, 1).reshape(own_rows, GW, 3, 3, 3)
     )
     return (block_output, volume_grad, first_grad, group_grad, third_grad)
 

time: 100 us -> 100 us (level)
    select_n x14 -> x17, other arithmetic: 0.25 us -> 2.48 us  [tree_sum(): jnp.where(upper, jnp.concatenate([other, pieces[n]]), jnp.concatenate([pi...]
    mul x3 -> x2, other arithmetic: 2.22 us -> 0.02 us  [tree_sum(): pieces = [piece * scale for piece in pieces]]
where the time goes in v16:
time: 100 us; the launch traced here: 99.7 us
  starting transfers between devices  41 us (41%)
  waiting for transfers between devices  18 us (18%)
  Pallas kernels  14.6 us (15%)
  local copies, waits for them, and re-layouts  9.86 us (10%)
  matrix products  8.62 us (9%)
  other arithmetic  6.01 us (6%)
  between operations  1.65 us (2%)
    ppermute x4, starting transfers between devices, tree_sum(): got = lax.ppermute(jnp.concatenate(sends), axis, pairs)  12.6 us
    pallas_call x2, Pallas kernels, conv_call(): pl.pallas_call(conv_body, out_shape=jax.ShapeDtypeStruct((height, channel...  10.2 us
    ppermute x4, waiting for transfers between devices, tree_sum(): got = lax.ppermute(jnp.concatenate(sends), axis, pairs)  8.74 us
    ppermute x4, waiting for transfers between devices, tree_sum(): lax.ppermute(jnp.concatenate([pieces[n] for n in members]), axis, pairs)  8.62 us
    ppermute x4, starting transfers between devices, tree_sum(): lax.ppermute(jnp.concatenate([pieces[n] for n in members]), axis, pairs)  6.85 us
    ppermute x2, starting transfers between devices, halo(): before = lax.ppermute(last, 'sub', up)  6.72 us
    ppermute x2, starting transfers between devices, per_device(): near = [lax.ppermute(volume, 'grp', up), lax.ppermute(volume, 'grp', down)]  6.36 us
    ppermute x1, starting transfers between devices, halo(): below = lax.ppermute(block[depth - 1:], 'grp', up)  4.55 us
  transfers between devices with their start and end apart: 16, of which 9 were waited for; matrix products, arithmetic and copies ran while one was open for 15% of the time, Pallas kernels for 4%

profile of v16, /device:TPU:0, one launch (start us, length us, event | category | flops | bytes accessed | tf_op | source)
XLA Modules:
  0.0 99.7 jit_solution(9043923378530310468)
XLA Ops:
  0.7 5.1 %collective-permute-start = (bf16[256,1,2,128]{3,2,1,0:T(2,128)(2,1)}, bf16[256,1,2,128]{3,2,1,0:T(2,128)(2,1)S(1)}, u32[]{:S(2)}, u32[]{:S(2)}) collective-permute-start(bf16[256,1,2,128]{3,2,1,0:T(2,128)(2,1)} %param.5), channel_id=1, source_target_pairs={{0,4},{4,8},{8,12},{1,5},{5,9},{9,13},{2,6},{6,10},{10,14},{3,7},{... | collective-permute-start | bytes 393224 | tf_op jit(solution)/shard_map/ppermute | solution.py:250
  5.7 1.3 %collective-permute-start.1 = (bf16[256,1,2,128]{3,2,1,0:T(2,128)(2,1)}, bf16[256,1,2,128]{3,2,1,0:T(2,128)(2,1)S(1)}, u32[]{:S(2)}, u32[]{:S(2)}) collective-permute-start(bf16[256,1,2,128]{3,2,1,0:T(2,128)(2,1)} %param.5), channel_id=1, source_target_pairs={{4,0},{8,4},{12,8},{5,1},{9,5},{13,9},{6,2},{10,6},{14,10},{7,3},{... | collective-permute-start | bytes 393224 | tf_op jit(solution)/shard_map/ppermute | solution.py:250
  7.0 1.0 %copy.80 = bf16[256,1,2,128]{0,3,2,1:T(8,128)(2,1)S(1)} copy(bf16[256,1,2,128]{3,2,1,0:T(2,128)(2,1)} %param.5) | data formatting | bytes 262144 | tf_op args[0]
  8.1 3.8 %convolution_convert_fusion.1 = bf16[256,256,27]{0,1,2:T(8,128)(2,1)} fusion(bf16[256,8,27]{0,1,2:T(8,128)(2,1)} %bitcast.132, s32[256]{0:T(256)S(1)} %and_select_fusion), kind=kOutput, calls=%fused_computation.1 | convolution fusion | flops 30083072 | bytes 3650560 | tf_op jit(solution)/shard_map/ojt,ji->toi/dot_general | solution.py:216
  11.9 0.2 reduce-precision_convert_fusion.4
  12.4 0.3 reduce-precision_convert_fusion.3
  12.8 0.3 reduce-precision_convert_fusion.2
  13.3 1.3 %collective-permute-start.3 = (bf16[3,1,256,128]{3,2,1,0:T(8,128)(2,1)S(1)}, bf16[3,1,256,128]{3,2,1,0:T(8,128)(2,1)S(1)}, u32[]{:S(2)}, u32[]{:S(2)}) collective-permute-start(bf16[3,1,256,128]{3,2,1,0:T(8,128)(2,1)S(1)} %pad_maximum_fusion.3), channel_id=1, source_target_pairs={{1,0},{2,1},{3,2},{5,4},{6,5},{7,6},{9,8},{10,9},{11,10},{13,12},{... | collective-permute-start | bytes 589832 | tf_op jit(solution)/shard_map/ppermute | solution.py:193
  14.7 3.2 %collective-permute-start.2 = (bf16[3,1,256,128]{3,2,1,0:T(8,128)(2,1)S(1)}, bf16[3,1,256,128]{3,2,1,0:T(8,128)(2,1)S(1)}, u32[]{:S(2)}, u32[]{:S(2)}) collective-permute-start(bf16[3,1,256,128]{3,2,1,0:T(8,128)(2,1)S(1)} %pad_maximum_fusion.2), channel_id=1, source_target_pairs={{0,1},{1,2},{2,3},{4,5},{5,6},{6,7},{8,9},{9,10},{10,11},{12,13},{... | collective-permute-start | bytes 589832 | tf_op jit(solution)/shard_map/ppermute | solution.py:192
  17.9 2.9 %convolution_convert_fusion = bf16[256,256,27]{1,0,2:T(8,128)(2,1)} fusion(bf16[256,8,27]{0,1,2:T(8,128)(2,1)S(1)} %bitcast.133, s32[256]{0:T(256)S(1)} %and_select_fusion), kind=kOutput, calls=%fused_computation | convolution fusion | flops 30138368 | bytes 3650560 | tf_op jit(solution)/shard_map/ji,ojt->tio/dot_general | solution.py:217
  20.8 0.6 copy-done.8
  21.5 5.1 %shard_map.92 = f32[2,256,128]{2,1,0:T(8,128)} custom-call(bf16[1,2,256,128]{3,2,1,0:T(8,128)(2,1)} %bitcast.112, bf16[1,2,256,128]{3,2,1,0:T(8,128)(2,1)} %bitcast.115, bf16[1,2,256,128]{3,2,1,0:T(8,128)(2,1)} %bitcast.109, bf16[3,1,256,128]{3,2,1,0:T(8,128)(2,1)} %copy-done.9, bf16[3,1,256,128]{3,2,1,0:T(8,128)(2,1)} %copy-done.8, ...), custom_call_target="tpu_custom_call" | custom-call | flops 905969664 | bytes 4587520 | tf_op jit(solution)/shard_map/pallas_call | solution.py:60
  26.6 1.1 %fusion.22 = bf16[256,2,128]{2,0,1:T(8,128)(2,1)S(1)} fusion(f32[2,256,128]{2,1,0:T(8,128)} %shard_map.92), kind=kLoop, calls=%fused_computation.54 | loop fusion | flops 393216 | bytes 393216 | tf_op jit(solution)/shard_map/transpose | solution.py:239
  27.8 0.3 fusion.10
  28.5 0.8 fusion.6.delta_ref
  29.2 4.6 %collective-permute-start.4 = (bf16[1,2,256,128]{3,2,1,0:T(8,128)(2,1)}, bf16[1,2,256,128]{3,2,1,0:T(8,128)(2,1)S(1)}, u32[]{:S(2)}, u32[]{:S(2)}) collective-permute-start(bf16[1,2,256,128]{3,2,1,0:T(8,128)(2,1)} %bitcast.20.block_ref), channel_id=1, source_target_pairs={{0,4},{4,8},{8,12},{1,5},{5,9},{9,13},{2,6},{6,10},{10,14},{3,7},{... | collective-permute-start | bytes 393224 | tf_op jit(solution)/shard_map/ppermute | solution.py:183
  33.8 1.3 %collective-permute-start.5 = (bf16[1,2,256,128]{3,2,1,0:T(8,128)(2,1)}, bf16[1,2,256,128]{3,2,1,0:T(8,128)(2,1)S(1)}, u32[]{:S(2)}, u32[]{:S(2)}) collective-permute-start(bf16[1,2,256,128]{3,2,1,0:T(8,128)(2,1)} %bitcast.20.block_ref), channel_id=1, source_target_pairs={{4,0},{8,4},{12,8},{5,1},{9,5},{13,9},{6,2},{10,6},{14,10},{7,3},{... | collective-permute-start | bytes 393224 | tf_op jit(solution)/shard_map/ppermute | solution.py:184
  35.1 0.2 fusion.46
  35.3 4.4 %shard_map.94 = f32[2,256,128]{2,1,0:T(8,128)} custom-call(bf16[1,2,256,128]{3,2,1,0:T(8,128)(2,1)} %bitcast.113, bf16[1,2,256,128]{3,2,1,0:T(8,128)(2,1)} %bitcast.116, bf16[1,2,256,128]{3,2,1,0:T(8,128)(2,1)} %bitcast.110, bf16[3,1,256,128]{3,2,1,0:T(8,128)(2,1)} %copy-done.9, bf16[3,1,256,128]{3,2,1,0:T(8,128)(2,1)} %copy-done.8, ...), custom_call_target="tpu_custom_call" | custom-call | flops 1358954496 | bytes 1179648 | tf_op jit(solution)/shard_map/pallas_call | solution.py:117
  39.7 1.1 %copy.93 = f32[256,2,128]{0,2,1:T(8,128)S(1)} copy(f32[256,2,128]{2,0,1:T(8,128)} %bitcast.134) | data formatting | bytes 524288 | tf_op jit(solution)/shard_map/transpose | solution.py:128
  42.1 0.9 fusion.39
  43.1 1.3 %collective-permute-start.7 = (bf16[3,1,256,128]{3,2,1,0:T(8,128)(2,1)S(1)}, bf16[3,1,256,128]{3,2,1,0:T(8,128)(2,1)S(1)}, u32[]{:S(2)}, u32[]{:S(2)}) collective-permute-start(bf16[3,1,256,128]{3,2,1,0:T(8,128)(2,1)S(1)} %pad_maximum_fusion.5), channel_id=1, source_target_pairs={{1,0},{2,1},{3,2},{5,4},{6,5},{7,6},{9,8},{10,9},{11,10},{13,12},{... | collective-permute-start | bytes 589832 | tf_op jit(solution)/shard_map/ppermute | solution.py:193
  44.4 3.5 %collective-permute-start.6 = (bf16[3,1,256,128]{3,2,1,0:T(8,128)(2,1)S(1)}, bf16[3,1,256,128]{3,2,1,0:T(8,128)(2,1)S(1)}, u32[]{:S(2)}, u32[]{:S(2)}) collective-permute-start(bf16[3,1,256,128]{3,2,1,0:T(8,128)(2,1)S(1)} %pad_maximum_fusion.4), channel_id=1, source_target_pairs={{0,1},{1,2},{2,3},{4,5},{5,6},{6,7},{8,9},{9,10},{10,11},{12,13},{... | collective-permute-start | bytes 589832 | tf_op jit(solution)/shard_map/ppermute | solution.py:192
  48.2 0.6 collective-permute-done.6.before_ref
  48.8 0.6 copy-done.11
  49.5 5.1 %shard_map.93 = f32[2,256,128]{2,1,0:T(8,128)} custom-call(bf16[1,2,256,128]{3,2,1,0:T(8,128)(2,1)} %bitcast.20.block_ref, bf16[1,2,256,128]{3,2,1,0:T(8,128)(2,1)} %copy-done.5, bf16[1,2,256,128]{3,2,1,0:T(8,128)(2,1)} %copy-done.6, bf16[3,1,256,128]{3,2,1,0:T(8,128)(2,1)} %copy-done.11, bf16[3,1,256,128]{3,2,1,0:T(8,128)(2,1)} %copy-done.10, ...), custom_call_target="tpu_custom_call" | custom-call | flops 905969664 | bytes 4587520 | tf_op jit(solution)/shard_map/pallas_call | solution.py:60
  54.6 1.0 convert_bitcast_fusion
  56.3 4.0 %collective-permute-start.8 = (f32[93184]{0:T(1024)S(1)}, f32[93184]{0:T(1024)S(1)}, u32[]{:S(2)}, u32[]{:S(2)}) collective-permute-start(f32[93184]{0:T(1024)S(1)} %pad_maximum_fusion), channel_id=1, source_target_pairs={{0,1},{1,0},{2,3},{3,2},{4,5},{5,4},{6,7},{7,6},{8,9},{9,8},{10,11... | collective-permute-start | bytes 1118216 | tf_op jit(solution)/shard_map/ppermute | solution.py:152
  60.7 0.9 collective-permute-done.8
  61.7 2.8 %collective-permute-start.9 = (f32[46592]{0:T(1024)S(1)}, f32[46592]{0:T(1024)S(1)}, u32[]{:S(2)}, u32[]{:S(2)}) collective-permute-start(f32[46592]{0:T(1024)S(1)} %pad_maximum_fusion.6), channel_id=1, source_target_pairs={{0,2},{1,3},{2,0},{3,1},{4,6},{5,7},{6,4},{7,5},{8,10},{9,11},{10,... | collective-permute-start | bytes 559112 | tf_op jit(solution)/shard_map/ppermute | solution.py:152
  64.5 5.0 %collective-permute-done.9 = f32[46592]{0:T(1024)S(1)} collective-permute-done((f32[46592]{0:T(1024)S(1)}, f32[46592]{0:T(1024)S(1)}, u32[]{:S(2)}, u32[]{:S(2)}) %collective-permute-start.9) | collective-permute-done | bytes 186400 | tf_op jit(solution)/shard_map/ppermute | solution.py:152
  69.7 2.7 %collective-permute-start.10 = (f32[23296]{0:T(1024)S(1)}, f32[23296]{0:T(1024)S(1)}, u32[]{:S(2)}, u32[]{:S(2)}) collective-permute-start(f32[23296]{0:T(1024)S(1)} %pad_maximum_fusion.8), channel_id=1, source_target_pairs={{0,4},{4,0},{8,12},{12,8},{1,5},{5,1},{9,13},{13,9},{2,6},{6,2},{1... | collective-permute-start | bytes 279560 | tf_op jit(solution)/shard_map/ppermute | solution.py:152
  72.4 0.8 copy.107
  73.2 1.8 %collective-permute-done.10 = f32[23296]{0:T(1024)S(1)} collective-permute-done((f32[23296]{0:T(1024)S(1)}, f32[23296]{0:T(1024)S(1)}, u32[]{:S(2)}, u32[]{:S(2)}) %collective-permute-start.10) | collective-permute-done | bytes 93216 | tf_op jit(solution)/shard_map/ppermute | solution.py:152
  75.0 3.1 %collective-permute-start.11 = (f32[11648]{0:T(1024)S(1)}, f32[11648]{0:T(1024)S(1)}, u32[]{:S(2)}, u32[]{:S(2)}) collective-permute-start(f32[11648]{0:T(1024)S(1)} %pad_maximum_fusion.12), channel_id=1, source_target_pairs={{0,8},{4,12},{8,0},{12,4},{1,9},{5,13},{9,1},{13,5},{2,10},{6,14},... | collective-permute-start | bytes 139784 | tf_op jit(solution)/shard_map/ppermute | solution.py:152
  78.3 0.8 copy.108
  79.1 1.1 %collective-permute-done.11 = f32[11648]{0:T(1024)S(1)} collective-permute-done((f32[11648]{0:T(1024)S(1)}, f32[11648]{0:T(1024)S(1)}, u32[]{:S(2)}, u32[]{:S(2)}) %collective-permute-start.11) | collective-permute-done | bytes 46624 | tf_op jit(solution)/shard_map/ppermute | solution.py:152
  80.2 3.0 %collective-permute-start.12 = (f32[8192]{0:T(1024)S(1)}, f32[8192]{0:T(1024)S(1)}, u32[]{:S(2)}, u32[]{:S(2)}) collective-permute-start(f32[8192]{0:T(1024)S(1)} %pad_maximum_fusion.14), channel_id=1, source_target_pairs={{0,8},{4,12},{8,0},{12,4},{1,9},{5,13},{9,1},{13,5},{2,10},{6,14},... | collective-permute-start | bytes 98312 | tf_op jit(solution)/shard_map/ppermute | solution.py:163
  83.6 1.7 %collective-permute-done.12 = f32[8192]{0:T(1024)S(1)} collective-permute-done((f32[8192]{0:T(1024)S(1)}, f32[8192]{0:T(1024)S(1)}, u32[]{:S(2)}, u32[]{:S(2)}) %collective-permute-start.12) | collective-permute-done | bytes 32800 | tf_op jit(solution)/shard_map/ppermute | solution.py:163
  85.3 1.9 %collective-permute-start.13 = (f32[16384]{0:T(1024)S(1)}, f32[16384]{0:T(1024)S(1)}, u32[]{:S(2)}, u32[]{:S(2)}) collective-permute-start(f32[16384]{0:T(1024)S(1)} %pad_maximum_fusion.10), channel_id=1, source_target_pairs={{0,4},{4,0},{8,12},{12,8},{1,5},{5,1},{9,13},{13,9},{2,6},{6,2},{1... | collective-permute-start | bytes 196616 | tf_op jit(solution)/shard_map/ppermute | solution.py:163
  87.2 2.4 %collective-permute-done.13 = f32[16384]{0:T(1024)S(1)} collective-permute-done((f32[16384]{0:T(1024)S(1)}, f32[16384]{0:T(1024)S(1)}, u32[]{:S(2)}, u32[]{:S(2)}) %collective-permute-start.13) | collective-permute-done | bytes 65568 | tf_op jit(solution)/shard_map/ppermute | solution.py:163
  89.7 1.8 %collective-permute-start.14 = (f32[36224]{0:T(1024)S(1)}, f32[36224]{0:T(1024)S(1)}, u32[]{:S(2)}, u32[]{:S(2)}) collective-permute-start(f32[36224]{0:T(1024)S(1)} %pad_maximum_fusion.7), channel_id=1, source_target_pairs={{0,2},{1,3},{2,0},{3,1},{4,6},{5,7},{6,4},{7,5},{8,10},{9,11},{10,... | collective-permute-start | bytes 434696 | tf_op jit(solution)/shard_map/ppermute | solution.py:163
  91.6 3.3 %collective-permute-done.14 = f32[36224]{0:T(1024)S(1)} collective-permute-done((f32[36224]{0:T(1024)S(1)}, f32[36224]{0:T(1024)S(1)}, u32[]{:S(2)}, u32[]{:S(2)}) %collective-permute-start.14) | collective-permute-done | bytes 144928 | tf_op jit(solution)/shard_map/ppermute | solution.py:163
  95.7 1.2 %collective-permute-done.15 = f32[72448]{0:T(1024)S(1)} collective-permute-done((f32[72448]{0:T(1024)S(1)}, f32[72448]{0:T(1024)S(1)}, u32[]{:S(2)}, u32[]{:S(2)}) %collective-permute-start.15) | collective-permute-done | bytes 289824 | tf_op jit(solution)/shard_map/ppermute | solution.py:163
  97.1 0.3 copy.105
  97.5 0.7 maximum_select_fusion.1
  98.2 0.8 maximum_select_fusion.7
  99.0 0.7 maximum_select_fusion
  (139 shorter events, 5.5 us)
Async XLA Ops:
  0.6 11.2 %copy-start = (bf16[256,256]{1,0:T(8,128)(2,1)S(1)}, bf16[256,256]{1,0:T(8,128)(2,1)}, u32[]{:S(2)}) copy-start(bf16[256,256]{1,0:T(8,128)(2,1)} %param.7) | copy-start | bytes 393220
  0.6 11.6 %copy-start.12 = (bf16[256,1,2,128]{3,2,1,0:T(2,128)(2,1)S(1)}, bf16[256,1,2,128]{3,2,1,0:T(2,128)(2,1)}, u32[]{:S(2)}) copy-start(bf16[256,1,2,128]{3,2,1,0:T(2,128)(2,1)} %param.6) | copy-start | bytes 393220
  0.7 11.7 %collective-permute-start = (bf16[256,1,2,128]{3,2,1,0:T(2,128)(2,1)}, bf16[256,1,2,128]{3,2,1,0:T(2,128)(2,1)S(1)}, u32[]{:S(2)}, u32[]{:S(2)}) collective-permute-start(bf16[256,1,2,128]{3,2,1,0:T(2,128)(2,1)} %param.5), channel_id=1, source_target_pairs={{0,4},{4,8},{8,12},{1,5},{5,9},{9,13},{2,6},{6,10},{10,14},{3,7},{... | collective-permute-start | bytes 393224 | tf_op jit(solution)/shard_map/ppermute | solution.py:250
  5.7 7.1 %collective-permute-start.1 = (bf16[256,1,2,128]{3,2,1,0:T(2,128)(2,1)}, bf16[256,1,2,128]{3,2,1,0:T(2,128)(2,1)S(1)}, u32[]{:S(2)}, u32[]{:S(2)}) collective-permute-start(bf16[256,1,2,128]{3,2,1,0:T(2,128)(2,1)} %param.5), channel_id=1, source_target_pairs={{4,0},{8,4},{12,8},{5,1},{9,5},{13,9},{6,2},{10,6},{14,10},{7,3},{... | collective-permute-start | bytes 393224 | tf_op jit(solution)/shard_map/ppermute | solution.py:250
  11.9 6.0 %copy-start.7 = (bf16[256,8,3,3,3]{0,1,4,3,2:T(8,128)(2,1)S(1)}, bf16[256,8,3,3,3]{0,1,4,3,2:T(8,128)(2,1)}, u32[]{:S(2)}) copy-start(bf16[256,8,3,3,3]{0,1,4,3,2:T(8,128)(2,1)} %param.8) | copy-start | bytes 331780
  12.2 8.5 %copy-start.3 = (bf16[256,1,2,128]{3,0,2,1:T(8,128)(2,1)}, bf16[256,1,2,128]{3,0,2,1:T(8,128)(2,1)S(1)}, u32[]{:S(2)}) copy-start(bf16[256,1,2,128]{3,0,2,1:T(8,128)(2,1)S(1)} %copy.81) | copy-start | bytes 393220
  12.8 8.0 %copy-start.4 = (bf16[256,1,2,128]{3,0,2,1:T(8,128)(2,1)}, bf16[256,1,2,128]{3,0,2,1:T(8,128)(2,1)S(1)}, u32[]{:S(2)}) copy-start(bf16[256,1,2,128]{3,0,2,1:T(8,128)(2,1)S(1)} %copy.82) | copy-start | bytes 393220
  13.2 7.5 %copy-start.2 = (bf16[256,1,2,128]{3,0,2,1:T(8,128)(2,1)}, bf16[256,1,2,128]{3,0,2,1:T(8,128)(2,1)S(1)}, u32[]{:S(2)}) copy-start(bf16[256,1,2,128]{3,0,2,1:T(8,128)(2,1)S(1)} %copy.83) | copy-start | bytes 393220
  13.3 7.4 %collective-permute-start.3 = (bf16[3,1,256,128]{3,2,1,0:T(8,128)(2,1)S(1)}, bf16[3,1,256,128]{3,2,1,0:T(8,128)(2,1)S(1)}, u32[]{:S(2)}, u32[]{:S(2)}) collective-permute-start(bf16[3,1,256,128]{3,2,1,0:T(8,128)(2,1)S(1)} %pad_maximum_fusion.3), channel_id=1, source_target_pairs={{1,0},{2,1},{3,2},{5,4},{6,5},{7,6},{9,8},{10,9},{11,10},{13,12},{... | collective-permute-start | bytes 589832 | tf_op jit(solution)/shard_map/ppermute | solution.py:193
  14.6 13.2 %copy-start.13 = (bf16[256,256]{1,0:T(8,128)(2,1)S(1)}, bf16[256,256]{1,0:T(8,128)(2,1)}, u32[]{:S(2)}) copy-start(bf16[256,256]{1,0:T(8,128)(2,1)} %param.9) | copy-start | bytes 393220
  14.7 6.1 %collective-permute-start.2 = (bf16[3,1,256,128]{3,2,1,0:T(8,128)(2,1)S(1)}, bf16[3,1,256,128]{3,2,1,0:T(8,128)(2,1)S(1)}, u32[]{:S(2)}, u32[]{:S(2)}) collective-permute-start(bf16[3,1,256,128]{3,2,1,0:T(8,128)(2,1)S(1)} %pad_maximum_fusion.2), channel_id=1, source_target_pairs={{0,1},{1,2},{2,3},{4,5},{5,6},{6,7},{8,9},{9,10},{10,11},{12,13},{... | collective-permute-start | bytes 589832 | tf_op jit(solution)/shard_map/ppermute | solution.py:192
  20.7 0.7 copy-start.8
  20.7 0.7 copy-start.9
  26.6 1.9 %copy-start.1 = (f32[2,256,128]{2,1,0:T(8,128)S(1)}, f32[2,256,128]{2,1,0:T(8,128)}, u32[]{:S(2)}) copy-start(f32[2,256,128]{2,1,0:T(8,128)} %shard_map.92) | copy-start | bytes 786436
  29.2 13.7 %collective-permute-start.4 = (bf16[1,2,256,128]{3,2,1,0:T(8,128)(2,1)}, bf16[1,2,256,128]{3,2,1,0:T(8,128)(2,1)S(1)}, u32[]{:S(2)}, u32[]{:S(2)}) collective-permute-start(bf16[1,2,256,128]{3,2,1,0:T(8,128)(2,1)} %bitcast.20.block_ref), channel_id=1, source_target_pairs={{0,4},{4,8},{8,12},{1,5},{5,9},{9,13},{2,6},{6,10},{10,14},{3,7},{... | collective-permute-start | bytes 393224 | tf_op jit(solution)/shard_map/ppermute | solution.py:183
  33.8 9.2 %collective-permute-start.5 = (bf16[1,2,256,128]{3,2,1,0:T(8,128)(2,1)}, bf16[1,2,256,128]{3,2,1,0:T(8,128)(2,1)S(1)}, u32[]{:S(2)}, u32[]{:S(2)}) collective-permute-start(bf16[1,2,256,128]{3,2,1,0:T(8,128)(2,1)} %bitcast.20.block_ref), channel_id=1, source_target_pairs={{4,0},{8,4},{12,8},{5,1},{9,5},{13,9},{6,2},{10,6},{14,10},{7,3},{... | collective-permute-start | bytes 393224 | tf_op jit(solution)/shard_map/ppermute | solution.py:184
  43.0 5.9 %copy-start.5 = (bf16[1,2,256,128]{3,2,1,0:T(8,128)(2,1)}, bf16[1,2,256,128]{3,2,1,0:T(8,128)(2,1)S(1)}, u32[]{:S(2)}) copy-start(bf16[1,2,256,128]{3,2,1,0:T(8,128)(2,1)S(1)} %collective-permute-done.4.below_ref) | copy-start | bytes 393220
  43.0 5.8 %copy-start.6 = (bf16[1,2,256,128]{3,2,1,0:T(8,128)(2,1)}, bf16[1,2,256,128]{3,2,1,0:T(8,128)(2,1)S(1)}, u32[]{:S(2)}) copy-start(bf16[1,2,256,128]{3,2,1,0:T(8,128)(2,1)S(1)} %collective-permute-done.5.above_ref) | copy-start | bytes 393220
  43.1 5.1 %collective-permute-start.7 = (bf16[3,1,256,128]{3,2,1,0:T(8,128)(2,1)S(1)}, bf16[3,1,256,128]{3,2,1,0:T(8,128)(2,1)S(1)}, u32[]{:S(2)}, u32[]{:S(2)}) collective-permute-start(bf16[3,1,256,128]{3,2,1,0:T(8,128)(2,1)S(1)} %pad_maximum_fusion.5), channel_id=1, source_target_pairs={{1,0},{2,1},{3,2},{5,4},{6,5},{7,6},{9,8},{10,9},{11,10},{13,12},{... | collective-permute-start | bytes 589832 | tf_op jit(solution)/shard_map/ppermute | solution.py:193
  44.4 4.4 %collective-permute-start.6 = (bf16[3,1,256,128]{3,2,1,0:T(8,128)(2,1)S(1)}, bf16[3,1,256,128]{3,2,1,0:T(8,128)(2,1)S(1)}, u32[]{:S(2)}, u32[]{:S(2)}) collective-permute-start(bf16[3,1,256,128]{3,2,1,0:T(8,128)(2,1)S(1)} %pad_maximum_fusion.4), channel_id=1, source_target_pairs={{0,1},{1,2},{2,3},{4,5},{5,6},{6,7},{8,9},{9,10},{10,11},{12,13},{... | collective-permute-start | bytes 589832 | tf_op jit(solution)/shard_map/ppermute | solution.py:192
  48.2 0.7 copy-start.10
  48.8 0.7 copy-start.11
  56.3 5.3 %collective-permute-start.8 = (f32[93184]{0:T(1024)S(1)}, f32[93184]{0:T(1024)S(1)}, u32[]{:S(2)}, u32[]{:S(2)}) collective-permute-start(f32[93184]{0:T(1024)S(1)} %pad_maximum_fusion), channel_id=1, source_target_pairs={{0,1},{1,0},{2,3},{3,2},{4,5},{5,4},{6,7},{7,6},{8,9},{9,8},{10,11... | collective-permute-start | bytes 1118216 | tf_op jit(solution)/shard_map/ppermute | solution.py:152
  61.7 7.8 %collective-permute-start.9 = (f32[46592]{0:T(1024)S(1)}, f32[46592]{0:T(1024)S(1)}, u32[]{:S(2)}, u32[]{:S(2)}) collective-permute-start(f32[46592]{0:T(1024)S(1)} %pad_maximum_fusion.6), channel_id=1, source_target_pairs={{0,2},{1,3},{2,0},{3,1},{4,6},{5,7},{6,4},{7,5},{8,10},{9,11},{10,... | collective-permute-start | bytes 559112 | tf_op jit(solution)/shard_map/ppermute | solution.py:152
  69.7 5.3 %collective-permute-start.10 = (f32[23296]{0:T(1024)S(1)}, f32[23296]{0:T(1024)S(1)}, u32[]{:S(2)}, u32[]{:S(2)}) collective-permute-start(f32[23296]{0:T(1024)S(1)} %pad_maximum_fusion.8), channel_id=1, source_target_pairs={{0,4},{4,0},{8,12},{12,8},{1,5},{5,1},{9,13},{13,9},{2,6},{6,2},{1... | collective-permute-start | bytes 279560 | tf_op jit(solution)/shard_map/ppermute | solution.py:152
  75.0 5.2 %collective-permute-start.11 = (f32[11648]{0:T(1024)S(1)}, f32[11648]{0:T(1024)S(1)}, u32[]{:S(2)}, u32[]{:S(2)}) collective-permute-start(f32[11648]{0:T(1024)S(1)} %pad_maximum_fusion.12), channel_id=1, source_target_pairs={{0,8},{4,12},{8,0},{12,4},{1,9},{5,13},{9,1},{13,5},{2,10},{6,14},... | collective-permute-start | bytes 139784 | tf_op jit(solution)/shard_map/ppermute | solution.py:152
  80.2 5.0 %collective-permute-start.12 = (f32[8192]{0:T(1024)S(1)}, f32[8192]{0:T(1024)S(1)}, u32[]{:S(2)}, u32[]{:S(2)}) collective-permute-start(f32[8192]{0:T(1024)S(1)} %pad_maximum_fusion.14), channel_id=1, source_target_pairs={{0,8},{4,12},{8,0},{12,4},{1,9},{5,13},{9,1},{13,5},{2,10},{6,14},... | collective-permute-start | bytes 98312 | tf_op jit(solution)/shard_map/ppermute | solution.py:163
  85.3 4.3 %collective-permute-start.13 = (f32[16384]{0:T(1024)S(1)}, f32[16384]{0:T(1024)S(1)}, u32[]{:S(2)}, u32[]{:S(2)}) collective-permute-start(f32[16384]{0:T(1024)S(1)} %pad_maximum_fusion.10), channel_id=1, source_target_pairs={{0,4},{4,0},{8,12},{12,8},{1,5},{5,1},{9,13},{13,9},{2,6},{6,2},{1... | collective-permute-start | bytes 196616 | tf_op jit(solution)/shard_map/ppermute | solution.py:163
  89.7 5.2 %collective-permute-start.14 = (f32[36224]{0:T(1024)S(1)}, f32[36224]{0:T(1024)S(1)}, u32[]{:S(2)}, u32[]{:S(2)}) collective-permute-start(f32[36224]{0:T(1024)S(1)} %pad_maximum_fusion.7), channel_id=1, source_target_pairs={{0,2},{1,3},{2,0},{3,1},{4,6},{5,7},{6,4},{7,5},{8,10},{9,11},{10,... | collective-permute-start | bytes 434696 | tf_op jit(solution)/shard_map/ppermute | solution.py:163
  95.2 1.6 %collective-permute-start.15 = (f32[72448]{0:T(1024)S(1)}, f32[72448]{0:T(1024)S(1)}, u32[]{:S(2)}, u32[]{:S(2)}) collective-permute-start(f32[72448]{0:T(1024)S(1)} %pad_maximum_fusion.1), channel_id=1, source_target_pairs={{0,1},{1,0},{2,3},{3,2},{4,5},{5,4},{6,7},{7,6},{8,9},{9,8},{10,11... | collective-permute-start | bytes 869384 | tf_op jit(solution)/shard_map/ppermute | solution.py:163

commit v17 on v16

--- a/solution.py
+++ b/solution.py
@@ -166,11 +166,11 @@
             size = pieces[n].shape[0]
             other = got[offset : offset + size]
             offset += size
-            pieces[n] = jnp.where(
-                upper,
-                jnp.concatenate([other, pieces[n]]),
-                jnp.concatenate([pieces[n], other]),
+            mine = upper.astype(jnp.int32) * size
+            joined = lax.dynamic_update_slice_in_dim(
+                jnp.concatenate([other, other]), pieces[n], mine, 0
             )
+            pieces[n] = joined
     return pieces
 
 

time: 100 us -> 107 us (1.070)
  local copies, waits for them, and re-layouts: 9.86 us -> 18.5 us
  other arithmetic: 6.01 us -> 3.63 us
    dynamic_update_slice x0 -> x10, local copies, waits for them, and re-layouts: none -> 6.86 us  [tree_sum(): lax.dynamic_update_slice_in_dim(jnp.concatenate([other, other]), pieces[n...]
    select_n x17 -> x0, other arithmetic: 2.48 us -> none  [tree_sum(): jnp.where(upper, jnp.concatenate([other, pieces[n]]), jnp.concatenate([pi...]
    reshape x0 -> x3, local copies, waits for them, and re-layouts: none -> 1.85 us  [the longest x1 0.78 us: per_device(): third_grad = third_sum.reshape(third_part.shape)]
    ppermute x4, waiting for transfers between devices: 8.74 us -> 10.5 us  [tree_sum(): got = lax.ppermute(jnp.concatenate(sends), axis, pairs)]
    transpose x0 -> x1, local copies, waits for them, and re-layouts: none -> 1.16 us  [per_device(): group_sum.reshape(own_rows, 27, GW).transpose(0, 2, 1)]
  transfers between devices with their start and end apart: 16 -> 16, of which waited for: 9 -> 8; matrix products, arithmetic and copies ran while one was open for 15% -> 13% of each run, Pallas kernels for 4% -> 4%
where the time goes in v17:
time: 107 us
  starting transfers between devices  41 us (38%)
  waiting for transfers between devices  18.8 us (18%)
  local copies, waits for them, and re-layouts  18.5 us (17%)
  Pallas kernels  14.6 us (14%)
  matrix products  8.63 us (8%)
  other arithmetic  3.63 us (3%)
  between operations  1.62 us (2%)
    ppermute x4, starting transfers between devices, tree_sum(): got = lax.ppermute(jnp.concatenate(sends), axis, pairs)  12.6 us
    ppermute x4, waiting for transfers between devices, tree_sum(): got = lax.ppermute(jnp.concatenate(sends), axis, pairs)  10.5 us
    pallas_call x2, Pallas kernels, conv_call(): pl.pallas_call(conv_body, out_shape=jax.ShapeDtypeStruct((height, channel...  10.2 us
    ppermute x4, waiting for transfers between devices, tree_sum(): lax.ppermute(jnp.concatenate([pieces[n] for n in members]), axis, pairs)  7.61 us
    ppermute x4, starting transfers between devices, tree_sum(): lax.ppermute(jnp.concatenate([pieces[n] for n in members]), axis, pairs)  6.92 us
    dynamic_update_slice x10, local copies, waits for them, and re-layouts, tree_sum(): lax.dynamic_update_slice_in_dim(jnp.concatenate([other, other]), pieces[n...  6.86 us
    ppermute x2, starting transfers between devices, halo(): before = lax.ppermute(last, 'sub', up)  6.72 us
    ppermute x2, starting transfers between devices, per_device(): near = [lax.ppermute(volume, 'grp', up), lax.ppermute(volume, 'grp', down)]  6.36 us
  transfers between devices with their start and end apart: 16, of which 8 were waited for; matrix products, arithmetic and copies ran while one was open for 13% of the time, Pallas kernels for 4%

profile of v17, /device:TPU:0, one launch (start us, length us, event | category | flops | bytes accessed | tf_op | source)
XLA Modules:
  0.0 106.8 jit_solution(6766267808024679359)
XLA Ops:
  0.7 5.1 %collective-permute-start = (bf16[256,1,2,128]{3,2,1,0:T(2,128)(2,1)}, bf16[256,1,2,128]{3,2,1,0:T(2,128)(2,1)S(1)}, u32[]{:S(2)}, u32[]{:S(2)}) collective-permute-start(bf16[256,1,2,128]{3,2,1,0:T(2,128)(2,1)} %param.5), channel_id=1, source_target_pairs={{0,4},{4,8},{8,12},{1,5},{5,9},{9,13},{2,6},{6,10},{10,14},{3,7},{... | collective-permute-start | bytes 393224 | tf_op jit(solution)/shard_map/ppermute | solution.py:250
  5.7 1.3 %collective-permute-start.1 = (bf16[256,1,2,128]{3,2,1,0:T(2,128)(2,1)}, bf16[256,1,2,128]{3,2,1,0:T(2,128)(2,1)S(1)}, u32[]{:S(2)}, u32[]{:S(2)}) collective-permute-start(bf16[256,1,2,128]{3,2,1,0:T(2,128)(2,1)} %param.5), channel_id=1, source_target_pairs={{4,0},{8,4},{12,8},{5,1},{9,5},{13,9},{6,2},{10,6},{14,10},{7,3},{... | collective-permute-start | bytes 393224 | tf_op jit(solution)/shard_map/ppermute | solution.py:250
  7.0 1.0 copy.56
  8.1 3.8 %convolution_convert_fusion.1 = bf16[256,256,27]{0,1,2:T(8,128)(2,1)} fusion(bf16[256,8,27]{0,1,2:T(8,128)(2,1)} %bitcast.132, s32[256]{0:T(256)S(1)} %and_select_fusion), kind=kOutput, calls=%fused_computation.1 | convolution fusion | flops 30083072 | bytes 3650560 | tf_op jit(solution)/shard_map/ojt,ji->toi/dot_general | solution.py:216
  13.3 1.3 %collective-permute-start.3 = (bf16[3,1,256,128]{3,2,1,0:T(8,128)(2,1)S(1)}, bf16[3,1,256,128]{3,2,1,0:T(8,128)(2,1)S(1)}, u32[]{:S(2)}, u32[]{:S(2)}) collective-permute-start(bf16[3,1,256,128]{3,2,1,0:T(8,128)(2,1)S(1)} %pad_maximum_fusion.5), channel_id=1, source_target_pairs={{1,0},{2,1},{3,2},{5,4},{6,5},{7,6},{9,8},{10,9},{11,10},{13,12},{... | collective-permute-start | bytes 589832 | tf_op jit(solution)/shard_map/ppermute | solution.py:193
  14.7 3.2 %collective-permute-start.2 = (bf16[3,1,256,128]{3,2,1,0:T(8,128)(2,1)S(1)}, bf16[3,1,256,128]{3,2,1,0:T(8,128)(2,1)S(1)}, u32[]{:S(2)}, u32[]{:S(2)}) collective-permute-start(bf16[3,1,256,128]{3,2,1,0:T(8,128)(2,1)S(1)} %pad_maximum_fusion.4), channel_id=1, source_target_pairs={{0,1},{1,2},{2,3},{4,5},{5,6},{6,7},{8,9},{9,10},{10,11},{12,13},{... | collective-permute-start | bytes 589832 | tf_op jit(solution)/shard_map/ppermute | solution.py:192
  17.9 2.9 %convolution_convert_fusion = bf16[256,256,27]{1,0,2:T(8,128)(2,1)} fusion(bf16[256,8,27]{0,1,2:T(8,128)(2,1)S(1)} %bitcast.133, s32[256]{0:T(256)S(1)} %and_select_fusion), kind=kOutput, calls=%fused_computation | convolution fusion | flops 30138368 | bytes 3650560 | tf_op jit(solution)/shard_map/ji,ojt->tio/dot_general | solution.py:217
  20.8 0.6 copy-done.8
  21.5 5.1 %shard_map.92 = f32[2,256,128]{2,1,0:T(8,128)} custom-call(bf16[1,2,256,128]{3,2,1,0:T(8,128)(2,1)} %bitcast.112, bf16[1,2,256,128]{3,2,1,0:T(8,128)(2,1)} %bitcast.115, bf16[1,2,256,128]{3,2,1,0:T(8,128)(2,1)} %bitcast.109, bf16[3,1,256,128]{3,2,1,0:T(8,128)(2,1)} %copy-done.9, bf16[3,1,256,128]{3,2,1,0:T(8,128)(2,1)} %copy-done.8, ...), custom_call_target="tpu_custom_call" | custom-call | flops 905969664 | bytes 4587520 | tf_op jit(solution)/shard_map/pallas_call | solution.py:60
  26.6 1.1 %fusion.22 = bf16[256,2,128]{2,0,1:T(8,128)(2,1)S(1)} fusion(f32[2,256,128]{2,1,0:T(8,128)} %shard_map.92), kind=kLoop, calls=%fused_computation.52 | loop fusion | flops 393216 | bytes 393216 | tf_op jit(solution)/shard_map/transpose | solution.py:239
  28.5 0.8 fusion.6.delta_ref
  29.2 4.6 %collective-permute-start.4 = (bf16[1,2,256,128]{3,2,1,0:T(8,128)(2,1)}, bf16[1,2,256,128]{3,2,1,0:T(8,128)(2,1)S(1)}, u32[]{:S(2)}, u32[]{:S(2)}) collective-permute-start(bf16[1,2,256,128]{3,2,1,0:T(8,128)(2,1)} %bitcast.20.block_ref), channel_id=1, source_target_pairs={{0,4},{4,8},{8,12},{1,5},{5,9},{9,13},{2,6},{6,10},{10,14},{3,7},{... | collective-permute-start | bytes 393224 | tf_op jit(solution)/shard_map/ppermute | solution.py:183
  33.8 1.3 %collective-permute-start.5 = (bf16[1,2,256,128]{3,2,1,0:T(8,128)(2,1)}, bf16[1,2,256,128]{3,2,1,0:T(8,128)(2,1)S(1)}, u32[]{:S(2)}, u32[]{:S(2)}) collective-permute-start(bf16[1,2,256,128]{3,2,1,0:T(8,128)(2,1)} %bitcast.20.block_ref), channel_id=1, source_target_pairs={{4,0},{8,4},{12,8},{5,1},{9,5},{13,9},{6,2},{10,6},{14,10},{7,3},{... | collective-permute-start | bytes 393224 | tf_op jit(solution)/shard_map/ppermute | solution.py:184
  35.3 4.4 %shard_map.94 = f32[2,256,128]{2,1,0:T(8,128)} custom-call(bf16[1,2,256,128]{3,2,1,0:T(8,128)(2,1)} %bitcast.113, bf16[1,2,256,128]{3,2,1,0:T(8,128)(2,1)} %bitcast.116, bf16[1,2,256,128]{3,2,1,0:T(8,128)(2,1)} %bitcast.110, bf16[3,1,256,128]{3,2,1,0:T(8,128)(2,1)} %copy-done.9, bf16[3,1,256,128]{3,2,1,0:T(8,128)(2,1)} %copy-done.8, ...), custom_call_target="tpu_custom_call" | custom-call | flops 1358954496 | bytes 1179648 | tf_op jit(solution)/shard_map/pallas_call | solution.py:117
  39.7 1.1 %copy.69 = f32[256,2,128]{0,2,1:T(8,128)S(1)} copy(f32[256,2,128]{2,0,1:T(8,128)} %bitcast.134) | data formatting | bytes 524288 | tf_op jit(solution)/shard_map/transpose | solution.py:128
  42.1 0.9 fusion.35
  43.1 1.3 %collective-permute-start.7 = (bf16[3,1,256,128]{3,2,1,0:T(8,128)(2,1)S(1)}, bf16[3,1,256,128]{3,2,1,0:T(8,128)(2,1)S(1)}, u32[]{:S(2)}, u32[]{:S(2)}) collective-permute-start(bf16[3,1,256,128]{3,2,1,0:T(8,128)(2,1)S(1)} %pad_maximum_fusion.7), channel_id=1, source_target_pairs={{1,0},{2,1},{3,2},{5,4},{6,5},{7,6},{9,8},{10,9},{11,10},{13,12},{... | collective-permute-start | bytes 589832 | tf_op jit(solution)/shard_map/ppermute | solution.py:193
  44.4 3.5 %collective-permute-start.6 = (bf16[3,1,256,128]{3,2,1,0:T(8,128)(2,1)S(1)}, bf16[3,1,256,128]{3,2,1,0:T(8,128)(2,1)S(1)}, u32[]{:S(2)}, u32[]{:S(2)}) collective-permute-start(bf16[3,1,256,128]{3,2,1,0:T(8,128)(2,1)S(1)} %pad_maximum_fusion.6), channel_id=1, source_target_pairs={{0,1},{1,2},{2,3},{4,5},{5,6},{6,7},{8,9},{9,10},{10,11},{12,13},{... | collective-permute-start | bytes 589832 | tf_op jit(solution)/shard_map/ppermute | solution.py:192
  48.2 0.6 collective-permute-done.6.before_ref
  48.8 0.6 copy-done.11
  49.5 5.1 %shard_map.93 = f32[2,256,128]{2,1,0:T(8,128)} custom-call(bf16[1,2,256,128]{3,2,1,0:T(8,128)(2,1)} %bitcast.20.block_ref, bf16[1,2,256,128]{3,2,1,0:T(8,128)(2,1)} %copy-done.5, bf16[1,2,256,128]{3,2,1,0:T(8,128)(2,1)} %copy-done.6, bf16[3,1,256,128]{3,2,1,0:T(8,128)(2,1)} %copy-done.11, bf16[3,1,256,128]{3,2,1,0:T(8,128)(2,1)} %copy-done.10, ...), custom_call_target="tpu_custom_call" | custom-call | flops 905969664 | bytes 4587520 | tf_op jit(solution)/shard_map/pallas_call | solution.py:60
  54.6 1.0 convert_bitcast_fusion
  56.3 4.0 %collective-permute-start.8 = (f32[93184]{0:T(1024)S(1)}, f32[93184]{0:T(1024)S(1)}, u32[]{:S(2)}, u32[]{:S(2)}) collective-permute-start(f32[93184]{0:T(1024)S(1)} %pad_maximum_fusion), channel_id=1, source_target_pairs={{0,1},{1,0},{2,3},{3,2},{4,5},{5,4},{6,7},{7,6},{8,9},{9,8},{10,11... | collective-permute-start | bytes 1118216 | tf_op jit(solution)/shard_map/ppermute | solution.py:152
  60.7 0.9 collective-permute-done.8
  61.7 2.8 %collective-permute-start.9 = (f32[46592]{0:T(1024)S(1)}, f32[46592]{0:T(1024)S(1)}, u32[]{:S(2)}, u32[]{:S(2)}) collective-permute-start(f32[46592]{0:T(1024)S(1)} %pad_maximum_fusion.8), channel_id=1, source_target_pairs={{0,2},{1,3},{2,0},{3,1},{4,6},{5,7},{6,4},{7,5},{8,10},{9,11},{10,... | collective-permute-start | bytes 559112 | tf_op jit(solution)/shard_map/ppermute | solution.py:152
  64.5 5.0 %collective-permute-done.9 = f32[46592]{0:T(1024)S(1)} collective-permute-done((f32[46592]{0:T(1024)S(1)}, f32[46592]{0:T(1024)S(1)}, u32[]{:S(2)}, u32[]{:S(2)}) %collective-permute-start.9) | collective-permute-done | bytes 186400 | tf_op jit(solution)/shard_map/ppermute | solution.py:152
  69.7 2.7 %collective-permute-start.10 = (f32[23296]{0:T(1024)S(1)}, f32[23296]{0:T(1024)S(1)}, u32[]{:S(2)}, u32[]{:S(2)}) collective-permute-start(f32[23296]{0:T(1024)S(1)} %pad_maximum_fusion.12), channel_id=1, source_target_pairs={{0,4},{4,0},{8,12},{12,8},{1,5},{5,1},{9,13},{13,9},{2,6},{6,2},{1... | collective-permute-start | bytes 279560 | tf_op jit(solution)/shard_map/ppermute | solution.py:152
  72.4 2.6 %collective-permute-done.10 = f32[23296]{0:T(1024)S(1)} collective-permute-done((f32[23296]{0:T(1024)S(1)}, f32[23296]{0:T(1024)S(1)}, u32[]{:S(2)}, u32[]{:S(2)}) %collective-permute-start.10) | collective-permute-done | bytes 93216 | tf_op jit(solution)/shard_map/ppermute | solution.py:152
  75.0 3.1 %collective-permute-start.11 = (f32[11648]{0:T(1024)S(1)}, f32[11648]{0:T(1024)S(1)}, u32[]{:S(2)}, u32[]{:S(2)}) collective-permute-start(f32[11648]{0:T(1024)S(1)} %pad_maximum_fusion.17), channel_id=1, source_target_pairs={{0,8},{4,12},{8,0},{12,4},{1,9},{5,13},{9,1},{13,5},{2,10},{6,14},... | collective-permute-start | bytes 139784 | tf_op jit(solution)/shard_map/ppermute | solution.py:152
  78.1 2.1 %collective-permute-done.11 = f32[11648]{0:T(1024)S(1)} collective-permute-done((f32[11648]{0:T(1024)S(1)}, f32[11648]{0:T(1024)S(1)}, u32[]{:S(2)}, u32[]{:S(2)}) %collective-permute-start.11) | collective-permute-done | bytes 46624 | tf_op jit(solution)/shard_map/ppermute | solution.py:152
  80.2 3.0 %collective-permute-start.12 = (f32[8192]{0:T(1024)S(1)}, f32[8192]{0:T(1024)S(1)}, u32[]{:S(2)}, u32[]{:S(2)}) collective-permute-start(f32[8192]{0:T(1024)S(1)} %pad_maximum_fusion.18), channel_id=1, source_target_pairs={{0,8},{4,12},{8,0},{12,4},{1,9},{5,13},{9,1},{13,5},{2,10},{6,14},... | collective-permute-start | bytes 98312 | tf_op jit(solution)/shard_map/ppermute | solution.py:163
  83.2 1.9 %collective-permute-done.12 = f32[8192]{0:T(1024)S(1)} collective-permute-done((f32[8192]{0:T(1024)S(1)}, f32[8192]{0:T(1024)S(1)}, u32[]{:S(2)}, u32[]{:S(2)}) %collective-permute-start.12) | collective-permute-done | bytes 32800 | tf_op jit(solution)/shard_map/ppermute | solution.py:163
  86.0 2.0 %collective-permute-start.13 = (f32[16384]{0:T(1024)S(1)}, f32[16384]{0:T(1024)S(1)}, u32[]{:S(2)}, u32[]{:S(2)}) collective-permute-start(f32[16384]{0:T(1024)S(1)} %pad_maximum_fusion.13), channel_id=1, source_target_pairs={{0,4},{4,0},{8,12},{12,8},{1,5},{5,1},{9,13},{13,9},{2,6},{6,2},{1... | collective-permute-start | bytes 196616 | tf_op jit(solution)/shard_map/ppermute | solution.py:163
  88.0 2.3 %collective-permute-done.13 = f32[16384]{0:T(1024)S(1)} collective-permute-done((f32[16384]{0:T(1024)S(1)}, f32[16384]{0:T(1024)S(1)}, u32[]{:S(2)}, u32[]{:S(2)}) %collective-permute-start.13) | collective-permute-done | bytes 65568 | tf_op jit(solution)/shard_map/ppermute | solution.py:163
  90.4 0.6 dynamic_update_slice.32
  90.9 0.6 dynamic_update_slice.33
  91.5 1.8 %collective-permute-start.14 = (f32[36224]{0:T(1024)S(1)}, f32[36224]{0:T(1024)S(1)}, u32[]{:S(2)}, u32[]{:S(2)}) collective-permute-start(f32[36224]{0:T(1024)S(1)} %pad_maximum_fusion.9), channel_id=1, source_target_pairs={{0,2},{1,3},{2,0},{3,1},{4,6},{5,7},{6,4},{7,5},{8,10},{9,11},{10,... | collective-permute-start | bytes 434696 | tf_op jit(solution)/shard_map/ppermute | solution.py:163
  93.3 3.4 %collective-permute-done.14 = f32[36224]{0:T(1024)S(1)} collective-permute-done((f32[36224]{0:T(1024)S(1)}, f32[36224]{0:T(1024)S(1)}, u32[]{:S(2)}, u32[]{:S(2)}) %collective-permute-start.14) | collective-permute-done | bytes 144928 | tf_op jit(solution)/shard_map/ppermute | solution.py:163
  96.8 0.8 dynamic_update_slice.34
  97.6 0.8 dynamic_update_slice.35
  98.9 0.8 copy.78
  99.9 0.8 copy.79
  100.7 1.2 %dynamic_update_slice.39 = f32[65536]{0:T(1024)S(1)} dynamic-update-slice(f32[65536]{0:T(1024)S(1)} %pad_maximum_fusion.3, f32[32768]{0:T(1024)S(1)} %dynamic_update_slice.35, s32[]{:T(128)S(6)} %mul.100) | dynamic-update-slice | bytes 262148 | tf_op jit(solution)/shard_map/dynamic_update_slice | solution.py:170
  102.0 0.8 reshape.129
  102.8 0.5 dynamic_update_slice.38
  103.6 1.2 %copy.77 = f32[64,8,27]{0,1,2:T(8,128)} copy(f32[64,8,27]{1,2,0:T(8,128)S(1)} %bitcast.106) | data formatting | bytes 110592 | tf_op jit(solution)/shard_map/transpose | solution.py:313
  104.8 1.2 %dynamic_update_slice.37 = f32[65536]{0:T(1024)S(1)} dynamic-update-slice(f32[65536]{0:T(1024)S(1)} %pad_maximum_fusion.2, f32[32768]{0:T(1024)S(1)} %dynamic_update_slice.34, s32[]{:T(128)S(6)} %mul.100) | dynamic-update-slice | bytes 262148 | tf_op jit(solution)/shard_map/dynamic_update_slice | solution.py:170
  106.0 0.8 reshape.126
  (130 shorter events, 7.2 us)
Async XLA Ops:
  0.6 11.2 %copy-start = (bf16[256,256]{1,0:T(8,128)(2,1)S(1)}, bf16[256,256]{1,0:T(8,128)(2,1)}, u32[]{:S(2)}) copy-start(bf16[256,256]{1,0:T(8,128)(2,1)} %param.7) | copy-start | bytes 393220
  0.6 11.6 %copy-start.12 = (bf16[256,1,2,128]{3,2,1,0:T(2,128)(2,1)S(1)}, bf16[256,1,2,128]{3,2,1,0:T(2,128)(2,1)}, u32[]{:S(2)}) copy-start(bf16[256,1,2,128]{3,2,1,0:T(2,128)(2,1)} %param.6) | copy-start | bytes 393220
  0.7 11.7 %collective-permute-start = (bf16[256,1,2,128]{3,2,1,0:T(2,128)(2,1)}, bf16[256,1,2,128]{3,2,1,0:T(2,128)(2,1)S(1)}, u32[]{:S(2)}, u32[]{:S(2)}) collective-permute-start(bf16[256,1,2,128]{3,2,1,0:T(2,128)(2,1)} %param.5), channel_id=1, source_target_pairs={{0,4},{4,8},{8,12},{1,5},{5,9},{9,13},{2,6},{6,10},{10,14},{3,7},{... | collective-permute-start | bytes 393224 | tf_op jit(solution)/shard_map/ppermute | solution.py:250
  5.7 7.1 %collective-permute-start.1 = (bf16[256,1,2,128]{3,2,1,0:T(2,128)(2,1)}, bf16[256,1,2,128]{3,2,1,0:T(2,128)(2,1)S(1)}, u32[]{:S(2)}, u32[]{:S(2)}) collective-permute-start(bf16[256,1,2,128]{3,2,1,0:T(2,128)(2,1)} %param.5), channel_id=1, source_target_pairs={{4,0},{8,4},{12,8},{5,1},{9,5},{13,9},{6,2},{10,6},{14,10},{7,3},{... | collective-permute-start | bytes 393224 | tf_op jit(solution)/shard_map/ppermute | solution.py:250
  11.9 6.0 %copy-start.7 = (bf16[256,8,3,3,3]{0,1,4,3,2:T(8,128)(2,1)S(1)}, bf16[256,8,3,3,3]{0,1,4,3,2:T(8,128)(2,1)}, u32[]{:S(2)}) copy-start(bf16[256,8,3,3,3]{0,1,4,3,2:T(8,128)(2,1)} %param.8) | copy-start | bytes 331780
  12.2 8.5 %copy-start.3 = (bf16[256,1,2,128]{3,0,2,1:T(8,128)(2,1)}, bf16[256,1,2,128]{3,0,2,1:T(8,128)(2,1)S(1)}, u32[]{:S(2)}) copy-start(bf16[256,1,2,128]{3,0,2,1:T(8,128)(2,1)S(1)} %copy.57) | copy-start | bytes 393220
  12.8 8.0 %copy-start.4 = (bf16[256,1,2,128]{3,0,2,1:T(8,128)(2,1)}, bf16[256,1,2,128]{3,0,2,1:T(8,128)(2,1)S(1)}, u32[]{:S(2)}) copy-start(bf16[256,1,2,128]{3,0,2,1:T(8,128)(2,1)S(1)} %copy.58) | copy-start | bytes 393220
  13.2 7.5 %copy-start.2 = (bf16[256,1,2,128]{3,0,2,1:T(8,128)(2,1)}, bf16[256,1,2,128]{3,0,2,1:T(8,128)(2,1)S(1)}, u32[]{:S(2)}) copy-start(bf16[256,1,2,128]{3,0,2,1:T(8,128)(2,1)S(1)} %copy.59) | copy-start | bytes 393220
  13.3 7.4 %collective-permute-start.3 = (bf16[3,1,256,128]{3,2,1,0:T(8,128)(2,1)S(1)}, bf16[3,1,256,128]{3,2,1,0:T(8,128)(2,1)S(1)}, u32[]{:S(2)}, u32[]{:S(2)}) collective-permute-start(bf16[3,1,256,128]{3,2,1,0:T(8,128)(2,1)S(1)} %pad_maximum_fusion.5), channel_id=1, source_target_pairs={{1,0},{2,1},{3,2},{5,4},{6,5},{7,6},{9,8},{10,9},{11,10},{13,12},{... | collective-permute-start | bytes 589832 | tf_op jit(solution)/shard_map/ppermute | solution.py:193
  14.6 13.2 %copy-start.13 = (bf16[256,256]{1,0:T(8,128)(2,1)S(1)}, bf16[256,256]{1,0:T(8,128)(2,1)}, u32[]{:S(2)}) copy-start(bf16[256,256]{1,0:T(8,128)(2,1)} %param.9) | copy-start | bytes 393220
  14.7 6.1 %collective-permute-start.2 = (bf16[3,1,256,128]{3,2,1,0:T(8,128)(2,1)S(1)}, bf16[3,1,256,128]{3,2,1,0:T(8,128)(2,1)S(1)}, u32[]{:S(2)}, u32[]{:S(2)}) collective-permute-start(bf16[3,1,256,128]{3,2,1,0:T(8,128)(2,1)S(1)} %pad_maximum_fusion.4), channel_id=1, source_target_pairs={{0,1},{1,2},{2,3},{4,5},{5,6},{6,7},{8,9},{9,10},{10,11},{12,13},{... | collective-permute-start | bytes 589832 | tf_op jit(solution)/shard_map/ppermute | solution.py:192
  20.7 0.7 copy-start.8
  20.7 0.7 copy-start.9
  26.6 1.9 %copy-start.1 = (f32[2,256,128]{2,1,0:T(8,128)S(1)}, f32[2,256,128]{2,1,0:T(8,128)}, u32[]{:S(2)}) copy-start(f32[2,256,128]{2,1,0:T(8,128)} %shard_map.92) | copy-start | bytes 786436
  29.2 13.7 %collective-permute-start.4 = (bf16[1,2,256,128]{3,2,1,0:T(8,128)(2,1)}, bf16[1,2,256,128]{3,2,1,0:T(8,128)(2,1)S(1)}, u32[]{:S(2)}, u32[]{:S(2)}) collective-permute-start(bf16[1,2,256,128]{3,2,1,0:T(8,128)(2,1)} %bitcast.20.block_ref), channel_id=1, source_target_pairs={{0,4},{4,8},{8,12},{1,5},{5,9},{9,13},{2,6},{6,10},{10,14},{3,7},{... | collective-permute-start | bytes 393224 | tf_op jit(solution)/shard_map/ppermute | solution.py:183
  33.8 9.2 %collective-permute-start.5 = (bf16[1,2,256,128]{3,2,1,0:T(8,128)(2,1)}, bf16[1,2,256,128]{3,2,1,0:T(8,128)(2,1)S(1)}, u32[]{:S(2)}, u32[]{:S(2)}) collective-permute-start(bf16[1,2,256,128]{3,2,1,0:T(8,128)(2,1)} %bitcast.20.block_ref), channel_id=1, source_target_pairs={{4,0},{8,4},{12,8},{5,1},{9,5},{13,9},{6,2},{10,6},{14,10},{7,3},{... | collective-permute-start | bytes 393224 | tf_op jit(solution)/shard_map/ppermute | solution.py:184
  43.0 5.9 %copy-start.5 = (bf16[1,2,256,128]{3,2,1,0:T(8,128)(2,1)}, bf16[1,2,256,128]{3,2,1,0:T(8,128)(2,1)S(1)}, u32[]{:S(2)}) copy-start(bf16[1,2,256,128]{3,2,1,0:T(8,128)(2,1)S(1)} %collective-permute-done.4.below_ref) | copy-start | bytes 393220
  43.0 5.8 %copy-start.6 = (bf16[1,2,256,128]{3,2,1,0:T(8,128)(2,1)}, bf16[1,2,256,128]{3,2,1,0:T(8,128)(2,1)S(1)}, u32[]{:S(2)}) copy-start(bf16[1,2,256,128]{3,2,1,0:T(8,128)(2,1)S(1)} %collective-permute-done.5.above_ref) | copy-start | bytes 393220
  43.1 5.1 %collective-permute-start.7 = (bf16[3,1,256,128]{3,2,1,0:T(8,128)(2,1)S(1)}, bf16[3,1,256,128]{3,2,1,0:T(8,128)(2,1)S(1)}, u32[]{:S(2)}, u32[]{:S(2)}) collective-permute-start(bf16[3,1,256,128]{3,2,1,0:T(8,128)(2,1)S(1)} %pad_maximum_fusion.7), channel_id=1, source_target_pairs={{1,0},{2,1},{3,2},{5,4},{6,5},{7,6},{9,8},{10,9},{11,10},{13,12},{... | collective-permute-start | bytes 589832 | tf_op jit(solution)/shard_map/ppermute | solution.py:193
  44.4 4.4 %collective-permute-start.6 = (bf16[3,1,256,128]{3,2,1,0:T(8,128)(2,1)S(1)}, bf16[3,1,256,128]{3,2,1,0:T(8,128)(2,1)S(1)}, u32[]{:S(2)}, u32[]{:S(2)}) collective-permute-start(bf16[3,1,256,128]{3,2,1,0:T(8,128)(2,1)S(1)} %pad_maximum_fusion.6), channel_id=1, source_target_pairs={{0,1},{1,2},{2,3},{4,5},{5,6},{6,7},{8,9},{9,10},{10,11},{12,13},{... | collective-permute-start | bytes 589832 | tf_op jit(solution)/shard_map/ppermute | solution.py:192
  48.2 0.7 copy-start.10
  48.8 0.7 copy-start.11
  56.3 5.3 %collective-permute-start.8 = (f32[93184]{0:T(1024)S(1)}, f32[93184]{0:T(1024)S(1)}, u32[]{:S(2)}, u32[]{:S(2)}) collective-permute-start(f32[93184]{0:T(1024)S(1)} %pad_maximum_fusion), channel_id=1, source_target_pairs={{0,1},{1,0},{2,3},{3,2},{4,5},{5,4},{6,7},{7,6},{8,9},{9,8},{10,11... | collective-permute-start | bytes 1118216 | tf_op jit(solution)/shard_map/ppermute | solution.py:152
  61.7 7.8 %collective-permute-start.9 = (f32[46592]{0:T(1024)S(1)}, f32[46592]{0:T(1024)S(1)}, u32[]{:S(2)}, u32[]{:S(2)}) collective-permute-start(f32[46592]{0:T(1024)S(1)} %pad_maximum_fusion.8), channel_id=1, source_target_pairs={{0,2},{1,3},{2,0},{3,1},{4,6},{5,7},{6,4},{7,5},{8,10},{9,11},{10,... | collective-permute-start | bytes 559112 | tf_op jit(solution)/shard_map/ppermute | solution.py:152
  69.7 5.3 %collective-permute-start.10 = (f32[23296]{0:T(1024)S(1)}, f32[23296]{0:T(1024)S(1)}, u32[]{:S(2)}, u32[]{:S(2)}) collective-permute-start(f32[23296]{0:T(1024)S(1)} %pad_maximum_fusion.12), channel_id=1, source_target_pairs={{0,4},{4,0},{8,12},{12,8},{1,5},{5,1},{9,13},{13,9},{2,6},{6,2},{1... | collective-permute-start | bytes 279560 | tf_op jit(solution)/shard_map/ppermute | solution.py:152
  75.0 5.2 %collective-permute-start.11 = (f32[11648]{0:T(1024)S(1)}, f32[11648]{0:T(1024)S(1)}, u32[]{:S(2)}, u32[]{:S(2)}) collective-permute-start(f32[11648]{0:T(1024)S(1)} %pad_maximum_fusion.17), channel_id=1, source_target_pairs={{0,8},{4,12},{8,0},{12,4},{1,9},{5,13},{9,1},{13,5},{2,10},{6,14},... | collective-permute-start | bytes 139784 | tf_op jit(solution)/shard_map/ppermute | solution.py:152
  80.2 4.9 %collective-permute-start.12 = (f32[8192]{0:T(1024)S(1)}, f32[8192]{0:T(1024)S(1)}, u32[]{:S(2)}, u32[]{:S(2)}) collective-permute-start(f32[8192]{0:T(1024)S(1)} %pad_maximum_fusion.18), channel_id=1, source_target_pairs={{0,8},{4,12},{8,0},{12,4},{1,9},{5,13},{9,1},{13,5},{2,10},{6,14},... | collective-permute-start | bytes 98312 | tf_op jit(solution)/shard_map/ppermute | solution.py:163
  86.0 4.3 %collective-permute-start.13 = (f32[16384]{0:T(1024)S(1)}, f32[16384]{0:T(1024)S(1)}, u32[]{:S(2)}, u32[]{:S(2)}) collective-permute-start(f32[16384]{0:T(1024)S(1)} %pad_maximum_fusion.13), channel_id=1, source_target_pairs={{0,4},{4,0},{8,12},{12,8},{1,5},{5,1},{9,13},{13,9},{2,6},{6,2},{1... | collective-permute-start | bytes 196616 | tf_op jit(solution)/shard_map/ppermute | solution.py:163
  91.5 5.2 %collective-permute-start.14 = (f32[36224]{0:T(1024)S(1)}, f32[36224]{0:T(1024)S(1)}, u32[]{:S(2)}, u32[]{:S(2)}) collective-permute-start(f32[36224]{0:T(1024)S(1)} %pad_maximum_fusion.9), channel_id=1, source_target_pairs={{0,2},{1,3},{2,0},{3,1},{4,6},{5,7},{6,4},{7,5},{8,10},{9,11},{10,... | collective-permute-start | bytes 434696 | tf_op jit(solution)/shard_map/ppermute | solution.py:163
  98.8 1.9 %collective-permute-start.15 = (f32[72448]{0:T(1024)S(1)}, f32[72448]{0:T(1024)S(1)}, u32[]{:S(2)}, u32[]{:S(2)}) collective-permute-start(f32[72448]{0:T(1024)S(1)} %pad_maximum_fusion.1), channel_id=1, source_target_pairs={{0,1},{1,0},{2,3},{3,2},{4,5},{5,4},{6,7},{7,6},{8,9},{9,8},{10,11... | collective-permute-start | bytes 869384 | tf_op jit(solution)/shard_map/ppermute | solution.py:163

commit v18 on v17

--- a/solution.py
+++ b/solution.py
@@ -166,11 +166,9 @@
             size = pieces[n].shape[0]
             other = got[offset : offset + size]
             offset += size
-            mine = upper.astype(jnp.int32) * size
-            joined = lax.dynamic_update_slice_in_dim(
-                jnp.concatenate([other, other]), pieces[n], mine, 0
+            pieces[n] = jnp.concatenate(
+                [jnp.where(upper, other, pieces[n]), jnp.where(upper, pieces[n], other)]
             )
-            pieces[n] = joined
     return pieces
 
 

time: 107 us -> 101 us (0.944)
  local copies, waits for them, and re-layouts: 18.5 us -> 12.2 us
  other arithmetic: 3.63 us -> 4.97 us
    dynamic_update_slice x10 -> x0, local copies, waits for them, and re-layouts: 6.86 us -> none  [tree_sum(): lax.dynamic_update_slice_in_dim(jnp.concatenate([other, other]), pieces[n...]
    reshape x3 -> x0, local copies, waits for them, and re-layouts: 1.85 us -> none  [the longest x1 0.78 us: per_device(): third_grad = third_sum.reshape(third_part.shape)]
    unnamed x35 -> x38, local copies, waits for them, and re-layouts: 4.29 us -> 5.98 us
    transpose x1 -> x0, local copies, waits for them, and re-layouts: 1.16 us -> none  [per_device(): group_sum.reshape(own_rows, 27, GW).transpose(0, 2, 1)]
  transfers between devices with their start and end apart: 16 -> 16, of which waited for: 8 -> 9; matrix products, arithmetic and copies ran while one was open for 13% -> 15% of each run, Pallas kernels for 4% -> 4%
where the time goes in v18:
time: 101 us
  starting transfers between devices  40.9 us (40%)
  waiting for transfers between devices  17.8 us (18%)
  Pallas kernels  14.6 us (14%)
  local copies, waits for them, and re-layouts  12.2 us (12%)
  matrix products  8.61 us (9%)
  other arithmetic  4.97 us (5%)
  between operations  1.74 us (2%)
    ppermute x4, starting transfers between devices, tree_sum(): got = lax.ppermute(jnp.concatenate(sends), axis, pairs)  12.6 us
    pallas_call x2, Pallas kernels, conv_call(): pl.pallas_call(conv_body, out_shape=jax.ShapeDtypeStruct((height, channel...  10.2 us
    ppermute x4, waiting for transfers between devices, tree_sum(): got = lax.ppermute(jnp.concatenate(sends), axis, pairs)  9.74 us
    ppermute x4, waiting for transfers between devices, tree_sum(): lax.ppermute(jnp.concatenate([pieces[n] for n in members]), axis, pairs)  7.44 us
    ppermute x4, starting transfers between devices, tree_sum(): lax.ppermute(jnp.concatenate([pieces[n] for n in members]), axis, pairs)  6.81 us
    ppermute x2, starting transfers between devices, halo(): before = lax.ppermute(last, 'sub', up)  6.72 us
    ppermute x2, starting transfers between devices, per_device(): near = [lax.ppermute(volume, 'grp', up), lax.ppermute(volume, 'grp', down)]  6.36 us
    unnamed x38, local copies, waits for them, and re-layouts  5.98 us
  transfers between devices with their start and end apart: 16, of which 9 were waited for; matrix products, arithmetic and copies ran while one was open for 15% of the time, Pallas kernels for 4%

profile of v18, /device:TPU:0, one launch (start us, length us, event | category | flops | bytes accessed | tf_op | source)
XLA Modules:
  0.0 100.9 jit_solution(485697816470404063)
XLA Ops:
  0.7 5.1 %collective-permute-start = (bf16[256,1,2,128]{3,2,1,0:T(2,128)(2,1)}, bf16[256,1,2,128]{3,2,1,0:T(2,128)(2,1)S(1)}, u32[]{:S(2)}, u32[]{:S(2)}) collective-permute-start(bf16[256,1,2,128]{3,2,1,0:T(2,128)(2,1)} %param.5), channel_id=1, source_target_pairs={{0,4},{4,8},{8,12},{1,5},{5,9},{9,13},{2,6},{6,10},{10,14},{3,7},{... | collective-permute-start | bytes 393224 | tf_op jit(solution)/shard_map/ppermute | solution.py:248
  5.7 1.3 %collective-permute-start.1 = (bf16[256,1,2,128]{3,2,1,0:T(2,128)(2,1)}, bf16[256,1,2,128]{3,2,1,0:T(2,128)(2,1)S(1)}, u32[]{:S(2)}, u32[]{:S(2)}) collective-permute-start(bf16[256,1,2,128]{3,2,1,0:T(2,128)(2,1)} %param.5), channel_id=1, source_target_pairs={{4,0},{8,4},{12,8},{5,1},{9,5},{13,9},{6,2},{10,6},{14,10},{7,3},{... | collective-permute-start | bytes 393224 | tf_op jit(solution)/shard_map/ppermute | solution.py:248
  7.0 1.0 %copy.183 = bf16[256,1,2,128]{0,3,2,1:T(8,128)(2,1)S(1)} copy(bf16[256,1,2,128]{3,2,1,0:T(2,128)(2,1)} %param.5) | data formatting | bytes 262144 | tf_op args[0]
  8.1 3.8 %convolution_convert_fusion.1 = bf16[256,256,27]{0,1,2:T(8,128)(2,1)} fusion(bf16[256,8,27]{0,1,2:T(8,128)(2,1)} %bitcast.132, s32[256]{0:T(256)S(1)} %and_select_fusion), kind=kOutput, calls=%fused_computation.1 | convolution fusion | flops 30083072 | bytes 3650560 | tf_op jit(solution)/shard_map/ojt,ji->toi/dot_general | solution.py:214
  11.9 0.2 reduce-precision_convert_fusion.4
  12.4 0.3 reduce-precision_convert_fusion.3
  12.8 0.3 reduce-precision_convert_fusion.2
  13.3 1.3 %collective-permute-start.3 = (bf16[3,1,256,128]{3,2,1,0:T(8,128)(2,1)S(1)}, bf16[3,1,256,128]{3,2,1,0:T(8,128)(2,1)S(1)}, u32[]{:S(2)}, u32[]{:S(2)}) collective-permute-start(bf16[3,1,256,128]{3,2,1,0:T(8,128)(2,1)S(1)} %pad_maximum_fusion.4), channel_id=1, source_target_pairs={{1,0},{2,1},{3,2},{5,4},{6,5},{7,6},{9,8},{10,9},{11,10},{13,12},{... | collective-permute-start | bytes 589832 | tf_op jit(solution)/shard_map/ppermute | solution.py:191
  14.6 3.2 %collective-permute-start.2 = (bf16[3,1,256,128]{3,2,1,0:T(8,128)(2,1)S(1)}, bf16[3,1,256,128]{3,2,1,0:T(8,128)(2,1)S(1)}, u32[]{:S(2)}, u32[]{:S(2)}) collective-permute-start(bf16[3,1,256,128]{3,2,1,0:T(8,128)(2,1)S(1)} %pad_maximum_fusion.3), channel_id=1, source_target_pairs={{0,1},{1,2},{2,3},{4,5},{5,6},{6,7},{8,9},{9,10},{10,11},{12,13},{... | collective-permute-start | bytes 589832 | tf_op jit(solution)/shard_map/ppermute | solution.py:190
  17.8 2.9 %convolution_convert_fusion = bf16[256,256,27]{1,0,2:T(8,128)(2,1)} fusion(bf16[256,8,27]{0,1,2:T(8,128)(2,1)S(1)} %bitcast.133, s32[256]{0:T(256)S(1)} %and_select_fusion), kind=kOutput, calls=%fused_computation | convolution fusion | flops 30138368 | bytes 3650560 | tf_op jit(solution)/shard_map/ji,ojt->tio/dot_general | solution.py:215
  20.8 0.6 copy-done.8
  21.5 5.1 %shard_map.92 = f32[2,256,128]{2,1,0:T(8,128)} custom-call(bf16[1,2,256,128]{3,2,1,0:T(8,128)(2,1)} %bitcast.112, bf16[1,2,256,128]{3,2,1,0:T(8,128)(2,1)} %bitcast.115, bf16[1,2,256,128]{3,2,1,0:T(8,128)(2,1)} %bitcast.109, bf16[3,1,256,128]{3,2,1,0:T(8,128)(2,1)} %copy-done.9, bf16[3,1,256,128]{3,2,1,0:T(8,128)(2,1)} %copy-done.8, ...), custom_call_target="tpu_custom_call" | custom-call | flops 905969664 | bytes 4587520 | tf_op jit(solution)/shard_map/pallas_call | solution.py:60
  26.6 1.1 %fusion.22 = bf16[256,2,128]{2,0,1:T(8,128)(2,1)S(1)} fusion(f32[2,256,128]{2,1,0:T(8,128)} %shard_map.92), kind=kLoop, calls=%fused_computation.54 | loop fusion | flops 393216 | bytes 393216 | tf_op jit(solution)/shard_map/transpose | solution.py:237
  27.8 0.3 fusion.10
  28.5 0.8 fusion.6.delta_ref
  29.2 4.5 %collective-permute-start.4 = (bf16[1,2,256,128]{3,2,1,0:T(8,128)(2,1)}, bf16[1,2,256,128]{3,2,1,0:T(8,128)(2,1)S(1)}, u32[]{:S(2)}, u32[]{:S(2)}) collective-permute-start(bf16[1,2,256,128]{3,2,1,0:T(8,128)(2,1)} %bitcast.20.block_ref), channel_id=1, source_target_pairs={{0,4},{4,8},{8,12},{1,5},{5,9},{9,13},{2,6},{6,10},{10,14},{3,7},{... | collective-permute-start | bytes 393224 | tf_op jit(solution)/shard_map/ppermute | solution.py:181
  33.8 1.3 %collective-permute-start.5 = (bf16[1,2,256,128]{3,2,1,0:T(8,128)(2,1)}, bf16[1,2,256,128]{3,2,1,0:T(8,128)(2,1)S(1)}, u32[]{:S(2)}, u32[]{:S(2)}) collective-permute-start(bf16[1,2,256,128]{3,2,1,0:T(8,128)(2,1)} %bitcast.20.block_ref), channel_id=1, source_target_pairs={{4,0},{8,4},{12,8},{5,1},{9,5},{13,9},{6,2},{10,6},{14,10},{7,3},{... | collective-permute-start | bytes 393224 | tf_op jit(solution)/shard_map/ppermute | solution.py:182
  35.3 4.4 %shard_map.94 = f32[2,256,128]{2,1,0:T(8,128)} custom-call(bf16[1,2,256,128]{3,2,1,0:T(8,128)(2,1)} %bitcast.113, bf16[1,2,256,128]{3,2,1,0:T(8,128)(2,1)} %bitcast.116, bf16[1,2,256,128]{3,2,1,0:T(8,128)(2,1)} %bitcast.110, bf16[3,1,256,128]{3,2,1,0:T(8,128)(2,1)} %copy-done.9, bf16[3,1,256,128]{3,2,1,0:T(8,128)(2,1)} %copy-done.8, ...), custom_call_target="tpu_custom_call" | custom-call | flops 1358954496 | bytes 1179648 | tf_op jit(solution)/shard_map/pallas_call | solution.py:117
  39.7 1.1 %copy.196 = f32[256,2,128]{0,2,1:T(8,128)S(1)} copy(f32[256,2,128]{2,0,1:T(8,128)} %bitcast.134) | data formatting | bytes 524288 | tf_op jit(solution)/shard_map/transpose | solution.py:128
  42.0 0.9 fusion.44
  43.0 1.3 %collective-permute-start.7 = (bf16[3,1,256,128]{3,2,1,0:T(8,128)(2,1)S(1)}, bf16[3,1,256,128]{3,2,1,0:T(8,128)(2,1)S(1)}, u32[]{:S(2)}, u32[]{:S(2)}) collective-permute-start(bf16[3,1,256,128]{3,2,1,0:T(8,128)(2,1)S(1)} %pad_maximum_fusion.6), channel_id=1, source_target_pairs={{1,0},{2,1},{3,2},{5,4},{6,5},{7,6},{9,8},{10,9},{11,10},{13,12},{... | collective-permute-start | bytes 589832 | tf_op jit(solution)/shard_map/ppermute | solution.py:191
  44.4 3.5 %collective-permute-start.6 = (bf16[3,1,256,128]{3,2,1,0:T(8,128)(2,1)S(1)}, bf16[3,1,256,128]{3,2,1,0:T(8,128)(2,1)S(1)}, u32[]{:S(2)}, u32[]{:S(2)}) collective-permute-start(bf16[3,1,256,128]{3,2,1,0:T(8,128)(2,1)S(1)} %pad_maximum_fusion.5), channel_id=1, source_target_pairs={{0,1},{1,2},{2,3},{4,5},{5,6},{6,7},{8,9},{9,10},{10,11},{12,13},{... | collective-permute-start | bytes 589832 | tf_op jit(solution)/shard_map/ppermute | solution.py:190
  48.2 0.6 collective-permute-done.6.before_ref
  48.8 0.6 copy-done.11
  49.5 5.1 %shard_map.93 = f32[2,256,128]{2,1,0:T(8,128)} custom-call(bf16[1,2,256,128]{3,2,1,0:T(8,128)(2,1)} %bitcast.20.block_ref, bf16[1,2,256,128]{3,2,1,0:T(8,128)(2,1)} %copy-done.5, bf16[1,2,256,128]{3,2,1,0:T(8,128)(2,1)} %copy-done.6, bf16[3,1,256,128]{3,2,1,0:T(8,128)(2,1)} %copy-done.11, bf16[3,1,256,128]{3,2,1,0:T(8,128)(2,1)} %copy-done.10, ...), custom_call_target="tpu_custom_call" | custom-call | flops 905969664 | bytes 4587520 | tf_op jit(solution)/shard_map/pallas_call | solution.py:60
  54.6 1.0 convert_bitcast_fusion
  56.3 4.0 %collective-permute-start.8 = (f32[93184]{0:T(1024)S(1)}, f32[93184]{0:T(1024)S(1)}, u32[]{:S(2)}, u32[]{:S(2)}) collective-permute-start(f32[93184]{0:T(1024)S(1)} %pad_maximum_fusion), channel_id=1, source_target_pairs={{0,1},{1,0},{2,3},{3,2},{4,5},{5,4},{6,7},{7,6},{8,9},{9,8},{10,11... | collective-permute-start | bytes 1118216 | tf_op jit(solution)/shard_map/ppermute | solution.py:152
  60.7 0.9 collective-permute-done.8
  61.7 2.8 %collective-permute-start.9 = (f32[46592]{0:T(1024)S(1)}, f32[46592]{0:T(1024)S(1)}, u32[]{:S(2)}, u32[]{:S(2)}) collective-permute-start(f32[46592]{0:T(1024)S(1)} %pad_maximum_fusion.7), channel_id=1, source_target_pairs={{0,2},{1,3},{2,0},{3,1},{4,6},{5,7},{6,4},{7,5},{8,10},{9,11},{10,... | collective-permute-start | bytes 559112 | tf_op jit(solution)/shard_map/ppermute | solution.py:152
  64.5 5.0 %collective-permute-done.9 = f32[46592]{0:T(1024)S(1)} collective-permute-done((f32[46592]{0:T(1024)S(1)}, f32[46592]{0:T(1024)S(1)}, u32[]{:S(2)}, u32[]{:S(2)}) %collective-permute-start.9) | collective-permute-done | bytes 186400 | tf_op jit(solution)/shard_map/ppermute | solution.py:152
  69.7 2.7 %collective-permute-start.10 = (f32[23296]{0:T(1024)S(1)}, f32[23296]{0:T(1024)S(1)}, u32[]{:S(2)}, u32[]{:S(2)}) collective-permute-start(f32[23296]{0:T(1024)S(1)} %pad_maximum_fusion.13), channel_id=1, source_target_pairs={{0,4},{4,0},{8,12},{12,8},{1,5},{5,1},{9,13},{13,9},{2,6},{6,2},{1... | collective-permute-start | bytes 279560 | tf_op jit(solution)/shard_map/ppermute | solution.py:152
  72.4 2.6 %collective-permute-done.10 = f32[23296]{0:T(1024)S(1)} collective-permute-done((f32[23296]{0:T(1024)S(1)}, f32[23296]{0:T(1024)S(1)}, u32[]{:S(2)}, u32[]{:S(2)}) %collective-permute-start.10) | collective-permute-done | bytes 93216 | tf_op jit(solution)/shard_map/ppermute | solution.py:152
  75.0 3.1 %collective-permute-start.11 = (f32[11648]{0:T(1024)S(1)}, f32[11648]{0:T(1024)S(1)}, u32[]{:S(2)}, u32[]{:S(2)}) collective-permute-start(f32[11648]{0:T(1024)S(1)} %pad_maximum_fusion.17), channel_id=1, source_target_pairs={{0,8},{4,12},{8,0},{12,4},{1,9},{5,13},{9,1},{13,5},{2,10},{6,14},... | collective-permute-start | bytes 139784 | tf_op jit(solution)/shard_map/ppermute | solution.py:152
  78.1 0.8 copy.222
  78.9 1.3 %collective-permute-done.11 = f32[11648]{0:T(1024)S(1)} collective-permute-done((f32[11648]{0:T(1024)S(1)}, f32[11648]{0:T(1024)S(1)}, u32[]{:S(2)}, u32[]{:S(2)}) %collective-permute-start.11) | collective-permute-done | bytes 46624 | tf_op jit(solution)/shard_map/ppermute | solution.py:152
  80.2 3.0 %collective-permute-start.12 = (f32[8192]{0:T(1024)S(1)}, f32[8192]{0:T(1024)S(1)}, u32[]{:S(2)}, u32[]{:S(2)}) collective-permute-start(f32[8192]{0:T(1024)S(1)} %pad_maximum_fusion.18), channel_id=1, source_target_pairs={{0,8},{4,12},{8,0},{12,4},{1,9},{5,13},{9,1},{13,5},{2,10},{6,14},... | collective-permute-start | bytes 98312 | tf_op jit(solution)/shard_map/ppermute | solution.py:163
  83.4 0.8 copy.223
  84.2 1.0 collective-permute-done.12
  85.4 1.9 %collective-permute-start.13 = (f32[16384]{0:T(1024)S(1)}, f32[16384]{0:T(1024)S(1)}, u32[]{:S(2)}, u32[]{:S(2)}) collective-permute-start(f32[16384]{0:T(1024)S(1)} %pad_maximum_fusion.14), channel_id=1, source_target_pairs={{0,4},{4,0},{8,12},{12,8},{1,5},{5,1},{9,13},{13,9},{2,6},{6,2},{1... | collective-permute-start | bytes 196616 | tf_op jit(solution)/shard_map/ppermute | solution.py:163
  87.4 2.3 %collective-permute-done.13 = f32[16384]{0:T(1024)S(1)} collective-permute-done((f32[16384]{0:T(1024)S(1)}, f32[16384]{0:T(1024)S(1)}, u32[]{:S(2)}, u32[]{:S(2)}) %collective-permute-start.13) | collective-permute-done | bytes 65568 | tf_op jit(solution)/shard_map/ppermute | solution.py:163
  89.9 1.8 %collective-permute-start.14 = (f32[36224]{0:T(1024)S(1)}, f32[36224]{0:T(1024)S(1)}, u32[]{:S(2)}, u32[]{:S(2)}) collective-permute-start(f32[36224]{0:T(1024)S(1)} %get-tuple-element.39), channel_id=1, source_target_pairs={{0,2},{1,3},{2,0},{3,1},{4,6},{5,7},{6,4},{7,5},{8,10},{9,11},{10,... | collective-permute-start | bytes 434696 | tf_op jit(solution)/shard_map/ppermute | solution.py:163
  91.9 3.2 %collective-permute-done.14 = f32[36224]{0:T(1024)S(1)} collective-permute-done((f32[36224]{0:T(1024)S(1)}, f32[36224]{0:T(1024)S(1)}, u32[]{:S(2)}, u32[]{:S(2)}) %collective-permute-start.14) | collective-permute-done | bytes 144928 | tf_op jit(solution)/shard_map/ppermute | solution.py:163
  96.1 0.9 collective-permute-done.15
  97.3 0.8 copy.225
  98.5 0.3 copy.212
  98.8 0.3 copy.213
  99.3 0.8 copy.224
  100.1 0.7 pad_maximum_fusion.12
  (150 shorter events, 6.6 us)
Async XLA Ops:
  0.6 11.2 %copy-start = (bf16[256,256]{1,0:T(8,128)(2,1)S(1)}, bf16[256,256]{1,0:T(8,128)(2,1)}, u32[]{:S(2)}) copy-start(bf16[256,256]{1,0:T(8,128)(2,1)} %param.7) | copy-start | bytes 393220
  0.6 11.6 %copy-start.12 = (bf16[256,1,2,128]{3,2,1,0:T(2,128)(2,1)S(1)}, bf16[256,1,2,128]{3,2,1,0:T(2,128)(2,1)}, u32[]{:S(2)}) copy-start(bf16[256,1,2,128]{3,2,1,0:T(2,128)(2,1)} %param.6) | copy-start | bytes 393220
  0.7 11.7 %collective-permute-start = (bf16[256,1,2,128]{3,2,1,0:T(2,128)(2,1)}, bf16[256,1,2,128]{3,2,1,0:T(2,128)(2,1)S(1)}, u32[]{:S(2)}, u32[]{:S(2)}) collective-permute-start(bf16[256,1,2,128]{3,2,1,0:T(2,128)(2,1)} %param.5), channel_id=1, source_target_pairs={{0,4},{4,8},{8,12},{1,5},{5,9},{9,13},{2,6},{6,10},{10,14},{3,7},{... | collective-permute-start | bytes 393224 | tf_op jit(solution)/shard_map/ppermute | solution.py:248
  5.7 7.1 %collective-permute-start.1 = (bf16[256,1,2,128]{3,2,1,0:T(2,128)(2,1)}, bf16[256,1,2,128]{3,2,1,0:T(2,128)(2,1)S(1)}, u32[]{:S(2)}, u32[]{:S(2)}) collective-permute-start(bf16[256,1,2,128]{3,2,1,0:T(2,128)(2,1)} %param.5), channel_id=1, source_target_pairs={{4,0},{8,4},{12,8},{5,1},{9,5},{13,9},{6,2},{10,6},{14,10},{7,3},{... | collective-permute-start | bytes 393224 | tf_op jit(solution)/shard_map/ppermute | solution.py:248
  11.9 6.0 %copy-start.7 = (bf16[256,8,3,3,3]{0,1,4,3,2:T(8,128)(2,1)S(1)}, bf16[256,8,3,3,3]{0,1,4,3,2:T(8,128)(2,1)}, u32[]{:S(2)}) copy-start(bf16[256,8,3,3,3]{0,1,4,3,2:T(8,128)(2,1)} %param.8) | copy-start | bytes 331780
  12.2 8.5 %copy-start.3 = (bf16[256,1,2,128]{3,0,2,1:T(8,128)(2,1)}, bf16[256,1,2,128]{3,0,2,1:T(8,128)(2,1)S(1)}, u32[]{:S(2)}) copy-start(bf16[256,1,2,128]{3,0,2,1:T(8,128)(2,1)S(1)} %copy.184) | copy-start | bytes 393220
  12.8 8.0 %copy-start.4 = (bf16[256,1,2,128]{3,0,2,1:T(8,128)(2,1)}, bf16[256,1,2,128]{3,0,2,1:T(8,128)(2,1)S(1)}, u32[]{:S(2)}) copy-start(bf16[256,1,2,128]{3,0,2,1:T(8,128)(2,1)S(1)} %copy.185) | copy-start | bytes 393220
  13.2 7.6 %copy-start.2 = (bf16[256,1,2,128]{3,0,2,1:T(8,128)(2,1)}, bf16[256,1,2,128]{3,0,2,1:T(8,128)(2,1)S(1)}, u32[]{:S(2)}) copy-start(bf16[256,1,2,128]{3,0,2,1:T(8,128)(2,1)S(1)} %copy.186) | copy-start | bytes 393220
  13.3 7.4 %collective-permute-start.3 = (bf16[3,1,256,128]{3,2,1,0:T(8,128)(2,1)S(1)}, bf16[3,1,256,128]{3,2,1,0:T(8,128)(2,1)S(1)}, u32[]{:S(2)}, u32[]{:S(2)}) collective-permute-start(bf16[3,1,256,128]{3,2,1,0:T(8,128)(2,1)S(1)} %pad_maximum_fusion.4), channel_id=1, source_target_pairs={{1,0},{2,1},{3,2},{5,4},{6,5},{7,6},{9,8},{10,9},{11,10},{13,12},{... | collective-permute-start | bytes 589832 | tf_op jit(solution)/shard_map/ppermute | solution.py:191
  14.6 13.2 %copy-start.13 = (bf16[256,256]{1,0:T(8,128)(2,1)S(1)}, bf16[256,256]{1,0:T(8,128)(2,1)}, u32[]{:S(2)}) copy-start(bf16[256,256]{1,0:T(8,128)(2,1)} %param.9) | copy-start | bytes 393220
  14.6 6.1 %collective-permute-start.2 = (bf16[3,1,256,128]{3,2,1,0:T(8,128)(2,1)S(1)}, bf16[3,1,256,128]{3,2,1,0:T(8,128)(2,1)S(1)}, u32[]{:S(2)}, u32[]{:S(2)}) collective-permute-start(bf16[3,1,256,128]{3,2,1,0:T(8,128)(2,1)S(1)} %pad_maximum_fusion.3), channel_id=1, source_target_pairs={{0,1},{1,2},{2,3},{4,5},{5,6},{6,7},{8,9},{9,10},{10,11},{12,13},{... | collective-permute-start | bytes 589832 | tf_op jit(solution)/shard_map/ppermute | solution.py:190
  20.7 0.7 copy-start.8
  20.7 0.7 copy-start.9
  26.6 1.9 %copy-start.1 = (f32[2,256,128]{2,1,0:T(8,128)S(1)}, f32[2,256,128]{2,1,0:T(8,128)}, u32[]{:S(2)}) copy-start(f32[2,256,128]{2,1,0:T(8,128)} %shard_map.92) | copy-start | bytes 786436
  29.2 13.7 %collective-permute-start.4 = (bf16[1,2,256,128]{3,2,1,0:T(8,128)(2,1)}, bf16[1,2,256,128]{3,2,1,0:T(8,128)(2,1)S(1)}, u32[]{:S(2)}, u32[]{:S(2)}) collective-permute-start(bf16[1,2,256,128]{3,2,1,0:T(8,128)(2,1)} %bitcast.20.block_ref), channel_id=1, source_target_pairs={{0,4},{4,8},{8,12},{1,5},{5,9},{9,13},{2,6},{6,10},{10,14},{3,7},{... | collective-permute-start | bytes 393224 | tf_op jit(solution)/shard_map/ppermute | solution.py:181
  33.8 9.2 %collective-permute-start.5 = (bf16[1,2,256,128]{3,2,1,0:T(8,128)(2,1)}, bf16[1,2,256,128]{3,2,1,0:T(8,128)(2,1)S(1)}, u32[]{:S(2)}, u32[]{:S(2)}) collective-permute-start(bf16[1,2,256,128]{3,2,1,0:T(8,128)(2,1)} %bitcast.20.block_ref), channel_id=1, source_target_pairs={{4,0},{8,4},{12,8},{5,1},{9,5},{13,9},{6,2},{10,6},{14,10},{7,3},{... | collective-permute-start | bytes 393224 | tf_op jit(solution)/shard_map/ppermute | solution.py:182
  42.9 5.9 %copy-start.5 = (bf16[1,2,256,128]{3,2,1,0:T(8,128)(2,1)}, bf16[1,2,256,128]{3,2,1,0:T(8,128)(2,1)S(1)}, u32[]{:S(2)}) copy-start(bf16[1,2,256,128]{3,2,1,0:T(8,128)(2,1)S(1)} %collective-permute-done.4.below_ref) | copy-start | bytes 393220
  43.0 5.8 %copy-start.6 = (bf16[1,2,256,128]{3,2,1,0:T(8,128)(2,1)}, bf16[1,2,256,128]{3,2,1,0:T(8,128)(2,1)S(1)}, u32[]{:S(2)}) copy-start(bf16[1,2,256,128]{3,2,1,0:T(8,128)(2,1)S(1)} %collective-permute-done.5.above_ref) | copy-start | bytes 393220
  43.0 5.1 %collective-permute-start.7 = (bf16[3,1,256,128]{3,2,1,0:T(8,128)(2,1)S(1)}, bf16[3,1,256,128]{3,2,1,0:T(8,128)(2,1)S(1)}, u32[]{:S(2)}, u32[]{:S(2)}) collective-permute-start(bf16[3,1,256,128]{3,2,1,0:T(8,128)(2,1)S(1)} %pad_maximum_fusion.6), channel_id=1, source_target_pairs={{1,0},{2,1},{3,2},{5,4},{6,5},{7,6},{9,8},{10,9},{11,10},{13,12},{... | collective-permute-start | bytes 589832 | tf_op jit(solution)/shard_map/ppermute | solution.py:191
  44.4 4.4 %collective-permute-start.6 = (bf16[3,1,256,128]{3,2,1,0:T(8,128)(2,1)S(1)}, bf16[3,1,256,128]{3,2,1,0:T(8,128)(2,1)S(1)}, u32[]{:S(2)}, u32[]{:S(2)}) collective-permute-start(bf16[3,1,256,128]{3,2,1,0:T(8,128)(2,1)S(1)} %pad_maximum_fusion.5), channel_id=1, source_target_pairs={{0,1},{1,2},{2,3},{4,5},{5,6},{6,7},{8,9},{9,10},{10,11},{12,13},{... | collective-permute-start | bytes 589832 | tf_op jit(solution)/shard_map/ppermute | solution.py:190
  48.1 0.7 copy-start.10
  48.8 0.7 copy-start.11
  56.3 5.3 %collective-permute-start.8 = (f32[93184]{0:T(1024)S(1)}, f32[93184]{0:T(1024)S(1)}, u32[]{:S(2)}, u32[]{:S(2)}) collective-permute-start(f32[93184]{0:T(1024)S(1)} %pad_maximum_fusion), channel_id=1, source_target_pairs={{0,1},{1,0},{2,3},{3,2},{4,5},{5,4},{6,7},{7,6},{8,9},{9,8},{10,11... | collective-permute-start | bytes 1118216 | tf_op jit(solution)/shard_map/ppermute | solution.py:152
  61.7 7.8 %collective-permute-start.9 = (f32[46592]{0:T(1024)S(1)}, f32[46592]{0:T(1024)S(1)}, u32[]{:S(2)}, u32[]{:S(2)}) collective-permute-start(f32[46592]{0:T(1024)S(1)} %pad_maximum_fusion.7), channel_id=1, source_target_pairs={{0,2},{1,3},{2,0},{3,1},{4,6},{5,7},{6,4},{7,5},{8,10},{9,11},{10,... | collective-permute-start | bytes 559112 | tf_op jit(solution)/shard_map/ppermute | solution.py:152
  69.7 5.3 %collective-permute-start.10 = (f32[23296]{0:T(1024)S(1)}, f32[23296]{0:T(1024)S(1)}, u32[]{:S(2)}, u32[]{:S(2)}) collective-permute-start(f32[23296]{0:T(1024)S(1)} %pad_maximum_fusion.13), channel_id=1, source_target_pairs={{0,4},{4,0},{8,12},{12,8},{1,5},{5,1},{9,13},{13,9},{2,6},{6,2},{1... | collective-permute-start | bytes 279560 | tf_op jit(solution)/shard_map/ppermute | solution.py:152
  75.0 5.2 %collective-permute-start.11 = (f32[11648]{0:T(1024)S(1)}, f32[11648]{0:T(1024)S(1)}, u32[]{:S(2)}, u32[]{:S(2)}) collective-permute-start(f32[11648]{0:T(1024)S(1)} %pad_maximum_fusion.17), channel_id=1, source_target_pairs={{0,8},{4,12},{8,0},{12,4},{1,9},{5,13},{9,1},{13,5},{2,10},{6,14},... | collective-permute-start | bytes 139784 | tf_op jit(solution)/shard_map/ppermute | solution.py:152
  80.2 5.0 %collective-permute-start.12 = (f32[8192]{0:T(1024)S(1)}, f32[8192]{0:T(1024)S(1)}, u32[]{:S(2)}, u32[]{:S(2)}) collective-permute-start(f32[8192]{0:T(1024)S(1)} %pad_maximum_fusion.18), channel_id=1, source_target_pairs={{0,8},{4,12},{8,0},{12,4},{1,9},{5,13},{9,1},{13,5},{2,10},{6,14},... | collective-permute-start | bytes 98312 | tf_op jit(solution)/shard_map/ppermute | solution.py:163
  85.4 4.3 %collective-permute-start.13 = (f32[16384]{0:T(1024)S(1)}, f32[16384]{0:T(1024)S(1)}, u32[]{:S(2)}, u32[]{:S(2)}) collective-permute-start(f32[16384]{0:T(1024)S(1)} %pad_maximum_fusion.14), channel_id=1, source_target_pairs={{0,4},{4,0},{8,12},{12,8},{1,5},{5,1},{9,13},{13,9},{2,6},{6,2},{1... | collective-permute-start | bytes 196616 | tf_op jit(solution)/shard_map/ppermute | solution.py:163
  89.9 5.2 %collective-permute-start.14 = (f32[36224]{0:T(1024)S(1)}, f32[36224]{0:T(1024)S(1)}, u32[]{:S(2)}, u32[]{:S(2)}) collective-permute-start(f32[36224]{0:T(1024)S(1)} %get-tuple-element.39), channel_id=1, source_target_pairs={{0,2},{1,3},{2,0},{3,1},{4,6},{5,7},{6,4},{7,5},{8,10},{9,11},{10,... | collective-permute-start | bytes 434696 | tf_op jit(solution)/shard_map/ppermute | solution.py:163
  95.4 1.6 %collective-permute-start.15 = (f32[72448]{0:T(1024)S(1)}, f32[72448]{0:T(1024)S(1)}, u32[]{:S(2)}, u32[]{:S(2)}) collective-permute-start(f32[72448]{0:T(1024)S(1)} %get-tuple-element.35), channel_id=1, source_target_pairs={{0,1},{1,0},{2,3},{3,2},{4,5},{5,4},{6,7},{7,6},{8,9},{9,8},{10,11... | collective-permute-start | bytes 869384 | tf_op jit(solution)/shard_map/ppermute | solution.py:163
